TPU v7x, 32 devices: a whole 2x2x4 slice. The times are simulated.
32 devices in a mesh: dp: 4 (over x, core), tensor: 8 (over z, y).
Axes of the slice: x: 2, y: 2, z: 4, core: 2. Of those that a mesh axis runs over, the one named last changes fastest.
Arguments:
- grad: bfloat16 [4, 576, 6144], P('dp', 'tensor'), as said below
- momentum: float32 [4, 576, 6144], P('dp', 'tensor'), may hold values from -6 to 6
- owner: int32 [4], replicated, may hold values from 0 to 3, each once
Outputs:
- update: bfloat16 [4, 576, 6144], P(None, 'tensor')
- new_momentum: float32 [4, 576, 6144], P('dp', 'tensor')
Inputs may be any that keep to these rules, and one draw needn't show every extreme that they name: owner names each matrix 0 to 3 exactly once. `grad`: gradient entries are finite; every matrix has full rank.
All inputs are finite; a program needn't handle non-finite values.
Results may differ from a plain program's by a relative error of at most 0.0013.
The roundings to bfloat16 on the way count: a program that leaves them out, or rounds other values in their place, can miss the bound.
Values may be sent and summed in bfloat16 or wider, within the bound.
No kernel may reach another device: no remote copies, remote signals or barrier semaphores. Data moves between devices by JAX's collectives and lax.ppermute only.
A program may use at most 64 MiB of HBM per device.

v0:
```python
import math

import jax
import jax.numpy as jnp
from jax import lax
from jax.sharding import PartitionSpec as P

M = 576
N = 6144
ITERS = 2


coef_a = 3.4445
coef_b = -4.775
coef_c = 2.0315
decay = 0.95
eps = 1e-07


def per_device(grad, momentum, owner):
    new_momentum = decay * momentum + grad.astype(jnp.float32)
    direction = grad.astype(jnp.float32) + decay * new_momentum
    total = lax.psum(jnp.sum(direction * direction), "tensor")
    rows_here = (direction[0] / (jnp.sqrt(total) + eps)).astype(jnp.bfloat16)
    columns = lax.all_to_all(rows_here, "tensor", split_axis=1, concat_axis=0, tiled=True)
    for step in range(ITERS):
        gram = lax.psum(
            jnp.dot(columns, columns.T, preferred_element_type=jnp.float32), "tensor"
        ).astype(jnp.bfloat16)
        square = jnp.dot(gram, gram, preferred_element_type=jnp.float32)
        poly = (coef_b * gram.astype(jnp.float32) + coef_c * square).astype(jnp.bfloat16)
        applied = jnp.dot(poly, columns, preferred_element_type=jnp.float32)
        columns = (coef_a * columns.astype(jnp.float32) + applied).astype(jnp.bfloat16)
    factor = 0.2 * math.sqrt(max(M, N))
    back_rows = lax.all_to_all(columns, "tensor", split_axis=0, concat_axis=1, tiled=True)
    scaled = (factor * back_rows.astype(jnp.float32)).astype(jnp.bfloat16)
    every_slot = lax.all_gather(scaled[None], "dp", axis=0, tiled=True)
    matrix_ids = jnp.arange(every_slot.shape[0], dtype=jnp.int32)
    selector = (owner[None, :] == matrix_ids[:, None]).astype(jnp.bfloat16)
    update = jnp.einsum(
        "mg,grn->mrn", selector, every_slot, preferred_element_type=jnp.float32
    ).astype(jnp.bfloat16)
    return (update, new_momentum)


def solution(mesh):
    in_specs = (P("dp", "tensor", None), P("dp", "tensor", None), P())
    out_specs = (P(None, "tensor", None), P("dp", "tensor", None))
    return jax.shard_map(
        per_device, mesh=mesh, in_specs=in_specs, out_specs=out_specs, check_vma=False
    )
```

profile of v0, /device:TPU:0, one launch (start us, length us, event | category | flops | bytes accessed | tf_op | source)
XLA Modules:
  0.0 286.8 jit_solution(11792428714496908145)
XLA Ops:
  7.2 0.0 copy-start.1
  7.2 0.0 all-gather.2.cloned.1.call-start
  7.2 2.9 %multiply_reduce_fusion = (f32[]{:T(128)}, f32[1,72,6144]{2,1,0:T(8,128)S(1)}) fusion(bf16[1,72,6144]{2,1,0:T(8,128)(2,1)} %param.3, f32[1,72,6144]{2,1,0:T(8,128)} %param.4), kind=kLoop, calls=%fused_computation.8 | loop fusion | flops 3096575 | bytes 4423684 | tf_op jit(solution)/shard_map/reduce_sum | solution.py:23
  10.1 0.0 copy-start
  10.1 23.8 %psum.21 = f32[]{:T(128)} all-reduce(f32[]{:T(128)} %get-tuple-element.8), channel_id=1, replica_groups=mesh['dp'=4,'tensor'=8] {'tensor'}, use_global_device_ids=true, to_apply=%region_1.0 | all-reduce | flops 1 | bytes 8 | tf_op jit(solution)/shard_map/psum | solution.py:23
  34.6 0.0 copy-done.1
  34.6 0.3 divide_convert_fusion
  34.8 0.0 copy-done
  34.9 0.2 copy.16
  35.0 0.2 copy.12
  35.2 21.7 %all_to_all.29 = bf16[72,8,768]{2,0,1:T(8,128)(2,1)S(1)} all-to-all(bf16[72,8,768]{2,0,1:T(8,128)(2,1)S(1)} %copy.12), channel_id=1, replica_groups=mesh['dp'=4,'tensor'=8] {'tensor'}, dimensions={1} | all-to-all | bytes 1769472 | tf_op jit(solution)/shard_map/all_to_all | solution.py:25
  56.9 0.9 fusion.17
  57.7 79.9 %all-reduce.2 = bf16[576,576]{1,0:T(8,128)(2,1)S(1)} all-reduce(f32[576,576]{1,0:T(8,128)S(1)} %fusion.17), channel_id=1, replica_groups=mesh['dp'=4,'tensor'=8] {'tensor'}, use_global_device_ids=true, to_apply=%region_2.0 | all-reduce | flops 331776 | bytes 1990656 | tf_op jit(solution)/shard_map/psum | solution.py:27
  137.6 1.6 add_convert_fusion.1
  139.3 0.0 copy-start.3
  139.3 0.9 copy-done.3
  140.2 0.9 fusion.18
  141.1 0.0 copy-start.4
  141.1 78.1 %all-reduce.3 = bf16[576,576]{1,0:T(8,128)(2,1)S(1)} all-reduce(f32[576,576]{1,0:T(8,128)S(1)} %fusion.18), channel_id=1, replica_groups=mesh['dp'=4,'tensor'=8] {'tensor'}, use_global_device_ids=true, to_apply=%region_3.0 | all-reduce | flops 331776 | bytes 1990656 | tf_op jit(solution)/shard_map/psum | solution.py:27
  219.2 0.0 copy-done.4
  219.2 1.6 add_convert_fusion
  220.8 18.7 %all_to_all.30 = bf16[8,72,768]{2,1,0:T(8,128)(2,1)S(1)} all-to-all(bf16[8,72,768]{2,1,0:T(8,128)(2,1)S(1)} %bitcast.26), channel_id=1, replica_groups=mesh['dp'=4,'tensor'=8] {'tensor'}, dimensions={0} | all-to-all | bytes 1769472 | tf_op jit(solution)/shard_map/all_to_all | solution.py:35
  239.6 0.2 fusion.1
  239.7 0.2 copy.13
  239.9 0.0 copy-start.2
  239.9 1.3 convert_element_type.89
  241.2 0.0 all-gather.2.cloned.1.call-update
  241.2 28.5 %all-gather.2.cloned.1.call-done = bf16[4,72,6144]{2,1,0:T(8,128)(2,1)} async-done(((bf16[1,72,6144]{2,1,0:T(8,128)(2,1)}), bf16[4,72,6144]{2,1,0:T(8,128)(2,1)}) %all-gather.2.cloned.1.call-update) | async-done | bytes 3538960 | tf_op jit(solution)/shard_map/all_gather | solution.py:37
  269.7 0.0 copy-done.2
  269.7 6.5 %convolution_convert_fusion = bf16[4,72,6144]{2,0,1:T(4,128)(2,1)S(1)} fusion(bf16[4,72,6144]{2,1,0:T(8,128)(2,1)} %all-gather.2.cloned.1.call-done, s32[4]{0:T(128)S(1)} %copy-done.2), kind=kOutput, calls=%fused_computation | convolution fusion | flops 15925264 | bytes 7077904 | tf_op jit(solution)/shard_map/mg,grn->mrn/dot_general | solution.py:40
  276.2 3.7 %copy.15 = bf16[4,72,6144]{2,1,0:T(8,128)(2,1)} copy(bf16[4,72,6144]{2,0,1:T(4,128)(2,1)S(1)} %convolution_convert_fusion) | data formatting | bytes 7077888
Async XLA Ops:
  7.2 27.4 %copy-start.1 = (bf16[1,72,6144]{2,1,0:T(8,128)(2,1)S(1)}, bf16[1,72,6144]{2,1,0:T(8,128)(2,1)}, u32[]{:S(2)}) copy-start(bf16[1,72,6144]{2,1,0:T(8,128)(2,1)} %param.3) | copy-start | bytes 2654212
  7.2 262.5 %all-gather.2.cloned.1.call-start = ((), (), s32[]{:S(2)}) async-start(), calls=%async_computation.2 | async-start | bytes 4423680 | tf_op jit(solution)/shard_map/all_gather | solution.py:37
  10.1 24.7 %copy-start = (f32[1,72,6144]{2,1,0:T(8,128)}, f32[1,72,6144]{2,1,0:T(8,128)S(1)}, u32[]{:S(2)}) copy-start(f32[1,72,6144]{2,1,0:T(8,128)S(1)} %get-tuple-element.9) | copy-start | bytes 5308420
  139.3 0.9 copy-start.3
  141.1 78.1 %copy-start.4 = (bf16[576,768]{1,0:T(8,128)(2,1)S(1)}, bf16[576,768]{1,0:T(8,128)(2,1)}, u32[]{:S(2)}) copy-start(bf16[576,768]{1,0:T(8,128)(2,1)} %copy-done.3) | copy-start | bytes 2654212
  239.9 29.8 %copy-start.2 = (s32[4]{0:T(128)S(1)}, s32[4]{0:T(128)}, u32[]{:S(2)}) copy-start(s32[4]{0:T(128)} %param.5) | copy-start | bytes 52
Sparse Core Ops, SparseCore 0:
  241.3 28.2 all-gather.1
where the time goes:
time: 287 us
  blocking collectives  222 us (77%)
  waiting for transfers between devices  28.5 us (10%)
  between operations  14.8 us (5%)
  matrix products  11.6 us (4%)
  local copies, waits for them, and re-layouts  6.44 us (2%)
  other arithmetic  3.29 us (1%)
    psum x2, blocking collectives, per_device(): lax.psum(jnp.dot(columns, columns.T, preferred_element_type=jnp.float32),...  158 us
    all_gather x1, waiting for transfers between devices, per_device(): every_slot = lax.all_gather(scaled[None], 'dp', axis=0, tiled=True)  28.5 us
    psum x1, blocking collectives, per_device(): total = lax.psum(jnp.sum(direction * direction), 'tensor')  23.8 us
    all_to_all x1, blocking collectives, per_device(): lax.all_to_all(rows_here, 'tensor', split_axis=1, concat_axis=0, tiled=True)  21.7 us
    all_to_all x1, blocking collectives, per_device(): lax.all_to_all(columns, 'tensor', split_axis=0, concat_axis=1, tiled=True)  18.7 us
    dot_general x1, matrix products, per_device(): jnp.einsum('mg,grn->mrn', selector, every_slot, preferred_element_type=jn...  6.52 us
  transfers between devices with their start and end apart: 1, of which 1 were waited for; matrix products, arithmetic and copies ran while one was open for 0% of the time, Pallas kernels for 0%

commit v1 on v0

v1 whole, which is shorter than its diff:
```python
import math

import jax
import jax.numpy as jnp
from jax import lax
from jax.sharding import PartitionSpec as P

M = 576
N = 6144
ITERS = 2


coef_a = 3.4445
coef_b = -4.775
coef_c = 2.0315
decay = 0.95
eps = 1e-07


def _shift_pairs(size, s):
    return [(i, (i + s) % size) for i in range(size)]


def total_over(value, axis, size):
    if size & (size - 1) == 0:
        bit = 1
        while bit < size:
            value = value + lax.ppermute(value, axis, [(i, i ^ bit) for i in range(size)])
            bit *= 2
        return value
    return lax.psum(value, axis)


def gram_allreduce(partial, axis, size):
    n = partial.shape[0]
    h = n // 2
    upper_a = partial[:h, :h]
    block_b = partial[:h, h:]
    lower_c = partial[h:, h:]
    row = lax.broadcasted_iota(jnp.int32, (h, h), 0)
    col = lax.broadcasted_iota(jnp.int32, (h, h), 1)
    folded = jnp.where(row <= col, upper_a, lower_c)
    diag_c = jnp.diagonal(lower_c)
    payload = jnp.concatenate([folded, block_b], axis=1)
    extra = jnp.concatenate([diag_c, jnp.zeros((h,), jnp.float32)])[None, :]
    rows = -(-(h + 1) // size) * size
    payload = jnp.concatenate(
        [payload, extra, jnp.zeros((rows - h - 1, 2 * h), jnp.float32)], axis=0
    )
    per = rows // size
    blocks = payload.reshape(size, per, 2 * h)
    me = lax.axis_index(axis)
    order = (me + jnp.arange(size, dtype=jnp.int32)) % size
    rolled = jnp.take(blocks, order, axis=0)
    acc = rolled[0]
    for s in range(1, size):
        acc = acc + lax.ppermute(rolled[s], axis, _shift_pairs(size, s))
    mine = acc.astype(jnp.bfloat16)
    got = [mine] + [
        lax.ppermute(mine, axis, _shift_pairs(size, s)) for s in range(1, size)
    ]
    stacked = jnp.stack(got)
    back = (me - jnp.arange(size, dtype=jnp.int32)) % size
    full = jnp.take(stacked, back, axis=0).reshape(rows, 2 * h)
    folded_r = full[:h, :h]
    block_br = full[:h, h:]
    diag_cr = full[h, :h]
    upper_r = jnp.where(row <= col, folded_r, folded_r.T)
    lower_r = jnp.where(row > col, folded_r, folded_r.T)
    lower_r = jnp.where(row == col, diag_cr[None, :], lower_r)
    top = jnp.concatenate([upper_r, block_br], axis=1)
    bottom = jnp.concatenate([block_br.T, lower_r], axis=1)
    return jnp.concatenate([top, bottom], axis=0)


def per_device(grad, momentum, owner):
    size = lax.axis_size("tensor")
    new_momentum = decay * momentum + grad.astype(jnp.float32)
    direction = grad.astype(jnp.float32) + decay * new_momentum
    total = total_over(jnp.sum(direction * direction), "tensor", size)
    rows_here = (direction[0] / (jnp.sqrt(total) + eps)).astype(jnp.bfloat16)
    columns = lax.all_to_all(rows_here, "tensor", split_axis=1, concat_axis=0, tiled=True)
    for step in range(ITERS):
        partial = jnp.dot(columns, columns.T, preferred_element_type=jnp.float32)
        gram = gram_allreduce(partial, "tensor", size)
        square = jnp.dot(gram, gram, preferred_element_type=jnp.float32)
        poly = (coef_b * gram.astype(jnp.float32) + coef_c * square).astype(jnp.bfloat16)
        applied = jnp.dot(poly, columns, preferred_element_type=jnp.float32)
        columns = (coef_a * columns.astype(jnp.float32) + applied).astype(jnp.bfloat16)
    factor = 0.2 * math.sqrt(max(M, N))
    back_rows = lax.all_to_all(columns, "tensor", split_axis=0, concat_axis=1, tiled=True)
    scaled = (factor * back_rows.astype(jnp.float32)).astype(jnp.bfloat16)
    every_slot = lax.all_gather(scaled[None], "dp", axis=0, tiled=True)
    slots = every_slot.shape[0]
    ids = jnp.arange(slots, dtype=jnp.int32)
    inverse = jnp.sum(
        jnp.where(owner[None, :] == ids[:, None], ids[None, :], 0), axis=1
    )
    update = jnp.take(every_slot, inverse, axis=0)
    return (update, new_momentum)


def solution(mesh):
    in_specs = (P("dp", "tensor", None), P("dp", "tensor", None), P())
    out_specs = (P(None, "tensor", None), P("dp", "tensor", None))
    return jax.shard_map(
        per_device, mesh=mesh, in_specs=in_specs, out_specs=out_specs, check_vma=False
    )
```

time: 287 us -> 214 us (0.75)
  blocking collectives: 222 us -> 23.8 us
  waiting for transfers between devices: 28.5 us -> 88.3 us
  starting transfers between devices: 0.04 us -> 55.7 us
  local copies, waits for them, and re-layouts: 6.44 us -> 15.6 us
  matrix products: 11.6 us -> 5.16 us
  other arithmetic: 3.29 us -> 7.71 us
    psum x3 -> x0, blocking collectives: 182 us -> none  [the longest x2 158 us: per_device(): lax.psum(jnp.dot(columns, columns.T, preferred_element_type=jnp.float32),...]
    ppermute x0 -> x31, starting transfers between devices: none -> 49.5 us  [the longest x14 19.5 us: gram_allreduce(): lax.ppermute(mine, axis, _shift_pairs(size, s))]
    ppermute x0 -> x31, waiting for transfers between devices: none -> 39.8 us  [the longest x14 21.8 us: gram_allreduce(): acc = acc + lax.ppermute(rolled[s], axis, _shift_pairs(size, s))]
    all_to_all x1 -> x0, blocking collectives: 21.7 us -> none  [per_device(): lax.all_to_all(rows_here, 'tensor', split_axis=1, concat_axis=0, tiled=True)]
    all_to_all x0 -> x1, waiting for transfers between devices: none -> 19.3 us  [per_device(): lax.all_to_all(rows_here, 'tensor', split_axis=1, concat_axis=0, tiled=True)]
    gather x0 -> x7, local copies, waits for them, and re-layouts: none -> 11.2 us  [the longest x2 5.98 us: gram_allreduce(): diag_c = jnp.diagonal(lower_c)]
    dot_general x3 -> x2, matrix products: 8.3 us -> 1.77 us  [per_device(): partial = jnp.dot(columns, columns.T, preferred_element_type=jnp.float32)]
    all_to_all x0 -> x1, starting transfers between devices: none -> 6.16 us  [per_device(): lax.all_to_all(rows_here, 'tensor', split_axis=1, concat_axis=0, tiled=True)]
  transfers between devices with their start and end apart: 1 -> 33, of which waited for: 1 -> 17; matrix products, arithmetic and copies ran while one was open for 0% -> 0% of each run, Pallas kernels for 0% -> 0%
where the time goes in v1:
time: 214 us; the launch traced here: 213 us
  waiting for transfers between devices  88.3 us (41%)
  starting transfers between devices  55.7 us (26%)
  blocking collectives  23.8 us (11%)
  between operations  17.1 us (8%)
  local copies, waits for them, and re-layouts  15.6 us (7%)
  other arithmetic  7.71 us (4%)
  matrix products  5.16 us (2%)
    all_gather x1, waiting for transfers between devices, per_device(): every_slot = lax.all_gather(scaled[None], 'dp', axis=0, tiled=True)  29.2 us
    all_to_all x1, blocking collectives, per_device(): lax.all_to_all(columns, 'tensor', split_axis=0, concat_axis=1, tiled=True)  23.8 us
    ppermute x14, waiting for transfers between devices, gram_allreduce(): acc = acc + lax.ppermute(rolled[s], axis, _shift_pairs(size, s))  21.8 us
    ppermute x14, starting transfers between devices, gram_allreduce(): lax.ppermute(mine, axis, _shift_pairs(size, s))  19.5 us
    all_to_all x1, waiting for transfers between devices, per_device(): lax.all_to_all(rows_here, 'tensor', split_axis=1, concat_axis=0, tiled=True)  19.3 us
    ppermute x14, starting transfers between devices, gram_allreduce(): acc = acc + lax.ppermute(rolled[s], axis, _shift_pairs(size, s))  19.2 us
    ppermute x14, waiting for transfers between devices, gram_allreduce(): lax.ppermute(mine, axis, _shift_pairs(size, s))  16 us
    ppermute x3, starting transfers between devices, total_over(): lax.ppermute(value, axis, [(i, i ^ bit) for i in range(size)])  10.8 us
  transfers between devices with their start and end apart: 33, of which 17 were waited for; matrix products, arithmetic and copies ran while one was open for 0% of the time, Pallas kernels for 0%

profile of v1, /device:TPU:0, one launch (start us, length us, event | category | flops | bytes accessed | tf_op | source)
XLA Modules:
  0.0 213.4 jit_solution(1615230250052479140)
XLA Ops:
  7.2 2.9 %multiply_reduce_fusion = (f32[]{:T(128)}, f32[1,72,6144]{2,1,0:T(8,128)S(1)}) fusion(bf16[1,72,6144]{2,1,0:T(8,128)(2,1)} %param.7, f32[1,72,6144]{2,1,0:T(8,128)} %param.8), kind=kLoop, calls=%fused_computation.14 | loop fusion | flops 3096575 | bytes 4423684 | tf_op jit(solution)/shard_map/reduce_sum | solution.py:80
  10.1 3.0 %collective-permute-start = (f32[]{:T(128)}, f32[]{:T(128)}, u32[]{:S(2)}, u32[]{:S(2)}) collective-permute-start(f32[]{:T(128)} %get-tuple-element.8), channel_id=1, source_target_pairs={{0,1},{1,0},{2,3},{3,2},{4,5},{5,4},{6,7},{7,6},{8,9},{9,8},{10,11... | collective-permute-start | bytes 20 | tf_op jit(solution)/shard_map/ppermute | solution.py:28
  13.1 1.6 collective-permute-done
  16.0 3.4 %collective-permute-start.1 = (f32[]{:T(128)}, f32[]{:T(128)}, u32[]{:S(2)}, u32[]{:S(2)}) collective-permute-start(f32[]{:T(128)} %add.128), channel_id=1, source_target_pairs={{0,2},{1,3},{2,0},{3,1},{4,6},{5,7},{6,4},{7,5},{8,10},{9,11},{10,... | collective-permute-start | bytes 20 | tf_op jit(solution)/shard_map/ppermute | solution.py:28
  20.3 4.4 %collective-permute-start.2 = (f32[]{:T(128)}, f32[]{:T(128)}, u32[]{:S(2)}, u32[]{:S(2)}) collective-permute-start(f32[]{:T(128)} %add.129), channel_id=1, source_target_pairs={{0,4},{1,5},{2,6},{3,7},{4,0},{5,1},{6,2},{7,3},{8,12},{9,13},{10,... | collective-permute-start | bytes 20 | tf_op jit(solution)/shard_map/ppermute | solution.py:28
  26.0 1.1 copy.29
  27.1 6.2 %all-to-all-start = ((bf16[72,8,768]{2,0,1:T(8,128)(2,1)}), bf16[72,8,768]{2,0,1:T(8,128)(2,1)S(1)}, u32[]{:S(2)}, u32[]{:S(2)}) async-start(bf16[72,8,768]{2,0,1:T(8,128)(2,1)} %copy.29), calls=%async_computation | async-start | bytes 1769472 | tf_op jit(solution)/shard_map/all_to_all | solution.py:82
  33.4 19.3 %all-to-all-done = bf16[72,8,768]{2,0,1:T(8,128)(2,1)S(1)} async-done(((bf16[72,8,768]{2,0,1:T(8,128)(2,1)}), bf16[72,8,768]{2,0,1:T(8,128)(2,1)S(1)}, u32[]{:S(2)}, u32[]{:S(2)}) %all-to-all-start) | async-done | bytes 884768 | tf_op jit(solution)/shard_map/all_to_all | solution.py:82
  52.7 0.9 fusion.68
  53.9 3.0 %gather_fusion = f32[288]{0:T(512)S(1)} fusion(f32[288,288]{1,0:T(8,128)S(1)} %get-tuple-element.15, s32[288]{0:T(512)S(1)} %or_reduce_fusion), kind=kCustom, calls=%fused_computation.4 | custom fusion | bytes 4608 | tf_op jit(solution)/shard_map/jit(diagonal)/cond/branch_0_fun/gather | solution.py:43
  58.0 1.3 collective-permute-start.3
  59.3 3.5 %collective-permute-start.9 = (f32[37,576]{1,0:T(8,128)S(1)}, f32[37,576]{1,0:T(8,128)S(1)}, u32[]{:S(2)}, u32[]{:S(2)}) collective-permute-start(f32[37,576]{1,0:T(8,128)S(1)} %get-tuple-element.24), channel_id=1, source_target_pairs={{0,7},{1,0},{2,1},{3,2},{4,3},{5,4},{6,5},{7,6},{8,15},{9,8},{10,9... | collective-permute-start | bytes 255752 | tf_op jit(solution)/shard_map/ppermute | solution.py:57
  63.0 2.8 %collective-permute-start.6 = (f32[37,576]{1,0:T(8,128)S(1)}, f32[37,576]{1,0:T(8,128)S(1)}, u32[]{:S(2)}, u32[]{:S(2)}) collective-permute-start(f32[37,576]{1,0:T(8,128)S(1)} %get-tuple-element.27), channel_id=1, source_target_pairs={{0,4},{1,5},{2,6},{3,7},{4,0},{5,1},{6,2},{7,3},{8,12},{9,13},{10,... | collective-permute-start | bytes 255752 | tf_op jit(solution)/shard_map/ppermute | solution.py:57
  66.1 1.7 collective-permute-start.4
  67.9 0.6 collective-permute-done.8
  68.5 1.2 collective-permute-done.7
  69.6 8.3 %collective-permute-done.6 = f32[37,576]{1,0:T(8,128)S(1)} collective-permute-done((f32[37,576]{1,0:T(8,128)S(1)}, f32[37,576]{1,0:T(8,128)S(1)}, u32[]{:S(2)}, u32[]{:S(2)}) %collective-permute-start.6) | collective-permute-done | bytes 85280 | tf_op jit(solution)/shard_map/ppermute | solution.py:57
  78.5 1.2 collective-permute-start.15
  79.6 4.0 %collective-permute-start.14 = (bf16[37,576]{1,0:T(8,128)(2,1)S(1)}, bf16[37,576]{1,0:T(8,128)(2,1)S(1)}, u32[]{:S(2)}, u32[]{:S(2)}) collective-permute-start(bf16[37,576]{1,0:T(8,128)(2,1)S(1)} %get-tuple-element.7), channel_id=1, source_target_pairs={{0,5},{1,6},{2,7},{3,0},{4,1},{5,2},{6,3},{7,4},{8,13},{9,14},{10,... | collective-permute-start | bytes 127880 | tf_op jit(solution)/shard_map/ppermute | solution.py:60
  83.7 2.3 %collective-permute-start.13 = (bf16[37,576]{1,0:T(8,128)(2,1)S(1)}, bf16[37,576]{1,0:T(8,128)(2,1)S(1)}, u32[]{:S(2)}, u32[]{:S(2)}) collective-permute-start(bf16[37,576]{1,0:T(8,128)(2,1)S(1)} %get-tuple-element.7), channel_id=1, source_target_pairs={{0,4},{1,5},{2,6},{3,7},{4,0},{5,1},{6,2},{7,3},{8,12},{9,13},{10,... | collective-permute-start | bytes 127880 | tf_op jit(solution)/shard_map/ppermute | solution.py:60
  86.0 0.6 collective-permute-start.11
  86.6 5.3 %collective-permute-done.11 = bf16[37,576]{1,0:T(8,128)(2,1)S(1)} collective-permute-done((bf16[37,576]{1,0:T(8,128)(2,1)S(1)}, bf16[37,576]{1,0:T(8,128)(2,1)S(1)}, u32[]{:S(2)}, u32[]{:S(2)}) %collective-permute-start.11) | collective-permute-done | bytes 42656 | tf_op jit(solution)/shard_map/ppermute | solution.py:60
  91.9 1.5 collective-permute-start.16
  93.5 2.6 %collective-permute-done.16 = bf16[37,576]{1,0:T(8,128)(2,1)S(1)} collective-permute-done((bf16[37,576]{1,0:T(8,128)(2,1)S(1)}, bf16[37,576]{1,0:T(8,128)(2,1)S(1)}, u32[]{:S(2)}, u32[]{:S(2)}) %collective-permute-start.16) | collective-permute-done | bytes 42656 | tf_op jit(solution)/shard_map/ppermute | solution.py:60
  96.1 0.6 gather_fusion.4
  97.6 1.7 add_convert_fusion.1
  99.3 0.9 fusion.69
  100.5 3.0 %gather_fusion.1 = f32[288]{0:T(512)S(1)} fusion(f32[288,288]{1,0:T(8,128)S(1)} %get-tuple-element.12, s32[288]{0:T(512)S(1)} %or_reduce_fusion), kind=kCustom, calls=%fused_computation.5 | custom fusion | bytes 4608 | tf_op jit(solution)/shard_map/jit(diagonal)/cond/branch_0_fun/gather | solution.py:43
  103.8 0.6 gather_fusion.5
  104.6 3.0 %collective-permute-start.17 = (f32[37,576]{1,0:T(8,128)S(1)}, f32[37,576]{1,0:T(8,128)S(1)}, u32[]{:S(2)}, u32[]{:S(2)}) collective-permute-start(f32[37,576]{1,0:T(8,128)S(1)} %get-tuple-element.16), channel_id=1, source_target_pairs={{0,1},{1,2},{2,3},{3,4},{4,5},{5,6},{6,7},{7,0},{8,9},{9,10},{10,1... | collective-permute-start | bytes 255752 | tf_op jit(solution)/shard_map/ppermute | solution.py:57
  107.6 1.8 collective-permute-start.23
  109.6 4.2 %collective-permute-start.20 = (f32[37,576]{1,0:T(8,128)S(1)}, f32[37,576]{1,0:T(8,128)S(1)}, u32[]{:S(2)}, u32[]{:S(2)}) collective-permute-start(f32[37,576]{1,0:T(8,128)S(1)} %get-tuple-element.20), channel_id=1, source_target_pairs={{0,4},{1,5},{2,6},{3,7},{4,0},{5,1},{6,2},{7,3},{8,12},{9,13},{10,... | collective-permute-start | bytes 255752 | tf_op jit(solution)/shard_map/ppermute | solution.py:57
  113.7 0.6 collective-permute-start.18
  114.4 1.8 collective-permute-done.22
  116.2 8.8 %collective-permute-done.20 = f32[37,576]{1,0:T(8,128)S(1)} collective-permute-done((f32[37,576]{1,0:T(8,128)S(1)}, f32[37,576]{1,0:T(8,128)S(1)}, u32[]{:S(2)}, u32[]{:S(2)}) %collective-permute-start.20) | collective-permute-done | bytes 85280 | tf_op jit(solution)/shard_map/ppermute | solution.py:57
  125.0 0.6 collective-permute-done.19
  125.8 4.2 %collective-permute-start.28 = (bf16[37,576]{1,0:T(8,128)(2,1)S(1)}, bf16[37,576]{1,0:T(8,128)(2,1)S(1)}, u32[]{:S(2)}, u32[]{:S(2)}) collective-permute-start(bf16[37,576]{1,0:T(8,128)(2,1)S(1)} %get-tuple-element.5), channel_id=1, source_target_pairs={{0,5},{1,6},{2,7},{3,0},{4,1},{5,2},{6,3},{7,4},{8,13},{9,14},{10,... | collective-permute-start | bytes 127880 | tf_op jit(solution)/shard_map/ppermute | solution.py:60
  130.0 3.3 %collective-permute-start.27 = (bf16[37,576]{1,0:T(8,128)(2,1)S(1)}, bf16[37,576]{1,0:T(8,128)(2,1)S(1)}, u32[]{:S(2)}, u32[]{:S(2)}) collective-permute-start(bf16[37,576]{1,0:T(8,128)(2,1)S(1)} %get-tuple-element.5), channel_id=1, source_target_pairs={{0,4},{1,5},{2,6},{3,7},{4,0},{5,1},{6,2},{7,3},{8,12},{9,13},{10,... | collective-permute-start | bytes 127880 | tf_op jit(solution)/shard_map/ppermute | solution.py:60
  133.9 5.4 %collective-permute-done.25 = bf16[37,576]{1,0:T(8,128)(2,1)S(1)} collective-permute-done((bf16[37,576]{1,0:T(8,128)(2,1)S(1)}, bf16[37,576]{1,0:T(8,128)(2,1)S(1)}, u32[]{:S(2)}, u32[]{:S(2)}) %collective-permute-start.25) | collective-permute-done | bytes 42656 | tf_op jit(solution)/shard_map/ppermute | solution.py:60
  139.4 1.4 collective-permute-start.30
  140.8 2.6 %collective-permute-done.30 = bf16[37,576]{1,0:T(8,128)(2,1)S(1)} collective-permute-done((bf16[37,576]{1,0:T(8,128)(2,1)S(1)}, bf16[37,576]{1,0:T(8,128)(2,1)S(1)}, u32[]{:S(2)}, u32[]{:S(2)}) %collective-permute-start.30) | collective-permute-done | bytes 42656 | tf_op jit(solution)/shard_map/ppermute | solution.py:60
  143.5 0.6 gather_fusion.6
  145.0 1.7 add_convert_fusion
  146.7 23.8 %all_to_all.29 = bf16[8,72,768]{2,1,0:T(8,128)(2,1)S(1)} all-to-all(bf16[8,72,768]{2,1,0:T(8,128)(2,1)S(1)} %bitcast.130), channel_id=1, replica_groups=mesh['dp'=4,'tensor'=8] {'tensor'}, dimensions={0} | all-to-all | bytes 1769472 | tf_op jit(solution)/shard_map/all_to_all | solution.py:91
  170.9 1.3 convert_element_type.85
  172.4 29.2 %all-gather.2.cloned.1.call-done = bf16[4,72,6144]{2,1,0:T(8,128)(2,1)} async-done(((bf16[1,72,6144]{2,1,0:T(8,128)(2,1)}), bf16[4,72,6144]{2,1,0:T(8,128)(2,1)}) %all-gather.2.cloned.1.call-update) | async-done | bytes 3538960 | tf_op jit(solution)/shard_map/all_gather | solution.py:93
  201.6 2.8 %gather_fusion.2 = bf16[4,72,6144]{2,1,0:T(8,128)(2,1)S(1)} fusion(bf16[4,72,6144]{2,1,0:T(8,128)(2,1)} %all-gather.2.cloned.1.call-done, s32[1024]{0:T(1024)S(1)} %pad_clamp_fusion), kind=kCustom, calls=%fused_computation.6 | custom fusion | bytes 7077904 | tf_op jit(solution)/shard_map/jit(_take)/gather | solution.py:99
  204.4 2.2 %broadcast_select_fusion = bf16[4,72,6144]{2,1,0:T(8,128)(2,1)} fusion(bf16[4,72,6144]{2,1,0:T(8,128)(2,1)S(1)} %gather_fusion.2, pred[4]{0:T(512)(128)(4,1)S(1)} %compare_and_fusion.2), kind=kLoop, calls=%fused_computation.7 | loop fusion | flops 1769472 | bytes 7077892 | tf_op jit(solution)/shard_map/jit(_take)/select_n | solution.py:99
  (102 shorter events, 7.5 us)
Async XLA Ops:
  7.2 18.4 %copy-start.1 = (bf16[1,72,6144]{2,1,0:T(8,128)(2,1)S(1)}, bf16[1,72,6144]{2,1,0:T(8,128)(2,1)}, u32[]{:S(2)}) copy-start(bf16[1,72,6144]{2,1,0:T(8,128)(2,1)} %param.7) | copy-start | bytes 2654212
  10.1 15.8 %copy-start = (f32[1,72,6144]{2,1,0:T(8,128)}, f32[1,72,6144]{2,1,0:T(8,128)S(1)}, u32[]{:S(2)}) copy-start(f32[1,72,6144]{2,1,0:T(8,128)S(1)} %get-tuple-element.9) | copy-start | bytes 5308420
  10.1 4.6 %collective-permute-start = (f32[]{:T(128)}, f32[]{:T(128)}, u32[]{:S(2)}, u32[]{:S(2)}) collective-permute-start(f32[]{:T(128)} %get-tuple-element.8), channel_id=1, source_target_pairs={{0,1},{1,0},{2,3},{3,2},{4,5},{5,4},{6,7},{7,6},{8,9},{9,8},{10,11... | collective-permute-start | bytes 20 | tf_op jit(solution)/shard_map/ppermute | solution.py:28
  16.0 3.6 %collective-permute-start.1 = (f32[]{:T(128)}, f32[]{:T(128)}, u32[]{:S(2)}, u32[]{:S(2)}) collective-permute-start(f32[]{:T(128)} %add.128), channel_id=1, source_target_pairs={{0,2},{1,3},{2,0},{3,1},{4,6},{5,7},{6,4},{7,5},{8,10},{9,11},{10,... | collective-permute-start | bytes 20 | tf_op jit(solution)/shard_map/ppermute | solution.py:28
  20.3 4.6 %collective-permute-start.2 = (f32[]{:T(128)}, f32[]{:T(128)}, u32[]{:S(2)}, u32[]{:S(2)}) collective-permute-start(f32[]{:T(128)} %add.129), channel_id=1, source_target_pairs={{0,4},{1,5},{2,6},{3,7},{4,0},{5,1},{6,2},{7,3},{8,12},{9,13},{10,... | collective-permute-start | bytes 20 | tf_op jit(solution)/shard_map/ppermute | solution.py:28
  27.1 25.6 %all-to-all-start = ((bf16[72,8,768]{2,0,1:T(8,128)(2,1)}), bf16[72,8,768]{2,0,1:T(8,128)(2,1)S(1)}, u32[]{:S(2)}, u32[]{:S(2)}) async-start(bf16[72,8,768]{2,0,1:T(8,128)(2,1)} %copy.29), calls=%async_computation | async-start | bytes 1769472 | tf_op jit(solution)/shard_map/all_to_all | solution.py:82
  33.2 168.4 %all-gather.2.cloned.1.call-start = ((), (), s32[]{:S(2)}) async-start(), calls=%async_computation.2 | async-start | bytes 4423680 | tf_op jit(solution)/shard_map/all_gather | solution.py:93
  58.0 8.1 %collective-permute-start.3 = (f32[37,576]{1,0:T(8,128)S(1)}, f32[37,576]{1,0:T(8,128)S(1)}, u32[]{:S(2)}, u32[]{:S(2)}) collective-permute-start(f32[37,576]{1,0:T(8,128)S(1)} %get-tuple-element.23), channel_id=1, source_target_pairs={{0,1},{1,2},{2,3},{3,4},{4,5},{5,6},{6,7},{7,0},{8,9},{9,10},{10,1... | collective-permute-start | bytes 255752 | tf_op jit(solution)/shard_map/ppermute | solution.py:57
  59.3 6.8 %collective-permute-start.9 = (f32[37,576]{1,0:T(8,128)S(1)}, f32[37,576]{1,0:T(8,128)S(1)}, u32[]{:S(2)}, u32[]{:S(2)}) collective-permute-start(f32[37,576]{1,0:T(8,128)S(1)} %get-tuple-element.24), channel_id=1, source_target_pairs={{0,7},{1,0},{2,1},{3,2},{4,3},{5,4},{6,5},{7,6},{8,15},{9,8},{10,9... | collective-permute-start | bytes 255752 | tf_op jit(solution)/shard_map/ppermute | solution.py:57
  62.8 5.6 %collective-permute-start.8 = (f32[37,576]{1,0:T(8,128)S(1)}, f32[37,576]{1,0:T(8,128)S(1)}, u32[]{:S(2)}, u32[]{:S(2)}) collective-permute-start(f32[37,576]{1,0:T(8,128)S(1)} %get-tuple-element.25), channel_id=1, source_target_pairs={{0,6},{1,7},{2,0},{3,1},{4,2},{5,3},{6,4},{7,5},{8,14},{9,15},{10,... | collective-permute-start | bytes 255752 | tf_op jit(solution)/shard_map/ppermute | solution.py:57
  62.9 6.7 %collective-permute-start.7 = (f32[37,576]{1,0:T(8,128)S(1)}, f32[37,576]{1,0:T(8,128)S(1)}, u32[]{:S(2)}, u32[]{:S(2)}) collective-permute-start(f32[37,576]{1,0:T(8,128)S(1)} %get-tuple-element.26), channel_id=1, source_target_pairs={{0,5},{1,6},{2,7},{3,0},{4,1},{5,2},{6,3},{7,4},{8,13},{9,14},{10,... | collective-permute-start | bytes 255752 | tf_op jit(solution)/shard_map/ppermute | solution.py:57
  63.0 15.0 %collective-permute-start.6 = (f32[37,576]{1,0:T(8,128)S(1)}, f32[37,576]{1,0:T(8,128)S(1)}, u32[]{:S(2)}, u32[]{:S(2)}) collective-permute-start(f32[37,576]{1,0:T(8,128)S(1)} %get-tuple-element.27), channel_id=1, source_target_pairs={{0,4},{1,5},{2,6},{3,7},{4,0},{5,1},{6,2},{7,3},{8,12},{9,13},{10,... | collective-permute-start | bytes 255752 | tf_op jit(solution)/shard_map/ppermute | solution.py:57
  66.1 12.0 %collective-permute-start.5 = (f32[37,576]{1,0:T(8,128)S(1)}, f32[37,576]{1,0:T(8,128)S(1)}, u32[]{:S(2)}, u32[]{:S(2)}) collective-permute-start(f32[37,576]{1,0:T(8,128)S(1)} %get-tuple-element.28), channel_id=1, source_target_pairs={{0,3},{1,4},{2,5},{3,6},{4,7},{5,0},{6,1},{7,2},{8,11},{9,12},{10,... | collective-permute-start | bytes 255752 | tf_op jit(solution)/shard_map/ppermute | solution.py:57
  66.1 12.0 %collective-permute-start.4 = (f32[37,576]{1,0:T(8,128)S(1)}, f32[37,576]{1,0:T(8,128)S(1)}, u32[]{:S(2)}, u32[]{:S(2)}) collective-permute-start(f32[37,576]{1,0:T(8,128)S(1)} %get-tuple-element.29), channel_id=1, source_target_pairs={{0,2},{1,3},{2,4},{3,5},{4,6},{5,7},{6,0},{7,1},{8,10},{9,11},{10,... | collective-permute-start | bytes 255752 | tf_op jit(solution)/shard_map/ppermute | solution.py:57
  78.2 7.8 %collective-permute-start.10 = (bf16[37,576]{1,0:T(8,128)(2,1)S(1)}, bf16[37,576]{1,0:T(8,128)(2,1)S(1)}, u32[]{:S(2)}, u32[]{:S(2)}) collective-permute-start(bf16[37,576]{1,0:T(8,128)(2,1)S(1)} %get-tuple-element.7), channel_id=1, source_target_pairs={{0,1},{1,2},{2,3},{3,4},{4,5},{5,6},{6,7},{7,0},{8,9},{9,10},{10,1... | collective-permute-start | bytes 127880 | tf_op jit(solution)/shard_map/ppermute | solution.py:60
  78.5 15.0 %collective-permute-start.15 = (bf16[37,576]{1,0:T(8,128)(2,1)S(1)}, bf16[37,576]{1,0:T(8,128)(2,1)S(1)}, u32[]{:S(2)}, u32[]{:S(2)}) collective-permute-start(bf16[37,576]{1,0:T(8,128)(2,1)S(1)} %get-tuple-element.7), channel_id=1, source_target_pairs={{0,6},{1,7},{2,0},{3,1},{4,2},{5,3},{6,4},{7,5},{8,14},{9,15},{10,... | collective-permute-start | bytes 127880 | tf_op jit(solution)/shard_map/ppermute | solution.py:60
  79.6 13.8 %collective-permute-start.14 = (bf16[37,576]{1,0:T(8,128)(2,1)S(1)}, bf16[37,576]{1,0:T(8,128)(2,1)S(1)}, u32[]{:S(2)}, u32[]{:S(2)}) collective-permute-start(bf16[37,576]{1,0:T(8,128)(2,1)S(1)} %get-tuple-element.7), channel_id=1, source_target_pairs={{0,5},{1,6},{2,7},{3,0},{4,1},{5,2},{6,3},{7,4},{8,13},{9,14},{10,... | collective-permute-start | bytes 127880 | tf_op jit(solution)/shard_map/ppermute | solution.py:60
  83.7 9.7 %collective-permute-start.13 = (bf16[37,576]{1,0:T(8,128)(2,1)S(1)}, bf16[37,576]{1,0:T(8,128)(2,1)S(1)}, u32[]{:S(2)}, u32[]{:S(2)}) collective-permute-start(bf16[37,576]{1,0:T(8,128)(2,1)S(1)} %get-tuple-element.7), channel_id=1, source_target_pairs={{0,4},{1,5},{2,6},{3,7},{4,0},{5,1},{6,2},{7,3},{8,12},{9,13},{10,... | collective-permute-start | bytes 127880 | tf_op jit(solution)/shard_map/ppermute | solution.py:60
  86.0 7.4 %collective-permute-start.12 = (bf16[37,576]{1,0:T(8,128)(2,1)S(1)}, bf16[37,576]{1,0:T(8,128)(2,1)S(1)}, u32[]{:S(2)}, u32[]{:S(2)}) collective-permute-start(bf16[37,576]{1,0:T(8,128)(2,1)S(1)} %get-tuple-element.7), channel_id=1, source_target_pairs={{0,3},{1,4},{2,5},{3,6},{4,7},{5,0},{6,1},{7,2},{8,11},{9,12},{10,... | collective-permute-start | bytes 127880 | tf_op jit(solution)/shard_map/ppermute | solution.py:60
  86.0 5.9 %collective-permute-start.11 = (bf16[37,576]{1,0:T(8,128)(2,1)S(1)}, bf16[37,576]{1,0:T(8,128)(2,1)S(1)}, u32[]{:S(2)}, u32[]{:S(2)}) collective-permute-start(bf16[37,576]{1,0:T(8,128)(2,1)S(1)} %get-tuple-element.7), channel_id=1, source_target_pairs={{0,2},{1,3},{2,4},{3,5},{4,6},{5,7},{6,0},{7,1},{8,10},{9,11},{10,... | collective-permute-start | bytes 127880 | tf_op jit(solution)/shard_map/ppermute | solution.py:60
  91.9 4.2 %collective-permute-start.16 = (bf16[37,576]{1,0:T(8,128)(2,1)S(1)}, bf16[37,576]{1,0:T(8,128)(2,1)S(1)}, u32[]{:S(2)}, u32[]{:S(2)}) collective-permute-start(bf16[37,576]{1,0:T(8,128)(2,1)S(1)} %get-tuple-element.7), channel_id=1, source_target_pairs={{0,7},{1,0},{2,1},{3,2},{4,3},{5,4},{6,5},{7,6},{8,15},{9,8},{10,9... | collective-permute-start | bytes 127880 | tf_op jit(solution)/shard_map/ppermute | solution.py:60
  104.6 9.1 %collective-permute-start.17 = (f32[37,576]{1,0:T(8,128)S(1)}, f32[37,576]{1,0:T(8,128)S(1)}, u32[]{:S(2)}, u32[]{:S(2)}) collective-permute-start(f32[37,576]{1,0:T(8,128)S(1)} %get-tuple-element.16), channel_id=1, source_target_pairs={{0,1},{1,2},{2,3},{3,4},{4,5},{5,6},{6,7},{7,0},{8,9},{9,10},{10,1... | collective-permute-start | bytes 255752 | tf_op jit(solution)/shard_map/ppermute | solution.py:57
  107.6 6.2 %collective-permute-start.23 = (f32[37,576]{1,0:T(8,128)S(1)}, f32[37,576]{1,0:T(8,128)S(1)}, u32[]{:S(2)}, u32[]{:S(2)}) collective-permute-start(f32[37,576]{1,0:T(8,128)S(1)} %get-tuple-element.17), channel_id=1, source_target_pairs={{0,7},{1,0},{2,1},{3,2},{4,3},{5,4},{6,5},{7,6},{8,15},{9,8},{10,9... | collective-permute-start | bytes 255752 | tf_op jit(solution)/shard_map/ppermute | solution.py:57
  109.4 6.8 %collective-permute-start.22 = (f32[37,576]{1,0:T(8,128)S(1)}, f32[37,576]{1,0:T(8,128)S(1)}, u32[]{:S(2)}, u32[]{:S(2)}) collective-permute-start(f32[37,576]{1,0:T(8,128)S(1)} %get-tuple-element.18), channel_id=1, source_target_pairs={{0,6},{1,7},{2,0},{3,1},{4,2},{5,3},{6,4},{7,5},{8,14},{9,15},{10,... | collective-permute-start | bytes 255752 | tf_op jit(solution)/shard_map/ppermute | solution.py:57
  109.4 6.8 %collective-permute-start.21 = (f32[37,576]{1,0:T(8,128)S(1)}, f32[37,576]{1,0:T(8,128)S(1)}, u32[]{:S(2)}, u32[]{:S(2)}) collective-permute-start(f32[37,576]{1,0:T(8,128)S(1)} %get-tuple-element.19), channel_id=1, source_target_pairs={{0,5},{1,6},{2,7},{3,0},{4,1},{5,2},{6,3},{7,4},{8,13},{9,14},{10,... | collective-permute-start | bytes 255752 | tf_op jit(solution)/shard_map/ppermute | solution.py:57
  109.6 15.4 %collective-permute-start.20 = (f32[37,576]{1,0:T(8,128)S(1)}, f32[37,576]{1,0:T(8,128)S(1)}, u32[]{:S(2)}, u32[]{:S(2)}) collective-permute-start(f32[37,576]{1,0:T(8,128)S(1)} %get-tuple-element.20), channel_id=1, source_target_pairs={{0,4},{1,5},{2,6},{3,7},{4,0},{5,1},{6,2},{7,3},{8,12},{9,13},{10,... | collective-permute-start | bytes 255752 | tf_op jit(solution)/shard_map/ppermute | solution.py:57
  113.7 11.8 %collective-permute-start.19 = (f32[37,576]{1,0:T(8,128)S(1)}, f32[37,576]{1,0:T(8,128)S(1)}, u32[]{:S(2)}, u32[]{:S(2)}) collective-permute-start(f32[37,576]{1,0:T(8,128)S(1)} %get-tuple-element.21), channel_id=1, source_target_pairs={{0,3},{1,4},{2,5},{3,6},{4,7},{5,0},{6,1},{7,2},{8,11},{9,12},{10,... | collective-permute-start | bytes 255752 | tf_op jit(solution)/shard_map/ppermute | solution.py:57
  113.7 11.8 %collective-permute-start.18 = (f32[37,576]{1,0:T(8,128)S(1)}, f32[37,576]{1,0:T(8,128)S(1)}, u32[]{:S(2)}, u32[]{:S(2)}) collective-permute-start(f32[37,576]{1,0:T(8,128)S(1)} %get-tuple-element.22), channel_id=1, source_target_pairs={{0,2},{1,3},{2,4},{3,5},{4,6},{5,7},{6,0},{7,1},{8,10},{9,11},{10,... | collective-permute-start | bytes 255752 | tf_op jit(solution)/shard_map/ppermute | solution.py:57
  125.6 7.7 %collective-permute-start.24 = (bf16[37,576]{1,0:T(8,128)(2,1)S(1)}, bf16[37,576]{1,0:T(8,128)(2,1)S(1)}, u32[]{:S(2)}, u32[]{:S(2)}) collective-permute-start(bf16[37,576]{1,0:T(8,128)(2,1)S(1)} %get-tuple-element.5), channel_id=1, source_target_pairs={{0,1},{1,2},{2,3},{3,4},{4,5},{5,6},{6,7},{7,0},{8,9},{9,10},{10,1... | collective-permute-start | bytes 127880 | tf_op jit(solution)/shard_map/ppermute | solution.py:60
  125.7 15.1 %collective-permute-start.29 = (bf16[37,576]{1,0:T(8,128)(2,1)S(1)}, bf16[37,576]{1,0:T(8,128)(2,1)S(1)}, u32[]{:S(2)}, u32[]{:S(2)}) collective-permute-start(bf16[37,576]{1,0:T(8,128)(2,1)S(1)} %get-tuple-element.5), channel_id=1, source_target_pairs={{0,6},{1,7},{2,0},{3,1},{4,2},{5,3},{6,4},{7,5},{8,14},{9,15},{10,... | collective-permute-start | bytes 127880 | tf_op jit(solution)/shard_map/ppermute | solution.py:60
  125.8 15.0 %collective-permute-start.28 = (bf16[37,576]{1,0:T(8,128)(2,1)S(1)}, bf16[37,576]{1,0:T(8,128)(2,1)S(1)}, u32[]{:S(2)}, u32[]{:S(2)}) collective-permute-start(bf16[37,576]{1,0:T(8,128)(2,1)S(1)} %get-tuple-element.5), channel_id=1, source_target_pairs={{0,5},{1,6},{2,7},{3,0},{4,1},{5,2},{6,3},{7,4},{8,13},{9,14},{10,... | collective-permute-start | bytes 127880 | tf_op jit(solution)/shard_map/ppermute | solution.py:60
  130.0 10.8 %collective-permute-start.27 = (bf16[37,576]{1,0:T(8,128)(2,1)S(1)}, bf16[37,576]{1,0:T(8,128)(2,1)S(1)}, u32[]{:S(2)}, u32[]{:S(2)}) collective-permute-start(bf16[37,576]{1,0:T(8,128)(2,1)S(1)} %get-tuple-element.5), channel_id=1, source_target_pairs={{0,4},{1,5},{2,6},{3,7},{4,0},{5,1},{6,2},{7,3},{8,12},{9,13},{10,... | collective-permute-start | bytes 127880 | tf_op jit(solution)/shard_map/ppermute | solution.py:60
  133.3 7.4 %collective-permute-start.26 = (bf16[37,576]{1,0:T(8,128)(2,1)S(1)}, bf16[37,576]{1,0:T(8,128)(2,1)S(1)}, u32[]{:S(2)}, u32[]{:S(2)}) collective-permute-start(bf16[37,576]{1,0:T(8,128)(2,1)S(1)} %get-tuple-element.5), channel_id=1, source_target_pairs={{0,3},{1,4},{2,5},{3,6},{4,7},{5,0},{6,1},{7,2},{8,11},{9,12},{10,... | collective-permute-start | bytes 127880 | tf_op jit(solution)/shard_map/ppermute | solution.py:60
  133.4 6.0 %collective-permute-start.25 = (bf16[37,576]{1,0:T(8,128)(2,1)S(1)}, bf16[37,576]{1,0:T(8,128)(2,1)S(1)}, u32[]{:S(2)}, u32[]{:S(2)}) collective-permute-start(bf16[37,576]{1,0:T(8,128)(2,1)S(1)} %get-tuple-element.5), channel_id=1, source_target_pairs={{0,2},{1,3},{2,4},{3,5},{4,6},{5,7},{6,0},{7,1},{8,10},{9,11},{10,... | collective-permute-start | bytes 127880 | tf_op jit(solution)/shard_map/ppermute | solution.py:60
  139.4 4.1 %collective-permute-start.30 = (bf16[37,576]{1,0:T(8,128)(2,1)S(1)}, bf16[37,576]{1,0:T(8,128)(2,1)S(1)}, u32[]{:S(2)}, u32[]{:S(2)}) collective-permute-start(bf16[37,576]{1,0:T(8,128)(2,1)S(1)} %get-tuple-element.5), channel_id=1, source_target_pairs={{0,7},{1,0},{2,1},{3,2},{4,3},{5,4},{6,5},{7,6},{8,15},{9,8},{10,9... | collective-permute-start | bytes 127880 | tf_op jit(solution)/shard_map/ppermute | solution.py:60
  170.9 1.4 copy-start.2
Sparse Core Ops, SparseCore 0:
  172.3 29.2 all-gather.1

commit v2 on v1

--- a/solution.py
+++ b/solution.py
@@ -88,9 +88,16 @@
         applied = jnp.dot(poly, columns, preferred_element_type=jnp.float32)
         columns = (coef_a * columns.astype(jnp.float32) + applied).astype(jnp.bfloat16)
     factor = 0.2 * math.sqrt(max(M, N))
-    back_rows = lax.all_to_all(columns, "tensor", split_axis=0, concat_axis=1, tiled=True)
-    scaled = (factor * back_rows.astype(jnp.float32)).astype(jnp.bfloat16)
-    every_slot = lax.all_gather(scaled[None], "dp", axis=0, tiled=True)
+    per = columns.shape[0] // size
+    half = per // 2
+    blocks = columns.reshape(size, per, columns.shape[1])
+    gathered = []
+    for lo, hi in ((0, half), (half, per)):
+        piece = blocks[:, lo:hi, :].reshape(size * (hi - lo), columns.shape[1])
+        back_rows = lax.all_to_all(piece, "tensor", split_axis=0, concat_axis=1, tiled=True)
+        scaled = (factor * back_rows.astype(jnp.float32)).astype(jnp.bfloat16)
+        gathered.append(lax.all_gather(scaled[None], "dp", axis=0, tiled=True))
+    every_slot = jnp.concatenate(gathered, axis=1)
     slots = every_slot.shape[0]
     ids = jnp.arange(slots, dtype=jnp.int32)
     inverse = jnp.sum(

time: 214 us -> 218 us (1.019)
  waiting for transfers between devices: 88.3 us -> 69.2 us
  starting transfers between devices: 55.7 us -> 67.3 us
  other arithmetic: 7.71 us -> 12.4 us
  blocking collectives: 23.8 us -> 27.6 us
  matrix products: 5.16 us -> 7.57 us
    ppermute x14, waiting for transfers between devices: 21.8 us -> 10.2 us  [gram_allreduce(): acc = acc + lax.ppermute(rolled[s], axis, _shift_pairs(size, s))]
    ppermute x14, starting transfers between devices: 19.5 us -> 30.1 us  [gram_allreduce(): lax.ppermute(mine, axis, _shift_pairs(size, s))]
    ppermute x14, waiting for transfers between devices: 16 us -> 8 us  [gram_allreduce(): lax.ppermute(mine, axis, _shift_pairs(size, s))]
    all_to_all x1 -> x2, blocking collectives: 23.8 us -> 27.6 us  [per_device(): lax.all_to_all(piece, 'tensor', split_axis=0, concat_axis=1, tiled=True)]
    concatenate x0 -> x1, other arithmetic: none -> 2.72 us  [per_device(): every_slot = jnp.concatenate(gathered, axis=1)]
    all_gather x1 -> x2, waiting for transfers between devices: 29.2 us -> 30.1 us  [per_device(): gathered.append(lax.all_gather(scaled[None], 'dp', axis=0, tiled=True))]
  transfers between devices with their start and end apart: 33 -> 34, of which waited for: 17 -> 18; matrix products, arithmetic and copies ran while one was open for 0% -> 1% of each run, Pallas kernels for 0% -> 0%
where the time goes in v2:
time: 218 us
  waiting for transfers between devices  69.2 us (32%)
  starting transfers between devices  67.3 us (31%)
  blocking collectives  27.6 us (13%)
  between operations  16.9 us (8%)
  local copies, waits for them, and re-layouts  16.7 us (8%)
  other arithmetic  12.4 us (6%)
  matrix products  7.57 us (3%)
    ppermute x14, starting transfers between devices, gram_allreduce(): lax.ppermute(mine, axis, _shift_pairs(size, s))  30.1 us
    all_gather x2, waiting for transfers between devices, per_device(): gathered.append(lax.all_gather(scaled[None], 'dp', axis=0, tiled=True))  30.1 us
    all_to_all x2, blocking collectives, per_device(): lax.all_to_all(piece, 'tensor', split_axis=0, concat_axis=1, tiled=True)  27.6 us
    ppermute x14, starting transfers between devices, gram_allreduce(): acc = acc + lax.ppermute(rolled[s], axis, _shift_pairs(size, s))  20 us
    all_to_all x1, waiting for transfers between devices, per_device(): lax.all_to_all(rows_here, 'tensor', split_axis=1, concat_axis=0, tiled=True)  18.4 us
    ppermute x3, starting transfers between devices, total_over(): lax.ppermute(value, axis, [(i, i ^ bit) for i in range(size)])  10.8 us
    ppermute x14, waiting for transfers between devices, gram_allreduce(): acc = acc + lax.ppermute(rolled[s], axis, _shift_pairs(size, s))  10.2 us
    ppermute x14, waiting for transfers between devices, gram_allreduce(): lax.ppermute(mine, axis, _shift_pairs(size, s))  8 us
  transfers between devices with their start and end apart: 34, of which 18 were waited for; matrix products, arithmetic and copies ran while one was open for 1% of the time, Pallas kernels for 0%

profile of v2, /device:TPU:0, one launch (start us, length us, event | category | flops | bytes accessed | tf_op | source)
XLA Modules:
  0.0 217.6 jit_solution(10814130053055024486)
XLA Ops:
  7.2 2.9 %multiply_reduce_fusion = (f32[]{:T(128)}, f32[1,72,6144]{2,1,0:T(8,128)S(1)}) fusion(bf16[1,72,6144]{2,1,0:T(8,128)(2,1)} %param.7, f32[1,72,6144]{2,1,0:T(8,128)} %param.8), kind=kLoop, calls=%fused_computation.14 | loop fusion | flops 3096575 | bytes 4423684 | tf_op jit(solution)/shard_map/reduce_sum | solution.py:80
  10.1 3.0 %collective-permute-start = (f32[]{:T(128)}, f32[]{:T(128)}, u32[]{:S(2)}, u32[]{:S(2)}) collective-permute-start(f32[]{:T(128)} %get-tuple-element.8), channel_id=1, source_target_pairs={{0,1},{1,0},{2,3},{3,2},{4,5},{5,4},{6,7},{7,6},{8,9},{9,8},{10,11... | collective-permute-start | bytes 20 | tf_op jit(solution)/shard_map/ppermute | solution.py:28
  13.1 1.8 collective-permute-done
  16.1 3.4 %collective-permute-start.1 = (f32[]{:T(128)}, f32[]{:T(128)}, u32[]{:S(2)}, u32[]{:S(2)}) collective-permute-start(f32[]{:T(128)} %add.128), channel_id=1, source_target_pairs={{0,2},{1,3},{2,0},{3,1},{4,6},{5,7},{6,4},{7,5},{8,10},{9,11},{10,... | collective-permute-start | bytes 20 | tf_op jit(solution)/shard_map/ppermute | solution.py:28
  20.4 4.4 %collective-permute-start.2 = (f32[]{:T(128)}, f32[]{:T(128)}, u32[]{:S(2)}, u32[]{:S(2)}) collective-permute-start(f32[]{:T(128)} %add.129), channel_id=1, source_target_pairs={{0,4},{1,5},{2,6},{3,7},{4,0},{5,1},{6,2},{7,3},{8,12},{9,13},{10,... | collective-permute-start | bytes 20 | tf_op jit(solution)/shard_map/ppermute | solution.py:28
  26.3 1.1 copy.31
  27.3 6.2 %all-to-all-start = ((bf16[72,8,768]{2,0,1:T(8,128)(2,1)}), bf16[72,8,768]{2,0,1:T(8,128)(2,1)S(1)}, u32[]{:S(2)}, u32[]{:S(2)}) async-start(bf16[72,8,768]{2,0,1:T(8,128)(2,1)} %copy.31), calls=%async_computation | async-start | bytes 1769472 | tf_op jit(solution)/shard_map/all_to_all | solution.py:82
  33.7 18.4 %all-to-all-done = bf16[72,8,768]{2,0,1:T(8,128)(2,1)S(1)} async-done(((bf16[72,8,768]{2,0,1:T(8,128)(2,1)}), bf16[72,8,768]{2,0,1:T(8,128)(2,1)S(1)}, u32[]{:S(2)}, u32[]{:S(2)}) %all-to-all-start) | async-done | bytes 884768 | tf_op jit(solution)/shard_map/all_to_all | solution.py:82
  53.2 3.0 %gather_fusion = f32[288]{0:T(512)S(1)} fusion(f32[288,288]{1,0:T(8,128)S(1)} %get-tuple-element.15, s32[288]{0:T(512)S(1)} %or_reduce_fusion), kind=kCustom, calls=%fused_computation.4 | custom fusion | bytes 4608 | tf_op jit(solution)/shard_map/jit(diagonal)/cond/branch_0_fun/gather | solution.py:43
  57.4 1.2 collective-permute-start.3
  58.6 2.0 collective-permute-start.5
  60.6 2.2 collective-permute-start.6
  62.8 1.8 collective-permute-start.7
  64.6 1.5 collective-permute-done.3
  66.4 1.3 collective-permute-start.9
  67.6 3.2 %collective-permute-done.5 = f32[37,576]{1,0:T(8,128)S(1)} collective-permute-done((f32[37,576]{1,0:T(8,128)S(1)}, f32[37,576]{1,0:T(8,128)S(1)}, u32[]{:S(2)}, u32[]{:S(2)}) %collective-permute-start.5) | collective-permute-done | bytes 85280 | tf_op jit(solution)/shard_map/ppermute | solution.py:57
  71.3 2.6 %collective-permute-done.8 = f32[37,576]{1,0:T(8,128)S(1)} collective-permute-done((f32[37,576]{1,0:T(8,128)S(1)}, f32[37,576]{1,0:T(8,128)S(1)}, u32[]{:S(2)}, u32[]{:S(2)}) %collective-permute-start.8) | collective-permute-done | bytes 85280 | tf_op jit(solution)/shard_map/ppermute | solution.py:57
  73.9 2.6 %collective-permute-start.10 = (bf16[37,576]{1,0:T(8,128)(2,1)S(1)}, bf16[37,576]{1,0:T(8,128)(2,1)S(1)}, u32[]{:S(2)}, u32[]{:S(2)}) collective-permute-start(bf16[37,576]{1,0:T(8,128)(2,1)S(1)} %get-tuple-element.7), channel_id=1, source_target_pairs={{0,1},{1,2},{2,3},{3,4},{4,5},{5,6},{6,7},{7,0},{8,9},{9,10},{10,1... | collective-permute-start | bytes 127880 | tf_op jit(solution)/shard_map/ppermute | solution.py:60
  76.5 2.9 %collective-permute-start.11 = (bf16[37,576]{1,0:T(8,128)(2,1)S(1)}, bf16[37,576]{1,0:T(8,128)(2,1)S(1)}, u32[]{:S(2)}, u32[]{:S(2)}) collective-permute-start(bf16[37,576]{1,0:T(8,128)(2,1)S(1)} %get-tuple-element.7), channel_id=1, source_target_pairs={{0,2},{1,3},{2,4},{3,5},{4,6},{5,7},{6,0},{7,1},{8,10},{9,11},{10,... | collective-permute-start | bytes 127880 | tf_op jit(solution)/shard_map/ppermute | solution.py:60
  79.5 1.7 collective-permute-start.12
  81.9 3.2 %collective-permute-start.14 = (bf16[37,576]{1,0:T(8,128)(2,1)S(1)}, bf16[37,576]{1,0:T(8,128)(2,1)S(1)}, u32[]{:S(2)}, u32[]{:S(2)}) collective-permute-start(bf16[37,576]{1,0:T(8,128)(2,1)S(1)} %get-tuple-element.7), channel_id=1, source_target_pairs={{0,5},{1,6},{2,7},{3,0},{4,1},{5,2},{6,3},{7,4},{8,13},{9,14},{10,... | collective-permute-start | bytes 127880 | tf_op jit(solution)/shard_map/ppermute | solution.py:60
  85.1 2.9 %collective-permute-start.15 = (bf16[37,576]{1,0:T(8,128)(2,1)S(1)}, bf16[37,576]{1,0:T(8,128)(2,1)S(1)}, u32[]{:S(2)}, u32[]{:S(2)}) collective-permute-start(bf16[37,576]{1,0:T(8,128)(2,1)S(1)} %get-tuple-element.7), channel_id=1, source_target_pairs={{0,6},{1,7},{2,0},{3,1},{4,2},{5,3},{6,4},{7,5},{8,14},{9,15},{10,... | collective-permute-start | bytes 127880 | tf_op jit(solution)/shard_map/ppermute | solution.py:60
  88.1 1.6 collective-permute-done.15
  89.7 2.4 %collective-permute-done.16 = bf16[37,576]{1,0:T(8,128)(2,1)S(1)} collective-permute-done((bf16[37,576]{1,0:T(8,128)(2,1)S(1)}, bf16[37,576]{1,0:T(8,128)(2,1)S(1)}, u32[]{:S(2)}, u32[]{:S(2)}) %collective-permute-start.16) | collective-permute-done | bytes 42656 | tf_op jit(solution)/shard_map/ppermute | solution.py:60
  93.6 2.6 %add_convert_fusion.1 = bf16[576,768]{1,0:T(8,128)(2,1)} fusion(bf16[576,768]{1,0:T(8,128)(2,1)S(1)} %bitcast.132, bf16[288,288]{1,0:T(8,128)(2,1)S(1)} %get-tuple-element.35, bf16[288,288]{1,0:T(8,128)(2,1)S(1)} %copy.33, bf16[288,288]{1,0:T(8,128)(2,1)S(1)} %get-tuple-element.38, bf16[288,288]{1,0:T(8,128)(2,1)S(1)} %get-tuple-element.34), kind=kOutput, calls=%fused_computation.12 | convolution fusion | flops 900218880 | bytes 2433024 | tf_op jit(solution)/shard_map/dot_general | solution.py:88
  96.2 2.4 %fusion.71 = f32[576,576]{1,0:T(8,128)S(1)} fusion(bf16[576,768]{1,0:T(8,128)(2,1)} %add_convert_fusion.1), kind=kOutput, calls=%fused_computation.137 | convolution fusion | flops 509607936 | bytes 2211840 | tf_op jit(solution)/shard_map/dot_general | solution.py:84
  98.9 3.0 %gather_fusion.1 = f32[288]{0:T(512)S(1)} fusion(f32[288,288]{1,0:T(8,128)S(1)} %get-tuple-element.12, s32[288]{0:T(512)S(1)} %or_reduce_fusion), kind=kCustom, calls=%fused_computation.5 | custom fusion | bytes 4608 | tf_op jit(solution)/shard_map/jit(diagonal)/cond/branch_0_fun/gather | solution.py:43
  103.9 3.0 %collective-permute-start.19 = (f32[37,576]{1,0:T(8,128)S(1)}, f32[37,576]{1,0:T(8,128)S(1)}, u32[]{:S(2)}, u32[]{:S(2)}) collective-permute-start(f32[37,576]{1,0:T(8,128)S(1)} %get-tuple-element.23), channel_id=1, source_target_pairs={{0,3},{1,4},{2,5},{3,6},{4,7},{5,0},{6,1},{7,2},{8,11},{9,12},{10,... | collective-permute-start | bytes 255752 | tf_op jit(solution)/shard_map/ppermute | solution.py:57
  106.9 1.5 collective-permute-start.20
  108.4 2.8 %collective-permute-start.21 = (f32[37,576]{1,0:T(8,128)S(1)}, f32[37,576]{1,0:T(8,128)S(1)}, u32[]{:S(2)}, u32[]{:S(2)}) collective-permute-start(f32[37,576]{1,0:T(8,128)S(1)} %get-tuple-element.21), channel_id=1, source_target_pairs={{0,5},{1,6},{2,7},{3,0},{4,1},{5,2},{6,3},{7,4},{8,13},{9,14},{10,... | collective-permute-start | bytes 255752 | tf_op jit(solution)/shard_map/ppermute | solution.py:57
  111.5 3.1 %collective-permute-start.23 = (f32[37,576]{1,0:T(8,128)S(1)}, f32[37,576]{1,0:T(8,128)S(1)}, u32[]{:S(2)}, u32[]{:S(2)}) collective-permute-start(f32[37,576]{1,0:T(8,128)S(1)} %get-tuple-element.19), channel_id=1, source_target_pairs={{0,7},{1,0},{2,1},{3,2},{4,3},{5,4},{6,5},{7,6},{8,15},{9,8},{10,9... | collective-permute-start | bytes 255752 | tf_op jit(solution)/shard_map/ppermute | solution.py:57
  114.6 1.7 collective-permute-done.19
  116.9 3.4 %collective-permute-start.24 = (bf16[37,576]{1,0:T(8,128)(2,1)S(1)}, bf16[37,576]{1,0:T(8,128)(2,1)S(1)}, u32[]{:S(2)}, u32[]{:S(2)}) collective-permute-start(bf16[37,576]{1,0:T(8,128)(2,1)S(1)} %get-tuple-element.5), channel_id=1, source_target_pairs={{0,1},{1,2},{2,3},{3,4},{4,5},{5,6},{6,7},{7,0},{8,9},{9,10},{10,1... | collective-permute-start | bytes 127880 | tf_op jit(solution)/shard_map/ppermute | solution.py:60
  120.4 3.9 %collective-permute-start.25 = (bf16[37,576]{1,0:T(8,128)(2,1)S(1)}, bf16[37,576]{1,0:T(8,128)(2,1)S(1)}, u32[]{:S(2)}, u32[]{:S(2)}) collective-permute-start(bf16[37,576]{1,0:T(8,128)(2,1)S(1)} %get-tuple-element.5), channel_id=1, source_target_pairs={{0,2},{1,3},{2,4},{3,5},{4,6},{5,7},{6,0},{7,1},{8,10},{9,11},{10,... | collective-permute-start | bytes 127880 | tf_op jit(solution)/shard_map/ppermute | solution.py:60
  124.2 1.9 collective-permute-start.26
  127.1 2.9 %collective-permute-start.28 = (bf16[37,576]{1,0:T(8,128)(2,1)S(1)}, bf16[37,576]{1,0:T(8,128)(2,1)S(1)}, u32[]{:S(2)}, u32[]{:S(2)}) collective-permute-start(bf16[37,576]{1,0:T(8,128)(2,1)S(1)} %get-tuple-element.5), channel_id=1, source_target_pairs={{0,5},{1,6},{2,7},{3,0},{4,1},{5,2},{6,3},{7,4},{8,13},{9,14},{10,... | collective-permute-start | bytes 127880 | tf_op jit(solution)/shard_map/ppermute | solution.py:60
  130.0 2.9 %collective-permute-start.29 = (bf16[37,576]{1,0:T(8,128)(2,1)S(1)}, bf16[37,576]{1,0:T(8,128)(2,1)S(1)}, u32[]{:S(2)}, u32[]{:S(2)}) collective-permute-start(bf16[37,576]{1,0:T(8,128)(2,1)S(1)} %get-tuple-element.5), channel_id=1, source_target_pairs={{0,6},{1,7},{2,0},{3,1},{4,2},{5,3},{6,4},{7,5},{8,14},{9,15},{10,... | collective-permute-start | bytes 127880 | tf_op jit(solution)/shard_map/ppermute | solution.py:60
  133.2 1.4 collective-permute-done.29
  134.6 2.6 %collective-permute-done.30 = bf16[37,576]{1,0:T(8,128)(2,1)S(1)} collective-permute-done((bf16[37,576]{1,0:T(8,128)(2,1)S(1)}, bf16[37,576]{1,0:T(8,128)(2,1)S(1)}, u32[]{:S(2)}, u32[]{:S(2)}) %collective-permute-start.30) | collective-permute-done | bytes 42656 | tf_op jit(solution)/shard_map/ppermute | solution.py:60
  139.1 1.7 add_convert_fusion
  140.9 14.2 %all_to_all.36 = bf16[8,36,768]{2,1,0:T(8,128)(2,1)S(1)} all-to-all(bf16[8,36,768]{2,1,0:T(8,128)(2,1)S(1)} %get-tuple-element.16), channel_id=1, replica_groups=mesh['dp'=4,'tensor'=8] {'tensor'}, dimensions={0} | all-to-all | bytes 884736 | tf_op jit(solution)/shard_map/all_to_all | solution.py:97
  155.3 1.0 convert_element_type.113
  156.4 13.4 %all_to_all.37 = bf16[8,36,768]{2,1,0:T(8,128)(2,1)S(1)} all-to-all(bf16[8,36,768]{2,1,0:T(8,128)(2,1)S(1)} %get-tuple-element.17), channel_id=1, replica_groups=mesh['dp'=4,'tensor'=8] {'tensor'}, dimensions={0} | all-to-all | bytes 884736 | tf_op jit(solution)/shard_map/all_to_all | solution.py:97
  171.2 6.1 %all-gather.3.cloned.1.call-done = bf16[4,36,6144]{2,1,0:T(8,128)(2,1)} async-done(((bf16[1,36,6144]{2,1,0:T(8,128)(2,1)}), bf16[4,36,6144]{2,1,0:T(8,128)(2,1)}) %all-gather.3.cloned.1.call-update) | async-done | bytes 1769488 | tf_op jit(solution)/shard_map/all_gather | solution.py:99
  177.2 24.0 %all-gather.5.cloned.1.call-done = bf16[4,36,6144]{2,1,0:T(8,128)(2,1)} async-done(((bf16[1,36,6144]{2,1,0:T(8,128)(2,1)}), bf16[4,36,6144]{2,1,0:T(8,128)(2,1)}) %all-gather.5.cloned.1.call-update) | async-done | bytes 1769488 | tf_op jit(solution)/shard_map/all_gather | solution.py:99
  201.2 2.7 %pad_maximum_fusion = bf16[4,72,6144]{2,1,0:T(8,128)(2,1)S(1)} fusion(bf16[4,36,6144]{2,1,0:T(8,128)(2,1)} %all-gather.5.cloned.1.call-done, bf16[4,36,6144]{2,1,0:T(8,128)(2,1)} %all-gather.3.cloned.1.call-done), kind=kLoop, calls=%fused_computation.7 | loop fusion | flops 7077888 | bytes 7077888 | tf_op jit(solution)/shard_map/concatenate | solution.py:100
  204.0 2.6 %gather_fusion.2 = bf16[4,72,6144]{2,1,0:T(8,128)(2,1)} fusion(bf16[4,72,6144]{2,1,0:T(8,128)(2,1)S(1)} %pad_maximum_fusion, s32[1024]{0:T(1024)S(1)} %pad_clamp_fusion), kind=kCustom, calls=%fused_computation.6 | custom fusion | bytes 7077904 | tf_op jit(solution)/shard_map/jit(_take)/gather | solution.py:106
  206.5 4.2 %broadcast_select_fusion = bf16[4,72,6144]{2,1,0:T(8,128)(2,1)} fusion(bf16[4,72,6144]{2,1,0:T(8,128)(2,1)} %gather_fusion.2, pred[4]{0:T(512)(128)(4,1)S(1)} %compare_and_fusion.2), kind=kLoop, calls=%fused_computation.8 | loop fusion | flops 1769472 | bytes 7077892 | tf_op jit(solution)/shard_map/jit(_take)/select_n | solution.py:106
  (113 shorter events, 14.8 us)
Async XLA Ops:
  7.2 18.6 %copy-start.1 = (bf16[1,72,6144]{2,1,0:T(8,128)(2,1)S(1)}, bf16[1,72,6144]{2,1,0:T(8,128)(2,1)}, u32[]{:S(2)}) copy-start(bf16[1,72,6144]{2,1,0:T(8,128)(2,1)} %param.7) | copy-start | bytes 2654212
  10.1 16.0 %copy-start = (f32[1,72,6144]{2,1,0:T(8,128)}, f32[1,72,6144]{2,1,0:T(8,128)S(1)}, u32[]{:S(2)}) copy-start(f32[1,72,6144]{2,1,0:T(8,128)S(1)} %get-tuple-element.9) | copy-start | bytes 5308420
  10.1 4.8 %collective-permute-start = (f32[]{:T(128)}, f32[]{:T(128)}, u32[]{:S(2)}, u32[]{:S(2)}) collective-permute-start(f32[]{:T(128)} %get-tuple-element.8), channel_id=1, source_target_pairs={{0,1},{1,0},{2,3},{3,2},{4,5},{5,4},{6,7},{7,6},{8,9},{9,8},{10,11... | collective-permute-start | bytes 20 | tf_op jit(solution)/shard_map/ppermute | solution.py:28
  16.1 3.8 %collective-permute-start.1 = (f32[]{:T(128)}, f32[]{:T(128)}, u32[]{:S(2)}, u32[]{:S(2)}) collective-permute-start(f32[]{:T(128)} %add.128), channel_id=1, source_target_pairs={{0,2},{1,3},{2,0},{3,1},{4,6},{5,7},{6,4},{7,5},{8,10},{9,11},{10,... | collective-permute-start | bytes 20 | tf_op jit(solution)/shard_map/ppermute | solution.py:28
  20.4 4.8 %collective-permute-start.2 = (f32[]{:T(128)}, f32[]{:T(128)}, u32[]{:S(2)}, u32[]{:S(2)}) collective-permute-start(f32[]{:T(128)} %add.129), channel_id=1, source_target_pairs={{0,4},{1,5},{2,6},{3,7},{4,0},{5,1},{6,2},{7,3},{8,12},{9,13},{10,... | collective-permute-start | bytes 20 | tf_op jit(solution)/shard_map/ppermute | solution.py:28
  27.3 24.7 %all-to-all-start = ((bf16[72,8,768]{2,0,1:T(8,128)(2,1)}), bf16[72,8,768]{2,0,1:T(8,128)(2,1)S(1)}, u32[]{:S(2)}, u32[]{:S(2)}) async-start(bf16[72,8,768]{2,0,1:T(8,128)(2,1)} %copy.31), calls=%async_computation | async-start | bytes 1769472 | tf_op jit(solution)/shard_map/all_to_all | solution.py:82
  33.5 143.8 %all-gather.3.cloned.1.call-start = ((), (), s32[]{:S(2)}) async-start(), calls=%async_computation.3 | async-start | bytes 2457600 | tf_op jit(solution)/shard_map/all_gather | solution.py:99
  57.4 8.7 %collective-permute-start.3 = (f32[37,576]{1,0:T(8,128)S(1)}, f32[37,576]{1,0:T(8,128)S(1)}, u32[]{:S(2)}, u32[]{:S(2)}) collective-permute-start(f32[37,576]{1,0:T(8,128)S(1)} %get-tuple-element.25), channel_id=1, source_target_pairs={{0,1},{1,2},{2,3},{3,4},{4,5},{5,6},{6,7},{7,0},{8,9},{9,10},{10,1... | collective-permute-start | bytes 255752 | tf_op jit(solution)/shard_map/ppermute | solution.py:57
  58.6 7.7 %collective-permute-start.4 = (f32[37,576]{1,0:T(8,128)S(1)}, f32[37,576]{1,0:T(8,128)S(1)}, u32[]{:S(2)}, u32[]{:S(2)}) collective-permute-start(f32[37,576]{1,0:T(8,128)S(1)} %get-tuple-element.31), channel_id=1, source_target_pairs={{0,2},{1,3},{2,4},{3,5},{4,6},{5,7},{6,0},{7,1},{8,10},{9,11},{10,... | collective-permute-start | bytes 255752 | tf_op jit(solution)/shard_map/ppermute | solution.py:57
  58.6 12.2 %collective-permute-start.5 = (f32[37,576]{1,0:T(8,128)S(1)}, f32[37,576]{1,0:T(8,128)S(1)}, u32[]{:S(2)}, u32[]{:S(2)}) collective-permute-start(f32[37,576]{1,0:T(8,128)S(1)} %get-tuple-element.30), channel_id=1, source_target_pairs={{0,3},{1,4},{2,5},{3,6},{4,7},{5,0},{6,1},{7,2},{8,11},{9,12},{10,... | collective-permute-start | bytes 255752 | tf_op jit(solution)/shard_map/ppermute | solution.py:57
  60.6 10.6 %collective-permute-start.6 = (f32[37,576]{1,0:T(8,128)S(1)}, f32[37,576]{1,0:T(8,128)S(1)}, u32[]{:S(2)}, u32[]{:S(2)}) collective-permute-start(f32[37,576]{1,0:T(8,128)S(1)} %get-tuple-element.29), channel_id=1, source_target_pairs={{0,4},{1,5},{2,6},{3,7},{4,0},{5,1},{6,2},{7,3},{8,12},{9,13},{10,... | collective-permute-start | bytes 255752 | tf_op jit(solution)/shard_map/ppermute | solution.py:57
  62.8 8.5 %collective-permute-start.7 = (f32[37,576]{1,0:T(8,128)S(1)}, f32[37,576]{1,0:T(8,128)S(1)}, u32[]{:S(2)}, u32[]{:S(2)}) collective-permute-start(f32[37,576]{1,0:T(8,128)S(1)} %get-tuple-element.28), channel_id=1, source_target_pairs={{0,5},{1,6},{2,7},{3,0},{4,1},{5,2},{6,3},{7,4},{8,13},{9,14},{10,... | collective-permute-start | bytes 255752 | tf_op jit(solution)/shard_map/ppermute | solution.py:57
  66.0 7.8 %collective-permute-start.8 = (f32[37,576]{1,0:T(8,128)S(1)}, f32[37,576]{1,0:T(8,128)S(1)}, u32[]{:S(2)}, u32[]{:S(2)}) collective-permute-start(f32[37,576]{1,0:T(8,128)S(1)} %get-tuple-element.27), channel_id=1, source_target_pairs={{0,6},{1,7},{2,0},{3,1},{4,2},{5,3},{6,4},{7,5},{8,14},{9,15},{10,... | collective-permute-start | bytes 255752 | tf_op jit(solution)/shard_map/ppermute | solution.py:57
  66.4 7.5 %collective-permute-start.9 = (f32[37,576]{1,0:T(8,128)S(1)}, f32[37,576]{1,0:T(8,128)S(1)}, u32[]{:S(2)}, u32[]{:S(2)}) collective-permute-start(f32[37,576]{1,0:T(8,128)S(1)} %get-tuple-element.26), channel_id=1, source_target_pairs={{0,7},{1,0},{2,1},{3,2},{4,3},{5,4},{6,5},{7,6},{8,15},{9,8},{10,9... | collective-permute-start | bytes 255752 | tf_op jit(solution)/shard_map/ppermute | solution.py:57
  73.9 11.1 %collective-permute-start.10 = (bf16[37,576]{1,0:T(8,128)(2,1)S(1)}, bf16[37,576]{1,0:T(8,128)(2,1)S(1)}, u32[]{:S(2)}, u32[]{:S(2)}) collective-permute-start(bf16[37,576]{1,0:T(8,128)(2,1)S(1)} %get-tuple-element.7), channel_id=1, source_target_pairs={{0,1},{1,2},{2,3},{3,4},{4,5},{5,6},{6,7},{7,0},{8,9},{9,10},{10,1... | collective-permute-start | bytes 127880 | tf_op jit(solution)/shard_map/ppermute | solution.py:60
  76.5 11.4 %collective-permute-start.11 = (bf16[37,576]{1,0:T(8,128)(2,1)S(1)}, bf16[37,576]{1,0:T(8,128)(2,1)S(1)}, u32[]{:S(2)}, u32[]{:S(2)}) collective-permute-start(bf16[37,576]{1,0:T(8,128)(2,1)S(1)} %get-tuple-element.7), channel_id=1, source_target_pairs={{0,2},{1,3},{2,4},{3,5},{4,6},{5,7},{6,0},{7,1},{8,10},{9,11},{10,... | collective-permute-start | bytes 127880 | tf_op jit(solution)/shard_map/ppermute | solution.py:60
  79.5 8.6 %collective-permute-start.12 = (bf16[37,576]{1,0:T(8,128)(2,1)S(1)}, bf16[37,576]{1,0:T(8,128)(2,1)S(1)}, u32[]{:S(2)}, u32[]{:S(2)}) collective-permute-start(bf16[37,576]{1,0:T(8,128)(2,1)S(1)} %get-tuple-element.7), channel_id=1, source_target_pairs={{0,3},{1,4},{2,5},{3,6},{4,7},{5,0},{6,1},{7,2},{8,11},{9,12},{10,... | collective-permute-start | bytes 127880 | tf_op jit(solution)/shard_map/ppermute | solution.py:60
  81.2 6.9 %collective-permute-start.13 = (bf16[37,576]{1,0:T(8,128)(2,1)S(1)}, bf16[37,576]{1,0:T(8,128)(2,1)S(1)}, u32[]{:S(2)}, u32[]{:S(2)}) collective-permute-start(bf16[37,576]{1,0:T(8,128)(2,1)S(1)} %get-tuple-element.7), channel_id=1, source_target_pairs={{0,4},{1,5},{2,6},{3,7},{4,0},{5,1},{6,2},{7,3},{8,12},{9,13},{10,... | collective-permute-start | bytes 127880 | tf_op jit(solution)/shard_map/ppermute | solution.py:60
  81.9 6.2 %collective-permute-start.14 = (bf16[37,576]{1,0:T(8,128)(2,1)S(1)}, bf16[37,576]{1,0:T(8,128)(2,1)S(1)}, u32[]{:S(2)}, u32[]{:S(2)}) collective-permute-start(bf16[37,576]{1,0:T(8,128)(2,1)S(1)} %get-tuple-element.7), channel_id=1, source_target_pairs={{0,5},{1,6},{2,7},{3,0},{4,1},{5,2},{6,3},{7,4},{8,13},{9,14},{10,... | collective-permute-start | bytes 127880 | tf_op jit(solution)/shard_map/ppermute | solution.py:60
  85.1 4.6 %collective-permute-start.15 = (bf16[37,576]{1,0:T(8,128)(2,1)S(1)}, bf16[37,576]{1,0:T(8,128)(2,1)S(1)}, u32[]{:S(2)}, u32[]{:S(2)}) collective-permute-start(bf16[37,576]{1,0:T(8,128)(2,1)S(1)} %get-tuple-element.7), channel_id=1, source_target_pairs={{0,6},{1,7},{2,0},{3,1},{4,2},{5,3},{6,4},{7,5},{8,14},{9,15},{10,... | collective-permute-start | bytes 127880 | tf_op jit(solution)/shard_map/ppermute | solution.py:60
  87.9 4.2 %collective-permute-start.16 = (bf16[37,576]{1,0:T(8,128)(2,1)S(1)}, bf16[37,576]{1,0:T(8,128)(2,1)S(1)}, u32[]{:S(2)}, u32[]{:S(2)}) collective-permute-start(bf16[37,576]{1,0:T(8,128)(2,1)S(1)} %get-tuple-element.7), channel_id=1, source_target_pairs={{0,7},{1,0},{2,1},{3,2},{4,3},{5,4},{6,5},{7,6},{8,15},{9,8},{10,9... | collective-permute-start | bytes 127880 | tf_op jit(solution)/shard_map/ppermute | solution.py:60
  103.1 8.4 %collective-permute-start.17 = (f32[37,576]{1,0:T(8,128)S(1)}, f32[37,576]{1,0:T(8,128)S(1)}, u32[]{:S(2)}, u32[]{:S(2)}) collective-permute-start(f32[37,576]{1,0:T(8,128)S(1)} %get-tuple-element.18), channel_id=1, source_target_pairs={{0,1},{1,2},{2,3},{3,4},{4,5},{5,6},{6,7},{7,0},{8,9},{9,10},{10,1... | collective-permute-start | bytes 255752 | tf_op jit(solution)/shard_map/ppermute | solution.py:57
  103.1 8.4 %collective-permute-start.18 = (f32[37,576]{1,0:T(8,128)S(1)}, f32[37,576]{1,0:T(8,128)S(1)}, u32[]{:S(2)}, u32[]{:S(2)}) collective-permute-start(f32[37,576]{1,0:T(8,128)S(1)} %get-tuple-element.24), channel_id=1, source_target_pairs={{0,2},{1,3},{2,4},{3,5},{4,6},{5,7},{6,0},{7,1},{8,10},{9,11},{10,... | collective-permute-start | bytes 255752 | tf_op jit(solution)/shard_map/ppermute | solution.py:57
  103.9 12.4 %collective-permute-start.19 = (f32[37,576]{1,0:T(8,128)S(1)}, f32[37,576]{1,0:T(8,128)S(1)}, u32[]{:S(2)}, u32[]{:S(2)}) collective-permute-start(f32[37,576]{1,0:T(8,128)S(1)} %get-tuple-element.23), channel_id=1, source_target_pairs={{0,3},{1,4},{2,5},{3,6},{4,7},{5,0},{6,1},{7,2},{8,11},{9,12},{10,... | collective-permute-start | bytes 255752 | tf_op jit(solution)/shard_map/ppermute | solution.py:57
  106.9 9.6 %collective-permute-start.20 = (f32[37,576]{1,0:T(8,128)S(1)}, f32[37,576]{1,0:T(8,128)S(1)}, u32[]{:S(2)}, u32[]{:S(2)}) collective-permute-start(f32[37,576]{1,0:T(8,128)S(1)} %get-tuple-element.22), channel_id=1, source_target_pairs={{0,4},{1,5},{2,6},{3,7},{4,0},{5,1},{6,2},{7,3},{8,12},{9,13},{10,... | collective-permute-start | bytes 255752 | tf_op jit(solution)/shard_map/ppermute | solution.py:57
  108.4 8.1 %collective-permute-start.21 = (f32[37,576]{1,0:T(8,128)S(1)}, f32[37,576]{1,0:T(8,128)S(1)}, u32[]{:S(2)}, u32[]{:S(2)}) collective-permute-start(f32[37,576]{1,0:T(8,128)S(1)} %get-tuple-element.21), channel_id=1, source_target_pairs={{0,5},{1,6},{2,7},{3,0},{4,1},{5,2},{6,3},{7,4},{8,13},{9,14},{10,... | collective-permute-start | bytes 255752 | tf_op jit(solution)/shard_map/ppermute | solution.py:57
  111.5 5.0 %collective-permute-start.22 = (f32[37,576]{1,0:T(8,128)S(1)}, f32[37,576]{1,0:T(8,128)S(1)}, u32[]{:S(2)}, u32[]{:S(2)}) collective-permute-start(f32[37,576]{1,0:T(8,128)S(1)} %get-tuple-element.20), channel_id=1, source_target_pairs={{0,6},{1,7},{2,0},{3,1},{4,2},{5,3},{6,4},{7,5},{8,14},{9,15},{10,... | collective-permute-start | bytes 255752 | tf_op jit(solution)/shard_map/ppermute | solution.py:57
  111.5 5.3 %collective-permute-start.23 = (f32[37,576]{1,0:T(8,128)S(1)}, f32[37,576]{1,0:T(8,128)S(1)}, u32[]{:S(2)}, u32[]{:S(2)}) collective-permute-start(f32[37,576]{1,0:T(8,128)S(1)} %get-tuple-element.19), channel_id=1, source_target_pairs={{0,7},{1,0},{2,1},{3,2},{4,3},{5,4},{6,5},{7,6},{8,15},{9,8},{10,9... | collective-permute-start | bytes 255752 | tf_op jit(solution)/shard_map/ppermute | solution.py:57
  116.9 13.0 %collective-permute-start.24 = (bf16[37,576]{1,0:T(8,128)(2,1)S(1)}, bf16[37,576]{1,0:T(8,128)(2,1)S(1)}, u32[]{:S(2)}, u32[]{:S(2)}) collective-permute-start(bf16[37,576]{1,0:T(8,128)(2,1)S(1)} %get-tuple-element.5), channel_id=1, source_target_pairs={{0,1},{1,2},{2,3},{3,4},{4,5},{5,6},{6,7},{7,0},{8,9},{9,10},{10,1... | collective-permute-start | bytes 127880 | tf_op jit(solution)/shard_map/ppermute | solution.py:60
  120.4 12.5 %collective-permute-start.25 = (bf16[37,576]{1,0:T(8,128)(2,1)S(1)}, bf16[37,576]{1,0:T(8,128)(2,1)S(1)}, u32[]{:S(2)}, u32[]{:S(2)}) collective-permute-start(bf16[37,576]{1,0:T(8,128)(2,1)S(1)} %get-tuple-element.5), channel_id=1, source_target_pairs={{0,2},{1,3},{2,4},{3,5},{4,6},{5,7},{6,0},{7,1},{8,10},{9,11},{10,... | collective-permute-start | bytes 127880 | tf_op jit(solution)/shard_map/ppermute | solution.py:60
  124.2 8.9 %collective-permute-start.26 = (bf16[37,576]{1,0:T(8,128)(2,1)S(1)}, bf16[37,576]{1,0:T(8,128)(2,1)S(1)}, u32[]{:S(2)}, u32[]{:S(2)}) collective-permute-start(bf16[37,576]{1,0:T(8,128)(2,1)S(1)} %get-tuple-element.5), channel_id=1, source_target_pairs={{0,3},{1,4},{2,5},{3,6},{4,7},{5,0},{6,1},{7,2},{8,11},{9,12},{10,... | collective-permute-start | bytes 127880 | tf_op jit(solution)/shard_map/ppermute | solution.py:60
  126.1 7.0 %collective-permute-start.27 = (bf16[37,576]{1,0:T(8,128)(2,1)S(1)}, bf16[37,576]{1,0:T(8,128)(2,1)S(1)}, u32[]{:S(2)}, u32[]{:S(2)}) collective-permute-start(bf16[37,576]{1,0:T(8,128)(2,1)S(1)} %get-tuple-element.5), channel_id=1, source_target_pairs={{0,4},{1,5},{2,6},{3,7},{4,0},{5,1},{6,2},{7,3},{8,12},{9,13},{10,... | collective-permute-start | bytes 127880 | tf_op jit(solution)/shard_map/ppermute | solution.py:60
  127.1 6.1 %collective-permute-start.28 = (bf16[37,576]{1,0:T(8,128)(2,1)S(1)}, bf16[37,576]{1,0:T(8,128)(2,1)S(1)}, u32[]{:S(2)}, u32[]{:S(2)}) collective-permute-start(bf16[37,576]{1,0:T(8,128)(2,1)S(1)} %get-tuple-element.5), channel_id=1, source_target_pairs={{0,5},{1,6},{2,7},{3,0},{4,1},{5,2},{6,3},{7,4},{8,13},{9,14},{10,... | collective-permute-start | bytes 127880 | tf_op jit(solution)/shard_map/ppermute | solution.py:60
  130.0 4.6 %collective-permute-start.29 = (bf16[37,576]{1,0:T(8,128)(2,1)S(1)}, bf16[37,576]{1,0:T(8,128)(2,1)S(1)}, u32[]{:S(2)}, u32[]{:S(2)}) collective-permute-start(bf16[37,576]{1,0:T(8,128)(2,1)S(1)} %get-tuple-element.5), channel_id=1, source_target_pairs={{0,6},{1,7},{2,0},{3,1},{4,2},{5,3},{6,4},{7,5},{8,14},{9,15},{10,... | collective-permute-start | bytes 127880 | tf_op jit(solution)/shard_map/ppermute | solution.py:60
  132.8 4.3 %collective-permute-start.30 = (bf16[37,576]{1,0:T(8,128)(2,1)S(1)}, bf16[37,576]{1,0:T(8,128)(2,1)S(1)}, u32[]{:S(2)}, u32[]{:S(2)}) collective-permute-start(bf16[37,576]{1,0:T(8,128)(2,1)S(1)} %get-tuple-element.5), channel_id=1, source_target_pairs={{0,7},{1,0},{2,1},{3,2},{4,3},{5,4},{6,5},{7,6},{8,15},{9,8},{10,9... | collective-permute-start | bytes 127880 | tf_op jit(solution)/shard_map/ppermute | solution.py:60
  137.9 1.2 copy-start.3
  156.4 44.9 %all-gather.5.cloned.1.call-start = ((), (), s32[]{:S(2)}) async-start(), calls=%async_computation.4 | async-start | bytes 2457600 | tf_op jit(solution)/shard_map/all_gather | solution.py:99
  169.8 1.2 copy-start.2
Sparse Core Ops, SparseCore 0:
  156.5 20.7 all-gather.2
  179.4 21.8 all-gather.4

commit v3 on v1

--- a/solution.py
+++ b/solution.py
@@ -73,6 +73,23 @@
     return jnp.concatenate([top, bottom], axis=0)
 
 
+def gather_slots(mine, axis, size):
+    if size & (size - 1) != 0:
+        full = lax.all_gather(mine[None], axis, axis=0, tiled=True)
+        me = lax.axis_index(axis)
+        return jnp.take(full, jnp.arange(size, dtype=jnp.int32) ^ me, axis=0, mode="clip")
+    held = {0: mine}
+    bit = size // 2
+    while bit >= 1:
+        keys = sorted(held)
+        sent = jnp.stack([held[j] for j in keys])
+        got = lax.ppermute(sent, axis, [(i, i ^ bit) for i in range(size)])
+        for n, j in enumerate(keys):
+            held[j ^ bit] = got[n]
+        bit //= 2
+    return jnp.stack([held[j] for j in range(size)])
+
+
 def per_device(grad, momentum, owner):
     size = lax.axis_size("tensor")
     new_momentum = decay * momentum + grad.astype(jnp.float32)
@@ -88,15 +105,31 @@
         applied = jnp.dot(poly, columns, preferred_element_type=jnp.float32)
         columns = (coef_a * columns.astype(jnp.float32) + applied).astype(jnp.bfloat16)
     factor = 0.2 * math.sqrt(max(M, N))
-    back_rows = lax.all_to_all(columns, "tensor", split_axis=0, concat_axis=1, tiled=True)
-    scaled = (factor * back_rows.astype(jnp.float32)).astype(jnp.bfloat16)
-    every_slot = lax.all_gather(scaled[None], "dp", axis=0, tiled=True)
-    slots = every_slot.shape[0]
+    per = columns.shape[0] // size
+    half = per // 2
+    blocks = columns.reshape(size, per, columns.shape[1])
+    slots = lax.axis_size("dp")
     ids = jnp.arange(slots, dtype=jnp.int32)
     inverse = jnp.sum(
         jnp.where(owner[None, :] == ids[:, None], ids[None, :], 0), axis=1
     )
-    update = jnp.take(every_slot, inverse, axis=0)
+    where_from = inverse ^ lax.axis_index("dp")
+    pieces = []
+    for lo, hi in ((0, half), (half, per)):
+        piece = blocks[:, lo:hi, :].reshape(size * (hi - lo), columns.shape[1])
+        back_rows = lax.all_to_all(piece, "tensor", split_axis=0, concat_axis=1, tiled=True)
+        scaled = (factor * back_rows.astype(jnp.float32)).astype(jnp.bfloat16)
+        held = gather_slots(scaled, "dp", slots)
+        pieces.append(held)
+    rows = []
+    for m in range(slots):
+        rows.append(
+            jnp.concatenate(
+                [lax.dynamic_index_in_dim(p, where_from[m], 0, keepdims=True) for p in pieces],
+                axis=1,
+            )
+        )
+    update = jnp.concatenate(rows, axis=0)
     return (update, new_momentum)
 
 

time: 214 us -> 188 us (0.88)
  waiting for transfers between devices: 88.3 us -> 68.9 us
  blocking collectives: 23.8 us -> 15.2 us
  starting transfers between devices: 55.7 us -> 63 us
  between operations: 17.1 us -> 11.1 us
  other arithmetic: 7.71 us -> 10.1 us
    all_gather x1 -> x0, waiting for transfers between devices: 29.2 us -> none  [per_device(): every_slot = lax.all_gather(scaled[None], 'dp', axis=0, tiled=True)]
    all_to_all x1, blocking collectives: 23.8 us -> 15.2 us  [per_device(): lax.all_to_all(piece, 'tensor', split_axis=0, concat_axis=1, tiled=True)]
    all_to_all x0 -> x1, waiting for transfers between devices: none -> 7.8 us  [per_device(): lax.all_to_all(piece, 'tensor', split_axis=0, concat_axis=1, tiled=True)]
    ppermute x0 -> x4, starting transfers between devices: none -> 3.66 us  [gather_slots(): got = lax.ppermute(sent, axis, [(i, i ^ bit) for i in range(size)])]
    all_to_all x0 -> x1, starting transfers between devices: none -> 3.62 us  [per_device(): lax.all_to_all(piece, 'tensor', split_axis=0, concat_axis=1, tiled=True)]
    ppermute x0 -> x4, waiting for transfers between devices: none -> 3.03 us  [gather_slots(): got = lax.ppermute(sent, axis, [(i, i ^ bit) for i in range(size)])]
    concatenate x0 -> x1, other arithmetic: none -> 2.9 us  [per_device(): update = jnp.concatenate(rows, axis=0)]
    gather x1 -> x0, local copies, waits for them, and re-layouts: 2.77 us -> none  [per_device(): update = jnp.take(every_slot, inverse, axis=0)]
  transfers between devices with their start and end apart: 33 -> 37, of which waited for: 17 -> 20; matrix products, arithmetic and copies ran while one was open for 0% -> 2% of each run, Pallas kernels for 0% -> 0%
where the time goes in v3:
time: 188 us
  waiting for transfers between devices  68.9 us (37%)
  starting transfers between devices  63 us (34%)
  blocking collectives  15.2 us (8%)
  local copies, waits for them, and re-layouts  14.1 us (8%)
  between operations  11.1 us (6%)
  other arithmetic  10.1 us (5%)
  matrix products  5.17 us (3%)
    ppermute x14, waiting for transfers between devices, gram_allreduce(): acc = acc + lax.ppermute(rolled[s], axis, _shift_pairs(size, s))  21.1 us
    ppermute x14, starting transfers between devices, gram_allreduce(): acc = acc + lax.ppermute(rolled[s], axis, _shift_pairs(size, s))  19.4 us
    ppermute x14, starting transfers between devices, gram_allreduce(): lax.ppermute(mine, axis, _shift_pairs(size, s))  19.4 us
    all_to_all x1, waiting for transfers between devices, per_device(): lax.all_to_all(rows_here, 'tensor', split_axis=1, concat_axis=0, tiled=True)  18.4 us
    ppermute x14, waiting for transfers between devices, gram_allreduce(): lax.ppermute(mine, axis, _shift_pairs(size, s))  16 us
    all_to_all x1, blocking collectives, per_device(): lax.all_to_all(piece, 'tensor', split_axis=0, concat_axis=1, tiled=True)  15.2 us
    ppermute x3, starting transfers between devices, total_over(): lax.ppermute(value, axis, [(i, i ^ bit) for i in range(size)])  10.8 us
    all_to_all x1, waiting for transfers between devices, per_device(): lax.all_to_all(piece, 'tensor', split_axis=0, concat_axis=1, tiled=True)  7.8 us
  transfers between devices with their start and end apart: 37, of which 20 were waited for; matrix products, arithmetic and copies ran while one was open for 2% of the time, Pallas kernels for 0%

profile of v3, /device:TPU:0, one launch (start us, length us, event | category | flops | bytes accessed | tf_op | source)
XLA Modules:
  0.0 187.6 jit_solution(16320764303713601819)
XLA Ops:
  0.6 2.9 %multiply_reduce_fusion = (f32[]{:T(128)}, f32[1,72,6144]{2,1,0:T(8,128)S(1)}) fusion(bf16[1,72,6144]{2,1,0:T(8,128)(2,1)} %param.7, f32[1,72,6144]{2,1,0:T(8,128)} %param.8), kind=kLoop, calls=%fused_computation.14 | loop fusion | flops 3096575 | bytes 4423684 | tf_op jit(solution)/shard_map/reduce_sum | solution.py:97
  3.5 3.0 %collective-permute-start = (f32[]{:T(128)}, f32[]{:T(128)}, u32[]{:S(2)}, u32[]{:S(2)}) collective-permute-start(f32[]{:T(128)} %get-tuple-element.8), channel_id=1, source_target_pairs={{0,1},{1,0},{2,3},{3,2},{4,5},{5,4},{6,7},{7,6},{8,9},{9,8},{10,11... | collective-permute-start | bytes 20 | tf_op jit(solution)/shard_map/ppermute | solution.py:28
  6.5 1.8 collective-permute-done
  9.5 3.4 %collective-permute-start.1 = (f32[]{:T(128)}, f32[]{:T(128)}, u32[]{:S(2)}, u32[]{:S(2)}) collective-permute-start(f32[]{:T(128)} %add.129), channel_id=1, source_target_pairs={{0,2},{1,3},{2,0},{3,1},{4,6},{5,7},{6,4},{7,5},{8,10},{9,11},{10,... | collective-permute-start | bytes 20 | tf_op jit(solution)/shard_map/ppermute | solution.py:28
  13.9 4.4 %collective-permute-start.2 = (f32[]{:T(128)}, f32[]{:T(128)}, u32[]{:S(2)}, u32[]{:S(2)}) collective-permute-start(f32[]{:T(128)} %add.130), channel_id=1, source_target_pairs={{0,4},{1,5},{2,6},{3,7},{4,0},{5,1},{6,2},{7,3},{8,12},{9,13},{10,... | collective-permute-start | bytes 20 | tf_op jit(solution)/shard_map/ppermute | solution.py:28
  19.8 1.1 copy.23
  20.8 6.2 %all-to-all-start = ((bf16[72,8,768]{2,0,1:T(8,128)(2,1)}), bf16[72,8,768]{2,0,1:T(8,128)(2,1)S(1)}, u32[]{:S(2)}, u32[]{:S(2)}) async-start(bf16[72,8,768]{2,0,1:T(8,128)(2,1)} %copy.23), calls=%async_computation | async-start | bytes 1769472 | tf_op jit(solution)/shard_map/all_to_all | solution.py:99
  27.1 18.4 %all-to-all-done = bf16[72,8,768]{2,0,1:T(8,128)(2,1)S(1)} async-done(((bf16[72,8,768]{2,0,1:T(8,128)(2,1)}), bf16[72,8,768]{2,0,1:T(8,128)(2,1)S(1)}, u32[]{:S(2)}, u32[]{:S(2)}) %all-to-all-start) | async-done | bytes 884768 | tf_op jit(solution)/shard_map/all_to_all | solution.py:99
  45.5 0.9 fusion.72
  46.7 3.0 %gather_fusion = f32[288]{0:T(512)S(1)} fusion(f32[288,288]{1,0:T(8,128)S(1)} %get-tuple-element.23, s32[288]{0:T(512)S(1)} %or_reduce_fusion), kind=kCustom, calls=%fused_computation.4 | custom fusion | bytes 4608 | tf_op jit(solution)/shard_map/jit(diagonal)/cond/branch_0_fun/gather | solution.py:43
  50.9 1.3 collective-permute-start.3
  52.1 3.5 %collective-permute-start.9 = (f32[37,576]{1,0:T(8,128)S(1)}, f32[37,576]{1,0:T(8,128)S(1)}, u32[]{:S(2)}, u32[]{:S(2)}) collective-permute-start(f32[37,576]{1,0:T(8,128)S(1)} %get-tuple-element.38), channel_id=1, source_target_pairs={{0,7},{1,0},{2,1},{3,2},{4,3},{5,4},{6,5},{7,6},{8,15},{9,8},{10,9... | collective-permute-start | bytes 255752 | tf_op jit(solution)/shard_map/ppermute | solution.py:57
  55.8 2.8 %collective-permute-start.6 = (f32[37,576]{1,0:T(8,128)S(1)}, f32[37,576]{1,0:T(8,128)S(1)}, u32[]{:S(2)}, u32[]{:S(2)}) collective-permute-start(f32[37,576]{1,0:T(8,128)S(1)} %get-tuple-element.41), channel_id=1, source_target_pairs={{0,4},{1,5},{2,6},{3,7},{4,0},{5,1},{6,2},{7,3},{8,12},{9,13},{10,... | collective-permute-start | bytes 255752 | tf_op jit(solution)/shard_map/ppermute | solution.py:57
  58.7 0.8 collective-permute-done.3
  59.4 1.3 collective-permute-start.4
  60.7 0.8 collective-permute-done.8
  61.5 1.4 collective-permute-done.7
  62.9 7.2 %collective-permute-done.6 = f32[37,576]{1,0:T(8,128)S(1)} collective-permute-done((f32[37,576]{1,0:T(8,128)S(1)}, f32[37,576]{1,0:T(8,128)S(1)}, u32[]{:S(2)}, u32[]{:S(2)}) %collective-permute-start.6) | collective-permute-done | bytes 85280 | tf_op jit(solution)/shard_map/ppermute | solution.py:57
  71.1 0.8 collective-permute-start.15
  71.9 4.2 %collective-permute-start.14 = (bf16[37,576]{1,0:T(8,128)(2,1)S(1)}, bf16[37,576]{1,0:T(8,128)(2,1)S(1)}, u32[]{:S(2)}, u32[]{:S(2)}) collective-permute-start(bf16[37,576]{1,0:T(8,128)(2,1)S(1)} %get-tuple-element.7), channel_id=1, source_target_pairs={{0,5},{1,6},{2,7},{3,0},{4,1},{5,2},{6,3},{7,4},{8,13},{9,14},{10,... | collective-permute-start | bytes 127880 | tf_op jit(solution)/shard_map/ppermute | solution.py:60
  76.1 2.7 %collective-permute-start.13 = (bf16[37,576]{1,0:T(8,128)(2,1)S(1)}, bf16[37,576]{1,0:T(8,128)(2,1)S(1)}, u32[]{:S(2)}, u32[]{:S(2)}) collective-permute-start(bf16[37,576]{1,0:T(8,128)(2,1)S(1)} %get-tuple-element.7), channel_id=1, source_target_pairs={{0,4},{1,5},{2,6},{3,7},{4,0},{5,1},{6,2},{7,3},{8,12},{9,13},{10,... | collective-permute-start | bytes 127880 | tf_op jit(solution)/shard_map/ppermute | solution.py:60
  79.3 5.4 %collective-permute-done.11 = bf16[37,576]{1,0:T(8,128)(2,1)S(1)} collective-permute-done((bf16[37,576]{1,0:T(8,128)(2,1)S(1)}, bf16[37,576]{1,0:T(8,128)(2,1)S(1)}, u32[]{:S(2)}, u32[]{:S(2)}) %collective-permute-start.11) | collective-permute-done | bytes 42656 | tf_op jit(solution)/shard_map/ppermute | solution.py:60
  84.7 1.4 collective-permute-start.16
  86.2 2.6 %collective-permute-done.16 = bf16[37,576]{1,0:T(8,128)(2,1)S(1)} collective-permute-done((bf16[37,576]{1,0:T(8,128)(2,1)S(1)}, bf16[37,576]{1,0:T(8,128)(2,1)S(1)}, u32[]{:S(2)}, u32[]{:S(2)}) %collective-permute-start.16) | collective-permute-done | bytes 42656 | tf_op jit(solution)/shard_map/ppermute | solution.py:60
  90.3 1.7 add_convert_fusion.1
  92.0 0.9 fusion.73
  93.2 3.0 %gather_fusion.1 = f32[288]{0:T(512)S(1)} fusion(f32[288,288]{1,0:T(8,128)S(1)} %get-tuple-element.20, s32[288]{0:T(512)S(1)} %or_reduce_fusion), kind=kCustom, calls=%fused_computation.5 | custom fusion | bytes 4608 | tf_op jit(solution)/shard_map/jit(diagonal)/cond/branch_0_fun/gather | solution.py:43
  97.4 2.6 %collective-permute-start.17 = (f32[37,576]{1,0:T(8,128)S(1)}, f32[37,576]{1,0:T(8,128)S(1)}, u32[]{:S(2)}, u32[]{:S(2)}) collective-permute-start(f32[37,576]{1,0:T(8,128)S(1)} %get-tuple-element.30), channel_id=1, source_target_pairs={{0,1},{1,2},{2,3},{3,4},{4,5},{5,6},{6,7},{7,0},{8,9},{9,10},{10,1... | collective-permute-start | bytes 255752 | tf_op jit(solution)/shard_map/ppermute | solution.py:57
  100.0 2.1 %collective-permute-start.23 = (f32[37,576]{1,0:T(8,128)S(1)}, f32[37,576]{1,0:T(8,128)S(1)}, u32[]{:S(2)}, u32[]{:S(2)}) collective-permute-start(f32[37,576]{1,0:T(8,128)S(1)} %get-tuple-element.31), channel_id=1, source_target_pairs={{0,7},{1,0},{2,1},{3,2},{4,3},{5,4},{6,5},{7,6},{8,15},{9,8},{10,9... | collective-permute-start | bytes 255752 | tf_op jit(solution)/shard_map/ppermute | solution.py:57
  102.3 4.2 %collective-permute-start.20 = (f32[37,576]{1,0:T(8,128)S(1)}, f32[37,576]{1,0:T(8,128)S(1)}, u32[]{:S(2)}, u32[]{:S(2)}) collective-permute-start(f32[37,576]{1,0:T(8,128)S(1)} %get-tuple-element.34), channel_id=1, source_target_pairs={{0,4},{1,5},{2,6},{3,7},{4,0},{5,1},{6,2},{7,3},{8,12},{9,13},{10,... | collective-permute-start | bytes 255752 | tf_op jit(solution)/shard_map/ppermute | solution.py:57
  107.7 1.2 collective-permute-done.22
  109.1 8.2 %collective-permute-done.20 = f32[37,576]{1,0:T(8,128)S(1)} collective-permute-done((f32[37,576]{1,0:T(8,128)S(1)}, f32[37,576]{1,0:T(8,128)S(1)}, u32[]{:S(2)}, u32[]{:S(2)}) %collective-permute-start.20) | collective-permute-done | bytes 85280 | tf_op jit(solution)/shard_map/ppermute | solution.py:57
  118.6 3.7 %collective-permute-start.28 = (bf16[37,576]{1,0:T(8,128)(2,1)S(1)}, bf16[37,576]{1,0:T(8,128)(2,1)S(1)}, u32[]{:S(2)}, u32[]{:S(2)}) collective-permute-start(bf16[37,576]{1,0:T(8,128)(2,1)S(1)} %get-tuple-element.5), channel_id=1, source_target_pairs={{0,5},{1,6},{2,7},{3,0},{4,1},{5,2},{6,3},{7,4},{8,13},{9,14},{10,... | collective-permute-start | bytes 127880 | tf_op jit(solution)/shard_map/ppermute | solution.py:60
  122.3 3.4 %collective-permute-start.27 = (bf16[37,576]{1,0:T(8,128)(2,1)S(1)}, bf16[37,576]{1,0:T(8,128)(2,1)S(1)}, u32[]{:S(2)}, u32[]{:S(2)}) collective-permute-start(bf16[37,576]{1,0:T(8,128)(2,1)S(1)} %get-tuple-element.5), channel_id=1, source_target_pairs={{0,4},{1,5},{2,6},{3,7},{4,0},{5,1},{6,2},{7,3},{8,12},{9,13},{10,... | collective-permute-start | bytes 127880 | tf_op jit(solution)/shard_map/ppermute | solution.py:60
  126.3 5.4 %collective-permute-done.25 = bf16[37,576]{1,0:T(8,128)(2,1)S(1)} collective-permute-done((bf16[37,576]{1,0:T(8,128)(2,1)S(1)}, bf16[37,576]{1,0:T(8,128)(2,1)S(1)}, u32[]{:S(2)}, u32[]{:S(2)}) %collective-permute-start.25) | collective-permute-done | bytes 42656 | tf_op jit(solution)/shard_map/ppermute | solution.py:60
  131.7 1.4 collective-permute-start.30
  133.2 2.6 %collective-permute-done.30 = bf16[37,576]{1,0:T(8,128)(2,1)S(1)} collective-permute-done((bf16[37,576]{1,0:T(8,128)(2,1)S(1)}, bf16[37,576]{1,0:T(8,128)(2,1)S(1)}, u32[]{:S(2)}, u32[]{:S(2)}) %collective-permute-start.30) | collective-permute-done | bytes 42656 | tf_op jit(solution)/shard_map/ppermute | solution.py:60
  137.3 1.7 add_convert_fusion
  139.0 0.9 fusion.70
  139.9 15.2 %all_to_all.36 = bf16[8,36,768]{2,1,0:T(8,128)(2,1)S(1)} all-to-all(bf16[8,36,768]{2,1,0:T(8,128)(2,1)S(1)} %get-tuple-element.28), channel_id=1, replica_groups=mesh['dp'=4,'tensor'=8] {'tensor'}, dimensions={0} | all-to-all | bytes 884736 | tf_op jit(solution)/shard_map/all_to_all | solution.py:120
  155.2 3.6 %all-to-all-start.2 = ((bf16[8,36,768]{2,1,0:T(8,128)(2,1)}), bf16[8,36,768]{2,1,0:T(8,128)(2,1)S(1)}, u32[]{:S(2)}, u32[]{:S(2)}) async-start(bf16[8,36,768]{2,1,0:T(8,128)(2,1)} %get-tuple-element.29), calls=%async_computation.2 | async-start | bytes 983040 | tf_op jit(solution)/shard_map/all_to_all | solution.py:120
  159.2 1.5 collective-permute-start.31
  160.9 7.8 %all-to-all-done.2 = bf16[8,36,768]{2,1,0:T(8,128)(2,1)S(1)} async-done(((bf16[8,36,768]{2,1,0:T(8,128)(2,1)}), bf16[8,36,768]{2,1,0:T(8,128)(2,1)S(1)}, u32[]{:S(2)}, u32[]{:S(2)}) %all-to-all-start.2) | async-done | bytes 442400 | tf_op jit(solution)/shard_map/all_to_all | solution.py:120
  169.1 1.5 collective-permute-start.33
  170.7 1.4 collective-permute-done.31
  172.1 1.1 pad_maximum_fusion.2
  182.5 1.6 collective-permute-done.34
  184.7 2.9 %maximum_maximum_fusion = bf16[4,72,6144]{2,1,0:T(8,128)(2,1)} fusion(bf16[1,36,6144]{2,1,0:T(8,128)(2,1)S(1)} %get-tuple-element.15, bf16[1,36,6144]{2,1,0:T(8,128)(2,1)S(1)} %get-tuple-element.11, bf16[1,36,6144]{2,1,0:T(8,128)(2,1)S(1)} %get-tuple-element.16, bf16[1,36,6144]{2,1,0:T(8,128)(2,1)S(1)} %get-tuple-element.12, ...), kind=kLoop, calls=%fused_computation.6 | loop fusion | flops 28311552 | bytes 7077888 | tf_op jit(solution)/shard_map/concatenate | solution.py:132
  (119 shorter events, 15.6 us)
Async XLA Ops:
  0.6 18.7 %copy-start.1 = (bf16[1,72,6144]{2,1,0:T(8,128)(2,1)S(1)}, bf16[1,72,6144]{2,1,0:T(8,128)(2,1)}, u32[]{:S(2)}) copy-start(bf16[1,72,6144]{2,1,0:T(8,128)(2,1)} %param.7) | copy-start | bytes 2654212
  3.5 16.0 %copy-start = (f32[1,72,6144]{2,1,0:T(8,128)}, f32[1,72,6144]{2,1,0:T(8,128)S(1)}, u32[]{:S(2)}) copy-start(f32[1,72,6144]{2,1,0:T(8,128)S(1)} %get-tuple-element.9) | copy-start | bytes 5308420
  3.5 4.8 %collective-permute-start = (f32[]{:T(128)}, f32[]{:T(128)}, u32[]{:S(2)}, u32[]{:S(2)}) collective-permute-start(f32[]{:T(128)} %get-tuple-element.8), channel_id=1, source_target_pairs={{0,1},{1,0},{2,3},{3,2},{4,5},{5,4},{6,7},{7,6},{8,9},{9,8},{10,11... | collective-permute-start | bytes 20 | tf_op jit(solution)/shard_map/ppermute | solution.py:28
  9.5 3.8 %collective-permute-start.1 = (f32[]{:T(128)}, f32[]{:T(128)}, u32[]{:S(2)}, u32[]{:S(2)}) collective-permute-start(f32[]{:T(128)} %add.129), channel_id=1, source_target_pairs={{0,2},{1,3},{2,0},{3,1},{4,6},{5,7},{6,4},{7,5},{8,10},{9,11},{10,... | collective-permute-start | bytes 20 | tf_op jit(solution)/shard_map/ppermute | solution.py:28
  13.9 4.8 %collective-permute-start.2 = (f32[]{:T(128)}, f32[]{:T(128)}, u32[]{:S(2)}, u32[]{:S(2)}) collective-permute-start(f32[]{:T(128)} %add.130), channel_id=1, source_target_pairs={{0,4},{1,5},{2,6},{3,7},{4,0},{5,1},{6,2},{7,3},{8,12},{9,13},{10,... | collective-permute-start | bytes 20 | tf_op jit(solution)/shard_map/ppermute | solution.py:28
  20.8 24.7 %all-to-all-start = ((bf16[72,8,768]{2,0,1:T(8,128)(2,1)}), bf16[72,8,768]{2,0,1:T(8,128)(2,1)S(1)}, u32[]{:S(2)}, u32[]{:S(2)}) async-start(bf16[72,8,768]{2,0,1:T(8,128)(2,1)} %copy.23), calls=%async_computation | async-start | bytes 1769472 | tf_op jit(solution)/shard_map/all_to_all | solution.py:99
  50.9 8.5 %collective-permute-start.3 = (f32[37,576]{1,0:T(8,128)S(1)}, f32[37,576]{1,0:T(8,128)S(1)}, u32[]{:S(2)}, u32[]{:S(2)}) collective-permute-start(f32[37,576]{1,0:T(8,128)S(1)} %get-tuple-element.37), channel_id=1, source_target_pairs={{0,1},{1,2},{2,3},{3,4},{4,5},{5,6},{6,7},{7,0},{8,9},{9,10},{10,1... | collective-permute-start | bytes 255752 | tf_op jit(solution)/shard_map/ppermute | solution.py:57
  52.1 7.3 %collective-permute-start.9 = (f32[37,576]{1,0:T(8,128)S(1)}, f32[37,576]{1,0:T(8,128)S(1)}, u32[]{:S(2)}, u32[]{:S(2)}) collective-permute-start(f32[37,576]{1,0:T(8,128)S(1)} %get-tuple-element.38), channel_id=1, source_target_pairs={{0,7},{1,0},{2,1},{3,2},{4,3},{5,4},{6,5},{7,6},{8,15},{9,8},{10,9... | collective-permute-start | bytes 255752 | tf_op jit(solution)/shard_map/ppermute | solution.py:57
  55.7 5.8 %collective-permute-start.8 = (f32[37,576]{1,0:T(8,128)S(1)}, f32[37,576]{1,0:T(8,128)S(1)}, u32[]{:S(2)}, u32[]{:S(2)}) collective-permute-start(f32[37,576]{1,0:T(8,128)S(1)} %get-tuple-element.39), channel_id=1, source_target_pairs={{0,6},{1,7},{2,0},{3,1},{4,2},{5,3},{6,4},{7,5},{8,14},{9,15},{10,... | collective-permute-start | bytes 255752 | tf_op jit(solution)/shard_map/ppermute | solution.py:57
  55.7 7.2 %collective-permute-start.7 = (f32[37,576]{1,0:T(8,128)S(1)}, f32[37,576]{1,0:T(8,128)S(1)}, u32[]{:S(2)}, u32[]{:S(2)}) collective-permute-start(f32[37,576]{1,0:T(8,128)S(1)} %get-tuple-element.40), channel_id=1, source_target_pairs={{0,5},{1,6},{2,7},{3,0},{4,1},{5,2},{6,3},{7,4},{8,13},{9,14},{10,... | collective-permute-start | bytes 255752 | tf_op jit(solution)/shard_map/ppermute | solution.py:57
  55.8 14.4 %collective-permute-start.6 = (f32[37,576]{1,0:T(8,128)S(1)}, f32[37,576]{1,0:T(8,128)S(1)}, u32[]{:S(2)}, u32[]{:S(2)}) collective-permute-start(f32[37,576]{1,0:T(8,128)S(1)} %get-tuple-element.41), channel_id=1, source_target_pairs={{0,4},{1,5},{2,6},{3,7},{4,0},{5,1},{6,2},{7,3},{8,12},{9,13},{10,... | collective-permute-start | bytes 255752 | tf_op jit(solution)/shard_map/ppermute | solution.py:57
  59.4 11.5 %collective-permute-start.5 = (f32[37,576]{1,0:T(8,128)S(1)}, f32[37,576]{1,0:T(8,128)S(1)}, u32[]{:S(2)}, u32[]{:S(2)}) collective-permute-start(f32[37,576]{1,0:T(8,128)S(1)} %get-tuple-element.42), channel_id=1, source_target_pairs={{0,3},{1,4},{2,5},{3,6},{4,7},{5,0},{6,1},{7,2},{8,11},{9,12},{10,... | collective-permute-start | bytes 255752 | tf_op jit(solution)/shard_map/ppermute | solution.py:57
  59.4 11.5 %collective-permute-start.4 = (f32[37,576]{1,0:T(8,128)S(1)}, f32[37,576]{1,0:T(8,128)S(1)}, u32[]{:S(2)}, u32[]{:S(2)}) collective-permute-start(f32[37,576]{1,0:T(8,128)S(1)} %get-tuple-element.43), channel_id=1, source_target_pairs={{0,2},{1,3},{2,4},{3,5},{4,6},{5,7},{6,0},{7,1},{8,10},{9,11},{10,... | collective-permute-start | bytes 255752 | tf_op jit(solution)/shard_map/ppermute | solution.py:57
  71.0 7.8 %collective-permute-start.10 = (bf16[37,576]{1,0:T(8,128)(2,1)S(1)}, bf16[37,576]{1,0:T(8,128)(2,1)S(1)}, u32[]{:S(2)}, u32[]{:S(2)}) collective-permute-start(bf16[37,576]{1,0:T(8,128)(2,1)S(1)} %get-tuple-element.7), channel_id=1, source_target_pairs={{0,1},{1,2},{2,3},{3,4},{4,5},{5,6},{6,7},{7,0},{8,9},{9,10},{10,1... | collective-permute-start | bytes 127880 | tf_op jit(solution)/shard_map/ppermute | solution.py:60
  71.1 15.2 %collective-permute-start.15 = (bf16[37,576]{1,0:T(8,128)(2,1)S(1)}, bf16[37,576]{1,0:T(8,128)(2,1)S(1)}, u32[]{:S(2)}, u32[]{:S(2)}) collective-permute-start(bf16[37,576]{1,0:T(8,128)(2,1)S(1)} %get-tuple-element.7), channel_id=1, source_target_pairs={{0,6},{1,7},{2,0},{3,1},{4,2},{5,3},{6,4},{7,5},{8,14},{9,15},{10,... | collective-permute-start | bytes 127880 | tf_op jit(solution)/shard_map/ppermute | solution.py:60
  71.9 14.3 %collective-permute-start.14 = (bf16[37,576]{1,0:T(8,128)(2,1)S(1)}, bf16[37,576]{1,0:T(8,128)(2,1)S(1)}, u32[]{:S(2)}, u32[]{:S(2)}) collective-permute-start(bf16[37,576]{1,0:T(8,128)(2,1)S(1)} %get-tuple-element.7), channel_id=1, source_target_pairs={{0,5},{1,6},{2,7},{3,0},{4,1},{5,2},{6,3},{7,4},{8,13},{9,14},{10,... | collective-permute-start | bytes 127880 | tf_op jit(solution)/shard_map/ppermute | solution.py:60
  76.1 10.1 %collective-permute-start.13 = (bf16[37,576]{1,0:T(8,128)(2,1)S(1)}, bf16[37,576]{1,0:T(8,128)(2,1)S(1)}, u32[]{:S(2)}, u32[]{:S(2)}) collective-permute-start(bf16[37,576]{1,0:T(8,128)(2,1)S(1)} %get-tuple-element.7), channel_id=1, source_target_pairs={{0,4},{1,5},{2,6},{3,7},{4,0},{5,1},{6,2},{7,3},{8,12},{9,13},{10,... | collective-permute-start | bytes 127880 | tf_op jit(solution)/shard_map/ppermute | solution.py:60
  78.7 7.4 %collective-permute-start.12 = (bf16[37,576]{1,0:T(8,128)(2,1)S(1)}, bf16[37,576]{1,0:T(8,128)(2,1)S(1)}, u32[]{:S(2)}, u32[]{:S(2)}) collective-permute-start(bf16[37,576]{1,0:T(8,128)(2,1)S(1)} %get-tuple-element.7), channel_id=1, source_target_pairs={{0,3},{1,4},{2,5},{3,6},{4,7},{5,0},{6,1},{7,2},{8,11},{9,12},{10,... | collective-permute-start | bytes 127880 | tf_op jit(solution)/shard_map/ppermute | solution.py:60
  78.8 5.9 %collective-permute-start.11 = (bf16[37,576]{1,0:T(8,128)(2,1)S(1)}, bf16[37,576]{1,0:T(8,128)(2,1)S(1)}, u32[]{:S(2)}, u32[]{:S(2)}) collective-permute-start(bf16[37,576]{1,0:T(8,128)(2,1)S(1)} %get-tuple-element.7), channel_id=1, source_target_pairs={{0,2},{1,3},{2,4},{3,5},{4,6},{5,7},{6,0},{7,1},{8,10},{9,11},{10,... | collective-permute-start | bytes 127880 | tf_op jit(solution)/shard_map/ppermute | solution.py:60
  84.7 4.1 %collective-permute-start.16 = (bf16[37,576]{1,0:T(8,128)(2,1)S(1)}, bf16[37,576]{1,0:T(8,128)(2,1)S(1)}, u32[]{:S(2)}, u32[]{:S(2)}) collective-permute-start(bf16[37,576]{1,0:T(8,128)(2,1)S(1)} %get-tuple-element.7), channel_id=1, source_target_pairs={{0,7},{1,0},{2,1},{3,2},{4,3},{5,4},{6,5},{7,6},{8,15},{9,8},{10,9... | collective-permute-start | bytes 127880 | tf_op jit(solution)/shard_map/ppermute | solution.py:60
  97.4 9.1 %collective-permute-start.17 = (f32[37,576]{1,0:T(8,128)S(1)}, f32[37,576]{1,0:T(8,128)S(1)}, u32[]{:S(2)}, u32[]{:S(2)}) collective-permute-start(f32[37,576]{1,0:T(8,128)S(1)} %get-tuple-element.30), channel_id=1, source_target_pairs={{0,1},{1,2},{2,3},{3,4},{4,5},{5,6},{6,7},{7,0},{8,9},{9,10},{10,1... | collective-permute-start | bytes 255752 | tf_op jit(solution)/shard_map/ppermute | solution.py:57
  100.0 7.1 %collective-permute-start.23 = (f32[37,576]{1,0:T(8,128)S(1)}, f32[37,576]{1,0:T(8,128)S(1)}, u32[]{:S(2)}, u32[]{:S(2)}) collective-permute-start(f32[37,576]{1,0:T(8,128)S(1)} %get-tuple-element.31), channel_id=1, source_target_pairs={{0,7},{1,0},{2,1},{3,2},{4,3},{5,4},{6,5},{7,6},{8,15},{9,8},{10,9... | collective-permute-start | bytes 255752 | tf_op jit(solution)/shard_map/ppermute | solution.py:57
  102.2 6.8 %collective-permute-start.22 = (f32[37,576]{1,0:T(8,128)S(1)}, f32[37,576]{1,0:T(8,128)S(1)}, u32[]{:S(2)}, u32[]{:S(2)}) collective-permute-start(f32[37,576]{1,0:T(8,128)S(1)} %get-tuple-element.32), channel_id=1, source_target_pairs={{0,6},{1,7},{2,0},{3,1},{4,2},{5,3},{6,4},{7,5},{8,14},{9,15},{10,... | collective-permute-start | bytes 255752 | tf_op jit(solution)/shard_map/ppermute | solution.py:57
  102.2 6.9 %collective-permute-start.21 = (f32[37,576]{1,0:T(8,128)S(1)}, f32[37,576]{1,0:T(8,128)S(1)}, u32[]{:S(2)}, u32[]{:S(2)}) collective-permute-start(f32[37,576]{1,0:T(8,128)S(1)} %get-tuple-element.33), channel_id=1, source_target_pairs={{0,5},{1,6},{2,7},{3,0},{4,1},{5,2},{6,3},{7,4},{8,13},{9,14},{10,... | collective-permute-start | bytes 255752 | tf_op jit(solution)/shard_map/ppermute | solution.py:57
  102.3 14.9 %collective-permute-start.20 = (f32[37,576]{1,0:T(8,128)S(1)}, f32[37,576]{1,0:T(8,128)S(1)}, u32[]{:S(2)}, u32[]{:S(2)}) collective-permute-start(f32[37,576]{1,0:T(8,128)S(1)} %get-tuple-element.34), channel_id=1, source_target_pairs={{0,4},{1,5},{2,6},{3,7},{4,0},{5,1},{6,2},{7,3},{8,12},{9,13},{10,... | collective-permute-start | bytes 255752 | tf_op jit(solution)/shard_map/ppermute | solution.py:57
  106.5 11.4 %collective-permute-start.19 = (f32[37,576]{1,0:T(8,128)S(1)}, f32[37,576]{1,0:T(8,128)S(1)}, u32[]{:S(2)}, u32[]{:S(2)}) collective-permute-start(f32[37,576]{1,0:T(8,128)S(1)} %get-tuple-element.35), channel_id=1, source_target_pairs={{0,3},{1,4},{2,5},{3,6},{4,7},{5,0},{6,1},{7,2},{8,11},{9,12},{10,... | collective-permute-start | bytes 255752 | tf_op jit(solution)/shard_map/ppermute | solution.py:57
  107.1 10.8 %collective-permute-start.18 = (f32[37,576]{1,0:T(8,128)S(1)}, f32[37,576]{1,0:T(8,128)S(1)}, u32[]{:S(2)}, u32[]{:S(2)}) collective-permute-start(f32[37,576]{1,0:T(8,128)S(1)} %get-tuple-element.36), channel_id=1, source_target_pairs={{0,2},{1,3},{2,4},{3,5},{4,6},{5,7},{6,0},{7,1},{8,10},{9,11},{10,... | collective-permute-start | bytes 255752 | tf_op jit(solution)/shard_map/ppermute | solution.py:57
  118.0 7.7 %collective-permute-start.24 = (bf16[37,576]{1,0:T(8,128)(2,1)S(1)}, bf16[37,576]{1,0:T(8,128)(2,1)S(1)}, u32[]{:S(2)}, u32[]{:S(2)}) collective-permute-start(bf16[37,576]{1,0:T(8,128)(2,1)S(1)} %get-tuple-element.5), channel_id=1, source_target_pairs={{0,1},{1,2},{2,3},{3,4},{4,5},{5,6},{6,7},{7,0},{8,9},{9,10},{10,1... | collective-permute-start | bytes 127880 | tf_op jit(solution)/shard_map/ppermute | solution.py:60
  118.0 15.1 %collective-permute-start.29 = (bf16[37,576]{1,0:T(8,128)(2,1)S(1)}, bf16[37,576]{1,0:T(8,128)(2,1)S(1)}, u32[]{:S(2)}, u32[]{:S(2)}) collective-permute-start(bf16[37,576]{1,0:T(8,128)(2,1)S(1)} %get-tuple-element.5), channel_id=1, source_target_pairs={{0,6},{1,7},{2,0},{3,1},{4,2},{5,3},{6,4},{7,5},{8,14},{9,15},{10,... | collective-permute-start | bytes 127880 | tf_op jit(solution)/shard_map/ppermute | solution.py:60
  118.6 14.5 %collective-permute-start.28 = (bf16[37,576]{1,0:T(8,128)(2,1)S(1)}, bf16[37,576]{1,0:T(8,128)(2,1)S(1)}, u32[]{:S(2)}, u32[]{:S(2)}) collective-permute-start(bf16[37,576]{1,0:T(8,128)(2,1)S(1)} %get-tuple-element.5), channel_id=1, source_target_pairs={{0,5},{1,6},{2,7},{3,0},{4,1},{5,2},{6,3},{7,4},{8,13},{9,14},{10,... | collective-permute-start | bytes 127880 | tf_op jit(solution)/shard_map/ppermute | solution.py:60
  122.3 10.8 %collective-permute-start.27 = (bf16[37,576]{1,0:T(8,128)(2,1)S(1)}, bf16[37,576]{1,0:T(8,128)(2,1)S(1)}, u32[]{:S(2)}, u32[]{:S(2)}) collective-permute-start(bf16[37,576]{1,0:T(8,128)(2,1)S(1)} %get-tuple-element.5), channel_id=1, source_target_pairs={{0,4},{1,5},{2,6},{3,7},{4,0},{5,1},{6,2},{7,3},{8,12},{9,13},{10,... | collective-permute-start | bytes 127880 | tf_op jit(solution)/shard_map/ppermute | solution.py:60
  125.7 7.4 %collective-permute-start.26 = (bf16[37,576]{1,0:T(8,128)(2,1)S(1)}, bf16[37,576]{1,0:T(8,128)(2,1)S(1)}, u32[]{:S(2)}, u32[]{:S(2)}) collective-permute-start(bf16[37,576]{1,0:T(8,128)(2,1)S(1)} %get-tuple-element.5), channel_id=1, source_target_pairs={{0,3},{1,4},{2,5},{3,6},{4,7},{5,0},{6,1},{7,2},{8,11},{9,12},{10,... | collective-permute-start | bytes 127880 | tf_op jit(solution)/shard_map/ppermute | solution.py:60
  125.7 6.0 %collective-permute-start.25 = (bf16[37,576]{1,0:T(8,128)(2,1)S(1)}, bf16[37,576]{1,0:T(8,128)(2,1)S(1)}, u32[]{:S(2)}, u32[]{:S(2)}) collective-permute-start(bf16[37,576]{1,0:T(8,128)(2,1)S(1)} %get-tuple-element.5), channel_id=1, source_target_pairs={{0,2},{1,3},{2,4},{3,5},{4,6},{5,7},{6,0},{7,1},{8,10},{9,11},{10,... | collective-permute-start | bytes 127880 | tf_op jit(solution)/shard_map/ppermute | solution.py:60
  131.7 4.1 %collective-permute-start.30 = (bf16[37,576]{1,0:T(8,128)(2,1)S(1)}, bf16[37,576]{1,0:T(8,128)(2,1)S(1)}, u32[]{:S(2)}, u32[]{:S(2)}) collective-permute-start(bf16[37,576]{1,0:T(8,128)(2,1)S(1)} %get-tuple-element.5), channel_id=1, source_target_pairs={{0,7},{1,0},{2,1},{3,2},{4,3},{5,4},{6,5},{7,6},{8,15},{9,8},{10,9... | collective-permute-start | bytes 127880 | tf_op jit(solution)/shard_map/ppermute | solution.py:60
  155.2 5.6 %copy-start.2 = (s32[4]{0:T(128)S(1)}, s32[4]{0:T(128)}, u32[]{:S(2)}) copy-start(s32[4]{0:T(128)} %param.9) | copy-start | bytes 52
  155.2 13.5 %all-to-all-start.2 = ((bf16[8,36,768]{2,1,0:T(8,128)(2,1)}), bf16[8,36,768]{2,1,0:T(8,128)(2,1)S(1)}, u32[]{:S(2)}, u32[]{:S(2)}) async-start(bf16[8,36,768]{2,1,0:T(8,128)(2,1)} %get-tuple-element.29), calls=%async_computation.2 | async-start | bytes 983040 | tf_op jit(solution)/shard_map/all_to_all | solution.py:120
  159.2 12.8 %collective-permute-start.31 = (bf16[1,36,6144]{2,1,0:T(8,128)(2,1)S(1)}, bf16[1,36,6144]{2,1,0:T(8,128)(2,1)S(1)}, u32[]{:S(2)}, u32[]{:S(2)}) collective-permute-start(bf16[1,36,6144]{2,1,0:T(8,128)(2,1)S(1)} %convert_element_type.113), channel_id=1, source_target_pairs={{0,16},{8,24},{16,0},{24,8},{1,17},{9,25},{17,1},{25,9},{2,18},{10... | collective-permute-start | bytes 1327112 | tf_op jit(solution)/shard_map/ppermute | solution.py:86
  169.1 12.1 %collective-permute-start.33 = (bf16[1,36,6144]{2,1,0:T(8,128)(2,1)S(1)}, bf16[1,36,6144]{2,1,0:T(8,128)(2,1)S(1)}, u32[]{:S(2)}, u32[]{:S(2)}) collective-permute-start(bf16[1,36,6144]{2,1,0:T(8,128)(2,1)S(1)} %convert_element_type.117), channel_id=1, source_target_pairs={{0,16},{8,24},{16,0},{24,8},{1,17},{9,25},{17,1},{25,9},{2,18},{10... | collective-permute-start | bytes 1327112 | tf_op jit(solution)/shard_map/ppermute | solution.py:86
  173.1 8.9 %collective-permute-start.32 = (bf16[2,36,6144]{2,1,0:T(8,128)(2,1)}, bf16[2,36,6144]{2,1,0:T(8,128)(2,1)S(1)}, u32[]{:S(2)}, u32[]{:S(2)}) collective-permute-start(bf16[2,36,6144]{2,1,0:T(8,128)(2,1)} %pad_maximum_fusion.2), channel_id=1, source_target_pairs={{0,8},{8,0},{16,24},{24,16},{1,9},{9,1},{17,25},{25,17},{2,10},{10... | collective-permute-start | bytes 2654216 | tf_op jit(solution)/shard_map/ppermute | solution.py:86
  181.4 2.8 %collective-permute-start.34 = (bf16[2,36,6144]{2,1,0:T(8,128)(2,1)S(1)}, bf16[2,36,6144]{2,1,0:T(8,128)(2,1)S(1)}, u32[]{:S(2)}, u32[]{:S(2)}) collective-permute-start(bf16[2,36,6144]{2,1,0:T(8,128)(2,1)S(1)} %pad_maximum_fusion.3), channel_id=1, source_target_pairs={{0,8},{8,0},{16,24},{24,16},{1,9},{9,1},{17,25},{25,17},{2,10},{10... | collective-permute-start | bytes 2654216 | tf_op jit(solution)/shard_map/ppermute | solution.py:86

commit v4 on v3

--- a/solution.py
+++ b/solution.py
@@ -22,13 +22,9 @@
 
 
 def total_over(value, axis, size):
-    if size & (size - 1) == 0:
-        bit = 1
-        while bit < size:
-            value = value + lax.ppermute(value, axis, [(i, i ^ bit) for i in range(size)])
-            bit *= 2
-        return value
-    return lax.psum(value, axis)
+    spread = jnp.broadcast_to(value, (size, 1))
+    got = lax.all_to_all(spread, axis, split_axis=0, concat_axis=0, tiled=True)
+    return jnp.sum(got)
 
 
 def gram_allreduce(partial, axis, size):
@@ -56,12 +52,8 @@
     for s in range(1, size):
         acc = acc + lax.ppermute(rolled[s], axis, _shift_pairs(size, s))
     mine = acc.astype(jnp.bfloat16)
-    got = [mine] + [
-        lax.ppermute(mine, axis, _shift_pairs(size, s)) for s in range(1, size)
-    ]
-    stacked = jnp.stack(got)
-    back = (me - jnp.arange(size, dtype=jnp.int32)) % size
-    full = jnp.take(stacked, back, axis=0).reshape(rows, 2 * h)
+    spread = jnp.broadcast_to(mine[None], (size,) + mine.shape)
+    full = lax.all_to_all(spread, axis, split_axis=0, concat_axis=0, tiled=True).reshape(rows, 2 * h)
     folded_r = full[:h, :h]
     block_br = full[:h, h:]
     diag_cr = full[h, :h]

time: 188 us -> 190 us (1.011)
  blocking collectives: 15.2 us -> 62.3 us
  starting transfers between devices: 63 us -> 29.1 us
  waiting for transfers between devices: 68.9 us -> 58.4 us
    all_to_all x0 -> x3, blocking collectives: none -> 45.5 us  [the longest x2 31.9 us: gram_allreduce(): lax.all_to_all(spread, axis, split_axis=0, concat_axis=0, tiled=True)]
    ppermute x17 -> x0, starting transfers between devices: 30.2 us -> none  [the longest x14 19.4 us: gram_allreduce(): lax.ppermute(mine, axis, _shift_pairs(size, s))]
    ppermute x17 -> x0, waiting for transfers between devices: 18.5 us -> none  [the longest x14 16 us: gram_allreduce(): lax.ppermute(mine, axis, _shift_pairs(size, s))]
    all_to_all x1, waiting for transfers between devices: 7.8 us -> 11.3 us  [per_device(): lax.all_to_all(piece, 'tensor', split_axis=0, concat_axis=1, tiled=True)]
    all_to_all x1, waiting for transfers between devices: 18.4 us -> 21 us  [per_device(): lax.all_to_all(rows_here, 'tensor', split_axis=1, concat_axis=0, tiled=True)]
    all_to_all x1, starting transfers between devices: 6.16 us -> 3.55 us  [per_device(): lax.all_to_all(rows_here, 'tensor', split_axis=1, concat_axis=0, tiled=True)]
    ppermute x14, waiting for transfers between devices: 21.1 us -> 23.4 us  [gram_allreduce(): acc = acc + lax.ppermute(rolled[s], axis, _shift_pairs(size, s))]
  transfers between devices with their start and end apart: 37 -> 20, of which waited for: 20 -> 15; matrix products, arithmetic and copies ran while one was open for 2% -> 2% of each run, Pallas kernels for 0% -> 0%
where the time goes in v4:
time: 190 us
  blocking collectives  62.3 us (33%)
  waiting for transfers between devices  58.4 us (31%)
  starting transfers between devices  29.1 us (15%)
  local copies, waits for them, and re-layouts  14.7 us (8%)
  other arithmetic  10.5 us (6%)
  between operations  9.45 us (5%)
  matrix products  5.14 us (3%)
    all_to_all x2, blocking collectives, gram_allreduce(): lax.all_to_all(spread, axis, split_axis=0, concat_axis=0, tiled=True)  31.9 us
    ppermute x14, waiting for transfers between devices, gram_allreduce(): acc = acc + lax.ppermute(rolled[s], axis, _shift_pairs(size, s))  23.4 us
    all_to_all x1, waiting for transfers between devices, per_device(): lax.all_to_all(rows_here, 'tensor', split_axis=1, concat_axis=0, tiled=True)  21 us
    ppermute x14, starting transfers between devices, gram_allreduce(): acc = acc + lax.ppermute(rolled[s], axis, _shift_pairs(size, s))  18.5 us
    all_to_all x1, blocking collectives, per_device(): lax.all_to_all(piece, 'tensor', split_axis=0, concat_axis=1, tiled=True)  16.7 us
    all_to_all x1, blocking collectives, total_over(): got = lax.all_to_all(spread, axis, split_axis=0, concat_axis=0, tiled=True)  13.6 us
    all_to_all x1, waiting for transfers between devices, per_device(): lax.all_to_all(piece, 'tensor', split_axis=0, concat_axis=1, tiled=True)  11.3 us
    gather x2, local copies, waits for them, and re-layouts, gram_allreduce(): diag_c = jnp.diagonal(lower_c)  5.98 us
  transfers between devices with their start and end apart: 20, of which 15 were waited for; matrix products, arithmetic and copies ran while one was open for 2% of the time, Pallas kernels for 0%

profile of v4, /device:TPU:0, one launch (start us, length us, event | category | flops | bytes accessed | tf_op | source)
XLA Modules:
  0.0 189.5 jit_solution(2723451408957819853)
XLA Ops:
  0.6 2.9 %multiply_reduce_fusion = (f32[]{:T(128)}, f32[1,72,6144]{2,1,0:T(8,128)S(1)}) fusion(bf16[1,72,6144]{2,1,0:T(8,128)(2,1)} %param.5, f32[1,72,6144]{2,1,0:T(8,128)} %param.6), kind=kLoop, calls=%fused_computation.12 | loop fusion | flops 3096575 | bytes 4423684 | tf_op jit(solution)/shard_map/reduce_sum | solution.py:89
  3.5 0.6 broadcast_in_dim.68
  4.2 13.6 %all_to_all.52 = f32[8,1,1]{2,1,0:T(1,128)S(1)} all-to-all(f32[8,1,1]{2,1,0:T(1,128)S(1)} %broadcast_in_dim.68), channel_id=1, replica_groups=mesh['dp'=4,'tensor'=8] {'tensor'}, dimensions={0} | all-to-all | bytes 64 | tf_op jit(solution)/shard_map/all_to_all | solution.py:26
  17.8 0.6 reduce_sum.28
  19.5 1.1 copy.35
  20.6 3.6 %all-to-all-start.1 = ((bf16[72,8,768]{2,0,1:T(8,128)(2,1)}), bf16[72,8,768]{2,0,1:T(8,128)(2,1)S(1)}, u32[]{:S(2)}, u32[]{:S(2)}) async-start(bf16[72,8,768]{2,0,1:T(8,128)(2,1)} %copy.35), calls=%async_computation.1 | async-start | bytes 1769472 | tf_op jit(solution)/shard_map/all_to_all | solution.py:91
  24.3 21.0 %all-to-all-done.1 = bf16[72,8,768]{2,0,1:T(8,128)(2,1)S(1)} async-done(((bf16[72,8,768]{2,0,1:T(8,128)(2,1)}), bf16[72,8,768]{2,0,1:T(8,128)(2,1)S(1)}, u32[]{:S(2)}, u32[]{:S(2)}) %all-to-all-start.1) | async-done | bytes 884768 | tf_op jit(solution)/shard_map/all_to_all | solution.py:91
  45.4 0.9 fusion.69
  46.3 0.3 slice_select_fusion.1
  46.6 3.0 %gather_fusion = f32[288]{0:T(512)S(1)} fusion(f32[288,288]{1,0:T(8,128)S(1)} %get-tuple-element.18, s32[288]{0:T(512)S(1)} %or_reduce_fusion), kind=kCustom, calls=%fused_computation.2 | custom fusion | bytes 4608 | tf_op jit(solution)/shard_map/jit(diagonal)/cond/branch_0_fun/gather | solution.py:39
  49.9 0.6 gather_fusion.2
  50.7 1.3 collective-permute-start
  52.0 3.5 %collective-permute-start.6 = (f32[37,576]{1,0:T(8,128)S(1)}, f32[37,576]{1,0:T(8,128)S(1)}, u32[]{:S(2)}, u32[]{:S(2)}) collective-permute-start(f32[37,576]{1,0:T(8,128)S(1)} %get-tuple-element.33), channel_id=1, source_target_pairs={{0,7},{1,0},{2,1},{3,2},{4,3},{5,4},{6,5},{7,6},{8,15},{9,8},{10,9... | collective-permute-start | bytes 255752 | tf_op jit(solution)/shard_map/ppermute | solution.py:53
  55.5 2.9 %collective-permute-start.3 = (f32[37,576]{1,0:T(8,128)S(1)}, f32[37,576]{1,0:T(8,128)S(1)}, u32[]{:S(2)}, u32[]{:S(2)}) collective-permute-start(f32[37,576]{1,0:T(8,128)S(1)} %get-tuple-element.36), channel_id=1, source_target_pairs={{0,4},{1,5},{2,6},{3,7},{4,0},{5,1},{6,2},{7,3},{8,12},{9,13},{10,... | collective-permute-start | bytes 255752 | tf_op jit(solution)/shard_map/ppermute | solution.py:53
  58.7 1.7 collective-permute-start.1
  60.7 2.2 %collective-permute-done.4 = f32[37,576]{1,0:T(8,128)S(1)} collective-permute-done((f32[37,576]{1,0:T(8,128)S(1)}, f32[37,576]{1,0:T(8,128)S(1)}, u32[]{:S(2)}, u32[]{:S(2)}) %collective-permute-start.4) | collective-permute-done | bytes 85280 | tf_op jit(solution)/shard_map/ppermute | solution.py:53
  62.9 7.9 %collective-permute-done.3 = f32[37,576]{1,0:T(8,128)S(1)} collective-permute-done((f32[37,576]{1,0:T(8,128)S(1)}, f32[37,576]{1,0:T(8,128)S(1)}, u32[]{:S(2)}, u32[]{:S(2)}) %collective-permute-start.3) | collective-permute-done | bytes 85280 | tf_op jit(solution)/shard_map/ppermute | solution.py:53
  70.8 0.6 collective-permute-done.2
  71.5 16.0 %all_to_all.53 = bf16[8,37,576]{2,1,0:T(8,128)(2,1)S(1)} all-to-all(bf16[8,37,576]{2,1,0:T(8,128)(2,1)S(1)} %broadcast_in_dim.70), channel_id=1, replica_groups=mesh['dp'=4,'tensor'=8] {'tensor'}, dimensions={0} | all-to-all | bytes 681984 | tf_op jit(solution)/shard_map/all_to_all | solution.py:56
  88.4 1.7 add_convert_fusion.1
  90.1 0.9 copy-done.3
  91.0 0.9 fusion.70
  91.9 0.3 slice_select_fusion
  92.2 3.0 %gather_fusion.1 = f32[288]{0:T(512)S(1)} fusion(f32[288,288]{1,0:T(8,128)S(1)} %get-tuple-element.15, s32[288]{0:T(512)S(1)} %or_reduce_fusion), kind=kCustom, calls=%fused_computation.3 | custom fusion | bytes 4608 | tf_op jit(solution)/shard_map/jit(diagonal)/cond/branch_0_fun/gather | solution.py:39
  95.5 0.6 gather_fusion.3
  96.3 1.2 collective-permute-start.7
  97.5 3.6 %collective-permute-start.13 = (f32[37,576]{1,0:T(8,128)S(1)}, f32[37,576]{1,0:T(8,128)S(1)}, u32[]{:S(2)}, u32[]{:S(2)}) collective-permute-start(f32[37,576]{1,0:T(8,128)S(1)} %get-tuple-element.26), channel_id=1, source_target_pairs={{0,7},{1,0},{2,1},{3,2},{4,3},{5,4},{6,5},{7,6},{8,15},{9,8},{10,9... | collective-permute-start | bytes 255752 | tf_op jit(solution)/shard_map/ppermute | solution.py:53
  101.1 2.9 %collective-permute-start.10 = (f32[37,576]{1,0:T(8,128)S(1)}, f32[37,576]{1,0:T(8,128)S(1)}, u32[]{:S(2)}, u32[]{:S(2)}) collective-permute-start(f32[37,576]{1,0:T(8,128)S(1)} %get-tuple-element.29), channel_id=1, source_target_pairs={{0,4},{1,5},{2,6},{3,7},{4,0},{5,1},{6,2},{7,3},{8,12},{9,13},{10,... | collective-permute-start | bytes 255752 | tf_op jit(solution)/shard_map/ppermute | solution.py:53
  104.0 0.7 collective-permute-done.7
  104.8 1.4 collective-permute-start.8
  106.1 0.4 collective-permute-done.12
  106.6 2.2 %collective-permute-done.11 = f32[37,576]{1,0:T(8,128)S(1)} collective-permute-done((f32[37,576]{1,0:T(8,128)S(1)}, f32[37,576]{1,0:T(8,128)S(1)}, u32[]{:S(2)}, u32[]{:S(2)}) %collective-permute-start.11) | collective-permute-done | bytes 85280 | tf_op jit(solution)/shard_map/ppermute | solution.py:53
  108.8 8.6 %collective-permute-done.10 = f32[37,576]{1,0:T(8,128)S(1)} collective-permute-done((f32[37,576]{1,0:T(8,128)S(1)}, f32[37,576]{1,0:T(8,128)S(1)}, u32[]{:S(2)}, u32[]{:S(2)}) %collective-permute-start.10) | collective-permute-done | bytes 85280 | tf_op jit(solution)/shard_map/ppermute | solution.py:53
  117.6 15.9 %all_to_all.54 = bf16[8,37,576]{2,1,0:T(8,128)(2,1)S(1)} all-to-all(bf16[8,37,576]{2,1,0:T(8,128)(2,1)S(1)} %broadcast_in_dim.74), channel_id=1, replica_groups=mesh['dp'=4,'tensor'=8] {'tensor'}, dimensions={0} | all-to-all | bytes 681984 | tf_op jit(solution)/shard_map/all_to_all | solution.py:56
  134.3 0.4 copy-done.4
  134.7 1.7 add_convert_fusion
  136.4 0.9 fusion.67
  137.3 16.7 %all_to_all.55 = bf16[8,36,768]{2,1,0:T(8,128)(2,1)S(1)} all-to-all(bf16[8,36,768]{2,1,0:T(8,128)(2,1)S(1)} %get-tuple-element.23), channel_id=1, replica_groups=mesh['dp'=4,'tensor'=8] {'tensor'}, dimensions={0} | all-to-all | bytes 884736 | tf_op jit(solution)/shard_map/all_to_all | solution.py:112
  154.0 3.8 %all-to-all-start.5 = ((bf16[8,36,768]{2,1,0:T(8,128)(2,1)}), bf16[8,36,768]{2,1,0:T(8,128)(2,1)S(1)}, u32[]{:S(2)}, u32[]{:S(2)}) async-start(bf16[8,36,768]{2,1,0:T(8,128)(2,1)} %get-tuple-element.24), calls=%async_computation.5 | async-start | bytes 983040 | tf_op jit(solution)/shard_map/all_to_all | solution.py:112
  158.2 1.6 collective-permute-start.14
  159.9 11.3 %all-to-all-done.5 = bf16[8,36,768]{2,1,0:T(8,128)(2,1)S(1)} async-done(((bf16[8,36,768]{2,1,0:T(8,128)(2,1)}), bf16[8,36,768]{2,1,0:T(8,128)(2,1)S(1)}, u32[]{:S(2)}, u32[]{:S(2)}) %all-to-all-start.5) | async-done | bytes 442400 | tf_op jit(solution)/shard_map/all_to_all | solution.py:112
  171.7 1.6 collective-permute-start.16
  173.3 1.1 pad_maximum_fusion.2
  174.3 0.7 fusion.68
  182.7 0.6 collective-permute-done.16
  184.1 2.0 %collective-permute-done.17 = bf16[2,36,6144]{2,1,0:T(8,128)(2,1)S(1)} collective-permute-done((bf16[2,36,6144]{2,1,0:T(8,128)(2,1)S(1)}, bf16[2,36,6144]{2,1,0:T(8,128)(2,1)S(1)}, u32[]{:S(2)}, u32[]{:S(2)}) %collective-permute-start.17) | collective-permute-done | bytes 884768 | tf_op jit(solution)/shard_map/ppermute | solution.py:78
  186.2 0.3 pad_maximum_fusion.1
  186.6 2.9 %maximum_maximum_fusion = bf16[4,72,6144]{2,1,0:T(8,128)(2,1)} fusion(bf16[1,36,6144]{2,1,0:T(8,128)(2,1)S(1)} %get-tuple-element.10, bf16[1,36,6144]{2,1,0:T(8,128)(2,1)S(1)} %get-tuple-element.6, bf16[1,36,6144]{2,1,0:T(8,128)(2,1)S(1)} %get-tuple-element.11, bf16[1,36,6144]{2,1,0:T(8,128)(2,1)S(1)} %get-tuple-element.7, ...), kind=kLoop, calls=%fused_computation.4 | loop fusion | flops 28311552 | bytes 7077888 | tf_op jit(solution)/shard_map/concatenate | solution.py:124
  (75 shorter events, 5.9 us)
Async XLA Ops:
  0.6 18.5 %copy-start.1 = (bf16[1,72,6144]{2,1,0:T(8,128)(2,1)S(1)}, bf16[1,72,6144]{2,1,0:T(8,128)(2,1)}, u32[]{:S(2)}) copy-start(bf16[1,72,6144]{2,1,0:T(8,128)(2,1)} %param.5) | copy-start | bytes 2654212
  3.5 15.8 %copy-start = (f32[1,72,6144]{2,1,0:T(8,128)}, f32[1,72,6144]{2,1,0:T(8,128)S(1)}, u32[]{:S(2)}) copy-start(f32[1,72,6144]{2,1,0:T(8,128)S(1)} %get-tuple-element.4) | copy-start | bytes 5308420
  20.6 24.8 %all-to-all-start.1 = ((bf16[72,8,768]{2,0,1:T(8,128)(2,1)}), bf16[72,8,768]{2,0,1:T(8,128)(2,1)S(1)}, u32[]{:S(2)}, u32[]{:S(2)}) async-start(bf16[72,8,768]{2,0,1:T(8,128)(2,1)} %copy.35), calls=%async_computation.1 | async-start | bytes 1769472 | tf_op jit(solution)/shard_map/all_to_all | solution.py:91
  50.7 7.9 %collective-permute-start = (f32[37,576]{1,0:T(8,128)S(1)}, f32[37,576]{1,0:T(8,128)S(1)}, u32[]{:S(2)}, u32[]{:S(2)}) collective-permute-start(f32[37,576]{1,0:T(8,128)S(1)} %get-tuple-element.32), channel_id=1, source_target_pairs={{0,1},{1,2},{2,3},{3,4},{4,5},{5,6},{6,7},{7,0},{8,9},{9,10},{10,1... | collective-permute-start | bytes 255752 | tf_op jit(solution)/shard_map/ppermute | solution.py:53
  52.0 6.7 %collective-permute-start.6 = (f32[37,576]{1,0:T(8,128)S(1)}, f32[37,576]{1,0:T(8,128)S(1)}, u32[]{:S(2)}, u32[]{:S(2)}) collective-permute-start(f32[37,576]{1,0:T(8,128)S(1)} %get-tuple-element.33), channel_id=1, source_target_pairs={{0,7},{1,0},{2,1},{3,2},{4,3},{5,4},{6,5},{7,6},{8,15},{9,8},{10,9... | collective-permute-start | bytes 255752 | tf_op jit(solution)/shard_map/ppermute | solution.py:53
  55.5 5.2 %collective-permute-start.5 = (f32[37,576]{1,0:T(8,128)S(1)}, f32[37,576]{1,0:T(8,128)S(1)}, u32[]{:S(2)}, u32[]{:S(2)}) collective-permute-start(f32[37,576]{1,0:T(8,128)S(1)} %get-tuple-element.34), channel_id=1, source_target_pairs={{0,6},{1,7},{2,0},{3,1},{4,2},{5,3},{6,4},{7,5},{8,14},{9,15},{10,... | collective-permute-start | bytes 255752 | tf_op jit(solution)/shard_map/ppermute | solution.py:53
  55.5 7.4 %collective-permute-start.4 = (f32[37,576]{1,0:T(8,128)S(1)}, f32[37,576]{1,0:T(8,128)S(1)}, u32[]{:S(2)}, u32[]{:S(2)}) collective-permute-start(f32[37,576]{1,0:T(8,128)S(1)} %get-tuple-element.35), channel_id=1, source_target_pairs={{0,5},{1,6},{2,7},{3,0},{4,1},{5,2},{6,3},{7,4},{8,13},{9,14},{10,... | collective-permute-start | bytes 255752 | tf_op jit(solution)/shard_map/ppermute | solution.py:53
  55.5 15.3 %collective-permute-start.3 = (f32[37,576]{1,0:T(8,128)S(1)}, f32[37,576]{1,0:T(8,128)S(1)}, u32[]{:S(2)}, u32[]{:S(2)}) collective-permute-start(f32[37,576]{1,0:T(8,128)S(1)} %get-tuple-element.36), channel_id=1, source_target_pairs={{0,4},{1,5},{2,6},{3,7},{4,0},{5,1},{6,2},{7,3},{8,12},{9,13},{10,... | collective-permute-start | bytes 255752 | tf_op jit(solution)/shard_map/ppermute | solution.py:53
  58.6 12.8 %collective-permute-start.2 = (f32[37,576]{1,0:T(8,128)S(1)}, f32[37,576]{1,0:T(8,128)S(1)}, u32[]{:S(2)}, u32[]{:S(2)}) collective-permute-start(f32[37,576]{1,0:T(8,128)S(1)} %get-tuple-element.37), channel_id=1, source_target_pairs={{0,3},{1,4},{2,5},{3,6},{4,7},{5,0},{6,1},{7,2},{8,11},{9,12},{10,... | collective-permute-start | bytes 255752 | tf_op jit(solution)/shard_map/ppermute | solution.py:53
  58.7 12.7 %collective-permute-start.1 = (f32[37,576]{1,0:T(8,128)S(1)}, f32[37,576]{1,0:T(8,128)S(1)}, u32[]{:S(2)}, u32[]{:S(2)}) collective-permute-start(f32[37,576]{1,0:T(8,128)S(1)} %get-tuple-element.38), channel_id=1, source_target_pairs={{0,2},{1,3},{2,4},{3,5},{4,6},{5,7},{6,0},{7,1},{8,10},{9,11},{10,... | collective-permute-start | bytes 255752 | tf_op jit(solution)/shard_map/ppermute | solution.py:53
  90.1 0.9 copy-start.3
  96.3 8.4 %collective-permute-start.7 = (f32[37,576]{1,0:T(8,128)S(1)}, f32[37,576]{1,0:T(8,128)S(1)}, u32[]{:S(2)}, u32[]{:S(2)}) collective-permute-start(f32[37,576]{1,0:T(8,128)S(1)} %get-tuple-element.25), channel_id=1, source_target_pairs={{0,1},{1,2},{2,3},{3,4},{4,5},{5,6},{6,7},{7,0},{8,9},{9,10},{10,1... | collective-permute-start | bytes 255752 | tf_op jit(solution)/shard_map/ppermute | solution.py:53
  97.5 7.2 %collective-permute-start.13 = (f32[37,576]{1,0:T(8,128)S(1)}, f32[37,576]{1,0:T(8,128)S(1)}, u32[]{:S(2)}, u32[]{:S(2)}) collective-permute-start(f32[37,576]{1,0:T(8,128)S(1)} %get-tuple-element.26), channel_id=1, source_target_pairs={{0,7},{1,0},{2,1},{3,2},{4,3},{5,4},{6,5},{7,6},{8,15},{9,8},{10,9... | collective-permute-start | bytes 255752 | tf_op jit(solution)/shard_map/ppermute | solution.py:53
  101.1 5.5 %collective-permute-start.12 = (f32[37,576]{1,0:T(8,128)S(1)}, f32[37,576]{1,0:T(8,128)S(1)}, u32[]{:S(2)}, u32[]{:S(2)}) collective-permute-start(f32[37,576]{1,0:T(8,128)S(1)} %get-tuple-element.27), channel_id=1, source_target_pairs={{0,6},{1,7},{2,0},{3,1},{4,2},{5,3},{6,4},{7,5},{8,14},{9,15},{10,... | collective-permute-start | bytes 255752 | tf_op jit(solution)/shard_map/ppermute | solution.py:53
  101.1 7.7 %collective-permute-start.11 = (f32[37,576]{1,0:T(8,128)S(1)}, f32[37,576]{1,0:T(8,128)S(1)}, u32[]{:S(2)}, u32[]{:S(2)}) collective-permute-start(f32[37,576]{1,0:T(8,128)S(1)} %get-tuple-element.28), channel_id=1, source_target_pairs={{0,5},{1,6},{2,7},{3,0},{4,1},{5,2},{6,3},{7,4},{8,13},{9,14},{10,... | collective-permute-start | bytes 255752 | tf_op jit(solution)/shard_map/ppermute | solution.py:53
  101.1 16.3 %collective-permute-start.10 = (f32[37,576]{1,0:T(8,128)S(1)}, f32[37,576]{1,0:T(8,128)S(1)}, u32[]{:S(2)}, u32[]{:S(2)}) collective-permute-start(f32[37,576]{1,0:T(8,128)S(1)} %get-tuple-element.29), channel_id=1, source_target_pairs={{0,4},{1,5},{2,6},{3,7},{4,0},{5,1},{6,2},{7,3},{8,12},{9,13},{10,... | collective-permute-start | bytes 255752 | tf_op jit(solution)/shard_map/ppermute | solution.py:53
  104.8 12.8 %collective-permute-start.9 = (f32[37,576]{1,0:T(8,128)S(1)}, f32[37,576]{1,0:T(8,128)S(1)}, u32[]{:S(2)}, u32[]{:S(2)}) collective-permute-start(f32[37,576]{1,0:T(8,128)S(1)} %get-tuple-element.30), channel_id=1, source_target_pairs={{0,3},{1,4},{2,5},{3,6},{4,7},{5,0},{6,1},{7,2},{8,11},{9,12},{10,... | collective-permute-start | bytes 255752 | tf_op jit(solution)/shard_map/ppermute | solution.py:53
  104.8 12.8 %collective-permute-start.8 = (f32[37,576]{1,0:T(8,128)S(1)}, f32[37,576]{1,0:T(8,128)S(1)}, u32[]{:S(2)}, u32[]{:S(2)}) collective-permute-start(f32[37,576]{1,0:T(8,128)S(1)} %get-tuple-element.31), channel_id=1, source_target_pairs={{0,2},{1,3},{2,4},{3,5},{4,6},{5,7},{6,0},{7,1},{8,10},{9,11},{10,... | collective-permute-start | bytes 255752 | tf_op jit(solution)/shard_map/ppermute | solution.py:53
  133.5 1.2 copy-start.4
  154.0 5.8 %copy-start.2 = (s32[4]{0:T(128)S(1)}, s32[4]{0:T(128)}, u32[]{:S(2)}) copy-start(s32[4]{0:T(128)} %param.7) | copy-start | bytes 52
  154.0 17.3 %all-to-all-start.5 = ((bf16[8,36,768]{2,1,0:T(8,128)(2,1)}), bf16[8,36,768]{2,1,0:T(8,128)(2,1)S(1)}, u32[]{:S(2)}, u32[]{:S(2)}) async-start(bf16[8,36,768]{2,1,0:T(8,128)(2,1)} %get-tuple-element.24), calls=%async_computation.5 | async-start | bytes 983040 | tf_op jit(solution)/shard_map/all_to_all | solution.py:112
  158.2 15.0 %collective-permute-start.14 = (bf16[1,36,6144]{2,1,0:T(8,128)(2,1)S(1)}, bf16[1,36,6144]{2,1,0:T(8,128)(2,1)S(1)}, u32[]{:S(2)}, u32[]{:S(2)}) collective-permute-start(bf16[1,36,6144]{2,1,0:T(8,128)(2,1)S(1)} %convert_element_type.113), channel_id=1, source_target_pairs={{0,16},{8,24},{16,0},{24,8},{1,17},{9,25},{17,1},{25,9},{2,18},{10... | collective-permute-start | bytes 1327112 | tf_op jit(solution)/shard_map/ppermute | solution.py:78
  171.7 11.6 %collective-permute-start.16 = (bf16[1,36,6144]{2,1,0:T(8,128)(2,1)S(1)}, bf16[1,36,6144]{2,1,0:T(8,128)(2,1)S(1)}, u32[]{:S(2)}, u32[]{:S(2)}) collective-permute-start(bf16[1,36,6144]{2,1,0:T(8,128)(2,1)S(1)} %convert_element_type.117), channel_id=1, source_target_pairs={{0,16},{8,24},{16,0},{24,8},{1,17},{9,25},{17,1},{25,9},{2,18},{10... | collective-permute-start | bytes 1327112 | tf_op jit(solution)/shard_map/ppermute | solution.py:78
  174.3 9.2 %collective-permute-start.15 = (bf16[2,36,6144]{2,1,0:T(8,128)(2,1)}, bf16[2,36,6144]{2,1,0:T(8,128)(2,1)S(1)}, u32[]{:S(2)}, u32[]{:S(2)}) collective-permute-start(bf16[2,36,6144]{2,1,0:T(8,128)(2,1)} %pad_maximum_fusion.2), channel_id=1, source_target_pairs={{0,8},{8,0},{16,24},{24,16},{1,9},{9,1},{17,25},{25,17},{2,10},{10... | collective-permute-start | bytes 2654216 | tf_op jit(solution)/shard_map/ppermute | solution.py:78
  183.5 2.6 %collective-permute-start.17 = (bf16[2,36,6144]{2,1,0:T(8,128)(2,1)S(1)}, bf16[2,36,6144]{2,1,0:T(8,128)(2,1)S(1)}, u32[]{:S(2)}, u32[]{:S(2)}) collective-permute-start(bf16[2,36,6144]{2,1,0:T(8,128)(2,1)S(1)} %pad_maximum_fusion.3), channel_id=1, source_target_pairs={{0,8},{8,0},{16,24},{24,16},{1,9},{9,1},{17,25},{25,17},{2,10},{10... | collective-permute-start | bytes 2654216 | tf_op jit(solution)/shard_map/ppermute | solution.py:78

commit v5 on v4

--- a/solution.py
+++ b/solution.py
@@ -46,11 +46,10 @@
     per = rows // size
     blocks = payload.reshape(size, per, 2 * h)
     me = lax.axis_index(axis)
-    order = (me + jnp.arange(size, dtype=jnp.int32)) % size
-    rolled = jnp.take(blocks, order, axis=0)
-    acc = rolled[0]
+    acc = lax.dynamic_index_in_dim(blocks, me, 0, keepdims=False)
     for s in range(1, size):
-        acc = acc + lax.ppermute(rolled[s], axis, _shift_pairs(size, s))
+        outgoing = lax.dynamic_index_in_dim(blocks, (me + s) % size, 0, keepdims=False)
+        acc = acc + lax.ppermute(outgoing, axis, _shift_pairs(size, s))
     mine = acc.astype(jnp.bfloat16)
     spread = jnp.broadcast_to(mine[None], (size,) + mine.shape)
     full = lax.all_to_all(spread, axis, split_axis=0, concat_axis=0, tiled=True).reshape(rows, 2 * h)

time: 190 us -> 189 us (level)
  no operation moved by 1% of the time
where the time goes in v5:
time: 189 us; the launch traced here: 188 us
  blocking collectives  62.3 us (33%)
  waiting for transfers between devices  58.4 us (31%)
  starting transfers between devices  29.1 us (15%)
  local copies, waits for them, and re-layouts  13.5 us (7%)
  other arithmetic  10.2 us (5%)
  between operations  9.5 us (5%)
  matrix products  5.14 us (3%)
    all_to_all x2, blocking collectives, gram_allreduce(): lax.all_to_all(spread, axis, split_axis=0, concat_axis=0, tiled=True)  32 us
    ppermute x14, waiting for transfers between devices, gram_allreduce(): acc = acc + lax.ppermute(outgoing, axis, _shift_pairs(size, s))  23.4 us
    all_to_all x1, waiting for transfers between devices, per_device(): lax.all_to_all(rows_here, 'tensor', split_axis=1, concat_axis=0, tiled=True)  21 us
    ppermute x14, starting transfers between devices, gram_allreduce(): acc = acc + lax.ppermute(outgoing, axis, _shift_pairs(size, s))  18.5 us
    all_to_all x1, blocking collectives, per_device(): lax.all_to_all(piece, 'tensor', split_axis=0, concat_axis=1, tiled=True)  16.7 us
    all_to_all x1, blocking collectives, total_over(): got = lax.all_to_all(spread, axis, split_axis=0, concat_axis=0, tiled=True)  13.6 us
    all_to_all x1, waiting for transfers between devices, per_device(): lax.all_to_all(piece, 'tensor', split_axis=0, concat_axis=1, tiled=True)  11.3 us
    gather x2, local copies, waits for them, and re-layouts, gram_allreduce(): diag_c = jnp.diagonal(lower_c)  5.98 us
  transfers between devices with their start and end apart: 20, of which 15 were waited for; matrix products, arithmetic and copies ran while one was open for 2% of the time, Pallas kernels for 0%

profile of v5, /device:TPU:0, one launch (start us, length us, event | category | flops | bytes accessed | tf_op | source)
XLA Modules:
  0.0 188.1 jit_solution(4399366720510347947)
XLA Ops:
  0.6 2.9 %multiply_reduce_fusion = (f32[]{:T(128)}, f32[1,72,6144]{2,1,0:T(8,128)S(1)}) fusion(bf16[1,72,6144]{2,1,0:T(8,128)(2,1)} %param.3, f32[1,72,6144]{2,1,0:T(8,128)} %param.4), kind=kLoop, calls=%fused_computation.10 | loop fusion | flops 3096575 | bytes 4423684 | tf_op jit(solution)/shard_map/reduce_sum | solution.py:88
  3.5 0.6 broadcast_in_dim.59
  4.2 13.6 %all_to_all.52 = f32[8,1,1]{2,1,0:T(1,128)S(1)} all-to-all(f32[8,1,1]{2,1,0:T(1,128)S(1)} %broadcast_in_dim.59), channel_id=1, replica_groups=mesh['dp'=4,'tensor'=8] {'tensor'}, dimensions={0} | all-to-all | bytes 64 | tf_op jit(solution)/shard_map/all_to_all | solution.py:26
  17.8 0.6 reduce_sum.28
  19.1 0.3 divide_convert_fusion
  19.5 1.1 copy.34
  20.6 3.6 %all-to-all-start.1 = ((bf16[72,8,768]{2,0,1:T(8,128)(2,1)}), bf16[72,8,768]{2,0,1:T(8,128)(2,1)S(1)}, u32[]{:S(2)}, u32[]{:S(2)}) async-start(bf16[72,8,768]{2,0,1:T(8,128)(2,1)} %copy.34), calls=%async_computation.1 | async-start | bytes 1769472 | tf_op jit(solution)/shard_map/all_to_all | solution.py:90
  24.4 21.0 %all-to-all-done.1 = bf16[72,8,768]{2,0,1:T(8,128)(2,1)S(1)} async-done(((bf16[72,8,768]{2,0,1:T(8,128)(2,1)}), bf16[72,8,768]{2,0,1:T(8,128)(2,1)S(1)}, u32[]{:S(2)}, u32[]{:S(2)}) %all-to-all-start.1) | async-done | bytes 884768 | tf_op jit(solution)/shard_map/all_to_all | solution.py:90
  45.4 0.9 fusion.66
  46.3 0.3 slice_select_fusion.1
  46.6 3.0 %gather_fusion = f32[288]{0:T(512)S(1)} fusion(f32[288,288]{1,0:T(8,128)S(1)} %get-tuple-element.17, s32[288]{0:T(512)S(1)} %or_reduce_fusion), kind=kCustom, calls=%fused_computation | custom fusion | bytes 4608 | tf_op jit(solution)/shard_map/jit(diagonal)/cond/branch_0_fun/gather | solution.py:39
  50.0 1.3 collective-permute-start
  51.3 3.5 %collective-permute-start.6 = (f32[37,576]{1,0:T(8,128)S(1)}, f32[37,576]{1,0:T(8,128)S(1)}, u32[]{:S(2)}, u32[]{:S(2)}) collective-permute-start(f32[37,576]{1,0:T(8,128)S(1)} %get-tuple-element.32), channel_id=1, source_target_pairs={{0,7},{1,0},{2,1},{3,2},{4,3},{5,4},{6,5},{7,6},{8,15},{9,8},{10,9... | collective-permute-start | bytes 255752 | tf_op jit(solution)/shard_map/ppermute | solution.py:52
  54.8 2.9 %collective-permute-start.3 = (f32[37,576]{1,0:T(8,128)S(1)}, f32[37,576]{1,0:T(8,128)S(1)}, u32[]{:S(2)}, u32[]{:S(2)}) collective-permute-start(f32[37,576]{1,0:T(8,128)S(1)} %get-tuple-element.35), channel_id=1, source_target_pairs={{0,4},{1,5},{2,6},{3,7},{4,0},{5,1},{6,2},{7,3},{8,12},{9,13},{10,... | collective-permute-start | bytes 255752 | tf_op jit(solution)/shard_map/ppermute | solution.py:52
  58.0 1.7 collective-permute-start.1
  60.0 2.2 %collective-permute-done.4 = f32[37,576]{1,0:T(8,128)S(1)} collective-permute-done((f32[37,576]{1,0:T(8,128)S(1)}, f32[37,576]{1,0:T(8,128)S(1)}, u32[]{:S(2)}, u32[]{:S(2)}) %collective-permute-start.4) | collective-permute-done | bytes 85280 | tf_op jit(solution)/shard_map/ppermute | solution.py:52
  62.2 7.9 %collective-permute-done.3 = f32[37,576]{1,0:T(8,128)S(1)} collective-permute-done((f32[37,576]{1,0:T(8,128)S(1)}, f32[37,576]{1,0:T(8,128)S(1)}, u32[]{:S(2)}, u32[]{:S(2)}) %collective-permute-start.3) | collective-permute-done | bytes 85280 | tf_op jit(solution)/shard_map/ppermute | solution.py:52
  70.1 0.6 collective-permute-done.2
  70.8 16.0 %all_to_all.53 = bf16[8,37,576]{2,1,0:T(8,128)(2,1)S(1)} all-to-all(bf16[8,37,576]{2,1,0:T(8,128)(2,1)S(1)} %broadcast_in_dim.61), channel_id=1, replica_groups=mesh['dp'=4,'tensor'=8] {'tensor'}, dimensions={0} | all-to-all | bytes 681984 | tf_op jit(solution)/shard_map/all_to_all | solution.py:55
  87.6 1.7 add_convert_fusion.1
  89.4 0.9 copy-done.3
  90.3 0.9 fusion.67
  91.2 0.3 slice_select_fusion
  91.5 3.0 %gather_fusion.1 = f32[288]{0:T(512)S(1)} fusion(f32[288,288]{1,0:T(8,128)S(1)} %get-tuple-element.14, s32[288]{0:T(512)S(1)} %or_reduce_fusion), kind=kCustom, calls=%fused_computation.1 | custom fusion | bytes 4608 | tf_op jit(solution)/shard_map/jit(diagonal)/cond/branch_0_fun/gather | solution.py:39
  94.9 1.2 collective-permute-start.7
  96.1 3.6 %collective-permute-start.13 = (f32[37,576]{1,0:T(8,128)S(1)}, f32[37,576]{1,0:T(8,128)S(1)}, u32[]{:S(2)}, u32[]{:S(2)}) collective-permute-start(f32[37,576]{1,0:T(8,128)S(1)} %get-tuple-element.25), channel_id=1, source_target_pairs={{0,7},{1,0},{2,1},{3,2},{4,3},{5,4},{6,5},{7,6},{8,15},{9,8},{10,9... | collective-permute-start | bytes 255752 | tf_op jit(solution)/shard_map/ppermute | solution.py:52
  99.7 2.9 %collective-permute-start.10 = (f32[37,576]{1,0:T(8,128)S(1)}, f32[37,576]{1,0:T(8,128)S(1)}, u32[]{:S(2)}, u32[]{:S(2)}) collective-permute-start(f32[37,576]{1,0:T(8,128)S(1)} %get-tuple-element.28), channel_id=1, source_target_pairs={{0,4},{1,5},{2,6},{3,7},{4,0},{5,1},{6,2},{7,3},{8,12},{9,13},{10,... | collective-permute-start | bytes 255752 | tf_op jit(solution)/shard_map/ppermute | solution.py:52
  102.6 0.7 collective-permute-done.7
  103.3 1.4 collective-permute-start.8
  104.7 0.4 collective-permute-done.12
  105.1 2.2 %collective-permute-done.11 = f32[37,576]{1,0:T(8,128)S(1)} collective-permute-done((f32[37,576]{1,0:T(8,128)S(1)}, f32[37,576]{1,0:T(8,128)S(1)}, u32[]{:S(2)}, u32[]{:S(2)}) %collective-permute-start.11) | collective-permute-done | bytes 85280 | tf_op jit(solution)/shard_map/ppermute | solution.py:52
  107.3 8.7 %collective-permute-done.10 = f32[37,576]{1,0:T(8,128)S(1)} collective-permute-done((f32[37,576]{1,0:T(8,128)S(1)}, f32[37,576]{1,0:T(8,128)S(1)}, u32[]{:S(2)}, u32[]{:S(2)}) %collective-permute-start.10) | collective-permute-done | bytes 85280 | tf_op jit(solution)/shard_map/ppermute | solution.py:52
  116.2 15.9 %all_to_all.54 = bf16[8,37,576]{2,1,0:T(8,128)(2,1)S(1)} all-to-all(bf16[8,37,576]{2,1,0:T(8,128)(2,1)S(1)} %broadcast_in_dim.65), channel_id=1, replica_groups=mesh['dp'=4,'tensor'=8] {'tensor'}, dimensions={0} | all-to-all | bytes 681984 | tf_op jit(solution)/shard_map/all_to_all | solution.py:55
  132.9 0.4 copy-done.4
  133.3 1.7 add_convert_fusion
  135.0 0.9 fusion.64
  135.8 16.7 %all_to_all.55 = bf16[8,36,768]{2,1,0:T(8,128)(2,1)S(1)} all-to-all(bf16[8,36,768]{2,1,0:T(8,128)(2,1)S(1)} %get-tuple-element.22), channel_id=1, replica_groups=mesh['dp'=4,'tensor'=8] {'tensor'}, dimensions={0} | all-to-all | bytes 884736 | tf_op jit(solution)/shard_map/all_to_all | solution.py:111
  152.6 3.8 %all-to-all-start.5 = ((bf16[8,36,768]{2,1,0:T(8,128)(2,1)}), bf16[8,36,768]{2,1,0:T(8,128)(2,1)S(1)}, u32[]{:S(2)}, u32[]{:S(2)}) async-start(bf16[8,36,768]{2,1,0:T(8,128)(2,1)} %get-tuple-element.23), calls=%async_computation.5 | async-start | bytes 983040 | tf_op jit(solution)/shard_map/all_to_all | solution.py:111
  156.8 1.6 collective-permute-start.14
  158.5 11.3 %all-to-all-done.5 = bf16[8,36,768]{2,1,0:T(8,128)(2,1)S(1)} async-done(((bf16[8,36,768]{2,1,0:T(8,128)(2,1)}), bf16[8,36,768]{2,1,0:T(8,128)(2,1)S(1)}, u32[]{:S(2)}, u32[]{:S(2)}) %all-to-all-start.5) | async-done | bytes 442400 | tf_op jit(solution)/shard_map/all_to_all | solution.py:111
  170.3 1.6 collective-permute-start.16
  171.8 1.1 pad_maximum_fusion.2
  172.9 0.7 fusion.65
  181.3 0.7 collective-permute-done.16
  182.2 0.3 pad_maximum_fusion
  182.7 2.0 %collective-permute-done.17 = bf16[2,36,6144]{2,1,0:T(8,128)(2,1)S(1)} collective-permute-done((bf16[2,36,6144]{2,1,0:T(8,128)(2,1)S(1)}, bf16[2,36,6144]{2,1,0:T(8,128)(2,1)S(1)}, u32[]{:S(2)}, u32[]{:S(2)}) %collective-permute-start.17) | collective-permute-done | bytes 884768 | tf_op jit(solution)/shard_map/ppermute | solution.py:77
  184.7 0.3 pad_maximum_fusion.1
  185.2 2.9 %maximum_maximum_fusion = bf16[4,72,6144]{2,1,0:T(8,128)(2,1)} fusion(bf16[1,36,6144]{2,1,0:T(8,128)(2,1)S(1)} %get-tuple-element.9, bf16[1,36,6144]{2,1,0:T(8,128)(2,1)S(1)} %get-tuple-element.5, bf16[1,36,6144]{2,1,0:T(8,128)(2,1)S(1)} %get-tuple-element.10, bf16[1,36,6144]{2,1,0:T(8,128)(2,1)S(1)} %get-tuple-element.6, ...), kind=kLoop, calls=%fused_computation.2 | loop fusion | flops 28311552 | bytes 7077888 | tf_op jit(solution)/shard_map/concatenate | solution.py:123
  (68 shorter events, 5.1 us)
Async XLA Ops:
  0.6 18.5 %copy-start.1 = (bf16[1,72,6144]{2,1,0:T(8,128)(2,1)S(1)}, bf16[1,72,6144]{2,1,0:T(8,128)(2,1)}, u32[]{:S(2)}) copy-start(bf16[1,72,6144]{2,1,0:T(8,128)(2,1)} %param.3) | copy-start | bytes 2654212
  3.5 15.8 %copy-start = (f32[1,72,6144]{2,1,0:T(8,128)}, f32[1,72,6144]{2,1,0:T(8,128)S(1)}, u32[]{:S(2)}) copy-start(f32[1,72,6144]{2,1,0:T(8,128)S(1)} %get-tuple-element.3) | copy-start | bytes 5308420
  20.6 24.8 %all-to-all-start.1 = ((bf16[72,8,768]{2,0,1:T(8,128)(2,1)}), bf16[72,8,768]{2,0,1:T(8,128)(2,1)S(1)}, u32[]{:S(2)}, u32[]{:S(2)}) async-start(bf16[72,8,768]{2,0,1:T(8,128)(2,1)} %copy.34), calls=%async_computation.1 | async-start | bytes 1769472 | tf_op jit(solution)/shard_map/all_to_all | solution.py:90
  50.0 7.9 %collective-permute-start = (f32[37,576]{1,0:T(8,128)S(1)}, f32[37,576]{1,0:T(8,128)S(1)}, u32[]{:S(2)}, u32[]{:S(2)}) collective-permute-start(f32[37,576]{1,0:T(8,128)S(1)} %get-tuple-element.31), channel_id=1, source_target_pairs={{0,1},{1,2},{2,3},{3,4},{4,5},{5,6},{6,7},{7,0},{8,9},{9,10},{10,1... | collective-permute-start | bytes 255752 | tf_op jit(solution)/shard_map/ppermute | solution.py:52
  51.3 6.7 %collective-permute-start.6 = (f32[37,576]{1,0:T(8,128)S(1)}, f32[37,576]{1,0:T(8,128)S(1)}, u32[]{:S(2)}, u32[]{:S(2)}) collective-permute-start(f32[37,576]{1,0:T(8,128)S(1)} %get-tuple-element.32), channel_id=1, source_target_pairs={{0,7},{1,0},{2,1},{3,2},{4,3},{5,4},{6,5},{7,6},{8,15},{9,8},{10,9... | collective-permute-start | bytes 255752 | tf_op jit(solution)/shard_map/ppermute | solution.py:52
  54.8 5.2 %collective-permute-start.5 = (f32[37,576]{1,0:T(8,128)S(1)}, f32[37,576]{1,0:T(8,128)S(1)}, u32[]{:S(2)}, u32[]{:S(2)}) collective-permute-start(f32[37,576]{1,0:T(8,128)S(1)} %get-tuple-element.33), channel_id=1, source_target_pairs={{0,6},{1,7},{2,0},{3,1},{4,2},{5,3},{6,4},{7,5},{8,14},{9,15},{10,... | collective-permute-start | bytes 255752 | tf_op jit(solution)/shard_map/ppermute | solution.py:52
  54.8 7.4 %collective-permute-start.4 = (f32[37,576]{1,0:T(8,128)S(1)}, f32[37,576]{1,0:T(8,128)S(1)}, u32[]{:S(2)}, u32[]{:S(2)}) collective-permute-start(f32[37,576]{1,0:T(8,128)S(1)} %get-tuple-element.34), channel_id=1, source_target_pairs={{0,5},{1,6},{2,7},{3,0},{4,1},{5,2},{6,3},{7,4},{8,13},{9,14},{10,... | collective-permute-start | bytes 255752 | tf_op jit(solution)/shard_map/ppermute | solution.py:52
  54.8 15.3 %collective-permute-start.3 = (f32[37,576]{1,0:T(8,128)S(1)}, f32[37,576]{1,0:T(8,128)S(1)}, u32[]{:S(2)}, u32[]{:S(2)}) collective-permute-start(f32[37,576]{1,0:T(8,128)S(1)} %get-tuple-element.35), channel_id=1, source_target_pairs={{0,4},{1,5},{2,6},{3,7},{4,0},{5,1},{6,2},{7,3},{8,12},{9,13},{10,... | collective-permute-start | bytes 255752 | tf_op jit(solution)/shard_map/ppermute | solution.py:52
  57.9 12.8 %collective-permute-start.2 = (f32[37,576]{1,0:T(8,128)S(1)}, f32[37,576]{1,0:T(8,128)S(1)}, u32[]{:S(2)}, u32[]{:S(2)}) collective-permute-start(f32[37,576]{1,0:T(8,128)S(1)} %get-tuple-element.36), channel_id=1, source_target_pairs={{0,3},{1,4},{2,5},{3,6},{4,7},{5,0},{6,1},{7,2},{8,11},{9,12},{10,... | collective-permute-start | bytes 255752 | tf_op jit(solution)/shard_map/ppermute | solution.py:52
  58.0 12.7 %collective-permute-start.1 = (f32[37,576]{1,0:T(8,128)S(1)}, f32[37,576]{1,0:T(8,128)S(1)}, u32[]{:S(2)}, u32[]{:S(2)}) collective-permute-start(f32[37,576]{1,0:T(8,128)S(1)} %get-tuple-element.37), channel_id=1, source_target_pairs={{0,2},{1,3},{2,4},{3,5},{4,6},{5,7},{6,0},{7,1},{8,10},{9,11},{10,... | collective-permute-start | bytes 255752 | tf_op jit(solution)/shard_map/ppermute | solution.py:52
  89.4 0.9 copy-start.3
  94.9 8.4 %collective-permute-start.7 = (f32[37,576]{1,0:T(8,128)S(1)}, f32[37,576]{1,0:T(8,128)S(1)}, u32[]{:S(2)}, u32[]{:S(2)}) collective-permute-start(f32[37,576]{1,0:T(8,128)S(1)} %get-tuple-element.24), channel_id=1, source_target_pairs={{0,1},{1,2},{2,3},{3,4},{4,5},{5,6},{6,7},{7,0},{8,9},{9,10},{10,1... | collective-permute-start | bytes 255752 | tf_op jit(solution)/shard_map/ppermute | solution.py:52
  96.1 7.2 %collective-permute-start.13 = (f32[37,576]{1,0:T(8,128)S(1)}, f32[37,576]{1,0:T(8,128)S(1)}, u32[]{:S(2)}, u32[]{:S(2)}) collective-permute-start(f32[37,576]{1,0:T(8,128)S(1)} %get-tuple-element.25), channel_id=1, source_target_pairs={{0,7},{1,0},{2,1},{3,2},{4,3},{5,4},{6,5},{7,6},{8,15},{9,8},{10,9... | collective-permute-start | bytes 255752 | tf_op jit(solution)/shard_map/ppermute | solution.py:52
  99.7 5.5 %collective-permute-start.12 = (f32[37,576]{1,0:T(8,128)S(1)}, f32[37,576]{1,0:T(8,128)S(1)}, u32[]{:S(2)}, u32[]{:S(2)}) collective-permute-start(f32[37,576]{1,0:T(8,128)S(1)} %get-tuple-element.26), channel_id=1, source_target_pairs={{0,6},{1,7},{2,0},{3,1},{4,2},{5,3},{6,4},{7,5},{8,14},{9,15},{10,... | collective-permute-start | bytes 255752 | tf_op jit(solution)/shard_map/ppermute | solution.py:52
  99.7 7.7 %collective-permute-start.11 = (f32[37,576]{1,0:T(8,128)S(1)}, f32[37,576]{1,0:T(8,128)S(1)}, u32[]{:S(2)}, u32[]{:S(2)}) collective-permute-start(f32[37,576]{1,0:T(8,128)S(1)} %get-tuple-element.27), channel_id=1, source_target_pairs={{0,5},{1,6},{2,7},{3,0},{4,1},{5,2},{6,3},{7,4},{8,13},{9,14},{10,... | collective-permute-start | bytes 255752 | tf_op jit(solution)/shard_map/ppermute | solution.py:52
  99.7 16.3 %collective-permute-start.10 = (f32[37,576]{1,0:T(8,128)S(1)}, f32[37,576]{1,0:T(8,128)S(1)}, u32[]{:S(2)}, u32[]{:S(2)}) collective-permute-start(f32[37,576]{1,0:T(8,128)S(1)} %get-tuple-element.28), channel_id=1, source_target_pairs={{0,4},{1,5},{2,6},{3,7},{4,0},{5,1},{6,2},{7,3},{8,12},{9,13},{10,... | collective-permute-start | bytes 255752 | tf_op jit(solution)/shard_map/ppermute | solution.py:52
  103.3 12.8 %collective-permute-start.9 = (f32[37,576]{1,0:T(8,128)S(1)}, f32[37,576]{1,0:T(8,128)S(1)}, u32[]{:S(2)}, u32[]{:S(2)}) collective-permute-start(f32[37,576]{1,0:T(8,128)S(1)} %get-tuple-element.29), channel_id=1, source_target_pairs={{0,3},{1,4},{2,5},{3,6},{4,7},{5,0},{6,1},{7,2},{8,11},{9,12},{10,... | collective-permute-start | bytes 255752 | tf_op jit(solution)/shard_map/ppermute | solution.py:52
  103.3 12.8 %collective-permute-start.8 = (f32[37,576]{1,0:T(8,128)S(1)}, f32[37,576]{1,0:T(8,128)S(1)}, u32[]{:S(2)}, u32[]{:S(2)}) collective-permute-start(f32[37,576]{1,0:T(8,128)S(1)} %get-tuple-element.30), channel_id=1, source_target_pairs={{0,2},{1,3},{2,4},{3,5},{4,6},{5,7},{6,0},{7,1},{8,10},{9,11},{10,... | collective-permute-start | bytes 255752 | tf_op jit(solution)/shard_map/ppermute | solution.py:52
  132.1 1.2 copy-start.4
  152.6 5.8 %copy-start.2 = (s32[4]{0:T(128)S(1)}, s32[4]{0:T(128)}, u32[]{:S(2)}) copy-start(s32[4]{0:T(128)} %param.5) | copy-start | bytes 52
  152.6 17.3 %all-to-all-start.5 = ((bf16[8,36,768]{2,1,0:T(8,128)(2,1)}), bf16[8,36,768]{2,1,0:T(8,128)(2,1)S(1)}, u32[]{:S(2)}, u32[]{:S(2)}) async-start(bf16[8,36,768]{2,1,0:T(8,128)(2,1)} %get-tuple-element.23), calls=%async_computation.5 | async-start | bytes 983040 | tf_op jit(solution)/shard_map/all_to_all | solution.py:111
  156.8 15.0 %collective-permute-start.14 = (bf16[1,36,6144]{2,1,0:T(8,128)(2,1)S(1)}, bf16[1,36,6144]{2,1,0:T(8,128)(2,1)S(1)}, u32[]{:S(2)}, u32[]{:S(2)}) collective-permute-start(bf16[1,36,6144]{2,1,0:T(8,128)(2,1)S(1)} %convert_element_type.113), channel_id=1, source_target_pairs={{0,16},{8,24},{16,0},{24,8},{1,17},{9,25},{17,1},{25,9},{2,18},{10... | collective-permute-start | bytes 1327112 | tf_op jit(solution)/shard_map/ppermute | solution.py:77
  170.3 11.6 %collective-permute-start.16 = (bf16[1,36,6144]{2,1,0:T(8,128)(2,1)S(1)}, bf16[1,36,6144]{2,1,0:T(8,128)(2,1)S(1)}, u32[]{:S(2)}, u32[]{:S(2)}) collective-permute-start(bf16[1,36,6144]{2,1,0:T(8,128)(2,1)S(1)} %convert_element_type.117), channel_id=1, source_target_pairs={{0,16},{8,24},{16,0},{24,8},{1,17},{9,25},{17,1},{25,9},{2,18},{10... | collective-permute-start | bytes 1327112 | tf_op jit(solution)/shard_map/ppermute | solution.py:77
  172.9 9.2 %collective-permute-start.15 = (bf16[2,36,6144]{2,1,0:T(8,128)(2,1)}, bf16[2,36,6144]{2,1,0:T(8,128)(2,1)S(1)}, u32[]{:S(2)}, u32[]{:S(2)}) collective-permute-start(bf16[2,36,6144]{2,1,0:T(8,128)(2,1)} %pad_maximum_fusion.2), channel_id=1, source_target_pairs={{0,8},{8,0},{16,24},{24,16},{1,9},{9,1},{17,25},{25,17},{2,10},{10... | collective-permute-start | bytes 2654216 | tf_op jit(solution)/shard_map/ppermute | solution.py:77
  182.0 2.6 %collective-permute-start.17 = (bf16[2,36,6144]{2,1,0:T(8,128)(2,1)S(1)}, bf16[2,36,6144]{2,1,0:T(8,128)(2,1)S(1)}, u32[]{:S(2)}, u32[]{:S(2)}) collective-permute-start(bf16[2,36,6144]{2,1,0:T(8,128)(2,1)S(1)} %pad_maximum_fusion.3), channel_id=1, source_target_pairs={{0,8},{8,0},{16,24},{24,16},{1,9},{9,1},{17,25},{25,17},{2,10},{10... | collective-permute-start | bytes 2654216 | tf_op jit(solution)/shard_map/ppermute | solution.py:77

commit v6 on v5

--- a/solution.py
+++ b/solution.py
@@ -36,7 +36,7 @@
     row = lax.broadcasted_iota(jnp.int32, (h, h), 0)
     col = lax.broadcasted_iota(jnp.int32, (h, h), 1)
     folded = jnp.where(row <= col, upper_a, lower_c)
-    diag_c = jnp.diagonal(lower_c)
+    diag_c = jnp.sum(jnp.where(row == col, lower_c, 0.0), axis=0)
     payload = jnp.concatenate([folded, block_b], axis=1)
     extra = jnp.concatenate([diag_c, jnp.zeros((h,), jnp.float32)])[None, :]
     rows = -(-(h + 1) // size) * size

time: 189 us -> 181 us (0.958)
  local copies, waits for them, and re-layouts: 13.5 us -> 6.24 us
    gather x2 -> x0, local copies, waits for them, and re-layouts: 5.98 us -> none  [gram_allreduce(): diag_c = jnp.diagonal(lower_c)]
where the time goes in v6:
time: 181 us
  blocking collectives  62.3 us (34%)
  waiting for transfers between devices  58.7 us (32%)
  starting transfers between devices  29.1 us (16%)
  other arithmetic  10.1 us (6%)
  between operations  9.23 us (5%)
  local copies, waits for them, and re-layouts  6.24 us (3%)
  matrix products  5.14 us (3%)
    all_to_all x2, blocking collectives, gram_allreduce(): lax.all_to_all(spread, axis, split_axis=0, concat_axis=0, tiled=True)  32 us
    ppermute x14, waiting for transfers between devices, gram_allreduce(): acc = acc + lax.ppermute(outgoing, axis, _shift_pairs(size, s))  23.4 us
    all_to_all x1, waiting for transfers between devices, per_device(): lax.all_to_all(rows_here, 'tensor', split_axis=1, concat_axis=0, tiled=True)  21 us
    ppermute x14, starting transfers between devices, gram_allreduce(): acc = acc + lax.ppermute(outgoing, axis, _shift_pairs(size, s))  18.5 us
    all_to_all x1, blocking collectives, per_device(): lax.all_to_all(piece, 'tensor', split_axis=0, concat_axis=1, tiled=True)  16.7 us
    all_to_all x1, blocking collectives, total_over(): got = lax.all_to_all(spread, axis, split_axis=0, concat_axis=0, tiled=True)  13.6 us
    all_to_all x1, waiting for transfers between devices, per_device(): lax.all_to_all(piece, 'tensor', split_axis=0, concat_axis=1, tiled=True)  11.3 us
    all_to_all x1, starting transfers between devices, per_device(): lax.all_to_all(piece, 'tensor', split_axis=0, concat_axis=1, tiled=True)  3.8 us
  transfers between devices with their start and end apart: 20, of which 15 were waited for; matrix products, arithmetic and copies ran while one was open for 2% of the time, Pallas kernels for 0%

profile of v6, /device:TPU:0, one launch (start us, length us, event | category | flops | bytes accessed | tf_op | source)
XLA Modules:
  0.0 180.7 jit_solution(6782484762427310521)
XLA Ops:
  0.6 2.9 %multiply_reduce_fusion = (f32[]{:T(128)}, f32[1,72,6144]{2,1,0:T(8,128)S(1)}) fusion(bf16[1,72,6144]{2,1,0:T(8,128)(2,1)} %param.3, f32[1,72,6144]{2,1,0:T(8,128)} %param.4), kind=kLoop, calls=%fused_computation.8 | loop fusion | flops 3096575 | bytes 4423684 | tf_op jit(solution)/shard_map/reduce_sum | solution.py:88
  3.5 0.6 broadcast_in_dim.58
  4.2 13.6 %all_to_all.52 = f32[8,1,1]{2,1,0:T(1,128)S(1)} all-to-all(f32[8,1,1]{2,1,0:T(1,128)S(1)} %broadcast_in_dim.58), channel_id=1, replica_groups=mesh['dp'=4,'tensor'=8] {'tensor'}, dimensions={0} | all-to-all | bytes 64 | tf_op jit(solution)/shard_map/all_to_all | solution.py:26
  17.8 0.6 reduce_sum.46
  19.1 0.3 divide_convert_fusion
  19.5 1.1 copy.35
  20.6 3.6 %all-to-all-start.1 = ((bf16[72,8,768]{2,0,1:T(8,128)(2,1)}), bf16[72,8,768]{2,0,1:T(8,128)(2,1)S(1)}, u32[]{:S(2)}, u32[]{:S(2)}) async-start(bf16[72,8,768]{2,0,1:T(8,128)(2,1)} %copy.35), calls=%async_computation.1 | async-start | bytes 1769472 | tf_op jit(solution)/shard_map/all_to_all | solution.py:90
  24.4 21.0 %all-to-all-done.1 = bf16[72,8,768]{2,0,1:T(8,128)(2,1)S(1)} async-done(((bf16[72,8,768]{2,0,1:T(8,128)(2,1)}), bf16[72,8,768]{2,0,1:T(8,128)(2,1)S(1)}, u32[]{:S(2)}, u32[]{:S(2)}) %all-to-all-start.1) | async-done | bytes 884768 | tf_op jit(solution)/shard_map/all_to_all | solution.py:90
  45.4 0.9 fusion.66
  46.3 0.2 slice_select_fusion.1
  46.5 0.2 maximum_maximum_fusion.1
  46.9 1.3 collective-permute-start
  48.2 3.5 %collective-permute-start.6 = (f32[37,576]{1,0:T(8,128)S(1)}, f32[37,576]{1,0:T(8,128)S(1)}, u32[]{:S(2)}, u32[]{:S(2)}) collective-permute-start(f32[37,576]{1,0:T(8,128)S(1)} %get-tuple-element.32), channel_id=1, source_target_pairs={{0,7},{1,0},{2,1},{3,2},{4,3},{5,4},{6,5},{7,6},{8,15},{9,8},{10,9... | collective-permute-start | bytes 255752 | tf_op jit(solution)/shard_map/ppermute | solution.py:52
  51.7 2.9 %collective-permute-start.3 = (f32[37,576]{1,0:T(8,128)S(1)}, f32[37,576]{1,0:T(8,128)S(1)}, u32[]{:S(2)}, u32[]{:S(2)}) collective-permute-start(f32[37,576]{1,0:T(8,128)S(1)} %get-tuple-element.35), channel_id=1, source_target_pairs={{0,4},{1,5},{2,6},{3,7},{4,0},{5,1},{6,2},{7,3},{8,12},{9,13},{10,... | collective-permute-start | bytes 255752 | tf_op jit(solution)/shard_map/ppermute | solution.py:52
  54.9 1.7 collective-permute-start.1
  56.7 0.3 collective-permute-done.5
  56.9 2.2 %collective-permute-done.4 = f32[37,576]{1,0:T(8,128)S(1)} collective-permute-done((f32[37,576]{1,0:T(8,128)S(1)}, f32[37,576]{1,0:T(8,128)S(1)}, u32[]{:S(2)}, u32[]{:S(2)}) %collective-permute-start.4) | collective-permute-done | bytes 85280 | tf_op jit(solution)/shard_map/ppermute | solution.py:52
  59.1 7.9 %collective-permute-done.3 = f32[37,576]{1,0:T(8,128)S(1)} collective-permute-done((f32[37,576]{1,0:T(8,128)S(1)}, f32[37,576]{1,0:T(8,128)S(1)}, u32[]{:S(2)}, u32[]{:S(2)}) %collective-permute-start.3) | collective-permute-done | bytes 85280 | tf_op jit(solution)/shard_map/ppermute | solution.py:52
  67.0 0.6 collective-permute-done.2
  67.8 16.0 %all_to_all.53 = bf16[8,37,576]{2,1,0:T(8,128)(2,1)S(1)} all-to-all(bf16[8,37,576]{2,1,0:T(8,128)(2,1)S(1)} %broadcast_in_dim.61), channel_id=1, replica_groups=mesh['dp'=4,'tensor'=8] {'tensor'}, dimensions={0} | all-to-all | bytes 681984 | tf_op jit(solution)/shard_map/all_to_all | solution.py:55
  84.6 1.7 add_convert_fusion.1
  86.3 0.9 fusion.67
  87.2 0.2 slice_select_fusion
  87.8 1.2 collective-permute-start.7
  89.0 3.6 %collective-permute-start.13 = (f32[37,576]{1,0:T(8,128)S(1)}, f32[37,576]{1,0:T(8,128)S(1)}, u32[]{:S(2)}, u32[]{:S(2)}) collective-permute-start(f32[37,576]{1,0:T(8,128)S(1)} %get-tuple-element.25), channel_id=1, source_target_pairs={{0,7},{1,0},{2,1},{3,2},{4,3},{5,4},{6,5},{7,6},{8,15},{9,8},{10,9... | collective-permute-start | bytes 255752 | tf_op jit(solution)/shard_map/ppermute | solution.py:52
  92.6 2.9 %collective-permute-start.10 = (f32[37,576]{1,0:T(8,128)S(1)}, f32[37,576]{1,0:T(8,128)S(1)}, u32[]{:S(2)}, u32[]{:S(2)}) collective-permute-start(f32[37,576]{1,0:T(8,128)S(1)} %get-tuple-element.28), channel_id=1, source_target_pairs={{0,4},{1,5},{2,6},{3,7},{4,0},{5,1},{6,2},{7,3},{8,12},{9,13},{10,... | collective-permute-start | bytes 255752 | tf_op jit(solution)/shard_map/ppermute | solution.py:52
  95.5 0.7 collective-permute-done.7
  96.3 1.4 collective-permute-start.8
  97.7 0.4 collective-permute-done.12
  98.1 2.2 %collective-permute-done.11 = f32[37,576]{1,0:T(8,128)S(1)} collective-permute-done((f32[37,576]{1,0:T(8,128)S(1)}, f32[37,576]{1,0:T(8,128)S(1)}, u32[]{:S(2)}, u32[]{:S(2)}) %collective-permute-start.11) | collective-permute-done | bytes 85280 | tf_op jit(solution)/shard_map/ppermute | solution.py:52
  100.3 8.7 %collective-permute-done.10 = f32[37,576]{1,0:T(8,128)S(1)} collective-permute-done((f32[37,576]{1,0:T(8,128)S(1)}, f32[37,576]{1,0:T(8,128)S(1)}, u32[]{:S(2)}, u32[]{:S(2)}) %collective-permute-start.10) | collective-permute-done | bytes 85280 | tf_op jit(solution)/shard_map/ppermute | solution.py:52
  109.2 15.9 %all_to_all.54 = bf16[8,37,576]{2,1,0:T(8,128)(2,1)S(1)} all-to-all(bf16[8,37,576]{2,1,0:T(8,128)(2,1)S(1)} %broadcast_in_dim.65), channel_id=1, replica_groups=mesh['dp'=4,'tensor'=8] {'tensor'}, dimensions={0} | all-to-all | bytes 681984 | tf_op jit(solution)/shard_map/all_to_all | solution.py:55
  125.9 1.7 add_convert_fusion
  127.6 0.9 fusion.64
  128.4 16.7 %all_to_all.55 = bf16[8,36,768]{2,1,0:T(8,128)(2,1)S(1)} all-to-all(bf16[8,36,768]{2,1,0:T(8,128)(2,1)S(1)} %get-tuple-element.22), channel_id=1, replica_groups=mesh['dp'=4,'tensor'=8] {'tensor'}, dimensions={0} | all-to-all | bytes 884736 | tf_op jit(solution)/shard_map/all_to_all | solution.py:111
  145.2 3.8 %all-to-all-start.5 = ((bf16[8,36,768]{2,1,0:T(8,128)(2,1)}), bf16[8,36,768]{2,1,0:T(8,128)(2,1)S(1)}, u32[]{:S(2)}, u32[]{:S(2)}) async-start(bf16[8,36,768]{2,1,0:T(8,128)(2,1)} %get-tuple-element.23), calls=%async_computation.5 | async-start | bytes 983040 | tf_op jit(solution)/shard_map/all_to_all | solution.py:111
  149.2 0.3 convert_element_type.113
  149.4 1.6 collective-permute-start.14
  151.1 11.3 %all-to-all-done.5 = bf16[8,36,768]{2,1,0:T(8,128)(2,1)S(1)} async-done(((bf16[8,36,768]{2,1,0:T(8,128)(2,1)}), bf16[8,36,768]{2,1,0:T(8,128)(2,1)S(1)}, u32[]{:S(2)}, u32[]{:S(2)}) %all-to-all-start.5) | async-done | bytes 442400 | tf_op jit(solution)/shard_map/all_to_all | solution.py:111
  162.6 0.3 convert_element_type.117
  162.9 1.6 collective-permute-start.16
  164.4 1.1 pad_maximum_fusion.2
  165.5 0.7 fusion.65
  173.6 0.9 collective-permute-done.16
  174.8 0.3 pad_maximum_fusion
  175.3 2.0 %collective-permute-done.17 = bf16[2,36,6144]{2,1,0:T(8,128)(2,1)S(1)} collective-permute-done((bf16[2,36,6144]{2,1,0:T(8,128)(2,1)S(1)}, bf16[2,36,6144]{2,1,0:T(8,128)(2,1)S(1)}, u32[]{:S(2)}, u32[]{:S(2)}) %collective-permute-start.17) | collective-permute-done | bytes 884768 | tf_op jit(solution)/shard_map/ppermute | solution.py:77
  177.3 0.3 pad_maximum_fusion.1
  177.8 2.9 %maximum_maximum_fusion = bf16[4,72,6144]{2,1,0:T(8,128)(2,1)} fusion(bf16[1,36,6144]{2,1,0:T(8,128)(2,1)S(1)} %get-tuple-element.9, bf16[1,36,6144]{2,1,0:T(8,128)(2,1)S(1)} %get-tuple-element.5, bf16[1,36,6144]{2,1,0:T(8,128)(2,1)S(1)} %get-tuple-element.10, bf16[1,36,6144]{2,1,0:T(8,128)(2,1)S(1)} %get-tuple-element.6, ...), kind=kLoop, calls=%fused_computation | loop fusion | flops 28311552 | bytes 7077888 | tf_op jit(solution)/shard_map/concatenate | solution.py:123
  (61 shorter events, 4.0 us)
Async XLA Ops:
  0.6 18.5 %copy-start.1 = (bf16[1,72,6144]{2,1,0:T(8,128)(2,1)S(1)}, bf16[1,72,6144]{2,1,0:T(8,128)(2,1)}, u32[]{:S(2)}) copy-start(bf16[1,72,6144]{2,1,0:T(8,128)(2,1)} %param.3) | copy-start | bytes 2654212
  3.5 15.8 %copy-start = (f32[1,72,6144]{2,1,0:T(8,128)}, f32[1,72,6144]{2,1,0:T(8,128)S(1)}, u32[]{:S(2)}) copy-start(f32[1,72,6144]{2,1,0:T(8,128)S(1)} %get-tuple-element.3) | copy-start | bytes 5308420
  20.6 24.8 %all-to-all-start.1 = ((bf16[72,8,768]{2,0,1:T(8,128)(2,1)}), bf16[72,8,768]{2,0,1:T(8,128)(2,1)S(1)}, u32[]{:S(2)}, u32[]{:S(2)}) async-start(bf16[72,8,768]{2,0,1:T(8,128)(2,1)} %copy.35), calls=%async_computation.1 | async-start | bytes 1769472 | tf_op jit(solution)/shard_map/all_to_all | solution.py:90
  46.9 7.9 %collective-permute-start = (f32[37,576]{1,0:T(8,128)S(1)}, f32[37,576]{1,0:T(8,128)S(1)}, u32[]{:S(2)}, u32[]{:S(2)}) collective-permute-start(f32[37,576]{1,0:T(8,128)S(1)} %get-tuple-element.31), channel_id=1, source_target_pairs={{0,1},{1,2},{2,3},{3,4},{4,5},{5,6},{6,7},{7,0},{8,9},{9,10},{10,1... | collective-permute-start | bytes 255752 | tf_op jit(solution)/shard_map/ppermute | solution.py:52
  48.2 6.7 %collective-permute-start.6 = (f32[37,576]{1,0:T(8,128)S(1)}, f32[37,576]{1,0:T(8,128)S(1)}, u32[]{:S(2)}, u32[]{:S(2)}) collective-permute-start(f32[37,576]{1,0:T(8,128)S(1)} %get-tuple-element.32), channel_id=1, source_target_pairs={{0,7},{1,0},{2,1},{3,2},{4,3},{5,4},{6,5},{7,6},{8,15},{9,8},{10,9... | collective-permute-start | bytes 255752 | tf_op jit(solution)/shard_map/ppermute | solution.py:52
  51.7 5.2 %collective-permute-start.5 = (f32[37,576]{1,0:T(8,128)S(1)}, f32[37,576]{1,0:T(8,128)S(1)}, u32[]{:S(2)}, u32[]{:S(2)}) collective-permute-start(f32[37,576]{1,0:T(8,128)S(1)} %get-tuple-element.33), channel_id=1, source_target_pairs={{0,6},{1,7},{2,0},{3,1},{4,2},{5,3},{6,4},{7,5},{8,14},{9,15},{10,... | collective-permute-start | bytes 255752 | tf_op jit(solution)/shard_map/ppermute | solution.py:52
  51.7 7.4 %collective-permute-start.4 = (f32[37,576]{1,0:T(8,128)S(1)}, f32[37,576]{1,0:T(8,128)S(1)}, u32[]{:S(2)}, u32[]{:S(2)}) collective-permute-start(f32[37,576]{1,0:T(8,128)S(1)} %get-tuple-element.34), channel_id=1, source_target_pairs={{0,5},{1,6},{2,7},{3,0},{4,1},{5,2},{6,3},{7,4},{8,13},{9,14},{10,... | collective-permute-start | bytes 255752 | tf_op jit(solution)/shard_map/ppermute | solution.py:52
  51.7 15.3 %collective-permute-start.3 = (f32[37,576]{1,0:T(8,128)S(1)}, f32[37,576]{1,0:T(8,128)S(1)}, u32[]{:S(2)}, u32[]{:S(2)}) collective-permute-start(f32[37,576]{1,0:T(8,128)S(1)} %get-tuple-element.35), channel_id=1, source_target_pairs={{0,4},{1,5},{2,6},{3,7},{4,0},{5,1},{6,2},{7,3},{8,12},{9,13},{10,... | collective-permute-start | bytes 255752 | tf_op jit(solution)/shard_map/ppermute | solution.py:52
  54.8 12.8 %collective-permute-start.2 = (f32[37,576]{1,0:T(8,128)S(1)}, f32[37,576]{1,0:T(8,128)S(1)}, u32[]{:S(2)}, u32[]{:S(2)}) collective-permute-start(f32[37,576]{1,0:T(8,128)S(1)} %get-tuple-element.36), channel_id=1, source_target_pairs={{0,3},{1,4},{2,5},{3,6},{4,7},{5,0},{6,1},{7,2},{8,11},{9,12},{10,... | collective-permute-start | bytes 255752 | tf_op jit(solution)/shard_map/ppermute | solution.py:52
  54.9 12.7 %collective-permute-start.1 = (f32[37,576]{1,0:T(8,128)S(1)}, f32[37,576]{1,0:T(8,128)S(1)}, u32[]{:S(2)}, u32[]{:S(2)}) collective-permute-start(f32[37,576]{1,0:T(8,128)S(1)} %get-tuple-element.37), channel_id=1, source_target_pairs={{0,2},{1,3},{2,4},{3,5},{4,6},{5,7},{6,0},{7,1},{8,10},{9,11},{10,... | collective-permute-start | bytes 255752 | tf_op jit(solution)/shard_map/ppermute | solution.py:52
  87.8 8.4 %collective-permute-start.7 = (f32[37,576]{1,0:T(8,128)S(1)}, f32[37,576]{1,0:T(8,128)S(1)}, u32[]{:S(2)}, u32[]{:S(2)}) collective-permute-start(f32[37,576]{1,0:T(8,128)S(1)} %get-tuple-element.24), channel_id=1, source_target_pairs={{0,1},{1,2},{2,3},{3,4},{4,5},{5,6},{6,7},{7,0},{8,9},{9,10},{10,1... | collective-permute-start | bytes 255752 | tf_op jit(solution)/shard_map/ppermute | solution.py:52
  89.0 7.2 %collective-permute-start.13 = (f32[37,576]{1,0:T(8,128)S(1)}, f32[37,576]{1,0:T(8,128)S(1)}, u32[]{:S(2)}, u32[]{:S(2)}) collective-permute-start(f32[37,576]{1,0:T(8,128)S(1)} %get-tuple-element.25), channel_id=1, source_target_pairs={{0,7},{1,0},{2,1},{3,2},{4,3},{5,4},{6,5},{7,6},{8,15},{9,8},{10,9... | collective-permute-start | bytes 255752 | tf_op jit(solution)/shard_map/ppermute | solution.py:52
  92.6 5.5 %collective-permute-start.12 = (f32[37,576]{1,0:T(8,128)S(1)}, f32[37,576]{1,0:T(8,128)S(1)}, u32[]{:S(2)}, u32[]{:S(2)}) collective-permute-start(f32[37,576]{1,0:T(8,128)S(1)} %get-tuple-element.26), channel_id=1, source_target_pairs={{0,6},{1,7},{2,0},{3,1},{4,2},{5,3},{6,4},{7,5},{8,14},{9,15},{10,... | collective-permute-start | bytes 255752 | tf_op jit(solution)/shard_map/ppermute | solution.py:52
  92.6 7.7 %collective-permute-start.11 = (f32[37,576]{1,0:T(8,128)S(1)}, f32[37,576]{1,0:T(8,128)S(1)}, u32[]{:S(2)}, u32[]{:S(2)}) collective-permute-start(f32[37,576]{1,0:T(8,128)S(1)} %get-tuple-element.27), channel_id=1, source_target_pairs={{0,5},{1,6},{2,7},{3,0},{4,1},{5,2},{6,3},{7,4},{8,13},{9,14},{10,... | collective-permute-start | bytes 255752 | tf_op jit(solution)/shard_map/ppermute | solution.py:52
  92.6 16.3 %collective-permute-start.10 = (f32[37,576]{1,0:T(8,128)S(1)}, f32[37,576]{1,0:T(8,128)S(1)}, u32[]{:S(2)}, u32[]{:S(2)}) collective-permute-start(f32[37,576]{1,0:T(8,128)S(1)} %get-tuple-element.28), channel_id=1, source_target_pairs={{0,4},{1,5},{2,6},{3,7},{4,0},{5,1},{6,2},{7,3},{8,12},{9,13},{10,... | collective-permute-start | bytes 255752 | tf_op jit(solution)/shard_map/ppermute | solution.py:52
  96.3 12.8 %collective-permute-start.9 = (f32[37,576]{1,0:T(8,128)S(1)}, f32[37,576]{1,0:T(8,128)S(1)}, u32[]{:S(2)}, u32[]{:S(2)}) collective-permute-start(f32[37,576]{1,0:T(8,128)S(1)} %get-tuple-element.29), channel_id=1, source_target_pairs={{0,3},{1,4},{2,5},{3,6},{4,7},{5,0},{6,1},{7,2},{8,11},{9,12},{10,... | collective-permute-start | bytes 255752 | tf_op jit(solution)/shard_map/ppermute | solution.py:52
  96.3 12.8 %collective-permute-start.8 = (f32[37,576]{1,0:T(8,128)S(1)}, f32[37,576]{1,0:T(8,128)S(1)}, u32[]{:S(2)}, u32[]{:S(2)}) collective-permute-start(f32[37,576]{1,0:T(8,128)S(1)} %get-tuple-element.30), channel_id=1, source_target_pairs={{0,2},{1,3},{2,4},{3,5},{4,6},{5,7},{6,0},{7,1},{8,10},{9,11},{10,... | collective-permute-start | bytes 255752 | tf_op jit(solution)/shard_map/ppermute | solution.py:52
  145.2 5.8 %copy-start.2 = (s32[4]{0:T(128)S(1)}, s32[4]{0:T(128)}, u32[]{:S(2)}) copy-start(s32[4]{0:T(128)} %param.5) | copy-start | bytes 52
  145.2 17.3 %all-to-all-start.5 = ((bf16[8,36,768]{2,1,0:T(8,128)(2,1)}), bf16[8,36,768]{2,1,0:T(8,128)(2,1)S(1)}, u32[]{:S(2)}, u32[]{:S(2)}) async-start(bf16[8,36,768]{2,1,0:T(8,128)(2,1)} %get-tuple-element.23), calls=%async_computation.5 | async-start | bytes 983040 | tf_op jit(solution)/shard_map/all_to_all | solution.py:111
  149.4 15.0 %collective-permute-start.14 = (bf16[1,36,6144]{2,1,0:T(8,128)(2,1)S(1)}, bf16[1,36,6144]{2,1,0:T(8,128)(2,1)S(1)}, u32[]{:S(2)}, u32[]{:S(2)}) collective-permute-start(bf16[1,36,6144]{2,1,0:T(8,128)(2,1)S(1)} %convert_element_type.113), channel_id=1, source_target_pairs={{0,16},{8,24},{16,0},{24,8},{1,17},{9,25},{17,1},{25,9},{2,18},{10... | collective-permute-start | bytes 1327112 | tf_op jit(solution)/shard_map/ppermute | solution.py:77
  162.9 11.6 %collective-permute-start.16 = (bf16[1,36,6144]{2,1,0:T(8,128)(2,1)S(1)}, bf16[1,36,6144]{2,1,0:T(8,128)(2,1)S(1)}, u32[]{:S(2)}, u32[]{:S(2)}) collective-permute-start(bf16[1,36,6144]{2,1,0:T(8,128)(2,1)S(1)} %convert_element_type.117), channel_id=1, source_target_pairs={{0,16},{8,24},{16,0},{24,8},{1,17},{9,25},{17,1},{25,9},{2,18},{10... | collective-permute-start | bytes 1327112 | tf_op jit(solution)/shard_map/ppermute | solution.py:77
  165.5 9.2 %collective-permute-start.15 = (bf16[2,36,6144]{2,1,0:T(8,128)(2,1)}, bf16[2,36,6144]{2,1,0:T(8,128)(2,1)S(1)}, u32[]{:S(2)}, u32[]{:S(2)}) collective-permute-start(bf16[2,36,6144]{2,1,0:T(8,128)(2,1)} %pad_maximum_fusion.2), channel_id=1, source_target_pairs={{0,8},{8,0},{16,24},{24,16},{1,9},{9,1},{17,25},{25,17},{2,10},{10... | collective-permute-start | bytes 2654216 | tf_op jit(solution)/shard_map/ppermute | solution.py:77
  174.6 2.6 %collective-permute-start.17 = (bf16[2,36,6144]{2,1,0:T(8,128)(2,1)S(1)}, bf16[2,36,6144]{2,1,0:T(8,128)(2,1)S(1)}, u32[]{:S(2)}, u32[]{:S(2)}) collective-permute-start(bf16[2,36,6144]{2,1,0:T(8,128)(2,1)S(1)} %pad_maximum_fusion.3), channel_id=1, source_target_pairs={{0,8},{8,0},{16,24},{24,16},{1,9},{9,1},{17,25},{25,17},{2,10},{10... | collective-permute-start | bytes 2654216 | tf_op jit(solution)/shard_map/ppermute | solution.py:77

commit v7 on v6

--- a/solution.py
+++ b/solution.py
@@ -46,13 +46,21 @@
     per = rows // size
     blocks = payload.reshape(size, per, 2 * h)
     me = lax.axis_index(axis)
-    acc = lax.dynamic_index_in_dim(blocks, me, 0, keepdims=False)
-    for s in range(1, size):
-        outgoing = lax.dynamic_index_in_dim(blocks, (me + s) % size, 0, keepdims=False)
-        acc = acc + lax.ppermute(outgoing, axis, _shift_pairs(size, s))
-    mine = acc.astype(jnp.bfloat16)
-    spread = jnp.broadcast_to(mine[None], (size,) + mine.shape)
-    full = lax.all_to_all(spread, axis, split_axis=0, concat_axis=0, tiled=True).reshape(rows, 2 * h)
+    cut = 8 * (per // 16)
+    chunks = [(0, cut), (cut, per)] if cut > 0 else [(0, per)]
+    reduced = []
+    for lo, hi in chunks:
+        part = blocks[:, lo:hi, :]
+        acc = lax.dynamic_index_in_dim(part, me, 0, keepdims=False)
+        for s in range(1, size):
+            outgoing = lax.dynamic_index_in_dim(part, (me + s) % size, 0, keepdims=False)
+            acc = acc + lax.ppermute(outgoing, axis, _shift_pairs(size, s))
+        reduced.append(acc.astype(jnp.bfloat16))
+    pieces = []
+    for mine in reduced:
+        spread = jnp.broadcast_to(mine[None], (size,) + mine.shape)
+        pieces.append(lax.all_to_all(spread, axis, split_axis=0, concat_axis=0, tiled=True))
+    full = jnp.concatenate(pieces, axis=1).reshape(rows, 2 * h)
     folded_r = full[:h, :h]
     block_br = full[:h, h:]
     diag_cr = full[h, :h]

time: 181 us -> 197 us (1.088)
  starting transfers between devices: 29.1 us -> 54.9 us
  blocking collectives: 62.3 us -> 53 us
  waiting for transfers between devices: 58.7 us -> 55.8 us
    ppermute x14 -> x28, starting transfers between devices: 18.5 us -> 35.7 us  [gram_allreduce(): acc = acc + lax.ppermute(outgoing, axis, _shift_pairs(size, s))]
    all_to_all x0 -> x2, waiting for transfers between devices: none -> 14.8 us  [gram_allreduce(): lax.all_to_all(spread, axis, split_axis=0, concat_axis=0, tiled=True)]
    ppermute x14 -> x28, waiting for transfers between devices: 23.4 us -> 10.5 us  [gram_allreduce(): acc = acc + lax.ppermute(outgoing, axis, _shift_pairs(size, s))]
    all_to_all x0 -> x2, starting transfers between devices: none -> 8.15 us  [gram_allreduce(): lax.all_to_all(spread, axis, split_axis=0, concat_axis=0, tiled=True)]
    all_to_all x2, blocking collectives: 32 us -> 24.2 us  [gram_allreduce(): lax.all_to_all(spread, axis, split_axis=0, concat_axis=0, tiled=True)]
    all_to_all x1, waiting for transfers between devices: 11.3 us -> 7.81 us  [per_device(): lax.all_to_all(piece, 'tensor', split_axis=0, concat_axis=1, tiled=True)]
  transfers between devices with their start and end apart: 20 -> 36, of which waited for: 15 -> 13; matrix products, arithmetic and copies ran while one was open for 2% -> 3% of each run, Pallas kernels for 0% -> 0%
where the time goes in v7:
time: 197 us; the launch traced here: 196 us
  waiting for transfers between devices  55.8 us (28%)
  starting transfers between devices  54.9 us (28%)
  blocking collectives  53 us (27%)
  other arithmetic  10.2 us (5%)
  between operations  9.35 us (5%)
  local copies, waits for them, and re-layouts  7.67 us (4%)
  matrix products  5.14 us (3%)
    ppermute x28, starting transfers between devices, gram_allreduce(): acc = acc + lax.ppermute(outgoing, axis, _shift_pairs(size, s))  35.7 us
    all_to_all x2, blocking collectives, gram_allreduce(): lax.all_to_all(spread, axis, split_axis=0, concat_axis=0, tiled=True)  24.2 us
    all_to_all x1, waiting for transfers between devices, per_device(): lax.all_to_all(rows_here, 'tensor', split_axis=1, concat_axis=0, tiled=True)  21 us
    all_to_all x1, blocking collectives, per_device(): lax.all_to_all(piece, 'tensor', split_axis=0, concat_axis=1, tiled=True)  15.2 us
    all_to_all x2, waiting for transfers between devices, gram_allreduce(): lax.all_to_all(spread, axis, split_axis=0, concat_axis=0, tiled=True)  14.8 us
    all_to_all x1, blocking collectives, total_over(): got = lax.all_to_all(spread, axis, split_axis=0, concat_axis=0, tiled=True)  13.6 us
    ppermute x28, waiting for transfers between devices, gram_allreduce(): acc = acc + lax.ppermute(outgoing, axis, _shift_pairs(size, s))  10.5 us
    all_to_all x2, starting transfers between devices, gram_allreduce(): lax.all_to_all(spread, axis, split_axis=0, concat_axis=0, tiled=True)  8.15 us
  transfers between devices with their start and end apart: 36, of which 13 were waited for; matrix products, arithmetic and copies ran while one was open for 3% of the time, Pallas kernels for 0%

profile of v7, /device:TPU:0, one launch (start us, length us, event | category | flops | bytes accessed | tf_op | source)
XLA Modules:
  0.0 196.0 jit_solution(2173952630704372431)
XLA Ops:
  0.6 2.9 %multiply_reduce_fusion = (f32[]{:T(128)}, f32[1,72,6144]{2,1,0:T(8,128)S(1)}) fusion(bf16[1,72,6144]{2,1,0:T(8,128)(2,1)} %param.3, f32[1,72,6144]{2,1,0:T(8,128)} %param.4), kind=kLoop, calls=%fused_computation.8 | loop fusion | flops 3096575 | bytes 4423684 | tf_op jit(solution)/shard_map/reduce_sum | solution.py:96
  4.2 13.6 %all_to_all.62 = f32[8,1,1]{2,1,0:T(1,128)S(1)} all-to-all(f32[8,1,1]{2,1,0:T(1,128)S(1)} %broadcast_in_dim.70), channel_id=1, replica_groups=mesh['dp'=4,'tensor'=8] {'tensor'}, dimensions={0} | all-to-all | bytes 64 | tf_op jit(solution)/shard_map/all_to_all | solution.py:26
  19.5 1.1 copy.36
  20.6 3.6 %all-to-all-start.1 = ((bf16[72,8,768]{2,0,1:T(8,128)(2,1)}), bf16[72,8,768]{2,0,1:T(8,128)(2,1)S(1)}, u32[]{:S(2)}, u32[]{:S(2)}) async-start(bf16[72,8,768]{2,0,1:T(8,128)(2,1)} %copy.36), calls=%async_computation.1 | async-start | bytes 1769472 | tf_op jit(solution)/shard_map/all_to_all | solution.py:98
  24.4 21.0 %all-to-all-done.1 = bf16[72,8,768]{2,0,1:T(8,128)(2,1)S(1)} async-done(((bf16[72,8,768]{2,0,1:T(8,128)(2,1)}), bf16[72,8,768]{2,0,1:T(8,128)(2,1)S(1)}, u32[]{:S(2)}, u32[]{:S(2)}) %all-to-all-start.1) | async-done | bytes 884768 | tf_op jit(solution)/shard_map/all_to_all | solution.py:98
  45.4 0.9 fusion.80
  47.0 1.3 collective-permute-start
  48.3 3.5 %collective-permute-start.6 = (f32[16,576]{1,0:T(8,128)S(1)}, f32[16,576]{1,0:T(8,128)S(1)}, u32[]{:S(2)}, u32[]{:S(2)}) collective-permute-start(f32[16,576]{1,0:T(8,128)S(1)} %get-tuple-element.53), channel_id=1, source_target_pairs={{0,7},{1,0},{2,1},{3,2},{4,3},{5,4},{6,5},{7,6},{8,15},{9,8},{10,9... | collective-permute-start | bytes 110600 | tf_op jit(solution)/shard_map/ppermute | solution.py:57
  51.8 0.8 collective-permute-start.7
  52.6 1.1 collective-permute-done
  53.8 2.8 %collective-permute-start.13 = (f32[21,576]{1,0:T(8,128)S(1)}, f32[21,576]{1,0:T(8,128)S(1)}, u32[]{:S(2)}, u32[]{:S(2)}) collective-permute-start(f32[21,576]{1,0:T(8,128)S(1)} %get-tuple-element.36), channel_id=1, source_target_pairs={{0,7},{1,0},{2,1},{3,2},{4,3},{5,4},{6,5},{7,6},{8,15},{9,8},{10,9... | collective-permute-start | bytes 145160 | tf_op jit(solution)/shard_map/ppermute | solution.py:57
  56.6 1.1 collective-permute-start.3
  57.7 1.4 collective-permute-start.2
  59.1 2.9 %collective-permute-done.3 = f32[16,576]{1,0:T(8,128)S(1)} collective-permute-done((f32[16,576]{1,0:T(8,128)S(1)}, f32[16,576]{1,0:T(8,128)S(1)}, u32[]{:S(2)}, u32[]{:S(2)}) %collective-permute-start.3) | collective-permute-done | bytes 36896 | tf_op jit(solution)/shard_map/ppermute | solution.py:57
  62.0 1.1 collective-permute-start.12
  63.1 1.3 collective-permute-done.2
  64.4 0.9 collective-permute-done.1
  65.3 2.7 %collective-permute-start.10 = (f32[21,576]{1,0:T(8,128)S(1)}, f32[21,576]{1,0:T(8,128)S(1)}, u32[]{:S(2)}, u32[]{:S(2)}) collective-permute-start(f32[21,576]{1,0:T(8,128)S(1)} %get-tuple-element.39), channel_id=1, source_target_pairs={{0,4},{1,5},{2,6},{3,7},{4,0},{5,1},{6,2},{7,3},{8,12},{9,13},{10,... | collective-permute-start | bytes 145160 | tf_op jit(solution)/shard_map/ppermute | solution.py:57
  68.5 1.7 collective-permute-start.8
  70.2 0.7 broadcast_in_dim.73
  70.9 4.0 %all-to-all-start.2 = ((bf16[8,16,576]{2,1,0:T(8,128)(2,1)}), bf16[8,16,576]{2,1,0:T(8,128)(2,1)S(1)}, u32[]{:S(2)}, u32[]{:S(2)}) async-start(bf16[8,16,576]{2,1,0:T(8,128)(2,1)} %broadcast_in_dim.73), calls=%async_computation.2 | async-start | bytes 327680 | tf_op jit(solution)/shard_map/all_to_all | solution.py:62
  75.2 7.3 %all-to-all-done.2 = bf16[8,16,576]{2,1,0:T(8,128)(2,1)S(1)} async-done(((bf16[8,16,576]{2,1,0:T(8,128)(2,1)}), bf16[8,16,576]{2,1,0:T(8,128)(2,1)S(1)}, u32[]{:S(2)}, u32[]{:S(2)}) %all-to-all-start.2) | async-done | bytes 147488 | tf_op jit(solution)/shard_map/all_to_all | solution.py:62
  82.6 10.5 %all_to_all.63 = bf16[8,21,576]{2,1,0:T(8,128)(2,1)S(1)} all-to-all(bf16[8,21,576]{2,1,0:T(8,128)(2,1)S(1)} %broadcast_in_dim.74), channel_id=1, replica_groups=mesh['dp'=4,'tensor'=8] {'tensor'}, dimensions={0} | all-to-all | bytes 387072 | tf_op jit(solution)/shard_map/all_to_all | solution.py:62
  93.9 1.7 add_convert_fusion.1
  95.6 0.9 fusion.81
  97.3 4.7 %collective-permute-start.20 = (f32[16,576]{1,0:T(8,128)S(1)}, f32[16,576]{1,0:T(8,128)S(1)}, u32[]{:S(2)}, u32[]{:S(2)}) collective-permute-start(f32[16,576]{1,0:T(8,128)S(1)} %get-tuple-element.46), channel_id=1, source_target_pairs={{0,7},{1,0},{2,1},{3,2},{4,3},{5,4},{6,5},{7,6},{8,15},{9,8},{10,9... | collective-permute-start | bytes 110600 | tf_op jit(solution)/shard_map/ppermute | solution.py:57
  102.0 1.8 collective-permute-start.21
  104.0 2.8 %collective-permute-start.27 = (f32[21,576]{1,0:T(8,128)S(1)}, f32[21,576]{1,0:T(8,128)S(1)}, u32[]{:S(2)}, u32[]{:S(2)}) collective-permute-start(f32[21,576]{1,0:T(8,128)S(1)} %get-tuple-element.29), channel_id=1, source_target_pairs={{0,7},{1,0},{2,1},{3,2},{4,3},{5,4},{6,5},{7,6},{8,15},{9,8},{10,9... | collective-permute-start | bytes 145160 | tf_op jit(solution)/shard_map/ppermute | solution.py:57
  106.8 1.1 collective-permute-start.17
  108.0 1.4 collective-permute-start.16
  109.4 3.5 %collective-permute-done.17 = f32[16,576]{1,0:T(8,128)S(1)} collective-permute-done((f32[16,576]{1,0:T(8,128)S(1)}, f32[16,576]{1,0:T(8,128)S(1)}, u32[]{:S(2)}, u32[]{:S(2)}) %collective-permute-start.17) | collective-permute-done | bytes 36896 | tf_op jit(solution)/shard_map/ppermute | solution.py:57
  112.9 1.4 collective-permute-start.26
  115.2 2.9 %collective-permute-start.24 = (f32[21,576]{1,0:T(8,128)S(1)}, f32[21,576]{1,0:T(8,128)S(1)}, u32[]{:S(2)}, u32[]{:S(2)}) collective-permute-start(f32[21,576]{1,0:T(8,128)S(1)} %get-tuple-element.32), channel_id=1, source_target_pairs={{0,4},{1,5},{2,6},{3,7},{4,0},{5,1},{6,2},{7,3},{8,12},{9,13},{10,... | collective-permute-start | bytes 145160 | tf_op jit(solution)/shard_map/ppermute | solution.py:57
  118.5 1.5 collective-permute-start.22
  120.1 0.7 broadcast_in_dim.78
  120.8 4.2 %all-to-all-start.4 = ((bf16[8,16,576]{2,1,0:T(8,128)(2,1)}), bf16[8,16,576]{2,1,0:T(8,128)(2,1)S(1)}, u32[]{:S(2)}, u32[]{:S(2)}) async-start(bf16[8,16,576]{2,1,0:T(8,128)(2,1)} %broadcast_in_dim.78), calls=%async_computation.4 | async-start | bytes 327680 | tf_op jit(solution)/shard_map/all_to_all | solution.py:62
  125.0 7.5 %all-to-all-done.4 = bf16[8,16,576]{2,1,0:T(8,128)(2,1)S(1)} async-done(((bf16[8,16,576]{2,1,0:T(8,128)(2,1)}), bf16[8,16,576]{2,1,0:T(8,128)(2,1)S(1)}, u32[]{:S(2)}, u32[]{:S(2)}) %all-to-all-start.4) | async-done | bytes 147488 | tf_op jit(solution)/shard_map/all_to_all | solution.py:62
  132.5 13.7 %all_to_all.64 = bf16[8,21,576]{2,1,0:T(8,128)(2,1)S(1)} all-to-all(bf16[8,21,576]{2,1,0:T(8,128)(2,1)S(1)} %broadcast_in_dim.79), channel_id=1, replica_groups=mesh['dp'=4,'tensor'=8] {'tensor'}, dimensions={0} | all-to-all | bytes 387072 | tf_op jit(solution)/shard_map/all_to_all | solution.py:62
  147.0 1.7 add_convert_fusion
  148.7 0.9 fusion.78
  149.6 15.2 %all_to_all.65 = bf16[8,36,768]{2,1,0:T(8,128)(2,1)S(1)} all-to-all(bf16[8,36,768]{2,1,0:T(8,128)(2,1)S(1)} %get-tuple-element.22), channel_id=1, replica_groups=mesh['dp'=4,'tensor'=8] {'tensor'}, dimensions={0} | all-to-all | bytes 884736 | tf_op jit(solution)/shard_map/all_to_all | solution.py:119
  164.8 3.8 %all-to-all-start.7 = ((bf16[8,36,768]{2,1,0:T(8,128)(2,1)}), bf16[8,36,768]{2,1,0:T(8,128)(2,1)S(1)}, u32[]{:S(2)}, u32[]{:S(2)}) async-start(bf16[8,36,768]{2,1,0:T(8,128)(2,1)} %get-tuple-element.23), calls=%async_computation.7 | async-start | bytes 983040 | tf_op jit(solution)/shard_map/all_to_all | solution.py:119
  169.0 1.6 collective-permute-start.28
  170.7 7.8 %all-to-all-done.7 = bf16[8,36,768]{2,1,0:T(8,128)(2,1)S(1)} async-done(((bf16[8,36,768]{2,1,0:T(8,128)(2,1)}), bf16[8,36,768]{2,1,0:T(8,128)(2,1)S(1)}, u32[]{:S(2)}, u32[]{:S(2)}) %all-to-all-start.7) | async-done | bytes 442400 | tf_op jit(solution)/shard_map/all_to_all | solution.py:119
  178.9 1.6 collective-permute-start.30
  180.5 1.1 pad_maximum_fusion.2
  191.0 1.6 collective-permute-done.31
  193.1 2.9 %maximum_maximum_fusion = bf16[4,72,6144]{2,1,0:T(8,128)(2,1)} fusion(bf16[1,36,6144]{2,1,0:T(8,128)(2,1)S(1)} %get-tuple-element.9, bf16[1,36,6144]{2,1,0:T(8,128)(2,1)S(1)} %get-tuple-element.5, bf16[1,36,6144]{2,1,0:T(8,128)(2,1)S(1)} %get-tuple-element.10, bf16[1,36,6144]{2,1,0:T(8,128)(2,1)S(1)} %get-tuple-element.6, ...), kind=kLoop, calls=%fused_computation | loop fusion | flops 28311552 | bytes 7077888 | tf_op jit(solution)/shard_map/concatenate | solution.py:131
  (105 shorter events, 10.6 us)
Async XLA Ops:
  0.6 18.5 %copy-start.1 = (bf16[1,72,6144]{2,1,0:T(8,128)(2,1)S(1)}, bf16[1,72,6144]{2,1,0:T(8,128)(2,1)}, u32[]{:S(2)}) copy-start(bf16[1,72,6144]{2,1,0:T(8,128)(2,1)} %param.3) | copy-start | bytes 2654212
  3.5 15.8 %copy-start = (f32[1,72,6144]{2,1,0:T(8,128)}, f32[1,72,6144]{2,1,0:T(8,128)S(1)}, u32[]{:S(2)}) copy-start(f32[1,72,6144]{2,1,0:T(8,128)S(1)} %get-tuple-element.3) | copy-start | bytes 5308420
  20.6 24.8 %all-to-all-start.1 = ((bf16[72,8,768]{2,0,1:T(8,128)(2,1)}), bf16[72,8,768]{2,0,1:T(8,128)(2,1)S(1)}, u32[]{:S(2)}, u32[]{:S(2)}) async-start(bf16[72,8,768]{2,0,1:T(8,128)(2,1)} %copy.36), calls=%async_computation.1 | async-start | bytes 1769472 | tf_op jit(solution)/shard_map/all_to_all | solution.py:98
  47.0 6.8 %collective-permute-start = (f32[16,576]{1,0:T(8,128)S(1)}, f32[16,576]{1,0:T(8,128)S(1)}, u32[]{:S(2)}, u32[]{:S(2)}) collective-permute-start(f32[16,576]{1,0:T(8,128)S(1)} %get-tuple-element.52), channel_id=1, source_target_pairs={{0,1},{1,2},{2,3},{3,4},{4,5},{5,6},{6,7},{7,0},{8,9},{9,10},{10,1... | collective-permute-start | bytes 110600 | tf_op jit(solution)/shard_map/ppermute | solution.py:57
  48.3 8.3 %collective-permute-start.6 = (f32[16,576]{1,0:T(8,128)S(1)}, f32[16,576]{1,0:T(8,128)S(1)}, u32[]{:S(2)}, u32[]{:S(2)}) collective-permute-start(f32[16,576]{1,0:T(8,128)S(1)} %get-tuple-element.53), channel_id=1, source_target_pairs={{0,7},{1,0},{2,1},{3,2},{4,3},{5,4},{6,5},{7,6},{8,15},{9,8},{10,9... | collective-permute-start | bytes 110600 | tf_op jit(solution)/shard_map/ppermute | solution.py:57
  51.8 6.0 %collective-permute-start.5 = (f32[16,576]{1,0:T(8,128)S(1)}, f32[16,576]{1,0:T(8,128)S(1)}, u32[]{:S(2)}, u32[]{:S(2)}) collective-permute-start(f32[16,576]{1,0:T(8,128)S(1)} %get-tuple-element.54), channel_id=1, source_target_pairs={{0,6},{1,7},{2,0},{3,1},{4,2},{5,3},{6,4},{7,5},{8,14},{9,15},{10,... | collective-permute-start | bytes 110600 | tf_op jit(solution)/shard_map/ppermute | solution.py:57
  51.8 7.4 %collective-permute-start.4 = (f32[16,576]{1,0:T(8,128)S(1)}, f32[16,576]{1,0:T(8,128)S(1)}, u32[]{:S(2)}, u32[]{:S(2)}) collective-permute-start(f32[16,576]{1,0:T(8,128)S(1)} %get-tuple-element.55), channel_id=1, source_target_pairs={{0,5},{1,6},{2,7},{3,0},{4,1},{5,2},{6,3},{7,4},{8,13},{9,14},{10,... | collective-permute-start | bytes 110600 | tf_op jit(solution)/shard_map/ppermute | solution.py:57
  51.8 16.2 %collective-permute-start.7 = (f32[21,576]{1,0:T(8,128)S(1)}, f32[21,576]{1,0:T(8,128)S(1)}, u32[]{:S(2)}, u32[]{:S(2)}) collective-permute-start(f32[21,576]{1,0:T(8,128)S(1)} %get-tuple-element.35), channel_id=1, source_target_pairs={{0,1},{1,2},{2,3},{3,4},{4,5},{5,6},{6,7},{7,0},{8,9},{9,10},{10,1... | collective-permute-start | bytes 145160 | tf_op jit(solution)/shard_map/ppermute | solution.py:57
  53.8 14.7 %collective-permute-start.13 = (f32[21,576]{1,0:T(8,128)S(1)}, f32[21,576]{1,0:T(8,128)S(1)}, u32[]{:S(2)}, u32[]{:S(2)}) collective-permute-start(f32[21,576]{1,0:T(8,128)S(1)} %get-tuple-element.36), channel_id=1, source_target_pairs={{0,7},{1,0},{2,1},{3,2},{4,3},{5,4},{6,5},{7,6},{8,15},{9,8},{10,9... | collective-permute-start | bytes 145160 | tf_op jit(solution)/shard_map/ppermute | solution.py:57
  56.6 5.4 %collective-permute-start.3 = (f32[16,576]{1,0:T(8,128)S(1)}, f32[16,576]{1,0:T(8,128)S(1)}, u32[]{:S(2)}, u32[]{:S(2)}) collective-permute-start(f32[16,576]{1,0:T(8,128)S(1)} %get-tuple-element.56), channel_id=1, source_target_pairs={{0,4},{1,5},{2,6},{3,7},{4,0},{5,1},{6,2},{7,3},{8,12},{9,13},{10,... | collective-permute-start | bytes 110600 | tf_op jit(solution)/shard_map/ppermute | solution.py:57
  57.7 6.7 %collective-permute-start.2 = (f32[16,576]{1,0:T(8,128)S(1)}, f32[16,576]{1,0:T(8,128)S(1)}, u32[]{:S(2)}, u32[]{:S(2)}) collective-permute-start(f32[16,576]{1,0:T(8,128)S(1)} %get-tuple-element.57), channel_id=1, source_target_pairs={{0,3},{1,4},{2,5},{3,6},{4,7},{5,0},{6,1},{7,2},{8,11},{9,12},{10,... | collective-permute-start | bytes 110600 | tf_op jit(solution)/shard_map/ppermute | solution.py:57
  59.1 6.1 %collective-permute-start.1 = (f32[16,576]{1,0:T(8,128)S(1)}, f32[16,576]{1,0:T(8,128)S(1)}, u32[]{:S(2)}, u32[]{:S(2)}) collective-permute-start(f32[16,576]{1,0:T(8,128)S(1)} %get-tuple-element.58), channel_id=1, source_target_pairs={{0,2},{1,3},{2,4},{3,5},{4,6},{5,7},{6,0},{7,1},{8,10},{9,11},{10,... | collective-permute-start | bytes 110600 | tf_op jit(solution)/shard_map/ppermute | solution.py:57
  62.0 12.9 %collective-permute-start.12 = (f32[21,576]{1,0:T(8,128)S(1)}, f32[21,576]{1,0:T(8,128)S(1)}, u32[]{:S(2)}, u32[]{:S(2)}) collective-permute-start(f32[21,576]{1,0:T(8,128)S(1)} %get-tuple-element.37), channel_id=1, source_target_pairs={{0,6},{1,7},{2,0},{3,1},{4,2},{5,3},{6,4},{7,5},{8,14},{9,15},{10,... | collective-permute-start | bytes 145160 | tf_op jit(solution)/shard_map/ppermute | solution.py:57
  64.4 10.5 %collective-permute-start.11 = (f32[21,576]{1,0:T(8,128)S(1)}, f32[21,576]{1,0:T(8,128)S(1)}, u32[]{:S(2)}, u32[]{:S(2)}) collective-permute-start(f32[21,576]{1,0:T(8,128)S(1)} %get-tuple-element.38), channel_id=1, source_target_pairs={{0,5},{1,6},{2,7},{3,0},{4,1},{5,2},{6,3},{7,4},{8,13},{9,14},{10,... | collective-permute-start | bytes 145160 | tf_op jit(solution)/shard_map/ppermute | solution.py:57
  65.3 9.7 %collective-permute-start.10 = (f32[21,576]{1,0:T(8,128)S(1)}, f32[21,576]{1,0:T(8,128)S(1)}, u32[]{:S(2)}, u32[]{:S(2)}) collective-permute-start(f32[21,576]{1,0:T(8,128)S(1)} %get-tuple-element.39), channel_id=1, source_target_pairs={{0,4},{1,5},{2,6},{3,7},{4,0},{5,1},{6,2},{7,3},{8,12},{9,13},{10,... | collective-permute-start | bytes 145160 | tf_op jit(solution)/shard_map/ppermute | solution.py:57
  68.0 6.9 %collective-permute-start.9 = (f32[21,576]{1,0:T(8,128)S(1)}, f32[21,576]{1,0:T(8,128)S(1)}, u32[]{:S(2)}, u32[]{:S(2)}) collective-permute-start(f32[21,576]{1,0:T(8,128)S(1)} %get-tuple-element.40), channel_id=1, source_target_pairs={{0,3},{1,4},{2,5},{3,6},{4,7},{5,0},{6,1},{7,2},{8,11},{9,12},{10,... | collective-permute-start | bytes 145160 | tf_op jit(solution)/shard_map/ppermute | solution.py:57
  68.5 6.7 %collective-permute-start.8 = (f32[21,576]{1,0:T(8,128)S(1)}, f32[21,576]{1,0:T(8,128)S(1)}, u32[]{:S(2)}, u32[]{:S(2)}) collective-permute-start(f32[21,576]{1,0:T(8,128)S(1)} %get-tuple-element.41), channel_id=1, source_target_pairs={{0,2},{1,3},{2,4},{3,5},{4,6},{5,7},{6,0},{7,1},{8,10},{9,11},{10,... | collective-permute-start | bytes 145160 | tf_op jit(solution)/shard_map/ppermute | solution.py:57
  70.9 11.7 %all-to-all-start.2 = ((bf16[8,16,576]{2,1,0:T(8,128)(2,1)}), bf16[8,16,576]{2,1,0:T(8,128)(2,1)S(1)}, u32[]{:S(2)}, u32[]{:S(2)}) async-start(bf16[8,16,576]{2,1,0:T(8,128)(2,1)} %broadcast_in_dim.73), calls=%async_computation.2 | async-start | bytes 327680 | tf_op jit(solution)/shard_map/all_to_all | solution.py:62
  97.2 6.8 %collective-permute-start.14 = (f32[16,576]{1,0:T(8,128)S(1)}, f32[16,576]{1,0:T(8,128)S(1)}, u32[]{:S(2)}, u32[]{:S(2)}) collective-permute-start(f32[16,576]{1,0:T(8,128)S(1)} %get-tuple-element.45), channel_id=1, source_target_pairs={{0,1},{1,2},{2,3},{3,4},{4,5},{5,6},{6,7},{7,0},{8,9},{9,10},{10,1... | collective-permute-start | bytes 110600 | tf_op jit(solution)/shard_map/ppermute | solution.py:57
  97.3 9.5 %collective-permute-start.20 = (f32[16,576]{1,0:T(8,128)S(1)}, f32[16,576]{1,0:T(8,128)S(1)}, u32[]{:S(2)}, u32[]{:S(2)}) collective-permute-start(f32[16,576]{1,0:T(8,128)S(1)} %get-tuple-element.46), channel_id=1, source_target_pairs={{0,7},{1,0},{2,1},{3,2},{4,3},{5,4},{6,5},{7,6},{8,15},{9,8},{10,9... | collective-permute-start | bytes 110600 | tf_op jit(solution)/shard_map/ppermute | solution.py:57
  102.0 6.0 %collective-permute-start.19 = (f32[16,576]{1,0:T(8,128)S(1)}, f32[16,576]{1,0:T(8,128)S(1)}, u32[]{:S(2)}, u32[]{:S(2)}) collective-permute-start(f32[16,576]{1,0:T(8,128)S(1)} %get-tuple-element.47), channel_id=1, source_target_pairs={{0,6},{1,7},{2,0},{3,1},{4,2},{5,3},{6,4},{7,5},{8,14},{9,15},{10,... | collective-permute-start | bytes 110600 | tf_op jit(solution)/shard_map/ppermute | solution.py:57
  102.0 7.3 %collective-permute-start.18 = (f32[16,576]{1,0:T(8,128)S(1)}, f32[16,576]{1,0:T(8,128)S(1)}, u32[]{:S(2)}, u32[]{:S(2)}) collective-permute-start(f32[16,576]{1,0:T(8,128)S(1)} %get-tuple-element.48), channel_id=1, source_target_pairs={{0,5},{1,6},{2,7},{3,0},{4,1},{5,2},{6,3},{7,4},{8,13},{9,14},{10,... | collective-permute-start | bytes 110600 | tf_op jit(solution)/shard_map/ppermute | solution.py:57
  102.0 16.1 %collective-permute-start.21 = (f32[21,576]{1,0:T(8,128)S(1)}, f32[21,576]{1,0:T(8,128)S(1)}, u32[]{:S(2)}, u32[]{:S(2)}) collective-permute-start(f32[21,576]{1,0:T(8,128)S(1)} %get-tuple-element.28), channel_id=1, source_target_pairs={{0,1},{1,2},{2,3},{3,4},{4,5},{5,6},{6,7},{7,0},{8,9},{9,10},{10,1... | collective-permute-start | bytes 145160 | tf_op jit(solution)/shard_map/ppermute | solution.py:57
  104.0 14.5 %collective-permute-start.27 = (f32[21,576]{1,0:T(8,128)S(1)}, f32[21,576]{1,0:T(8,128)S(1)}, u32[]{:S(2)}, u32[]{:S(2)}) collective-permute-start(f32[21,576]{1,0:T(8,128)S(1)} %get-tuple-element.29), channel_id=1, source_target_pairs={{0,7},{1,0},{2,1},{3,2},{4,3},{5,4},{6,5},{7,6},{8,15},{9,8},{10,9... | collective-permute-start | bytes 145160 | tf_op jit(solution)/shard_map/ppermute | solution.py:57
  106.8 6.1 %collective-permute-start.17 = (f32[16,576]{1,0:T(8,128)S(1)}, f32[16,576]{1,0:T(8,128)S(1)}, u32[]{:S(2)}, u32[]{:S(2)}) collective-permute-start(f32[16,576]{1,0:T(8,128)S(1)} %get-tuple-element.49), channel_id=1, source_target_pairs={{0,4},{1,5},{2,6},{3,7},{4,0},{5,1},{6,2},{7,3},{8,12},{9,13},{10,... | collective-permute-start | bytes 110600 | tf_op jit(solution)/shard_map/ppermute | solution.py:57
  108.0 6.7 %collective-permute-start.16 = (f32[16,576]{1,0:T(8,128)S(1)}, f32[16,576]{1,0:T(8,128)S(1)}, u32[]{:S(2)}, u32[]{:S(2)}) collective-permute-start(f32[16,576]{1,0:T(8,128)S(1)} %get-tuple-element.50), channel_id=1, source_target_pairs={{0,3},{1,4},{2,5},{3,6},{4,7},{5,0},{6,1},{7,2},{8,11},{9,12},{10,... | collective-permute-start | bytes 110600 | tf_op jit(solution)/shard_map/ppermute | solution.py:57
  109.4 5.9 %collective-permute-start.15 = (f32[16,576]{1,0:T(8,128)S(1)}, f32[16,576]{1,0:T(8,128)S(1)}, u32[]{:S(2)}, u32[]{:S(2)}) collective-permute-start(f32[16,576]{1,0:T(8,128)S(1)} %get-tuple-element.51), channel_id=1, source_target_pairs={{0,2},{1,3},{2,4},{3,5},{4,6},{5,7},{6,0},{7,1},{8,10},{9,11},{10,... | collective-permute-start | bytes 110600 | tf_op jit(solution)/shard_map/ppermute | solution.py:57
  112.9 12.0 %collective-permute-start.26 = (f32[21,576]{1,0:T(8,128)S(1)}, f32[21,576]{1,0:T(8,128)S(1)}, u32[]{:S(2)}, u32[]{:S(2)}) collective-permute-start(f32[21,576]{1,0:T(8,128)S(1)} %get-tuple-element.30), channel_id=1, source_target_pairs={{0,6},{1,7},{2,0},{3,1},{4,2},{5,3},{6,4},{7,5},{8,14},{9,15},{10,... | collective-permute-start | bytes 145160 | tf_op jit(solution)/shard_map/ppermute | solution.py:57
  114.6 10.3 %collective-permute-start.25 = (f32[21,576]{1,0:T(8,128)S(1)}, f32[21,576]{1,0:T(8,128)S(1)}, u32[]{:S(2)}, u32[]{:S(2)}) collective-permute-start(f32[21,576]{1,0:T(8,128)S(1)} %get-tuple-element.31), channel_id=1, source_target_pairs={{0,5},{1,6},{2,7},{3,0},{4,1},{5,2},{6,3},{7,4},{8,13},{9,14},{10,... | collective-permute-start | bytes 145160 | tf_op jit(solution)/shard_map/ppermute | solution.py:57
  115.2 9.7 %collective-permute-start.24 = (f32[21,576]{1,0:T(8,128)S(1)}, f32[21,576]{1,0:T(8,128)S(1)}, u32[]{:S(2)}, u32[]{:S(2)}) collective-permute-start(f32[21,576]{1,0:T(8,128)S(1)} %get-tuple-element.32), channel_id=1, source_target_pairs={{0,4},{1,5},{2,6},{3,7},{4,0},{5,1},{6,2},{7,3},{8,12},{9,13},{10,... | collective-permute-start | bytes 145160 | tf_op jit(solution)/shard_map/ppermute | solution.py:57
  118.1 6.8 %collective-permute-start.23 = (f32[21,576]{1,0:T(8,128)S(1)}, f32[21,576]{1,0:T(8,128)S(1)}, u32[]{:S(2)}, u32[]{:S(2)}) collective-permute-start(f32[21,576]{1,0:T(8,128)S(1)} %get-tuple-element.33), channel_id=1, source_target_pairs={{0,3},{1,4},{2,5},{3,6},{4,7},{5,0},{6,1},{7,2},{8,11},{9,12},{10,... | collective-permute-start | bytes 145160 | tf_op jit(solution)/shard_map/ppermute | solution.py:57
  118.5 6.4 %collective-permute-start.22 = (f32[21,576]{1,0:T(8,128)S(1)}, f32[21,576]{1,0:T(8,128)S(1)}, u32[]{:S(2)}, u32[]{:S(2)}) collective-permute-start(f32[21,576]{1,0:T(8,128)S(1)} %get-tuple-element.34), channel_id=1, source_target_pairs={{0,2},{1,3},{2,4},{3,5},{4,6},{5,7},{6,0},{7,1},{8,10},{9,11},{10,... | collective-permute-start | bytes 145160 | tf_op jit(solution)/shard_map/ppermute | solution.py:57
  120.8 11.7 %all-to-all-start.4 = ((bf16[8,16,576]{2,1,0:T(8,128)(2,1)}), bf16[8,16,576]{2,1,0:T(8,128)(2,1)S(1)}, u32[]{:S(2)}, u32[]{:S(2)}) async-start(bf16[8,16,576]{2,1,0:T(8,128)(2,1)} %broadcast_in_dim.78), calls=%async_computation.4 | async-start | bytes 327680 | tf_op jit(solution)/shard_map/all_to_all | solution.py:62
  164.8 5.8 %copy-start.2 = (s32[4]{0:T(128)S(1)}, s32[4]{0:T(128)}, u32[]{:S(2)}) copy-start(s32[4]{0:T(128)} %param.5) | copy-start | bytes 52
  164.8 13.7 %all-to-all-start.7 = ((bf16[8,36,768]{2,1,0:T(8,128)(2,1)}), bf16[8,36,768]{2,1,0:T(8,128)(2,1)S(1)}, u32[]{:S(2)}, u32[]{:S(2)}) async-start(bf16[8,36,768]{2,1,0:T(8,128)(2,1)} %get-tuple-element.23), calls=%async_computation.7 | async-start | bytes 983040 | tf_op jit(solution)/shard_map/all_to_all | solution.py:119
  169.0 11.5 %collective-permute-start.28 = (bf16[1,36,6144]{2,1,0:T(8,128)(2,1)S(1)}, bf16[1,36,6144]{2,1,0:T(8,128)(2,1)S(1)}, u32[]{:S(2)}, u32[]{:S(2)}) collective-permute-start(bf16[1,36,6144]{2,1,0:T(8,128)(2,1)S(1)} %convert_element_type.121), channel_id=1, source_target_pairs={{0,16},{8,24},{16,0},{24,8},{1,17},{9,25},{17,1},{25,9},{2,18},{10... | collective-permute-start | bytes 1327112 | tf_op jit(solution)/shard_map/ppermute | solution.py:85
  178.9 10.7 %collective-permute-start.30 = (bf16[1,36,6144]{2,1,0:T(8,128)(2,1)S(1)}, bf16[1,36,6144]{2,1,0:T(8,128)(2,1)S(1)}, u32[]{:S(2)}, u32[]{:S(2)}) collective-permute-start(bf16[1,36,6144]{2,1,0:T(8,128)(2,1)S(1)} %convert_element_type.125), channel_id=1, source_target_pairs={{0,16},{8,24},{16,0},{24,8},{1,17},{9,25},{17,1},{25,9},{2,18},{10... | collective-permute-start | bytes 1327112 | tf_op jit(solution)/shard_map/ppermute | solution.py:85
  181.6 8.8 %collective-permute-start.29 = (bf16[2,36,6144]{2,1,0:T(8,128)(2,1)}, bf16[2,36,6144]{2,1,0:T(8,128)(2,1)S(1)}, u32[]{:S(2)}, u32[]{:S(2)}) collective-permute-start(bf16[2,36,6144]{2,1,0:T(8,128)(2,1)} %pad_maximum_fusion.2), channel_id=1, source_target_pairs={{0,8},{8,0},{16,24},{24,16},{1,9},{9,1},{17,25},{25,17},{2,10},{10... | collective-permute-start | bytes 2654216 | tf_op jit(solution)/shard_map/ppermute | solution.py:85
  189.8 2.8 %collective-permute-start.31 = (bf16[2,36,6144]{2,1,0:T(8,128)(2,1)S(1)}, bf16[2,36,6144]{2,1,0:T(8,128)(2,1)S(1)}, u32[]{:S(2)}, u32[]{:S(2)}) collective-permute-start(bf16[2,36,6144]{2,1,0:T(8,128)(2,1)S(1)} %pad_maximum_fusion.3), channel_id=1, source_target_pairs={{0,8},{8,0},{16,24},{24,16},{1,9},{9,1},{17,25},{25,17},{2,10},{10... | collective-permute-start | bytes 2654216 | tf_op jit(solution)/shard_map/ppermute | solution.py:85

commit v8 on v6

--- a/solution.py
+++ b/solution.py
@@ -68,7 +68,10 @@
     if size & (size - 1) != 0:
         full = lax.all_gather(mine[None], axis, axis=0, tiled=True)
         me = lax.axis_index(axis)
-        return jnp.take(full, jnp.arange(size, dtype=jnp.int32) ^ me, axis=0, mode="clip")
+        for j in range(size):
+            yield j, lax.dynamic_index_in_dim(full, me ^ j, 0, keepdims=False)
+        return
+    yield 0, mine
     held = {0: mine}
     bit = size // 2
     while bit >= 1:
@@ -77,8 +80,8 @@
         got = lax.ppermute(sent, axis, [(i, i ^ bit) for i in range(size)])
         for n, j in enumerate(keys):
             held[j ^ bit] = got[n]
+            yield j ^ bit, got[n]
         bit //= 2
-    return jnp.stack([held[j] for j in range(size)])
 
 
 def per_device(grad, momentum, owner):
@@ -100,27 +103,14 @@
     half = per // 2
     blocks = columns.reshape(size, per, columns.shape[1])
     slots = lax.axis_size("dp")
-    ids = jnp.arange(slots, dtype=jnp.int32)
-    inverse = jnp.sum(
-        jnp.where(owner[None, :] == ids[:, None], ids[None, :], 0), axis=1
-    )
-    where_from = inverse ^ lax.axis_index("dp")
-    pieces = []
+    me_dp = lax.axis_index("dp")
+    update = jnp.zeros((slots, per, size * columns.shape[1]), jnp.bfloat16)
     for lo, hi in ((0, half), (half, per)):
         piece = blocks[:, lo:hi, :].reshape(size * (hi - lo), columns.shape[1])
         back_rows = lax.all_to_all(piece, "tensor", split_axis=0, concat_axis=1, tiled=True)
         scaled = (factor * back_rows.astype(jnp.float32)).astype(jnp.bfloat16)
-        held = gather_slots(scaled, "dp", slots)
-        pieces.append(held)
-    rows = []
-    for m in range(slots):
-        rows.append(
-            jnp.concatenate(
-                [lax.dynamic_index_in_dim(p, where_from[m], 0, keepdims=True) for p in pieces],
-                axis=1,
-            )
-        )
-    update = jnp.concatenate(rows, axis=0)
+        for j, block in gather_slots(scaled, "dp", slots):
+            update = lax.dynamic_update_slice(update, block[None], (owner[me_dp ^ j], lo, 0))
     return (update, new_momentum)
 
 

time: 181 us -> 203 us (1.12)
  local copies, waits for them, and re-layouts: 6.24 us -> 33.1 us
  other arithmetic: 10.1 us -> 7.47 us
  blocking collectives: 62.3 us -> 59.7 us
    dynamic_update_slice x0 -> x8, local copies, waits for them, and re-layouts: none -> 23.8 us  [per_device(): lax.dynamic_update_slice(update, block[None], (owner[me_dp ^ j], lo, 0))]
    ppermute x14, waiting for transfers between devices: 23.4 us -> 27.4 us  [gram_allreduce(): acc = acc + lax.ppermute(outgoing, axis, _shift_pairs(size, s))]
    concatenate x1 -> x0, other arithmetic: 2.9 us -> none  [per_device(): update = jnp.concatenate(rows, axis=0)]
    ppermute x4, waiting for transfers between devices: 2.89 us -> 0.01 us  [gather_slots(): got = lax.ppermute(sent, axis, [(i, i ^ bit) for i in range(size)])]
    all_to_all x2, blocking collectives: 32 us -> 29.5 us  [gram_allreduce(): lax.all_to_all(spread, axis, split_axis=0, concat_axis=0, tiled=True)]
    broadcast_in_dim x0 -> x1, local copies, waits for them, and re-layouts: none -> 2.2 us  [per_device(): update = jnp.zeros((slots, per, size * columns.shape[1]), jnp.bfloat16)]
    ppermute x14, starting transfers between devices: 18.5 us -> 16.5 us  [gram_allreduce(): acc = acc + lax.ppermute(outgoing, axis, _shift_pairs(size, s))]
  transfers between devices with their start and end apart: 20 -> 20, of which waited for: 15 -> 9; matrix products, arithmetic and copies ran while one was open for 2% -> 12% of each run, Pallas kernels for 0% -> 0%
where the time goes in v8:
time: 203 us; the launch traced here: 202 us
  waiting for transfers between devices  59.8 us (29%)
  blocking collectives  59.7 us (29%)
  local copies, waits for them, and re-layouts  33.1 us (16%)
  starting transfers between devices  27.4 us (13%)
  between operations  9.51 us (5%)
  other arithmetic  7.47 us (4%)
  matrix products  5.15 us (3%)
    all_to_all x2, blocking collectives, gram_allreduce(): lax.all_to_all(spread, axis, split_axis=0, concat_axis=0, tiled=True)  29.5 us
    ppermute x14, waiting for transfers between devices, gram_allreduce(): acc = acc + lax.ppermute(outgoing, axis, _shift_pairs(size, s))  27.4 us
    dynamic_update_slice x8, local copies, waits for them, and re-layouts, per_device(): lax.dynamic_update_slice(update, block[None], (owner[me_dp ^ j], lo, 0))  23.8 us
    all_to_all x1, waiting for transfers between devices, per_device(): lax.all_to_all(rows_here, 'tensor', split_axis=1, concat_axis=0, tiled=True)  21 us
    all_to_all x1, blocking collectives, per_device(): lax.all_to_all(piece, 'tensor', split_axis=0, concat_axis=1, tiled=True)  16.6 us
    ppermute x14, starting transfers between devices, gram_allreduce(): acc = acc + lax.ppermute(outgoing, axis, _shift_pairs(size, s))  16.5 us
    all_to_all x1, blocking collectives, total_over(): got = lax.all_to_all(spread, axis, split_axis=0, concat_axis=0, tiled=True)  13.6 us
    all_to_all x1, waiting for transfers between devices, per_device(): lax.all_to_all(piece, 'tensor', split_axis=0, concat_axis=1, tiled=True)  11.4 us
  transfers between devices with their start and end apart: 20, of which 9 were waited for; matrix products, arithmetic and copies ran while one was open for 12% of the time, Pallas kernels for 0%

profile of v8, /device:TPU:0, one launch (start us, length us, event | category | flops | bytes accessed | tf_op | source)
XLA Modules:
  0.0 202.1 jit_solution(4669359001191249638)
XLA Ops:
  0.6 2.9 %multiply_reduce_fusion = (f32[]{:T(128)}, f32[1,72,6144]{2,1,0:T(8,128)S(1)}) fusion(bf16[1,72,6144]{2,1,0:T(8,128)(2,1)} %param.3, f32[1,72,6144]{2,1,0:T(8,128)} %param.4), kind=kLoop, calls=%fused_computation.5 | loop fusion | flops 3096575 | bytes 4423684 | tf_op jit(solution)/shard_map/reduce_sum | solution.py:91
  3.5 0.6 broadcast_in_dim.49
  4.2 13.6 %all_to_all.52 = f32[8,1,1]{2,1,0:T(1,128)S(1)} all-to-all(f32[8,1,1]{2,1,0:T(1,128)S(1)} %broadcast_in_dim.49), channel_id=1, replica_groups=mesh['dp'=4,'tensor'=8] {'tensor'}, dimensions={0} | all-to-all | bytes 64 | tf_op jit(solution)/shard_map/all_to_all | solution.py:26
  19.5 1.1 copy.35
  20.6 3.6 %all-to-all-start.1 = ((bf16[72,8,768]{2,0,1:T(8,128)(2,1)}), bf16[72,8,768]{2,0,1:T(8,128)(2,1)S(1)}, u32[]{:S(2)}, u32[]{:S(2)}) async-start(bf16[72,8,768]{2,0,1:T(8,128)(2,1)} %copy.35), calls=%async_computation.1 | async-start | bytes 1769472 | tf_op jit(solution)/shard_map/all_to_all | solution.py:93
  24.3 21.0 %all-to-all-done.1 = bf16[72,8,768]{2,0,1:T(8,128)(2,1)S(1)} async-done(((bf16[72,8,768]{2,0,1:T(8,128)(2,1)}), bf16[72,8,768]{2,0,1:T(8,128)(2,1)S(1)}, u32[]{:S(2)}, u32[]{:S(2)}) %all-to-all-start.1) | async-done | bytes 884768 | tf_op jit(solution)/shard_map/all_to_all | solution.py:93
  45.4 0.9 fusion.66
  46.9 2.2 %collective-permute-start.6 = (f32[37,576]{1,0:T(8,128)S(1)}, f32[37,576]{1,0:T(8,128)S(1)}, u32[]{:S(2)}, u32[]{:S(2)}) collective-permute-start(f32[37,576]{1,0:T(8,128)S(1)} %get-tuple-element.24), channel_id=1, source_target_pairs={{0,7},{1,0},{2,1},{3,2},{4,3},{5,4},{6,5},{7,6},{8,15},{9,8},{10,9... | collective-permute-start | bytes 255752 | tf_op jit(solution)/shard_map/ppermute | solution.py:52
  49.1 0.8 collective-permute-start.4
  50.0 2.4 %collective-permute-start.3 = (f32[37,576]{1,0:T(8,128)S(1)}, f32[37,576]{1,0:T(8,128)S(1)}, u32[]{:S(2)}, u32[]{:S(2)}) collective-permute-start(f32[37,576]{1,0:T(8,128)S(1)} %get-tuple-element.27), channel_id=1, source_target_pairs={{0,4},{1,5},{2,6},{3,7},{4,0},{5,1},{6,2},{7,3},{8,12},{9,13},{10,... | collective-permute-start | bytes 255752 | tf_op jit(solution)/shard_map/ppermute | solution.py:52
  52.4 1.7 collective-permute-start.2
  54.1 1.1 collective-permute-done.5
  55.6 1.3 collective-permute-done.4
  56.8 9.2 %collective-permute-done.3 = f32[37,576]{1,0:T(8,128)S(1)} collective-permute-done((f32[37,576]{1,0:T(8,128)S(1)}, f32[37,576]{1,0:T(8,128)S(1)}, u32[]{:S(2)}, u32[]{:S(2)}) %collective-permute-start.3) | collective-permute-done | bytes 85280 | tf_op jit(solution)/shard_map/ppermute | solution.py:52
  66.0 2.8 %collective-permute-done.2 = f32[37,576]{1,0:T(8,128)S(1)} collective-permute-done((f32[37,576]{1,0:T(8,128)S(1)}, f32[37,576]{1,0:T(8,128)S(1)}, u32[]{:S(2)}, u32[]{:S(2)}) %collective-permute-start.2) | collective-permute-done | bytes 85280 | tf_op jit(solution)/shard_map/ppermute | solution.py:52
  69.0 15.0 %all_to_all.53 = bf16[8,37,576]{2,1,0:T(8,128)(2,1)S(1)} all-to-all(bf16[8,37,576]{2,1,0:T(8,128)(2,1)S(1)} %broadcast_in_dim.52), channel_id=1, replica_groups=mesh['dp'=4,'tensor'=8] {'tensor'}, dimensions={0} | all-to-all | bytes 681984 | tf_op jit(solution)/shard_map/all_to_all | solution.py:55
  84.7 1.7 add_convert_fusion.1
  86.4 0.9 fusion.67
  88.0 2.1 %collective-permute-start.13 = (f32[37,576]{1,0:T(8,128)S(1)}, f32[37,576]{1,0:T(8,128)S(1)}, u32[]{:S(2)}, u32[]{:S(2)}) collective-permute-start(f32[37,576]{1,0:T(8,128)S(1)} %get-tuple-element.17), channel_id=1, source_target_pairs={{0,7},{1,0},{2,1},{3,2},{4,3},{5,4},{6,5},{7,6},{8,15},{9,8},{10,9... | collective-permute-start | bytes 255752 | tf_op jit(solution)/shard_map/ppermute | solution.py:52
  90.2 1.7 collective-permute-start.11
  91.9 1.7 collective-permute-start.10
  93.6 1.4 collective-permute-start.9
  95.0 1.1 collective-permute-start.8
  96.1 0.9 collective-permute-start.7
  97.0 0.8 collective-permute-done.11
  97.8 10.2 %collective-permute-done.10 = f32[37,576]{1,0:T(8,128)S(1)} collective-permute-done((f32[37,576]{1,0:T(8,128)S(1)}, f32[37,576]{1,0:T(8,128)S(1)}, u32[]{:S(2)}, u32[]{:S(2)}) %collective-permute-start.10) | collective-permute-done | bytes 85280 | tf_op jit(solution)/shard_map/ppermute | solution.py:52
  108.0 1.9 collective-permute-done.9
  110.0 14.5 %all_to_all.54 = bf16[8,37,576]{2,1,0:T(8,128)(2,1)S(1)} all-to-all(bf16[8,37,576]{2,1,0:T(8,128)(2,1)S(1)} %broadcast_in_dim.56), channel_id=1, replica_groups=mesh['dp'=4,'tensor'=8] {'tensor'}, dimensions={0} | all-to-all | bytes 681984 | tf_op jit(solution)/shard_map/all_to_all | solution.py:55
  125.3 1.7 add_convert_fusion
  127.0 0.9 fusion.64
  127.9 16.6 %all_to_all.55 = bf16[8,36,768]{2,1,0:T(8,128)(2,1)S(1)} all-to-all(bf16[8,36,768]{2,1,0:T(8,128)(2,1)S(1)} %get-tuple-element.15), channel_id=1, replica_groups=mesh['dp'=4,'tensor'=8] {'tensor'}, dimensions={0} | all-to-all | bytes 884736 | tf_op jit(solution)/shard_map/all_to_all | solution.py:110
  144.5 3.7 %all-to-all-start.5 = ((bf16[8,36,768]{2,1,0:T(8,128)(2,1)}), bf16[8,36,768]{2,1,0:T(8,128)(2,1)S(1)}, u32[]{:S(2)}, u32[]{:S(2)}) async-start(bf16[8,36,768]{2,1,0:T(8,128)(2,1)} %get-tuple-element.14), calls=%async_computation.5 | async-start | bytes 983040 | tf_op jit(solution)/shard_map/all_to_all | solution.py:110
  148.6 1.6 collective-permute-start.14
  150.2 11.4 %all-to-all-done.5 = bf16[8,36,768]{2,1,0:T(8,128)(2,1)S(1)} async-done(((bf16[8,36,768]{2,1,0:T(8,128)(2,1)}), bf16[8,36,768]{2,1,0:T(8,128)(2,1)S(1)}, u32[]{:S(2)}, u32[]{:S(2)}) %all-to-all-start.5) | async-done | bytes 442400 | tf_op jit(solution)/shard_map/all_to_all | solution.py:110
  162.0 1.6 collective-permute-start.16
  163.6 1.1 pad_maximum_fusion
  164.6 0.7 fusion.65
  173.1 2.2 %broadcast_in_dim.48 = bf16[4,72,6144]{2,1,0:T(8,128)(2,1)} broadcast(bf16[]{:T(256)} %constant.107.clone.1), dimensions={} | broadcast | bytes 3538946 | tf_op jit(solution)/shard_map/broadcast_in_dim | solution.py:107
  175.3 3.0 %dynamic_update_slice.24 = bf16[4,72,6144]{2,1,0:T(8,128)(2,1)} dynamic-update-slice(bf16[4,72,6144]{2,1,0:T(8,128)(2,1)} %broadcast_in_dim.48, bf16[1,36,6144]{2,1,0:T(8,128)(2,1)S(1)} %convert_element_type.113, s32[]{:T(128)S(6)} %select_n.170, s32[]{:T(128)} %constant.113.clone.1, s32[]{:T(128)} %constant.113.clone.1) | dynamic-update-slice | bytes 884740 | tf_op jit(solution)/shard_map/dynamic_update_slice | solution.py:113
  178.3 1.1 pad_maximum_fusion.1
  179.9 3.0 %dynamic_update_slice.25 = bf16[4,72,6144]{2,1,0:T(8,128)(2,1)} dynamic-update-slice(bf16[4,72,6144]{2,1,0:T(8,128)(2,1)} %dynamic_update_slice.24, bf16[1,36,6144]{2,1,0:T(8,128)(2,1)S(1)} %collective-permute-done.14, s32[]{:T(128)S(6)} %select_n.172, s32[]{:T(128)} %constant.113.clone.1, s32[]{:T(128)} %constant.113.clone.1) | dynamic-update-slice | bytes 884740 | tf_op jit(solution)/shard_map/dynamic_update_slice | solution.py:113
  183.0 3.0 %dynamic_update_slice.26 = bf16[4,72,6144]{2,1,0:T(8,128)(2,1)} dynamic-update-slice(bf16[4,72,6144]{2,1,0:T(8,128)(2,1)} %dynamic_update_slice.25, bf16[1,36,6144]{2,1,0:T(8,128)(2,1)S(1)} %get-tuple-element.13, s32[]{:T(128)S(6)} %select_n.174, s32[]{:T(128)} %constant.113.clone.1, s32[]{:T(128)} %constant.113.clone.1) | dynamic-update-slice | bytes 884740 | tf_op jit(solution)/shard_map/dynamic_update_slice | solution.py:113
  186.0 3.0 %dynamic_update_slice.27 = bf16[4,72,6144]{2,1,0:T(8,128)(2,1)} dynamic-update-slice(bf16[4,72,6144]{2,1,0:T(8,128)(2,1)} %dynamic_update_slice.26, bf16[1,36,6144]{2,1,0:T(8,128)(2,1)S(1)} %get-tuple-element.12, s32[]{:T(128)S(6)} %select_n.176, s32[]{:T(128)} %constant.113.clone.1, s32[]{:T(128)} %constant.113.clone.1) | dynamic-update-slice | bytes 884740 | tf_op jit(solution)/shard_map/dynamic_update_slice | solution.py:113
  189.0 2.9 %dynamic_update_slice.28 = bf16[4,72,6144]{2,1,0:T(8,128)(2,1)} dynamic-update-slice(bf16[4,72,6144]{2,1,0:T(8,128)(2,1)} %dynamic_update_slice.27, bf16[1,36,6144]{2,1,0:T(8,128)(2,1)S(1)} %convert_element_type.117, s32[]{:T(128)S(6)} %select_n.170, s32[]{:T(128)} %constant.126.clone.1, s32[]{:T(128)} %constant.113.clone.1) | dynamic-update-slice | bytes 884740 | tf_op jit(solution)/shard_map/dynamic_update_slice | solution.py:113
  192.0 2.9 %dynamic_update_slice.29 = bf16[4,72,6144]{2,1,0:T(8,128)(2,1)} dynamic-update-slice(bf16[4,72,6144]{2,1,0:T(8,128)(2,1)} %dynamic_update_slice.28, bf16[1,36,6144]{2,1,0:T(8,128)(2,1)S(1)} %collective-permute-done.16, s32[]{:T(128)S(6)} %select_n.172, s32[]{:T(128)} %constant.126.clone.1, s32[]{:T(128)} %constant.113.clone.1) | dynamic-update-slice | bytes 884740 | tf_op jit(solution)/shard_map/dynamic_update_slice | solution.py:113
  194.9 1.2 fusion.62
  196.2 3.0 %dynamic_update_slice.30 = bf16[4,72,6144]{2,1,0:T(8,128)(2,1)} dynamic-update-slice(bf16[4,72,6144]{2,1,0:T(8,128)(2,1)} %dynamic_update_slice.29, bf16[1,36,6144]{2,1,0:T(8,128)(2,1)S(1)} %get-tuple-element.11, s32[]{:T(128)S(6)} %select_n.174, s32[]{:T(128)} %constant.126.clone.1, s32[]{:T(128)} %constant.113.clone.1) | dynamic-update-slice | bytes 884740 | tf_op jit(solution)/shard_map/dynamic_update_slice | solution.py:113
  199.1 2.9 %dynamic_update_slice.31 = bf16[4,72,6144]{2,1,0:T(8,128)(2,1)} dynamic-update-slice(bf16[4,72,6144]{2,1,0:T(8,128)(2,1)} %dynamic_update_slice.30, bf16[1,36,6144]{2,1,0:T(8,128)(2,1)S(1)} %get-tuple-element.10, s32[]{:T(128)S(6)} %select_n.176, s32[]{:T(128)} %constant.126.clone.1, s32[]{:T(128)} %constant.113.clone.1) | dynamic-update-slice | bytes 884740 | tf_op jit(solution)/shard_map/dynamic_update_slice | solution.py:113
  (63 shorter events, 6.0 us)
Async XLA Ops:
  0.6 18.5 %copy-start.1 = (bf16[1,72,6144]{2,1,0:T(8,128)(2,1)S(1)}, bf16[1,72,6144]{2,1,0:T(8,128)(2,1)}, u32[]{:S(2)}) copy-start(bf16[1,72,6144]{2,1,0:T(8,128)(2,1)} %param.3) | copy-start | bytes 2654212
  3.5 15.8 %copy-start = (f32[1,72,6144]{2,1,0:T(8,128)}, f32[1,72,6144]{2,1,0:T(8,128)S(1)}, u32[]{:S(2)}) copy-start(f32[1,72,6144]{2,1,0:T(8,128)S(1)} %get-tuple-element.3) | copy-start | bytes 5308420
  20.6 24.8 %all-to-all-start.1 = ((bf16[72,8,768]{2,0,1:T(8,128)(2,1)}), bf16[72,8,768]{2,0,1:T(8,128)(2,1)S(1)}, u32[]{:S(2)}, u32[]{:S(2)}) async-start(bf16[72,8,768]{2,0,1:T(8,128)(2,1)} %copy.35), calls=%async_computation.1 | async-start | bytes 1769472 | tf_op jit(solution)/shard_map/all_to_all | solution.py:93
  46.9 7.1 %collective-permute-start.6 = (f32[37,576]{1,0:T(8,128)S(1)}, f32[37,576]{1,0:T(8,128)S(1)}, u32[]{:S(2)}, u32[]{:S(2)}) collective-permute-start(f32[37,576]{1,0:T(8,128)S(1)} %get-tuple-element.24), channel_id=1, source_target_pairs={{0,7},{1,0},{2,1},{3,2},{4,3},{5,4},{6,5},{7,6},{8,15},{9,8},{10,9... | collective-permute-start | bytes 255752 | tf_op jit(solution)/shard_map/ppermute | solution.py:52
  49.1 6.1 %collective-permute-start.5 = (f32[37,576]{1,0:T(8,128)S(1)}, f32[37,576]{1,0:T(8,128)S(1)}, u32[]{:S(2)}, u32[]{:S(2)}) collective-permute-start(f32[37,576]{1,0:T(8,128)S(1)} %get-tuple-element.25), channel_id=1, source_target_pairs={{0,6},{1,7},{2,0},{3,1},{4,2},{5,3},{6,4},{7,5},{8,14},{9,15},{10,... | collective-permute-start | bytes 255752 | tf_op jit(solution)/shard_map/ppermute | solution.py:52
  49.1 7.7 %collective-permute-start.4 = (f32[37,576]{1,0:T(8,128)S(1)}, f32[37,576]{1,0:T(8,128)S(1)}, u32[]{:S(2)}, u32[]{:S(2)}) collective-permute-start(f32[37,576]{1,0:T(8,128)S(1)} %get-tuple-element.26), channel_id=1, source_target_pairs={{0,5},{1,6},{2,7},{3,0},{4,1},{5,2},{6,3},{7,4},{8,13},{9,14},{10,... | collective-permute-start | bytes 255752 | tf_op jit(solution)/shard_map/ppermute | solution.py:52
  50.0 16.0 %collective-permute-start.3 = (f32[37,576]{1,0:T(8,128)S(1)}, f32[37,576]{1,0:T(8,128)S(1)}, u32[]{:S(2)}, u32[]{:S(2)}) collective-permute-start(f32[37,576]{1,0:T(8,128)S(1)} %get-tuple-element.27), channel_id=1, source_target_pairs={{0,4},{1,5},{2,6},{3,7},{4,0},{5,1},{6,2},{7,3},{8,12},{9,13},{10,... | collective-permute-start | bytes 255752 | tf_op jit(solution)/shard_map/ppermute | solution.py:52
  52.4 16.4 %collective-permute-start.2 = (f32[37,576]{1,0:T(8,128)S(1)}, f32[37,576]{1,0:T(8,128)S(1)}, u32[]{:S(2)}, u32[]{:S(2)}) collective-permute-start(f32[37,576]{1,0:T(8,128)S(1)} %get-tuple-element.28), channel_id=1, source_target_pairs={{0,3},{1,4},{2,5},{3,6},{4,7},{5,0},{6,1},{7,2},{8,11},{9,12},{10,... | collective-permute-start | bytes 255752 | tf_op jit(solution)/shard_map/ppermute | solution.py:52
  54.1 14.8 %collective-permute-start.1 = (f32[37,576]{1,0:T(8,128)S(1)}, f32[37,576]{1,0:T(8,128)S(1)}, u32[]{:S(2)}, u32[]{:S(2)}) collective-permute-start(f32[37,576]{1,0:T(8,128)S(1)} %get-tuple-element.29), channel_id=1, source_target_pairs={{0,2},{1,3},{2,4},{3,5},{4,6},{5,7},{6,0},{7,1},{8,10},{9,11},{10,... | collective-permute-start | bytes 255752 | tf_op jit(solution)/shard_map/ppermute | solution.py:52
  55.2 13.6 %collective-permute-start = (f32[37,576]{1,0:T(8,128)S(1)}, f32[37,576]{1,0:T(8,128)S(1)}, u32[]{:S(2)}, u32[]{:S(2)}) collective-permute-start(f32[37,576]{1,0:T(8,128)S(1)} %get-tuple-element.23), channel_id=1, source_target_pairs={{0,1},{1,2},{2,3},{3,4},{4,5},{5,6},{6,7},{7,0},{8,9},{9,10},{10,1... | collective-permute-start | bytes 255752 | tf_op jit(solution)/shard_map/ppermute | solution.py:52
  88.0 7.1 %collective-permute-start.13 = (f32[37,576]{1,0:T(8,128)S(1)}, f32[37,576]{1,0:T(8,128)S(1)}, u32[]{:S(2)}, u32[]{:S(2)}) collective-permute-start(f32[37,576]{1,0:T(8,128)S(1)} %get-tuple-element.17), channel_id=1, source_target_pairs={{0,7},{1,0},{2,1},{3,2},{4,3},{5,4},{6,5},{7,6},{8,15},{9,8},{10,9... | collective-permute-start | bytes 255752 | tf_op jit(solution)/shard_map/ppermute | solution.py:52
  90.1 6.0 %collective-permute-start.12 = (f32[37,576]{1,0:T(8,128)S(1)}, f32[37,576]{1,0:T(8,128)S(1)}, u32[]{:S(2)}, u32[]{:S(2)}) collective-permute-start(f32[37,576]{1,0:T(8,128)S(1)} %get-tuple-element.18), channel_id=1, source_target_pairs={{0,6},{1,7},{2,0},{3,1},{4,2},{5,3},{6,4},{7,5},{8,14},{9,15},{10,... | collective-permute-start | bytes 255752 | tf_op jit(solution)/shard_map/ppermute | solution.py:52
  90.2 7.6 %collective-permute-start.11 = (f32[37,576]{1,0:T(8,128)S(1)}, f32[37,576]{1,0:T(8,128)S(1)}, u32[]{:S(2)}, u32[]{:S(2)}) collective-permute-start(f32[37,576]{1,0:T(8,128)S(1)} %get-tuple-element.19), channel_id=1, source_target_pairs={{0,5},{1,6},{2,7},{3,0},{4,1},{5,2},{6,3},{7,4},{8,13},{9,14},{10,... | collective-permute-start | bytes 255752 | tf_op jit(solution)/shard_map/ppermute | solution.py:52
  91.9 16.1 %collective-permute-start.10 = (f32[37,576]{1,0:T(8,128)S(1)}, f32[37,576]{1,0:T(8,128)S(1)}, u32[]{:S(2)}, u32[]{:S(2)}) collective-permute-start(f32[37,576]{1,0:T(8,128)S(1)} %get-tuple-element.20), channel_id=1, source_target_pairs={{0,4},{1,5},{2,6},{3,7},{4,0},{5,1},{6,2},{7,3},{8,12},{9,13},{10,... | collective-permute-start | bytes 255752 | tf_op jit(solution)/shard_map/ppermute | solution.py:52
  93.6 16.3 %collective-permute-start.9 = (f32[37,576]{1,0:T(8,128)S(1)}, f32[37,576]{1,0:T(8,128)S(1)}, u32[]{:S(2)}, u32[]{:S(2)}) collective-permute-start(f32[37,576]{1,0:T(8,128)S(1)} %get-tuple-element.21), channel_id=1, source_target_pairs={{0,3},{1,4},{2,5},{3,6},{4,7},{5,0},{6,1},{7,2},{8,11},{9,12},{10,... | collective-permute-start | bytes 255752 | tf_op jit(solution)/shard_map/ppermute | solution.py:52
  95.0 14.9 %collective-permute-start.8 = (f32[37,576]{1,0:T(8,128)S(1)}, f32[37,576]{1,0:T(8,128)S(1)}, u32[]{:S(2)}, u32[]{:S(2)}) collective-permute-start(f32[37,576]{1,0:T(8,128)S(1)} %get-tuple-element.22), channel_id=1, source_target_pairs={{0,2},{1,3},{2,4},{3,5},{4,6},{5,7},{6,0},{7,1},{8,10},{9,11},{10,... | collective-permute-start | bytes 255752 | tf_op jit(solution)/shard_map/ppermute | solution.py:52
  96.1 13.8 %collective-permute-start.7 = (f32[37,576]{1,0:T(8,128)S(1)}, f32[37,576]{1,0:T(8,128)S(1)}, u32[]{:S(2)}, u32[]{:S(2)}) collective-permute-start(f32[37,576]{1,0:T(8,128)S(1)} %get-tuple-element.16), channel_id=1, source_target_pairs={{0,1},{1,2},{2,3},{3,4},{4,5},{5,6},{6,7},{7,0},{8,9},{9,10},{10,1... | collective-permute-start | bytes 255752 | tf_op jit(solution)/shard_map/ppermute | solution.py:52
  144.5 17.0 %all-to-all-start.5 = ((bf16[8,36,768]{2,1,0:T(8,128)(2,1)}), bf16[8,36,768]{2,1,0:T(8,128)(2,1)S(1)}, u32[]{:S(2)}, u32[]{:S(2)}) async-start(bf16[8,36,768]{2,1,0:T(8,128)(2,1)} %get-tuple-element.14), calls=%async_computation.5 | async-start | bytes 983040 | tf_op jit(solution)/shard_map/all_to_all | solution.py:110
  148.6 15.0 %collective-permute-start.14 = (bf16[1,36,6144]{2,1,0:T(8,128)(2,1)S(1)}, bf16[1,36,6144]{2,1,0:T(8,128)(2,1)S(1)}, u32[]{:S(2)}, u32[]{:S(2)}) collective-permute-start(bf16[1,36,6144]{2,1,0:T(8,128)(2,1)S(1)} %convert_element_type.113), channel_id=1, source_target_pairs={{0,16},{8,24},{16,0},{24,8},{1,17},{9,25},{17,1},{25,9},{2,18},{10... | collective-permute-start | bytes 1327112 | tf_op jit(solution)/shard_map/ppermute | solution.py:80
  161.7 2.9 %copy-start.2 = (s32[4]{0:T(128)S(1)}, s32[4]{0:T(128)}, u32[]{:S(2)}) copy-start(s32[4]{0:T(128)} %param.5) | copy-start | bytes 52
  162.0 16.3 %collective-permute-start.16 = (bf16[1,36,6144]{2,1,0:T(8,128)(2,1)S(1)}, bf16[1,36,6144]{2,1,0:T(8,128)(2,1)S(1)}, u32[]{:S(2)}, u32[]{:S(2)}) collective-permute-start(bf16[1,36,6144]{2,1,0:T(8,128)(2,1)S(1)} %convert_element_type.117), channel_id=1, source_target_pairs={{0,16},{8,24},{16,0},{24,8},{1,17},{9,25},{17,1},{25,9},{2,18},{10... | collective-permute-start | bytes 1327112 | tf_op jit(solution)/shard_map/ppermute | solution.py:80
  164.6 18.3 %collective-permute-start.15 = (bf16[2,36,6144]{2,1,0:T(8,128)(2,1)}, bf16[2,36,6144]{2,1,0:T(8,128)(2,1)S(1)}, u32[]{:S(2)}, u32[]{:S(2)}) collective-permute-start(bf16[2,36,6144]{2,1,0:T(8,128)(2,1)} %pad_maximum_fusion), channel_id=1, source_target_pairs={{0,8},{8,0},{16,24},{24,16},{1,9},{9,1},{17,25},{25,17},{2,10},{10... | collective-permute-start | bytes 2654216 | tf_op jit(solution)/shard_map/ppermute | solution.py:80
  179.4 15.5 %collective-permute-start.17 = (bf16[2,36,6144]{2,1,0:T(8,128)(2,1)}, bf16[2,36,6144]{2,1,0:T(8,128)(2,1)}, u32[]{:S(2)}, u32[]{:S(2)}) collective-permute-start(bf16[2,36,6144]{2,1,0:T(8,128)(2,1)} %pad_maximum_fusion.1), channel_id=1, source_target_pairs={{0,8},{8,0},{16,24},{24,16},{1,9},{9,1},{17,25},{25,17},{2,10},{10... | collective-permute-start | bytes 2654216 | tf_op jit(solution)/shard_map/ppermute | solution.py:80

commit v9 on v6

--- a/solution.py
+++ b/solution.py
@@ -97,7 +97,7 @@
         columns = (coef_a * columns.astype(jnp.float32) + applied).astype(jnp.bfloat16)
     factor = 0.2 * math.sqrt(max(M, N))
     per = columns.shape[0] // size
-    half = per // 2
+    half = min(per, 8 * ((per * 9 + 64) // 128))
     blocks = columns.reshape(size, per, columns.shape[1])
     slots = lax.axis_size("dp")
     ids = jnp.arange(slots, dtype=jnp.int32)
@@ -106,7 +106,7 @@
     )
     where_from = inverse ^ lax.axis_index("dp")
     pieces = []
-    for lo, hi in ((0, half), (half, per)):
+    for lo, hi in ((0, half), (half, per)) if half < per else ((0, per),):
         piece = blocks[:, lo:hi, :].reshape(size * (hi - lo), columns.shape[1])
         back_rows = lax.all_to_all(piece, "tensor", split_axis=0, concat_axis=1, tiled=True)
         scaled = (factor * back_rows.astype(jnp.float32)).astype(jnp.bfloat16)

time: 181 us -> 179 us (0.989)
  blocking collectives: 62.3 us -> 45.6 us
  waiting for transfers between devices: 58.7 us -> 70.1 us
  starting transfers between devices: 29.1 us -> 32.5 us
  other arithmetic: 10.1 us -> 8.24 us
    all_to_all x1 -> x0, blocking collectives: 16.7 us -> none  [per_device(): lax.all_to_all(piece, 'tensor', split_axis=0, concat_axis=1, tiled=True)]
    all_to_all x1 -> x2, waiting for transfers between devices: 11.3 us -> 21.9 us  [per_device(): lax.all_to_all(piece, 'tensor', split_axis=0, concat_axis=1, tiled=True)]
    all_to_all x1 -> x2, starting transfers between devices: 3.8 us -> 7.12 us  [per_device(): lax.all_to_all(piece, 'tensor', split_axis=0, concat_axis=1, tiled=True)]
  transfers between devices with their start and end apart: 20 -> 21, of which waited for: 15 -> 16; matrix products, arithmetic and copies ran while one was open for 2% -> 2% of each run, Pallas kernels for 0% -> 0%
where the time goes in v9:
time: 179 us; the launch traced here: 178 us
  waiting for transfers between devices  70.1 us (39%)
  blocking collectives  45.6 us (25%)
  starting transfers between devices  32.5 us (18%)
  between operations  9.58 us (5%)
  other arithmetic  8.24 us (5%)
  local copies, waits for them, and re-layouts  6.93 us (4%)
  matrix products  5.16 us (3%)
    all_to_all x2, blocking collectives, gram_allreduce(): lax.all_to_all(spread, axis, split_axis=0, concat_axis=0, tiled=True)  32 us
    ppermute x14, waiting for transfers between devices, gram_allreduce(): acc = acc + lax.ppermute(outgoing, axis, _shift_pairs(size, s))  23.4 us
    all_to_all x2, waiting for transfers between devices, per_device(): lax.all_to_all(piece, 'tensor', split_axis=0, concat_axis=1, tiled=True)  21.9 us
    all_to_all x1, waiting for transfers between devices, per_device(): lax.all_to_all(rows_here, 'tensor', split_axis=1, concat_axis=0, tiled=True)  21 us
    ppermute x14, starting transfers between devices, gram_allreduce(): acc = acc + lax.ppermute(outgoing, axis, _shift_pairs(size, s))  18.5 us
    all_to_all x1, blocking collectives, total_over(): got = lax.all_to_all(spread, axis, split_axis=0, concat_axis=0, tiled=True)  13.6 us
    all_to_all x2, starting transfers between devices, per_device(): lax.all_to_all(piece, 'tensor', split_axis=0, concat_axis=1, tiled=True)  7.12 us
    ppermute x4, waiting for transfers between devices, gather_slots(): got = lax.ppermute(sent, axis, [(i, i ^ bit) for i in range(size)])  3.7 us
  transfers between devices with their start and end apart: 21, of which 16 were waited for; matrix products, arithmetic and copies ran while one was open for 2% of the time, Pallas kernels for 0%

profile of v9, /device:TPU:0, one launch (start us, length us, event | category | flops | bytes accessed | tf_op | source)
XLA Modules:
  0.0 178.0 jit_solution(6611797894835242285)
XLA Ops:
  0.6 2.9 %multiply_reduce_fusion = (f32[]{:T(128)}, f32[1,72,6144]{2,1,0:T(8,128)S(1)}) fusion(bf16[1,72,6144]{2,1,0:T(8,128)(2,1)} %param.3, f32[1,72,6144]{2,1,0:T(8,128)} %param.4), kind=kLoop, calls=%fused_computation.7 | loop fusion | flops 3096575 | bytes 4423684 | tf_op jit(solution)/shard_map/reduce_sum | solution.py:88
  3.5 0.6 broadcast_in_dim.58
  4.2 13.6 %all_to_all.52 = f32[8,1,1]{2,1,0:T(1,128)S(1)} all-to-all(f32[8,1,1]{2,1,0:T(1,128)S(1)} %broadcast_in_dim.58), channel_id=1, replica_groups=mesh['dp'=4,'tensor'=8] {'tensor'}, dimensions={0} | all-to-all | bytes 64 | tf_op jit(solution)/shard_map/all_to_all | solution.py:26
  17.8 0.6 reduce_sum.46
  19.1 0.3 divide_convert_fusion
  19.5 1.1 copy.35
  20.6 3.6 %all-to-all-start.1 = ((bf16[72,8,768]{2,0,1:T(8,128)(2,1)}), bf16[72,8,768]{2,0,1:T(8,128)(2,1)S(1)}, u32[]{:S(2)}, u32[]{:S(2)}) async-start(bf16[72,8,768]{2,0,1:T(8,128)(2,1)} %copy.35), calls=%async_computation.1 | async-start | bytes 1769472 | tf_op jit(solution)/shard_map/all_to_all | solution.py:90
  24.4 21.0 %all-to-all-done.1 = bf16[72,8,768]{2,0,1:T(8,128)(2,1)S(1)} async-done(((bf16[72,8,768]{2,0,1:T(8,128)(2,1)}), bf16[72,8,768]{2,0,1:T(8,128)(2,1)S(1)}, u32[]{:S(2)}, u32[]{:S(2)}) %all-to-all-start.1) | async-done | bytes 884768 | tf_op jit(solution)/shard_map/all_to_all | solution.py:90
  45.4 0.9 fusion.65
  46.3 0.2 slice_select_fusion.1
  46.5 0.2 maximum_maximum_fusion.1
  46.9 1.3 collective-permute-start
  48.2 3.5 %collective-permute-start.6 = (f32[37,576]{1,0:T(8,128)S(1)}, f32[37,576]{1,0:T(8,128)S(1)}, u32[]{:S(2)}, u32[]{:S(2)}) collective-permute-start(f32[37,576]{1,0:T(8,128)S(1)} %get-tuple-element.28), channel_id=1, source_target_pairs={{0,7},{1,0},{2,1},{3,2},{4,3},{5,4},{6,5},{7,6},{8,15},{9,8},{10,9... | collective-permute-start | bytes 255752 | tf_op jit(solution)/shard_map/ppermute | solution.py:52
  51.7 2.9 %collective-permute-start.3 = (f32[37,576]{1,0:T(8,128)S(1)}, f32[37,576]{1,0:T(8,128)S(1)}, u32[]{:S(2)}, u32[]{:S(2)}) collective-permute-start(f32[37,576]{1,0:T(8,128)S(1)} %get-tuple-element.31), channel_id=1, source_target_pairs={{0,4},{1,5},{2,6},{3,7},{4,0},{5,1},{6,2},{7,3},{8,12},{9,13},{10,... | collective-permute-start | bytes 255752 | tf_op jit(solution)/shard_map/ppermute | solution.py:52
  54.9 1.7 collective-permute-start.1
  56.7 0.3 collective-permute-done.5
  56.9 2.2 %collective-permute-done.4 = f32[37,576]{1,0:T(8,128)S(1)} collective-permute-done((f32[37,576]{1,0:T(8,128)S(1)}, f32[37,576]{1,0:T(8,128)S(1)}, u32[]{:S(2)}, u32[]{:S(2)}) %collective-permute-start.4) | collective-permute-done | bytes 85280 | tf_op jit(solution)/shard_map/ppermute | solution.py:52
  59.1 7.9 %collective-permute-done.3 = f32[37,576]{1,0:T(8,128)S(1)} collective-permute-done((f32[37,576]{1,0:T(8,128)S(1)}, f32[37,576]{1,0:T(8,128)S(1)}, u32[]{:S(2)}, u32[]{:S(2)}) %collective-permute-start.3) | collective-permute-done | bytes 85280 | tf_op jit(solution)/shard_map/ppermute | solution.py:52
  67.0 0.6 collective-permute-done.2
  67.8 16.0 %all_to_all.53 = bf16[8,37,576]{2,1,0:T(8,128)(2,1)S(1)} all-to-all(bf16[8,37,576]{2,1,0:T(8,128)(2,1)S(1)} %broadcast_in_dim.61), channel_id=1, replica_groups=mesh['dp'=4,'tensor'=8] {'tensor'}, dimensions={0} | all-to-all | bytes 681984 | tf_op jit(solution)/shard_map/all_to_all | solution.py:55
  84.6 1.7 add_convert_fusion.1
  86.3 0.9 fusion.66
  87.2 0.2 slice_select_fusion
  87.8 1.2 collective-permute-start.7
  89.0 3.6 %collective-permute-start.13 = (f32[37,576]{1,0:T(8,128)S(1)}, f32[37,576]{1,0:T(8,128)S(1)}, u32[]{:S(2)}, u32[]{:S(2)}) collective-permute-start(f32[37,576]{1,0:T(8,128)S(1)} %get-tuple-element.21), channel_id=1, source_target_pairs={{0,7},{1,0},{2,1},{3,2},{4,3},{5,4},{6,5},{7,6},{8,15},{9,8},{10,9... | collective-permute-start | bytes 255752 | tf_op jit(solution)/shard_map/ppermute | solution.py:52
  92.6 2.9 %collective-permute-start.10 = (f32[37,576]{1,0:T(8,128)S(1)}, f32[37,576]{1,0:T(8,128)S(1)}, u32[]{:S(2)}, u32[]{:S(2)}) collective-permute-start(f32[37,576]{1,0:T(8,128)S(1)} %get-tuple-element.24), channel_id=1, source_target_pairs={{0,4},{1,5},{2,6},{3,7},{4,0},{5,1},{6,2},{7,3},{8,12},{9,13},{10,... | collective-permute-start | bytes 255752 | tf_op jit(solution)/shard_map/ppermute | solution.py:52
  95.5 0.7 collective-permute-done.7
  96.3 1.4 collective-permute-start.8
  97.7 0.4 collective-permute-done.12
  98.1 2.2 %collective-permute-done.11 = f32[37,576]{1,0:T(8,128)S(1)} collective-permute-done((f32[37,576]{1,0:T(8,128)S(1)}, f32[37,576]{1,0:T(8,128)S(1)}, u32[]{:S(2)}, u32[]{:S(2)}) %collective-permute-start.11) | collective-permute-done | bytes 85280 | tf_op jit(solution)/shard_map/ppermute | solution.py:52
  100.3 8.7 %collective-permute-done.10 = f32[37,576]{1,0:T(8,128)S(1)} collective-permute-done((f32[37,576]{1,0:T(8,128)S(1)}, f32[37,576]{1,0:T(8,128)S(1)}, u32[]{:S(2)}, u32[]{:S(2)}) %collective-permute-start.10) | collective-permute-done | bytes 85280 | tf_op jit(solution)/shard_map/ppermute | solution.py:52
  109.2 15.9 %all_to_all.54 = bf16[8,37,576]{2,1,0:T(8,128)(2,1)S(1)} all-to-all(bf16[8,37,576]{2,1,0:T(8,128)(2,1)S(1)} %broadcast_in_dim.65), channel_id=1, replica_groups=mesh['dp'=4,'tensor'=8] {'tensor'}, dimensions={0} | all-to-all | bytes 681984 | tf_op jit(solution)/shard_map/all_to_all | solution.py:55
  125.9 1.7 add_convert_fusion
  127.6 0.8 slice.107
  128.4 3.5 %all-to-all-start.5 = ((bf16[8,32,768]{2,1,0:T(8,128)(2,1)}), bf16[8,32,768]{2,1,0:T(8,128)(2,1)S(1)}, u32[]{:S(2)}, u32[]{:S(2)}) async-start(bf16[8,32,768]{2,1,0:T(8,128)(2,1)} %slice.107), calls=%async_computation.5 | async-start | bytes 786432 | tf_op jit(solution)/shard_map/all_to_all | solution.py:111
  131.8 0.8 slice.104
  132.6 10.6 %all-to-all-done.5 = bf16[8,32,768]{2,1,0:T(8,128)(2,1)S(1)} async-done(((bf16[8,32,768]{2,1,0:T(8,128)(2,1)}), bf16[8,32,768]{2,1,0:T(8,128)(2,1)S(1)}, u32[]{:S(2)}, u32[]{:S(2)}) %all-to-all-start.5) | async-done | bytes 393248 | tf_op jit(solution)/shard_map/all_to_all | solution.py:111
  143.2 3.7 %all-to-all-start.4 = ((bf16[8,40,768]{2,1,0:T(8,128)(2,1)}), bf16[8,40,768]{2,1,0:T(8,128)(2,1)S(1)}, u32[]{:S(2)}, u32[]{:S(2)}) async-start(bf16[8,40,768]{2,1,0:T(8,128)(2,1)} %slice.104), calls=%async_computation.4 | async-start | bytes 983040 | tf_op jit(solution)/shard_map/all_to_all | solution.py:111
  147.1 0.2 copy.44
  147.5 1.6 collective-permute-start.16
  149.1 11.4 %all-to-all-done.4 = bf16[8,40,768]{2,1,0:T(8,128)(2,1)S(1)} async-done(((bf16[8,40,768]{2,1,0:T(8,128)(2,1)}), bf16[8,40,768]{2,1,0:T(8,128)(2,1)S(1)}, u32[]{:S(2)}, u32[]{:S(2)}) %all-to-all-start.4) | async-done | bytes 491552 | tf_op jit(solution)/shard_map/all_to_all | solution.py:111
  160.6 0.2 convert_element_type.113
  160.9 1.6 collective-permute-start.14
  162.6 0.7 fusion.64
  171.0 1.5 collective-permute-done.14
  173.1 2.1 %collective-permute-done.15 = bf16[2,40,6144]{2,1,0:T(8,128)(2,1)S(1)} collective-permute-done((bf16[2,40,6144]{2,1,0:T(8,128)(2,1)S(1)}, bf16[2,40,6144]{2,1,0:T(8,128)(2,1)S(1)}, u32[]{:S(2)}, u32[]{:S(2)}) %collective-permute-start.15) | collective-permute-done | bytes 983072 | tf_op jit(solution)/shard_map/ppermute | solution.py:77
  175.3 0.2 pad_maximum_fusion
  175.8 2.2 %maximum_maximum_fusion = bf16[4,72,6144]{2,1,0:T(8,128)(2,1)} fusion(bf16[1,32,6144]{2,1,0:T(8,128)(2,1)S(1)} %get-tuple-element.9, bf16[1,40,6144]{2,1,0:T(8,128)(2,1)S(1)} %get-tuple-element.5, bf16[1,32,6144]{2,1,0:T(8,128)(2,1)S(1)} %get-tuple-element.10, bf16[1,40,6144]{2,1,0:T(8,128)(2,1)S(1)} %get-tuple-element.6, ...), kind=kLoop, calls=%fused_computation | loop fusion | flops 28311552 | bytes 7077888 | tf_op jit(solution)/shard_map/concatenate | solution.py:123
  (63 shorter events, 4.4 us)
Async XLA Ops:
  0.6 18.5 %copy-start.1 = (bf16[1,72,6144]{2,1,0:T(8,128)(2,1)S(1)}, bf16[1,72,6144]{2,1,0:T(8,128)(2,1)}, u32[]{:S(2)}) copy-start(bf16[1,72,6144]{2,1,0:T(8,128)(2,1)} %param.3) | copy-start | bytes 2654212
  3.5 15.8 %copy-start = (f32[1,72,6144]{2,1,0:T(8,128)}, f32[1,72,6144]{2,1,0:T(8,128)S(1)}, u32[]{:S(2)}) copy-start(f32[1,72,6144]{2,1,0:T(8,128)S(1)} %get-tuple-element.3) | copy-start | bytes 5308420
  20.6 24.8 %all-to-all-start.1 = ((bf16[72,8,768]{2,0,1:T(8,128)(2,1)}), bf16[72,8,768]{2,0,1:T(8,128)(2,1)S(1)}, u32[]{:S(2)}, u32[]{:S(2)}) async-start(bf16[72,8,768]{2,0,1:T(8,128)(2,1)} %copy.35), calls=%async_computation.1 | async-start | bytes 1769472 | tf_op jit(solution)/shard_map/all_to_all | solution.py:90
  46.9 7.9 %collective-permute-start = (f32[37,576]{1,0:T(8,128)S(1)}, f32[37,576]{1,0:T(8,128)S(1)}, u32[]{:S(2)}, u32[]{:S(2)}) collective-permute-start(f32[37,576]{1,0:T(8,128)S(1)} %get-tuple-element.27), channel_id=1, source_target_pairs={{0,1},{1,2},{2,3},{3,4},{4,5},{5,6},{6,7},{7,0},{8,9},{9,10},{10,1... | collective-permute-start | bytes 255752 | tf_op jit(solution)/shard_map/ppermute | solution.py:52
  48.2 6.7 %collective-permute-start.6 = (f32[37,576]{1,0:T(8,128)S(1)}, f32[37,576]{1,0:T(8,128)S(1)}, u32[]{:S(2)}, u32[]{:S(2)}) collective-permute-start(f32[37,576]{1,0:T(8,128)S(1)} %get-tuple-element.28), channel_id=1, source_target_pairs={{0,7},{1,0},{2,1},{3,2},{4,3},{5,4},{6,5},{7,6},{8,15},{9,8},{10,9... | collective-permute-start | bytes 255752 | tf_op jit(solution)/shard_map/ppermute | solution.py:52
  51.7 5.2 %collective-permute-start.5 = (f32[37,576]{1,0:T(8,128)S(1)}, f32[37,576]{1,0:T(8,128)S(1)}, u32[]{:S(2)}, u32[]{:S(2)}) collective-permute-start(f32[37,576]{1,0:T(8,128)S(1)} %get-tuple-element.29), channel_id=1, source_target_pairs={{0,6},{1,7},{2,0},{3,1},{4,2},{5,3},{6,4},{7,5},{8,14},{9,15},{10,... | collective-permute-start | bytes 255752 | tf_op jit(solution)/shard_map/ppermute | solution.py:52
  51.7 7.4 %collective-permute-start.4 = (f32[37,576]{1,0:T(8,128)S(1)}, f32[37,576]{1,0:T(8,128)S(1)}, u32[]{:S(2)}, u32[]{:S(2)}) collective-permute-start(f32[37,576]{1,0:T(8,128)S(1)} %get-tuple-element.30), channel_id=1, source_target_pairs={{0,5},{1,6},{2,7},{3,0},{4,1},{5,2},{6,3},{7,4},{8,13},{9,14},{10,... | collective-permute-start | bytes 255752 | tf_op jit(solution)/shard_map/ppermute | solution.py:52
  51.7 15.3 %collective-permute-start.3 = (f32[37,576]{1,0:T(8,128)S(1)}, f32[37,576]{1,0:T(8,128)S(1)}, u32[]{:S(2)}, u32[]{:S(2)}) collective-permute-start(f32[37,576]{1,0:T(8,128)S(1)} %get-tuple-element.31), channel_id=1, source_target_pairs={{0,4},{1,5},{2,6},{3,7},{4,0},{5,1},{6,2},{7,3},{8,12},{9,13},{10,... | collective-permute-start | bytes 255752 | tf_op jit(solution)/shard_map/ppermute | solution.py:52
  54.8 12.8 %collective-permute-start.2 = (f32[37,576]{1,0:T(8,128)S(1)}, f32[37,576]{1,0:T(8,128)S(1)}, u32[]{:S(2)}, u32[]{:S(2)}) collective-permute-start(f32[37,576]{1,0:T(8,128)S(1)} %get-tuple-element.32), channel_id=1, source_target_pairs={{0,3},{1,4},{2,5},{3,6},{4,7},{5,0},{6,1},{7,2},{8,11},{9,12},{10,... | collective-permute-start | bytes 255752 | tf_op jit(solution)/shard_map/ppermute | solution.py:52
  54.9 12.7 %collective-permute-start.1 = (f32[37,576]{1,0:T(8,128)S(1)}, f32[37,576]{1,0:T(8,128)S(1)}, u32[]{:S(2)}, u32[]{:S(2)}) collective-permute-start(f32[37,576]{1,0:T(8,128)S(1)} %get-tuple-element.33), channel_id=1, source_target_pairs={{0,2},{1,3},{2,4},{3,5},{4,6},{5,7},{6,0},{7,1},{8,10},{9,11},{10,... | collective-permute-start | bytes 255752 | tf_op jit(solution)/shard_map/ppermute | solution.py:52
  87.8 8.4 %collective-permute-start.7 = (f32[37,576]{1,0:T(8,128)S(1)}, f32[37,576]{1,0:T(8,128)S(1)}, u32[]{:S(2)}, u32[]{:S(2)}) collective-permute-start(f32[37,576]{1,0:T(8,128)S(1)} %get-tuple-element.20), channel_id=1, source_target_pairs={{0,1},{1,2},{2,3},{3,4},{4,5},{5,6},{6,7},{7,0},{8,9},{9,10},{10,1... | collective-permute-start | bytes 255752 | tf_op jit(solution)/shard_map/ppermute | solution.py:52
  89.0 7.2 %collective-permute-start.13 = (f32[37,576]{1,0:T(8,128)S(1)}, f32[37,576]{1,0:T(8,128)S(1)}, u32[]{:S(2)}, u32[]{:S(2)}) collective-permute-start(f32[37,576]{1,0:T(8,128)S(1)} %get-tuple-element.21), channel_id=1, source_target_pairs={{0,7},{1,0},{2,1},{3,2},{4,3},{5,4},{6,5},{7,6},{8,15},{9,8},{10,9... | collective-permute-start | bytes 255752 | tf_op jit(solution)/shard_map/ppermute | solution.py:52
  92.6 5.5 %collective-permute-start.12 = (f32[37,576]{1,0:T(8,128)S(1)}, f32[37,576]{1,0:T(8,128)S(1)}, u32[]{:S(2)}, u32[]{:S(2)}) collective-permute-start(f32[37,576]{1,0:T(8,128)S(1)} %get-tuple-element.22), channel_id=1, source_target_pairs={{0,6},{1,7},{2,0},{3,1},{4,2},{5,3},{6,4},{7,5},{8,14},{9,15},{10,... | collective-permute-start | bytes 255752 | tf_op jit(solution)/shard_map/ppermute | solution.py:52
  92.6 7.7 %collective-permute-start.11 = (f32[37,576]{1,0:T(8,128)S(1)}, f32[37,576]{1,0:T(8,128)S(1)}, u32[]{:S(2)}, u32[]{:S(2)}) collective-permute-start(f32[37,576]{1,0:T(8,128)S(1)} %get-tuple-element.23), channel_id=1, source_target_pairs={{0,5},{1,6},{2,7},{3,0},{4,1},{5,2},{6,3},{7,4},{8,13},{9,14},{10,... | collective-permute-start | bytes 255752 | tf_op jit(solution)/shard_map/ppermute | solution.py:52
  92.6 16.3 %collective-permute-start.10 = (f32[37,576]{1,0:T(8,128)S(1)}, f32[37,576]{1,0:T(8,128)S(1)}, u32[]{:S(2)}, u32[]{:S(2)}) collective-permute-start(f32[37,576]{1,0:T(8,128)S(1)} %get-tuple-element.24), channel_id=1, source_target_pairs={{0,4},{1,5},{2,6},{3,7},{4,0},{5,1},{6,2},{7,3},{8,12},{9,13},{10,... | collective-permute-start | bytes 255752 | tf_op jit(solution)/shard_map/ppermute | solution.py:52
  96.3 12.8 %collective-permute-start.9 = (f32[37,576]{1,0:T(8,128)S(1)}, f32[37,576]{1,0:T(8,128)S(1)}, u32[]{:S(2)}, u32[]{:S(2)}) collective-permute-start(f32[37,576]{1,0:T(8,128)S(1)} %get-tuple-element.25), channel_id=1, source_target_pairs={{0,3},{1,4},{2,5},{3,6},{4,7},{5,0},{6,1},{7,2},{8,11},{9,12},{10,... | collective-permute-start | bytes 255752 | tf_op jit(solution)/shard_map/ppermute | solution.py:52
  96.3 12.8 %collective-permute-start.8 = (f32[37,576]{1,0:T(8,128)S(1)}, f32[37,576]{1,0:T(8,128)S(1)}, u32[]{:S(2)}, u32[]{:S(2)}) collective-permute-start(f32[37,576]{1,0:T(8,128)S(1)} %get-tuple-element.26), channel_id=1, source_target_pairs={{0,2},{1,3},{2,4},{3,5},{4,6},{5,7},{6,0},{7,1},{8,10},{9,11},{10,... | collective-permute-start | bytes 255752 | tf_op jit(solution)/shard_map/ppermute | solution.py:52
  127.6 19.3 %copy-start.2 = (s32[4]{0:T(128)S(1)}, s32[4]{0:T(128)}, u32[]{:S(2)}) copy-start(s32[4]{0:T(128)} %param.5) | copy-start | bytes 52
  128.4 14.8 %all-to-all-start.5 = ((bf16[8,32,768]{2,1,0:T(8,128)(2,1)}), bf16[8,32,768]{2,1,0:T(8,128)(2,1)S(1)}, u32[]{:S(2)}, u32[]{:S(2)}) async-start(bf16[8,32,768]{2,1,0:T(8,128)(2,1)} %slice.107), calls=%async_computation.5 | async-start | bytes 786432 | tf_op jit(solution)/shard_map/all_to_all | solution.py:111
  143.2 17.2 %all-to-all-start.4 = ((bf16[8,40,768]{2,1,0:T(8,128)(2,1)}), bf16[8,40,768]{2,1,0:T(8,128)(2,1)S(1)}, u32[]{:S(2)}, u32[]{:S(2)}) async-start(bf16[8,40,768]{2,1,0:T(8,128)(2,1)} %slice.104), calls=%async_computation.4 | async-start | bytes 983040 | tf_op jit(solution)/shard_map/all_to_all | solution.py:111
  147.5 14.9 %collective-permute-start.16 = (bf16[1,32,6144]{2,1,0:T(8,128)(2,1)S(1)}, bf16[1,32,6144]{2,1,0:T(8,128)(2,1)S(1)}, u32[]{:S(2)}, u32[]{:S(2)}) collective-permute-start(bf16[1,32,6144]{2,1,0:T(8,128)(2,1)S(1)} %convert_element_type.117), channel_id=1, source_target_pairs={{0,16},{8,24},{16,0},{24,8},{1,17},{9,25},{17,1},{25,9},{2,18},{10... | collective-permute-start | bytes 1179656 | tf_op jit(solution)/shard_map/ppermute | solution.py:77
  160.9 11.7 %collective-permute-start.14 = (bf16[1,40,6144]{2,1,0:T(8,128)(2,1)S(1)}, bf16[1,40,6144]{2,1,0:T(8,128)(2,1)S(1)}, u32[]{:S(2)}, u32[]{:S(2)}) collective-permute-start(bf16[1,40,6144]{2,1,0:T(8,128)(2,1)S(1)} %convert_element_type.113), channel_id=1, source_target_pairs={{0,16},{8,24},{16,0},{24,8},{1,17},{9,25},{17,1},{25,9},{2,18},{10... | collective-permute-start | bytes 1474568 | tf_op jit(solution)/shard_map/ppermute | solution.py:77
  162.5 10.2 %collective-permute-start.17 = (bf16[2,32,6144]{2,1,0:T(8,128)(2,1)S(1)}, bf16[2,32,6144]{2,1,0:T(8,128)(2,1)S(1)}, u32[]{:S(2)}, u32[]{:S(2)}) collective-permute-start(bf16[2,32,6144]{2,1,0:T(8,128)(2,1)S(1)} %pad_maximum_fusion.3), channel_id=1, source_target_pairs={{0,8},{8,0},{16,24},{24,16},{1,9},{9,1},{17,25},{25,17},{2,10},{10... | collective-permute-start | bytes 2359304 | tf_op jit(solution)/shard_map/ppermute | solution.py:77
  172.6 2.6 %collective-permute-start.15 = (bf16[2,40,6144]{2,1,0:T(8,128)(2,1)S(1)}, bf16[2,40,6144]{2,1,0:T(8,128)(2,1)S(1)}, u32[]{:S(2)}, u32[]{:S(2)}) collective-permute-start(bf16[2,40,6144]{2,1,0:T(8,128)(2,1)S(1)} %pad_maximum_fusion.2), channel_id=1, source_target_pairs={{0,8},{8,0},{16,24},{24,16},{1,9},{9,1},{17,25},{25,17},{2,10},{10... | collective-permute-start | bytes 2949128 | tf_op jit(solution)/shard_map/ppermute | solution.py:77

commit v10 on v9

--- a/solution.py
+++ b/solution.py
@@ -105,13 +105,17 @@
         jnp.where(owner[None, :] == ids[:, None], ids[None, :], 0), axis=1
     )
     where_from = inverse ^ lax.axis_index("dp")
+    bounds = ((0, half), (half, per)) if half < per else ((0, per),)
+    parts = [
+        blocks[:, lo:hi, :].reshape(size * (hi - lo), columns.shape[1]) for lo, hi in bounds
+    ]
     pieces = []
-    for lo, hi in ((0, half), (half, per)) if half < per else ((0, per),):
-        piece = blocks[:, lo:hi, :].reshape(size * (hi - lo), columns.shape[1])
-        back_rows = lax.all_to_all(piece, "tensor", split_axis=0, concat_axis=1, tiled=True)
+    for n in range(len(parts)):
+        back_rows = lax.all_to_all(parts[n], "tensor", split_axis=0, concat_axis=1, tiled=True)
+        if n + 1 < len(parts):
+            parts[n + 1], back_rows = lax.optimization_barrier((parts[n + 1], back_rows))
         scaled = (factor * back_rows.astype(jnp.float32)).astype(jnp.bfloat16)
-        held = gather_slots(scaled, "dp", slots)
-        pieces.append(held)
+        pieces.append(gather_slots(scaled, "dp", slots))
     rows = []
     for m in range(slots):
         rows.append(

time: 179 us -> 178 us (level)
    ppermute x4, waiting for transfers between devices: 3.7 us -> 1.52 us  [gather_slots(): got = lax.ppermute(sent, axis, [(i, i ^ bit) for i in range(size)])]
where the time goes in v10:
time: 178 us; the launch traced here: 177 us
  waiting for transfers between devices  68.4 us (38%)
  blocking collectives  45.6 us (26%)
  starting transfers between devices  32.9 us (18%)
  between operations  9.47 us (5%)
  other arithmetic  9.17 us (5%)
  local copies, waits for them, and re-layouts  6.65 us (4%)
  matrix products  5.16 us (3%)
    all_to_all x2, blocking collectives, gram_allreduce(): lax.all_to_all(spread, axis, split_axis=0, concat_axis=0, tiled=True)  32 us
    ppermute x14, waiting for transfers between devices, gram_allreduce(): acc = acc + lax.ppermute(outgoing, axis, _shift_pairs(size, s))  23.3 us
    all_to_all x2, waiting for transfers between devices, per_device(): lax.all_to_all(parts[n], 'tensor', split_axis=0, concat_axis=1, tiled=True)  22.5 us
    all_to_all x1, waiting for transfers between devices, per_device(): lax.all_to_all(rows_here, 'tensor', split_axis=1, concat_axis=0, tiled=True)  21 us
    ppermute x14, starting transfers between devices, gram_allreduce(): acc = acc + lax.ppermute(outgoing, axis, _shift_pairs(size, s))  18.6 us
    all_to_all x1, blocking collectives, total_over(): got = lax.all_to_all(spread, axis, split_axis=0, concat_axis=0, tiled=True)  13.6 us
    all_to_all x2, starting transfers between devices, per_device(): lax.all_to_all(parts[n], 'tensor', split_axis=0, concat_axis=1, tiled=True)  7.1 us
    ppermute x4, starting transfers between devices, gather_slots(): got = lax.ppermute(sent, axis, [(i, i ^ bit) for i in range(size)])  3.67 us
  transfers between devices with their start and end apart: 21, of which 16 were waited for; matrix products, arithmetic and copies ran while one was open for 2% of the time, Pallas kernels for 0%

profile of v10, /device:TPU:0, one launch (start us, length us, event | category | flops | bytes accessed | tf_op | source)
XLA Modules:
  0.0 177.3 jit_solution(12676490680244417356)
XLA Ops:
  0.6 2.9 %multiply_reduce_fusion = (f32[]{:T(128)}, f32[1,72,6144]{2,1,0:T(8,128)S(1)}) fusion(bf16[1,72,6144]{2,1,0:T(8,128)(2,1)} %param.3, f32[1,72,6144]{2,1,0:T(8,128)} %param.4), kind=kLoop, calls=%fused_computation.7 | loop fusion | flops 3096575 | bytes 4423684 | tf_op jit(solution)/shard_map/reduce_sum | solution.py:88
  3.5 0.6 broadcast_in_dim.58
  4.2 13.6 %all_to_all.61 = f32[8,1,1]{2,1,0:T(1,128)S(1)} all-to-all(f32[8,1,1]{2,1,0:T(1,128)S(1)} %broadcast_in_dim.58), channel_id=1, replica_groups=mesh['dp'=4,'tensor'=8] {'tensor'}, dimensions={0} | all-to-all | bytes 64 | tf_op jit(solution)/shard_map/all_to_all | solution.py:26
  17.8 0.6 reduce_sum.46
  19.1 0.3 divide_convert_fusion
  19.5 1.1 copy.43
  20.6 3.6 %all-to-all-start.1 = ((bf16[72,8,768]{2,0,1:T(8,128)(2,1)}), bf16[72,8,768]{2,0,1:T(8,128)(2,1)S(1)}, u32[]{:S(2)}, u32[]{:S(2)}) async-start(bf16[72,8,768]{2,0,1:T(8,128)(2,1)} %copy.43), calls=%async_computation.1 | async-start | bytes 1769472 | tf_op jit(solution)/shard_map/all_to_all | solution.py:90
  24.4 21.0 %all-to-all-done.1 = bf16[72,8,768]{2,0,1:T(8,128)(2,1)S(1)} async-done(((bf16[72,8,768]{2,0,1:T(8,128)(2,1)}), bf16[72,8,768]{2,0,1:T(8,128)(2,1)S(1)}, u32[]{:S(2)}, u32[]{:S(2)}) %all-to-all-start.1) | async-done | bytes 884768 | tf_op jit(solution)/shard_map/all_to_all | solution.py:90
  45.4 0.9 fusion.65
  46.3 0.2 slice_select_fusion.1
  46.5 0.2 maximum_maximum_fusion.1
  46.9 1.3 collective-permute-start
  48.2 3.5 %collective-permute-start.6 = (f32[37,576]{1,0:T(8,128)S(1)}, f32[37,576]{1,0:T(8,128)S(1)}, u32[]{:S(2)}, u32[]{:S(2)}) collective-permute-start(f32[37,576]{1,0:T(8,128)S(1)} %get-tuple-element.32), channel_id=1, source_target_pairs={{0,7},{1,0},{2,1},{3,2},{4,3},{5,4},{6,5},{7,6},{8,15},{9,8},{10,9... | collective-permute-start | bytes 255752 | tf_op jit(solution)/shard_map/ppermute | solution.py:52
  51.7 2.9 %collective-permute-start.3 = (f32[37,576]{1,0:T(8,128)S(1)}, f32[37,576]{1,0:T(8,128)S(1)}, u32[]{:S(2)}, u32[]{:S(2)}) collective-permute-start(f32[37,576]{1,0:T(8,128)S(1)} %get-tuple-element.35), channel_id=1, source_target_pairs={{0,4},{1,5},{2,6},{3,7},{4,0},{5,1},{6,2},{7,3},{8,12},{9,13},{10,... | collective-permute-start | bytes 255752 | tf_op jit(solution)/shard_map/ppermute | solution.py:52
  54.9 1.8 %collective-permute-start.1 = (f32[37,576]{1,0:T(8,128)S(1)}, f32[37,576]{1,0:T(8,128)S(1)}, u32[]{:S(2)}, u32[]{:S(2)}) collective-permute-start(f32[37,576]{1,0:T(8,128)S(1)} %get-tuple-element.37), channel_id=1, source_target_pairs={{0,2},{1,3},{2,4},{3,5},{4,6},{5,7},{6,0},{7,1},{8,10},{9,11},{10,... | collective-permute-start | bytes 255752 | tf_op jit(solution)/shard_map/ppermute | solution.py:52
  56.7 0.3 collective-permute-done.5
  56.9 2.2 %collective-permute-done.4 = f32[37,576]{1,0:T(8,128)S(1)} collective-permute-done((f32[37,576]{1,0:T(8,128)S(1)}, f32[37,576]{1,0:T(8,128)S(1)}, u32[]{:S(2)}, u32[]{:S(2)}) %collective-permute-start.4) | collective-permute-done | bytes 85280 | tf_op jit(solution)/shard_map/ppermute | solution.py:52
  59.1 7.9 %collective-permute-done.3 = f32[37,576]{1,0:T(8,128)S(1)} collective-permute-done((f32[37,576]{1,0:T(8,128)S(1)}, f32[37,576]{1,0:T(8,128)S(1)}, u32[]{:S(2)}, u32[]{:S(2)}) %collective-permute-start.3) | collective-permute-done | bytes 85280 | tf_op jit(solution)/shard_map/ppermute | solution.py:52
  67.0 0.7 collective-permute-done.2
  67.8 16.0 %all_to_all.62 = bf16[8,37,576]{2,1,0:T(8,128)(2,1)S(1)} all-to-all(bf16[8,37,576]{2,1,0:T(8,128)(2,1)S(1)} %broadcast_in_dim.61), channel_id=1, replica_groups=mesh['dp'=4,'tensor'=8] {'tensor'}, dimensions={0} | all-to-all | bytes 681984 | tf_op jit(solution)/shard_map/all_to_all | solution.py:55
  84.6 1.7 add_convert_fusion.1
  86.3 0.9 fusion.66
  87.2 0.2 slice_select_fusion
  87.8 1.2 collective-permute-start.7
  89.1 3.6 %collective-permute-start.13 = (f32[37,576]{1,0:T(8,128)S(1)}, f32[37,576]{1,0:T(8,128)S(1)}, u32[]{:S(2)}, u32[]{:S(2)}) collective-permute-start(f32[37,576]{1,0:T(8,128)S(1)} %get-tuple-element.25), channel_id=1, source_target_pairs={{0,7},{1,0},{2,1},{3,2},{4,3},{5,4},{6,5},{7,6},{8,15},{9,8},{10,9... | collective-permute-start | bytes 255752 | tf_op jit(solution)/shard_map/ppermute | solution.py:52
  92.6 2.9 %collective-permute-start.10 = (f32[37,576]{1,0:T(8,128)S(1)}, f32[37,576]{1,0:T(8,128)S(1)}, u32[]{:S(2)}, u32[]{:S(2)}) collective-permute-start(f32[37,576]{1,0:T(8,128)S(1)} %get-tuple-element.28), channel_id=1, source_target_pairs={{0,4},{1,5},{2,6},{3,7},{4,0},{5,1},{6,2},{7,3},{8,12},{9,13},{10,... | collective-permute-start | bytes 255752 | tf_op jit(solution)/shard_map/ppermute | solution.py:52
  95.6 0.7 collective-permute-done.7
  96.3 1.4 collective-permute-start.8
  97.7 0.4 collective-permute-done.12
  98.1 2.2 %collective-permute-done.11 = f32[37,576]{1,0:T(8,128)S(1)} collective-permute-done((f32[37,576]{1,0:T(8,128)S(1)}, f32[37,576]{1,0:T(8,128)S(1)}, u32[]{:S(2)}, u32[]{:S(2)}) %collective-permute-start.11) | collective-permute-done | bytes 85280 | tf_op jit(solution)/shard_map/ppermute | solution.py:52
  100.3 8.6 %collective-permute-done.10 = f32[37,576]{1,0:T(8,128)S(1)} collective-permute-done((f32[37,576]{1,0:T(8,128)S(1)}, f32[37,576]{1,0:T(8,128)S(1)}, u32[]{:S(2)}, u32[]{:S(2)}) %collective-permute-start.10) | collective-permute-done | bytes 85280 | tf_op jit(solution)/shard_map/ppermute | solution.py:52
  109.2 15.9 %all_to_all.63 = bf16[8,37,576]{2,1,0:T(8,128)(2,1)S(1)} all-to-all(bf16[8,37,576]{2,1,0:T(8,128)(2,1)S(1)} %broadcast_in_dim.65), channel_id=1, replica_groups=mesh['dp'=4,'tensor'=8] {'tensor'}, dimensions={0} | all-to-all | bytes 681984 | tf_op jit(solution)/shard_map/all_to_all | solution.py:55
  125.9 1.7 add_convert_fusion
  127.6 0.8 slice.105
  128.4 3.5 %all-to-all-start.4 = ((bf16[8,40,768]{2,1,0:T(8,128)(2,1)}), bf16[8,40,768]{2,1,0:T(8,128)(2,1)S(1)}, u32[]{:S(2)}, u32[]{:S(2)}) async-start(bf16[8,40,768]{2,1,0:T(8,128)(2,1)} %slice.105), calls=%async_computation.4 | async-start | bytes 983040 | tf_op jit(solution)/shard_map/all_to_all | solution.py:114
  131.9 0.8 slice.104
  132.7 12.7 %all-to-all-done.4 = bf16[8,40,768]{2,1,0:T(8,128)(2,1)S(1)} async-done(((bf16[8,40,768]{2,1,0:T(8,128)(2,1)}), bf16[8,40,768]{2,1,0:T(8,128)(2,1)S(1)}, u32[]{:S(2)}, u32[]{:S(2)}) %all-to-all-start.4) | async-done | bytes 491552 | tf_op jit(solution)/shard_map/all_to_all | solution.py:114
  145.4 3.6 %all-to-all-start.5 = ((bf16[8,32,768]{2,1,0:T(8,128)(2,1)}), bf16[8,32,768]{2,1,0:T(8,128)(2,1)S(1)}, u32[]{:S(2)}, u32[]{:S(2)}) async-start(bf16[8,32,768]{2,1,0:T(8,128)(2,1)} %bitcast.28), calls=%async_computation.5 | async-start | bytes 786432 | tf_op jit(solution)/shard_map/all_to_all | solution.py:114
  149.1 1.5 collective-permute-start.14
  150.7 9.9 %all-to-all-done.5 = bf16[8,32,768]{2,1,0:T(8,128)(2,1)S(1)} async-done(((bf16[8,32,768]{2,1,0:T(8,128)(2,1)}), bf16[8,32,768]{2,1,0:T(8,128)(2,1)S(1)}, u32[]{:S(2)}, u32[]{:S(2)}) %all-to-all-start.5) | async-done | bytes 393248 | tf_op jit(solution)/shard_map/all_to_all | solution.py:114
  160.7 0.2 copy.52
  161.1 1.5 collective-permute-start.16
  162.8 1.0 pad_maximum_fusion.2
  163.8 0.7 fusion.64
  172.3 0.6 collective-permute-start.17
  172.9 0.2 pad_maximum_fusion
  173.4 1.4 collective-permute-done.17
  175.1 2.2 %maximum_maximum_fusion = bf16[4,72,6144]{2,1,0:T(8,128)(2,1)} fusion(bf16[1,32,6144]{2,1,0:T(8,128)(2,1)S(1)} %get-tuple-element.13, bf16[1,40,6144]{2,1,0:T(8,128)(2,1)S(1)} %get-tuple-element.9, bf16[1,32,6144]{2,1,0:T(8,128)(2,1)S(1)} %get-tuple-element.14, bf16[1,40,6144]{2,1,0:T(8,128)(2,1)S(1)} %get-tuple-element.10, ...), kind=kLoop, calls=%fused_computation | loop fusion | flops 28311552 | bytes 7077888 | tf_op jit(solution)/shard_map/concatenate | solution.py:127
  (62 shorter events, 4.2 us)
Async XLA Ops:
  0.6 18.5 %copy-start.1 = (bf16[1,72,6144]{2,1,0:T(8,128)(2,1)S(1)}, bf16[1,72,6144]{2,1,0:T(8,128)(2,1)}, u32[]{:S(2)}) copy-start(bf16[1,72,6144]{2,1,0:T(8,128)(2,1)} %param.3) | copy-start | bytes 2654212
  3.5 15.8 %copy-start = (f32[1,72,6144]{2,1,0:T(8,128)}, f32[1,72,6144]{2,1,0:T(8,128)S(1)}, u32[]{:S(2)}) copy-start(f32[1,72,6144]{2,1,0:T(8,128)S(1)} %get-tuple-element.7) | copy-start | bytes 5308420
  20.6 24.8 %all-to-all-start.1 = ((bf16[72,8,768]{2,0,1:T(8,128)(2,1)}), bf16[72,8,768]{2,0,1:T(8,128)(2,1)S(1)}, u32[]{:S(2)}, u32[]{:S(2)}) async-start(bf16[72,8,768]{2,0,1:T(8,128)(2,1)} %copy.43), calls=%async_computation.1 | async-start | bytes 1769472 | tf_op jit(solution)/shard_map/all_to_all | solution.py:90
  46.9 7.9 %collective-permute-start = (f32[37,576]{1,0:T(8,128)S(1)}, f32[37,576]{1,0:T(8,128)S(1)}, u32[]{:S(2)}, u32[]{:S(2)}) collective-permute-start(f32[37,576]{1,0:T(8,128)S(1)} %get-tuple-element.31), channel_id=1, source_target_pairs={{0,1},{1,2},{2,3},{3,4},{4,5},{5,6},{6,7},{7,0},{8,9},{9,10},{10,1... | collective-permute-start | bytes 255752 | tf_op jit(solution)/shard_map/ppermute | solution.py:52
  48.2 6.7 %collective-permute-start.6 = (f32[37,576]{1,0:T(8,128)S(1)}, f32[37,576]{1,0:T(8,128)S(1)}, u32[]{:S(2)}, u32[]{:S(2)}) collective-permute-start(f32[37,576]{1,0:T(8,128)S(1)} %get-tuple-element.32), channel_id=1, source_target_pairs={{0,7},{1,0},{2,1},{3,2},{4,3},{5,4},{6,5},{7,6},{8,15},{9,8},{10,9... | collective-permute-start | bytes 255752 | tf_op jit(solution)/shard_map/ppermute | solution.py:52
  51.7 5.2 %collective-permute-start.5 = (f32[37,576]{1,0:T(8,128)S(1)}, f32[37,576]{1,0:T(8,128)S(1)}, u32[]{:S(2)}, u32[]{:S(2)}) collective-permute-start(f32[37,576]{1,0:T(8,128)S(1)} %get-tuple-element.33), channel_id=1, source_target_pairs={{0,6},{1,7},{2,0},{3,1},{4,2},{5,3},{6,4},{7,5},{8,14},{9,15},{10,... | collective-permute-start | bytes 255752 | tf_op jit(solution)/shard_map/ppermute | solution.py:52
  51.7 7.4 %collective-permute-start.4 = (f32[37,576]{1,0:T(8,128)S(1)}, f32[37,576]{1,0:T(8,128)S(1)}, u32[]{:S(2)}, u32[]{:S(2)}) collective-permute-start(f32[37,576]{1,0:T(8,128)S(1)} %get-tuple-element.34), channel_id=1, source_target_pairs={{0,5},{1,6},{2,7},{3,0},{4,1},{5,2},{6,3},{7,4},{8,13},{9,14},{10,... | collective-permute-start | bytes 255752 | tf_op jit(solution)/shard_map/ppermute | solution.py:52
  51.7 15.3 %collective-permute-start.3 = (f32[37,576]{1,0:T(8,128)S(1)}, f32[37,576]{1,0:T(8,128)S(1)}, u32[]{:S(2)}, u32[]{:S(2)}) collective-permute-start(f32[37,576]{1,0:T(8,128)S(1)} %get-tuple-element.35), channel_id=1, source_target_pairs={{0,4},{1,5},{2,6},{3,7},{4,0},{5,1},{6,2},{7,3},{8,12},{9,13},{10,... | collective-permute-start | bytes 255752 | tf_op jit(solution)/shard_map/ppermute | solution.py:52
  54.8 12.8 %collective-permute-start.2 = (f32[37,576]{1,0:T(8,128)S(1)}, f32[37,576]{1,0:T(8,128)S(1)}, u32[]{:S(2)}, u32[]{:S(2)}) collective-permute-start(f32[37,576]{1,0:T(8,128)S(1)} %get-tuple-element.36), channel_id=1, source_target_pairs={{0,3},{1,4},{2,5},{3,6},{4,7},{5,0},{6,1},{7,2},{8,11},{9,12},{10,... | collective-permute-start | bytes 255752 | tf_op jit(solution)/shard_map/ppermute | solution.py:52
  54.9 12.8 %collective-permute-start.1 = (f32[37,576]{1,0:T(8,128)S(1)}, f32[37,576]{1,0:T(8,128)S(1)}, u32[]{:S(2)}, u32[]{:S(2)}) collective-permute-start(f32[37,576]{1,0:T(8,128)S(1)} %get-tuple-element.37), channel_id=1, source_target_pairs={{0,2},{1,3},{2,4},{3,5},{4,6},{5,7},{6,0},{7,1},{8,10},{9,11},{10,... | collective-permute-start | bytes 255752 | tf_op jit(solution)/shard_map/ppermute | solution.py:52
  87.8 8.4 %collective-permute-start.7 = (f32[37,576]{1,0:T(8,128)S(1)}, f32[37,576]{1,0:T(8,128)S(1)}, u32[]{:S(2)}, u32[]{:S(2)}) collective-permute-start(f32[37,576]{1,0:T(8,128)S(1)} %get-tuple-element.24), channel_id=1, source_target_pairs={{0,1},{1,2},{2,3},{3,4},{4,5},{5,6},{6,7},{7,0},{8,9},{9,10},{10,1... | collective-permute-start | bytes 255752 | tf_op jit(solution)/shard_map/ppermute | solution.py:52
  89.1 7.2 %collective-permute-start.13 = (f32[37,576]{1,0:T(8,128)S(1)}, f32[37,576]{1,0:T(8,128)S(1)}, u32[]{:S(2)}, u32[]{:S(2)}) collective-permute-start(f32[37,576]{1,0:T(8,128)S(1)} %get-tuple-element.25), channel_id=1, source_target_pairs={{0,7},{1,0},{2,1},{3,2},{4,3},{5,4},{6,5},{7,6},{8,15},{9,8},{10,9... | collective-permute-start | bytes 255752 | tf_op jit(solution)/shard_map/ppermute | solution.py:52
  92.6 5.5 %collective-permute-start.12 = (f32[37,576]{1,0:T(8,128)S(1)}, f32[37,576]{1,0:T(8,128)S(1)}, u32[]{:S(2)}, u32[]{:S(2)}) collective-permute-start(f32[37,576]{1,0:T(8,128)S(1)} %get-tuple-element.26), channel_id=1, source_target_pairs={{0,6},{1,7},{2,0},{3,1},{4,2},{5,3},{6,4},{7,5},{8,14},{9,15},{10,... | collective-permute-start | bytes 255752 | tf_op jit(solution)/shard_map/ppermute | solution.py:52
  92.6 7.7 %collective-permute-start.11 = (f32[37,576]{1,0:T(8,128)S(1)}, f32[37,576]{1,0:T(8,128)S(1)}, u32[]{:S(2)}, u32[]{:S(2)}) collective-permute-start(f32[37,576]{1,0:T(8,128)S(1)} %get-tuple-element.27), channel_id=1, source_target_pairs={{0,5},{1,6},{2,7},{3,0},{4,1},{5,2},{6,3},{7,4},{8,13},{9,14},{10,... | collective-permute-start | bytes 255752 | tf_op jit(solution)/shard_map/ppermute | solution.py:52
  92.6 16.3 %collective-permute-start.10 = (f32[37,576]{1,0:T(8,128)S(1)}, f32[37,576]{1,0:T(8,128)S(1)}, u32[]{:S(2)}, u32[]{:S(2)}) collective-permute-start(f32[37,576]{1,0:T(8,128)S(1)} %get-tuple-element.28), channel_id=1, source_target_pairs={{0,4},{1,5},{2,6},{3,7},{4,0},{5,1},{6,2},{7,3},{8,12},{9,13},{10,... | collective-permute-start | bytes 255752 | tf_op jit(solution)/shard_map/ppermute | solution.py:52
  96.3 12.8 %collective-permute-start.9 = (f32[37,576]{1,0:T(8,128)S(1)}, f32[37,576]{1,0:T(8,128)S(1)}, u32[]{:S(2)}, u32[]{:S(2)}) collective-permute-start(f32[37,576]{1,0:T(8,128)S(1)} %get-tuple-element.29), channel_id=1, source_target_pairs={{0,3},{1,4},{2,5},{3,6},{4,7},{5,0},{6,1},{7,2},{8,11},{9,12},{10,... | collective-permute-start | bytes 255752 | tf_op jit(solution)/shard_map/ppermute | solution.py:52
  96.3 12.8 %collective-permute-start.8 = (f32[37,576]{1,0:T(8,128)S(1)}, f32[37,576]{1,0:T(8,128)S(1)}, u32[]{:S(2)}, u32[]{:S(2)}) collective-permute-start(f32[37,576]{1,0:T(8,128)S(1)} %get-tuple-element.30), channel_id=1, source_target_pairs={{0,2},{1,3},{2,4},{3,5},{4,6},{5,7},{6,0},{7,1},{8,10},{9,11},{10,... | collective-permute-start | bytes 255752 | tf_op jit(solution)/shard_map/ppermute | solution.py:52
  128.4 17.0 %all-to-all-start.4 = ((bf16[8,40,768]{2,1,0:T(8,128)(2,1)}), bf16[8,40,768]{2,1,0:T(8,128)(2,1)S(1)}, u32[]{:S(2)}, u32[]{:S(2)}) async-start(bf16[8,40,768]{2,1,0:T(8,128)(2,1)} %slice.105), calls=%async_computation.4 | async-start | bytes 983040 | tf_op jit(solution)/shard_map/all_to_all | solution.py:114
  131.9 18.8 %copy-start.2 = (s32[4]{0:T(128)S(1)}, s32[4]{0:T(128)}, u32[]{:S(2)}) copy-start(s32[4]{0:T(128)} %param.5) | copy-start | bytes 52
  145.4 15.2 %all-to-all-start.5 = ((bf16[8,32,768]{2,1,0:T(8,128)(2,1)}), bf16[8,32,768]{2,1,0:T(8,128)(2,1)S(1)}, u32[]{:S(2)}, u32[]{:S(2)}) async-start(bf16[8,32,768]{2,1,0:T(8,128)(2,1)} %bitcast.28), calls=%async_computation.5 | async-start | bytes 786432 | tf_op jit(solution)/shard_map/all_to_all | solution.py:114
  149.1 13.7 %collective-permute-start.14 = (bf16[1,40,6144]{2,1,0:T(8,128)(2,1)S(1)}, bf16[1,40,6144]{2,1,0:T(8,128)(2,1)S(1)}, u32[]{:S(2)}, u32[]{:S(2)}) collective-permute-start(bf16[1,40,6144]{2,1,0:T(8,128)(2,1)S(1)} %fusion.32), channel_id=1, source_target_pairs={{0,16},{8,24},{16,0},{24,8},{1,17},{9,25},{17,1},{25,9},{2,18},{10... | collective-permute-start | bytes 1474568 | tf_op jit(solution)/shard_map/ppermute | solution.py:77
  161.1 11.1 %collective-permute-start.16 = (bf16[1,32,6144]{2,1,0:T(8,128)(2,1)S(1)}, bf16[1,32,6144]{2,1,0:T(8,128)(2,1)S(1)}, u32[]{:S(2)}, u32[]{:S(2)}) collective-permute-start(bf16[1,32,6144]{2,1,0:T(8,128)(2,1)S(1)} %convert_element_type.93), channel_id=1, source_target_pairs={{0,16},{8,24},{16,0},{24,8},{1,17},{9,25},{17,1},{25,9},{2,18},{10... | collective-permute-start | bytes 1179656 | tf_op jit(solution)/shard_map/ppermute | solution.py:77
  163.8 9.0 %collective-permute-start.15 = (bf16[2,40,6144]{2,1,0:T(8,128)(2,1)}, bf16[2,40,6144]{2,1,0:T(8,128)(2,1)S(1)}, u32[]{:S(2)}, u32[]{:S(2)}) collective-permute-start(bf16[2,40,6144]{2,1,0:T(8,128)(2,1)} %pad_maximum_fusion.2), channel_id=1, source_target_pairs={{0,8},{8,0},{16,24},{24,16},{1,9},{9,1},{17,25},{25,17},{2,10},{10... | collective-permute-start | bytes 2949128 | tf_op jit(solution)/shard_map/ppermute | solution.py:77
  172.3 2.5 %collective-permute-start.17 = (bf16[2,32,6144]{2,1,0:T(8,128)(2,1)S(1)}, bf16[2,32,6144]{2,1,0:T(8,128)(2,1)S(1)}, u32[]{:S(2)}, u32[]{:S(2)}) collective-permute-start(bf16[2,32,6144]{2,1,0:T(8,128)(2,1)S(1)} %pad_maximum_fusion.3), channel_id=1, source_target_pairs={{0,8},{8,0},{16,24},{24,16},{1,9},{9,1},{17,25},{25,17},{2,10},{10... | collective-permute-start | bytes 2359304 | tf_op jit(solution)/shard_map/ppermute | solution.py:77

commit v11 on v10

--- a/solution.py
+++ b/solution.py
@@ -45,11 +45,10 @@
     )
     per = rows // size
     blocks = payload.reshape(size, per, 2 * h)
-    me = lax.axis_index(axis)
-    acc = lax.dynamic_index_in_dim(blocks, me, 0, keepdims=False)
+    received = lax.all_to_all(blocks, axis, split_axis=0, concat_axis=0, tiled=True)
+    acc = received[0]
     for s in range(1, size):
-        outgoing = lax.dynamic_index_in_dim(blocks, (me + s) % size, 0, keepdims=False)
-        acc = acc + lax.ppermute(outgoing, axis, _shift_pairs(size, s))
+        acc = acc + received[s]
     mine = acc.astype(jnp.bfloat16)
     spread = jnp.broadcast_to(mine[None], (size,) + mine.shape)
     full = lax.all_to_all(spread, axis, split_axis=0, concat_axis=0, tiled=True).reshape(rows, 2 * h)

time: 178 us -> 182 us (1.022)
  blocking collectives: 45.6 us -> 92.7 us
  waiting for transfers between devices: 68.4 us -> 45 us
  starting transfers between devices: 32.9 us -> 14.4 us
    all_to_all x0 -> x2, blocking collectives: none -> 49.4 us  [gram_allreduce(): lax.all_to_all(blocks, axis, split_axis=0, concat_axis=0, tiled=True)]
    ppermute x14 -> x0, waiting for transfers between devices: 23.3 us -> none  [gram_allreduce(): acc = acc + lax.ppermute(outgoing, axis, _shift_pairs(size, s))]
    ppermute x14 -> x0, starting transfers between devices: 18.6 us -> none  [gram_allreduce(): acc = acc + lax.ppermute(outgoing, axis, _shift_pairs(size, s))]
    all_to_all x2, blocking collectives: 32 us -> 29.7 us  [gram_allreduce(): lax.all_to_all(spread, axis, split_axis=0, concat_axis=0, tiled=True)]
  transfers between devices with their start and end apart: 21 -> 7, of which waited for: 16 -> 5; matrix products, arithmetic and copies ran while one was open for 2% -> 2% of each run, Pallas kernels for 0% -> 0%
where the time goes in v11:
time: 182 us
  blocking collectives  92.7 us (51%)
  waiting for transfers between devices  45 us (25%)
  starting transfers between devices  14.4 us (8%)
  other arithmetic  9.13 us (5%)
  between operations  8.91 us (5%)
  local copies, waits for them, and re-layouts  6.47 us (4%)
  matrix products  5.16 us (3%)
    all_to_all x2, blocking collectives, gram_allreduce(): lax.all_to_all(blocks, axis, split_axis=0, concat_axis=0, tiled=True)  49.4 us
    all_to_all x2, blocking collectives, gram_allreduce(): lax.all_to_all(spread, axis, split_axis=0, concat_axis=0, tiled=True)  29.7 us
    all_to_all x2, waiting for transfers between devices, per_device(): lax.all_to_all(parts[n], 'tensor', split_axis=0, concat_axis=1, tiled=True)  22.2 us
    all_to_all x1, waiting for transfers between devices, per_device(): lax.all_to_all(rows_here, 'tensor', split_axis=1, concat_axis=0, tiled=True)  21.1 us
    all_to_all x1, blocking collectives, total_over(): got = lax.all_to_all(spread, axis, split_axis=0, concat_axis=0, tiled=True)  13.6 us
    all_to_all x2, starting transfers between devices, per_device(): lax.all_to_all(parts[n], 'tensor', split_axis=0, concat_axis=1, tiled=True)  7.14 us
    ppermute x4, starting transfers between devices, gather_slots(): got = lax.ppermute(sent, axis, [(i, i ^ bit) for i in range(size)])  3.67 us
  transfers between devices with their start and end apart: 7, of which 5 were waited for; matrix products, arithmetic and copies ran while one was open for 2% of the time, Pallas kernels for 0%

profile of v11, /device:TPU:0, one launch (start us, length us, event | category | flops | bytes accessed | tf_op | source)
XLA Modules:
  0.0 181.7 jit_solution(1963484045356659401)
XLA Ops:
  0.6 2.9 %multiply_reduce_fusion = (f32[]{:T(128)}, f32[1,72,6144]{2,1,0:T(8,128)S(1)}) fusion(bf16[1,72,6144]{2,1,0:T(8,128)(2,1)} %param.3, f32[1,72,6144]{2,1,0:T(8,128)} %param.4), kind=kLoop, calls=%fused_computation.7 | loop fusion | flops 3096575 | bytes 4423684 | tf_op jit(solution)/shard_map/reduce_sum | solution.py:87
  3.5 0.6 broadcast_in_dim.62
  4.2 13.6 %all_to_all.71 = f32[8,1,1]{2,1,0:T(1,128)S(1)} all-to-all(f32[8,1,1]{2,1,0:T(1,128)S(1)} %broadcast_in_dim.62), channel_id=1, replica_groups=mesh['dp'=4,'tensor'=8] {'tensor'}, dimensions={0} | all-to-all | bytes 64 | tf_op jit(solution)/shard_map/all_to_all | solution.py:26
  17.8 0.6 reduce_sum.46
  19.1 0.3 divide_convert_fusion
  19.4 0.2 copy.57
  19.5 1.1 copy.43
  20.6 3.6 %all-to-all-start.1 = ((bf16[72,8,768]{2,0,1:T(8,128)(2,1)}), bf16[72,8,768]{2,0,1:T(8,128)(2,1)S(1)}, u32[]{:S(2)}, u32[]{:S(2)}) async-start(bf16[72,8,768]{2,0,1:T(8,128)(2,1)} %copy.43), calls=%async_computation.1 | async-start | bytes 1769472 | tf_op jit(solution)/shard_map/all_to_all | solution.py:89
  24.3 21.1 %all-to-all-done.1 = bf16[72,8,768]{2,0,1:T(8,128)(2,1)S(1)} async-done(((bf16[72,8,768]{2,0,1:T(8,128)(2,1)}), bf16[72,8,768]{2,0,1:T(8,128)(2,1)S(1)}, u32[]{:S(2)}, u32[]{:S(2)}) %all-to-all-start.1) | async-done | bytes 884768 | tf_op jit(solution)/shard_map/all_to_all | solution.py:89
  45.4 0.9 fusion.55
  46.3 0.2 slice_select_fusion.1
  46.5 0.2 maximum_maximum_fusion.1
  46.9 24.9 %all_to_all.72 = f32[8,37,576]{2,1,0:T(8,128)S(1)} all-to-all(f32[8,37,576]{2,1,0:T(8,128)S(1)} %reshape.61), channel_id=1, replica_groups=mesh['dp'=4,'tensor'=8] {'tensor'}, dimensions={0} | all-to-all | bytes 1363968 | tf_op jit(solution)/shard_map/all_to_all | solution.py:48
  71.9 15.0 %all_to_all.73 = bf16[8,37,576]{2,1,0:T(8,128)(2,1)S(1)} all-to-all(bf16[8,37,576]{2,1,0:T(8,128)(2,1)S(1)} %broadcast_in_dim.66), channel_id=1, replica_groups=mesh['dp'=4,'tensor'=8] {'tensor'}, dimensions={0} | all-to-all | bytes 681984 | tf_op jit(solution)/shard_map/all_to_all | solution.py:54
  86.9 0.2 reshape.62
  87.1 0.2 copy.44
  87.3 0.2 fusion.38
  87.4 0.2 copy.45
  87.6 1.7 add_convert_fusion.1
  89.3 0.9 fusion.56
  90.2 0.2 slice_select_fusion
  90.5 0.2 maximum_maximum_fusion.2
  90.8 24.5 %all_to_all.74 = f32[8,37,576]{2,1,0:T(8,128)S(1)} all-to-all(f32[8,37,576]{2,1,0:T(8,128)S(1)} %reshape.63), channel_id=1, replica_groups=mesh['dp'=4,'tensor'=8] {'tensor'}, dimensions={0} | all-to-all | bytes 1363968 | tf_op jit(solution)/shard_map/all_to_all | solution.py:48
  115.4 14.7 %all_to_all.75 = bf16[8,37,576]{2,1,0:T(8,128)(2,1)S(1)} all-to-all(bf16[8,37,576]{2,1,0:T(8,128)(2,1)S(1)} %broadcast_in_dim.71), channel_id=1, replica_groups=mesh['dp'=4,'tensor'=8] {'tensor'}, dimensions={0} | all-to-all | bytes 681984 | tf_op jit(solution)/shard_map/all_to_all | solution.py:54
  130.1 0.2 reshape.64
  130.3 0.2 copy.54
  130.5 0.2 fusion.37
  130.7 0.2 copy.55
  130.9 1.7 add_convert_fusion
  132.6 0.8 slice.185
  133.4 3.5 %all-to-all-start.6 = ((bf16[8,40,768]{2,1,0:T(8,128)(2,1)}), bf16[8,40,768]{2,1,0:T(8,128)(2,1)S(1)}, u32[]{:S(2)}, u32[]{:S(2)}) async-start(bf16[8,40,768]{2,1,0:T(8,128)(2,1)} %slice.185), calls=%async_computation.6 | async-start | bytes 983040 | tf_op jit(solution)/shard_map/all_to_all | solution.py:113
  136.9 0.8 slice.184
  137.7 12.5 %all-to-all-done.6 = bf16[8,40,768]{2,1,0:T(8,128)(2,1)S(1)} async-done(((bf16[8,40,768]{2,1,0:T(8,128)(2,1)}), bf16[8,40,768]{2,1,0:T(8,128)(2,1)S(1)}, u32[]{:S(2)}, u32[]{:S(2)}) %all-to-all-start.6) | async-done | bytes 491552 | tf_op jit(solution)/shard_map/all_to_all | solution.py:113
  150.2 3.7 %all-to-all-start.7 = ((bf16[8,32,768]{2,1,0:T(8,128)(2,1)}), bf16[8,32,768]{2,1,0:T(8,128)(2,1)S(1)}, u32[]{:S(2)}, u32[]{:S(2)}) async-start(bf16[8,32,768]{2,1,0:T(8,128)(2,1)} %bitcast.14), calls=%async_computation.7 | async-start | bytes 786432 | tf_op jit(solution)/shard_map/all_to_all | solution.py:113
  153.9 1.5 collective-permute-start
  155.6 9.7 %all-to-all-done.7 = bf16[8,32,768]{2,1,0:T(8,128)(2,1)S(1)} async-done(((bf16[8,32,768]{2,1,0:T(8,128)(2,1)}), bf16[8,32,768]{2,1,0:T(8,128)(2,1)S(1)}, u32[]{:S(2)}, u32[]{:S(2)}) %all-to-all-start.7) | async-done | bytes 393248 | tf_op jit(solution)/shard_map/all_to_all | solution.py:113
  165.4 0.2 copy.52
  165.6 0.2 convert_element_type.95
  165.8 1.5 collective-permute-start.2
  167.3 0.3 collective-permute-done
  167.6 1.0 pad_maximum_fusion.2
  168.7 0.6 fusion.54
  176.6 0.6 collective-permute-start.3
  177.3 0.2 pad_maximum_fusion
  177.5 0.2 constant_dynamic-slice_fusion.7
  177.7 1.4 collective-permute-done.3
  179.2 0.2 pad_maximum_fusion.1
  179.5 2.2 %maximum_maximum_fusion = bf16[4,72,6144]{2,1,0:T(8,128)(2,1)} fusion(bf16[1,32,6144]{2,1,0:T(8,128)(2,1)S(1)} %get-tuple-element.13, bf16[1,40,6144]{2,1,0:T(8,128)(2,1)S(1)} %get-tuple-element.9, bf16[1,32,6144]{2,1,0:T(8,128)(2,1)S(1)} %get-tuple-element.14, bf16[1,40,6144]{2,1,0:T(8,128)(2,1)S(1)} %get-tuple-element.10, ...), kind=kLoop, calls=%fused_computation | loop fusion | flops 28311552 | bytes 7077888 | tf_op jit(solution)/shard_map/concatenate | solution.py:126
  (34 shorter events, 1.2 us)
Async XLA Ops:
  0.6 18.5 %copy-start.1 = (bf16[1,72,6144]{2,1,0:T(8,128)(2,1)S(1)}, bf16[1,72,6144]{2,1,0:T(8,128)(2,1)}, u32[]{:S(2)}) copy-start(bf16[1,72,6144]{2,1,0:T(8,128)(2,1)} %param.3) | copy-start | bytes 2654212
  3.5 15.8 %copy-start = (f32[1,72,6144]{2,1,0:T(8,128)}, f32[1,72,6144]{2,1,0:T(8,128)S(1)}, u32[]{:S(2)}) copy-start(f32[1,72,6144]{2,1,0:T(8,128)S(1)} %get-tuple-element.7) | copy-start | bytes 5308420
  20.6 24.8 %all-to-all-start.1 = ((bf16[72,8,768]{2,0,1:T(8,128)(2,1)}), bf16[72,8,768]{2,0,1:T(8,128)(2,1)S(1)}, u32[]{:S(2)}, u32[]{:S(2)}) async-start(bf16[72,8,768]{2,0,1:T(8,128)(2,1)} %copy.43), calls=%async_computation.1 | async-start | bytes 1769472 | tf_op jit(solution)/shard_map/all_to_all | solution.py:89
  133.4 16.7 %all-to-all-start.6 = ((bf16[8,40,768]{2,1,0:T(8,128)(2,1)}), bf16[8,40,768]{2,1,0:T(8,128)(2,1)S(1)}, u32[]{:S(2)}, u32[]{:S(2)}) async-start(bf16[8,40,768]{2,1,0:T(8,128)(2,1)} %slice.185), calls=%async_computation.6 | async-start | bytes 983040 | tf_op jit(solution)/shard_map/all_to_all | solution.py:113
  136.9 18.6 %copy-start.2 = (s32[4]{0:T(128)S(1)}, s32[4]{0:T(128)}, u32[]{:S(2)}) copy-start(s32[4]{0:T(128)} %param.5) | copy-start | bytes 52
  150.2 15.1 %all-to-all-start.7 = ((bf16[8,32,768]{2,1,0:T(8,128)(2,1)}), bf16[8,32,768]{2,1,0:T(8,128)(2,1)S(1)}, u32[]{:S(2)}, u32[]{:S(2)}) async-start(bf16[8,32,768]{2,1,0:T(8,128)(2,1)} %bitcast.14), calls=%async_computation.7 | async-start | bytes 786432 | tf_op jit(solution)/shard_map/all_to_all | solution.py:113
  153.9 13.7 %collective-permute-start = (bf16[1,40,6144]{2,1,0:T(8,128)(2,1)S(1)}, bf16[1,40,6144]{2,1,0:T(8,128)(2,1)S(1)}, u32[]{:S(2)}, u32[]{:S(2)}) collective-permute-start(bf16[1,40,6144]{2,1,0:T(8,128)(2,1)S(1)} %fusion.32), channel_id=1, source_target_pairs={{0,16},{8,24},{16,0},{24,8},{1,17},{9,25},{17,1},{25,9},{2,18},{10... | collective-permute-start | bytes 1474568 | tf_op jit(solution)/shard_map/ppermute | solution.py:76
  165.8 10.7 %collective-permute-start.2 = (bf16[1,32,6144]{2,1,0:T(8,128)(2,1)S(1)}, bf16[1,32,6144]{2,1,0:T(8,128)(2,1)S(1)}, u32[]{:S(2)}, u32[]{:S(2)}) collective-permute-start(bf16[1,32,6144]{2,1,0:T(8,128)(2,1)S(1)} %convert_element_type.95), channel_id=1, source_target_pairs={{0,16},{8,24},{16,0},{24,8},{1,17},{9,25},{17,1},{25,9},{2,18},{10... | collective-permute-start | bytes 1179656 | tf_op jit(solution)/shard_map/ppermute | solution.py:76
  168.7 8.5 %collective-permute-start.1 = (bf16[2,40,6144]{2,1,0:T(8,128)(2,1)}, bf16[2,40,6144]{2,1,0:T(8,128)(2,1)S(1)}, u32[]{:S(2)}, u32[]{:S(2)}) collective-permute-start(bf16[2,40,6144]{2,1,0:T(8,128)(2,1)} %pad_maximum_fusion.2), channel_id=1, source_target_pairs={{0,8},{8,0},{16,24},{24,16},{1,9},{9,1},{17,25},{25,17},{2,10},{10... | collective-permute-start | bytes 2949128 | tf_op jit(solution)/shard_map/ppermute | solution.py:76
  176.6 2.5 %collective-permute-start.3 = (bf16[2,32,6144]{2,1,0:T(8,128)(2,1)S(1)}, bf16[2,32,6144]{2,1,0:T(8,128)(2,1)S(1)}, u32[]{:S(2)}, u32[]{:S(2)}) collective-permute-start(bf16[2,32,6144]{2,1,0:T(8,128)(2,1)S(1)} %pad_maximum_fusion.3), channel_id=1, source_target_pairs={{0,8},{8,0},{16,24},{24,16},{1,9},{9,1},{17,25},{25,17},{2,10},{10... | collective-permute-start | bytes 2359304 | tf_op jit(solution)/shard_map/ppermute | solution.py:76

commit v12 on v10

--- a/solution.py
+++ b/solution.py
@@ -97,7 +97,6 @@
         columns = (coef_a * columns.astype(jnp.float32) + applied).astype(jnp.bfloat16)
     factor = 0.2 * math.sqrt(max(M, N))
     per = columns.shape[0] // size
-    half = min(per, 8 * ((per * 9 + 64) // 128))
     blocks = columns.reshape(size, per, columns.shape[1])
     slots = lax.axis_size("dp")
     ids = jnp.arange(slots, dtype=jnp.int32)
@@ -105,7 +104,14 @@
         jnp.where(owner[None, :] == ids[:, None], ids[None, :], 0), axis=1
     )
     where_from = inverse ^ lax.axis_index("dp")
-    bounds = ((0, half), (half, per)) if half < per else ((0, per),)
+    bounds = []
+    lo = 0
+    for share in (4, 3):
+        hi = min(per, lo + 8 * ((per * share + 36) // 72))
+        if lo < hi < per:
+            bounds.append((lo, hi))
+            lo = hi
+    bounds.append((lo, per))
     parts = [
         blocks[:, lo:hi, :].reshape(size * (hi - lo), columns.shape[1]) for lo, hi in bounds
     ]

time: 178 us -> 179 us (level)
  starting transfers between devices: 32.9 us -> 38.4 us
  waiting for transfers between devices: 68.4 us -> 64.2 us
    all_to_all x2 -> x3, waiting for transfers between devices: 22.5 us -> 14.9 us  [per_device(): lax.all_to_all(parts[n], 'tensor', split_axis=0, concat_axis=1, tiled=True)]
    all_to_all x2 -> x3, starting transfers between devices: 7.1 us -> 11.4 us  [per_device(): lax.all_to_all(parts[n], 'tensor', split_axis=0, concat_axis=1, tiled=True)]
    ppermute x4 -> x6, waiting for transfers between devices: 1.52 us -> 5.02 us  [gather_slots(): got = lax.ppermute(sent, axis, [(i, i ^ bit) for i in range(size)])]
    ppermute x4 -> x6, starting transfers between devices: 3.67 us -> 4.79 us  [gather_slots(): got = lax.ppermute(sent, axis, [(i, i ^ bit) for i in range(size)])]
  transfers between devices with their start and end apart: 21 -> 24, of which waited for: 16 -> 17; matrix products, arithmetic and copies ran while one was open for 2% -> 2% of each run, Pallas kernels for 0% -> 0%
where the time goes in v12:
time: 179 us; the launch traced here: 178 us
  waiting for transfers between devices  64.2 us (36%)
  blocking collectives  45.6 us (25%)
  starting transfers between devices  38.4 us (21%)
  between operations  9.53 us (5%)
  other arithmetic  8.32 us (5%)
  local copies, waits for them, and re-layouts  7.02 us (4%)
  matrix products  5.16 us (3%)
    all_to_all x2, blocking collectives, gram_allreduce(): lax.all_to_all(spread, axis, split_axis=0, concat_axis=0, tiled=True)  32 us
    ppermute x14, waiting for transfers between devices, gram_allreduce(): acc = acc + lax.ppermute(outgoing, axis, _shift_pairs(size, s))  23.3 us
    all_to_all x1, waiting for transfers between devices, per_device(): lax.all_to_all(rows_here, 'tensor', split_axis=1, concat_axis=0, tiled=True)  21 us
    ppermute x14, starting transfers between devices, gram_allreduce(): acc = acc + lax.ppermute(outgoing, axis, _shift_pairs(size, s))  18.6 us
    all_to_all x3, waiting for transfers between devices, per_device(): lax.all_to_all(parts[n], 'tensor', split_axis=0, concat_axis=1, tiled=True)  14.9 us
    all_to_all x1, blocking collectives, total_over(): got = lax.all_to_all(spread, axis, split_axis=0, concat_axis=0, tiled=True)  13.6 us
    all_to_all x3, starting transfers between devices, per_device(): lax.all_to_all(parts[n], 'tensor', split_axis=0, concat_axis=1, tiled=True)  11.4 us
    ppermute x6, waiting for transfers between devices, gather_slots(): got = lax.ppermute(sent, axis, [(i, i ^ bit) for i in range(size)])  5.02 us
  transfers between devices with their start and end apart: 24, of which 17 were waited for; matrix products, arithmetic and copies ran while one was open for 2% of the time, Pallas kernels for 0%

profile of v12, /device:TPU:0, one launch (start us, length us, event | category | flops | bytes accessed | tf_op | source)
XLA Modules:
  0.0 178.2 jit_solution(16257768791877675165)
XLA Ops:
  0.6 2.9 %multiply_reduce_fusion = (f32[]{:T(128)}, f32[1,72,6144]{2,1,0:T(8,128)S(1)}) fusion(bf16[1,72,6144]{2,1,0:T(8,128)(2,1)} %param.3, f32[1,72,6144]{2,1,0:T(8,128)} %param.4), kind=kLoop, calls=%fused_computation.6 | loop fusion | flops 3096575 | bytes 4423684 | tf_op jit(solution)/shard_map/reduce_sum | solution.py:88
  3.5 0.6 broadcast_in_dim.58
  4.2 13.6 %all_to_all.80 = f32[8,1,1]{2,1,0:T(1,128)S(1)} all-to-all(f32[8,1,1]{2,1,0:T(1,128)S(1)} %broadcast_in_dim.58), channel_id=1, replica_groups=mesh['dp'=4,'tensor'=8] {'tensor'}, dimensions={0} | all-to-all | bytes 64 | tf_op jit(solution)/shard_map/all_to_all | solution.py:26
  17.8 0.6 reduce_sum.46
  19.1 0.3 divide_convert_fusion
  19.5 1.1 copy.45
  20.6 3.6 %all-to-all-start.1 = ((bf16[72,8,768]{2,0,1:T(8,128)(2,1)}), bf16[72,8,768]{2,0,1:T(8,128)(2,1)S(1)}, u32[]{:S(2)}, u32[]{:S(2)}) async-start(bf16[72,8,768]{2,0,1:T(8,128)(2,1)} %copy.45), calls=%async_computation.1 | async-start | bytes 1769472 | tf_op jit(solution)/shard_map/all_to_all | solution.py:90
  24.4 21.0 %all-to-all-done.1 = bf16[72,8,768]{2,0,1:T(8,128)(2,1)S(1)} async-done(((bf16[72,8,768]{2,0,1:T(8,128)(2,1)}), bf16[72,8,768]{2,0,1:T(8,128)(2,1)S(1)}, u32[]{:S(2)}, u32[]{:S(2)}) %all-to-all-start.1) | async-done | bytes 884768 | tf_op jit(solution)/shard_map/all_to_all | solution.py:90
  45.4 0.9 fusion.67
  46.3 0.2 slice_select_fusion.1
  46.9 1.3 collective-permute-start
  48.2 3.5 %collective-permute-start.6 = (f32[37,576]{1,0:T(8,128)S(1)}, f32[37,576]{1,0:T(8,128)S(1)}, u32[]{:S(2)}, u32[]{:S(2)}) collective-permute-start(f32[37,576]{1,0:T(8,128)S(1)} %get-tuple-element.34), channel_id=1, source_target_pairs={{0,7},{1,0},{2,1},{3,2},{4,3},{5,4},{6,5},{7,6},{8,15},{9,8},{10,9... | collective-permute-start | bytes 255752 | tf_op jit(solution)/shard_map/ppermute | solution.py:52
  51.7 2.9 %collective-permute-start.3 = (f32[37,576]{1,0:T(8,128)S(1)}, f32[37,576]{1,0:T(8,128)S(1)}, u32[]{:S(2)}, u32[]{:S(2)}) collective-permute-start(f32[37,576]{1,0:T(8,128)S(1)} %get-tuple-element.37), channel_id=1, source_target_pairs={{0,4},{1,5},{2,6},{3,7},{4,0},{5,1},{6,2},{7,3},{8,12},{9,13},{10,... | collective-permute-start | bytes 255752 | tf_op jit(solution)/shard_map/ppermute | solution.py:52
  54.9 1.8 %collective-permute-start.1 = (f32[37,576]{1,0:T(8,128)S(1)}, f32[37,576]{1,0:T(8,128)S(1)}, u32[]{:S(2)}, u32[]{:S(2)}) collective-permute-start(f32[37,576]{1,0:T(8,128)S(1)} %get-tuple-element.39), channel_id=1, source_target_pairs={{0,2},{1,3},{2,4},{3,5},{4,6},{5,7},{6,0},{7,1},{8,10},{9,11},{10,... | collective-permute-start | bytes 255752 | tf_op jit(solution)/shard_map/ppermute | solution.py:52
  56.7 0.3 collective-permute-done.5
  56.9 2.2 %collective-permute-done.4 = f32[37,576]{1,0:T(8,128)S(1)} collective-permute-done((f32[37,576]{1,0:T(8,128)S(1)}, f32[37,576]{1,0:T(8,128)S(1)}, u32[]{:S(2)}, u32[]{:S(2)}) %collective-permute-start.4) | collective-permute-done | bytes 85280 | tf_op jit(solution)/shard_map/ppermute | solution.py:52
  59.1 7.9 %collective-permute-done.3 = f32[37,576]{1,0:T(8,128)S(1)} collective-permute-done((f32[37,576]{1,0:T(8,128)S(1)}, f32[37,576]{1,0:T(8,128)S(1)}, u32[]{:S(2)}, u32[]{:S(2)}) %collective-permute-start.3) | collective-permute-done | bytes 85280 | tf_op jit(solution)/shard_map/ppermute | solution.py:52
  67.0 0.7 collective-permute-done.2
  67.8 16.0 %all_to_all.81 = bf16[8,37,576]{2,1,0:T(8,128)(2,1)S(1)} all-to-all(bf16[8,37,576]{2,1,0:T(8,128)(2,1)S(1)} %broadcast_in_dim.61), channel_id=1, replica_groups=mesh['dp'=4,'tensor'=8] {'tensor'}, dimensions={0} | all-to-all | bytes 681984 | tf_op jit(solution)/shard_map/all_to_all | solution.py:55
  84.6 1.7 add_convert_fusion.1
  86.3 0.9 fusion.68
  87.2 0.2 slice_select_fusion
  87.8 1.2 collective-permute-start.7
  89.1 3.6 %collective-permute-start.13 = (f32[37,576]{1,0:T(8,128)S(1)}, f32[37,576]{1,0:T(8,128)S(1)}, u32[]{:S(2)}, u32[]{:S(2)}) collective-permute-start(f32[37,576]{1,0:T(8,128)S(1)} %get-tuple-element.27), channel_id=1, source_target_pairs={{0,7},{1,0},{2,1},{3,2},{4,3},{5,4},{6,5},{7,6},{8,15},{9,8},{10,9... | collective-permute-start | bytes 255752 | tf_op jit(solution)/shard_map/ppermute | solution.py:52
  92.6 2.9 %collective-permute-start.10 = (f32[37,576]{1,0:T(8,128)S(1)}, f32[37,576]{1,0:T(8,128)S(1)}, u32[]{:S(2)}, u32[]{:S(2)}) collective-permute-start(f32[37,576]{1,0:T(8,128)S(1)} %get-tuple-element.30), channel_id=1, source_target_pairs={{0,4},{1,5},{2,6},{3,7},{4,0},{5,1},{6,2},{7,3},{8,12},{9,13},{10,... | collective-permute-start | bytes 255752 | tf_op jit(solution)/shard_map/ppermute | solution.py:52
  95.6 0.7 collective-permute-done.7
  96.3 1.4 collective-permute-start.8
  97.7 0.4 collective-permute-done.12
  98.1 2.2 %collective-permute-done.11 = f32[37,576]{1,0:T(8,128)S(1)} collective-permute-done((f32[37,576]{1,0:T(8,128)S(1)}, f32[37,576]{1,0:T(8,128)S(1)}, u32[]{:S(2)}, u32[]{:S(2)}) %collective-permute-start.11) | collective-permute-done | bytes 85280 | tf_op jit(solution)/shard_map/ppermute | solution.py:52
  100.3 8.6 %collective-permute-done.10 = f32[37,576]{1,0:T(8,128)S(1)} collective-permute-done((f32[37,576]{1,0:T(8,128)S(1)}, f32[37,576]{1,0:T(8,128)S(1)}, u32[]{:S(2)}, u32[]{:S(2)}) %collective-permute-start.10) | collective-permute-done | bytes 85280 | tf_op jit(solution)/shard_map/ppermute | solution.py:52
  109.2 15.9 %all_to_all.82 = bf16[8,37,576]{2,1,0:T(8,128)(2,1)S(1)} all-to-all(bf16[8,37,576]{2,1,0:T(8,128)(2,1)S(1)} %broadcast_in_dim.65), channel_id=1, replica_groups=mesh['dp'=4,'tensor'=8] {'tensor'}, dimensions={0} | all-to-all | bytes 681984 | tf_op jit(solution)/shard_map/all_to_all | solution.py:55
  125.9 1.7 add_convert_fusion
  127.6 0.8 slice.121
  128.3 3.5 %all-to-all-start.4 = ((bf16[8,32,768]{2,1,0:T(8,128)(2,1)}), bf16[8,32,768]{2,1,0:T(8,128)(2,1)S(1)}, u32[]{:S(2)}, u32[]{:S(2)}) async-start(bf16[8,32,768]{2,1,0:T(8,128)(2,1)} %slice.121), calls=%async_computation.4 | async-start | bytes 786432 | tf_op jit(solution)/shard_map/all_to_all | solution.py:120
  131.9 0.7 fusion.66
  140.3 0.7 slice.124
  141.0 0.7 slice.120
  141.7 1.5 all-to-all-done.4
  143.2 4.5 %all-to-all-start.5 = ((bf16[8,24,768]{2,1,0:T(8,128)(2,1)}), bf16[8,24,768]{2,1,0:T(8,128)(2,1)S(1)}, u32[]{:S(2)}, u32[]{:S(2)}) async-start(bf16[8,24,768]{2,1,0:T(8,128)(2,1)} %bitcast.29), calls=%async_computation.5 | async-start | bytes 589824 | tf_op jit(solution)/shard_map/all_to_all | solution.py:120
  147.8 1.5 collective-permute-start.14
  149.3 7.2 %all-to-all-done.5 = bf16[8,24,768]{2,1,0:T(8,128)(2,1)S(1)} async-done(((bf16[8,24,768]{2,1,0:T(8,128)(2,1)}), bf16[8,24,768]{2,1,0:T(8,128)(2,1)S(1)}, u32[]{:S(2)}, u32[]{:S(2)}) %all-to-all-start.5) | async-done | bytes 294944 | tf_op jit(solution)/shard_map/all_to_all | solution.py:120
  156.6 3.5 %all-to-all-start.6 = ((bf16[8,16,768]{2,1,0:T(8,128)(2,1)}), bf16[8,16,768]{2,1,0:T(8,128)(2,1)S(1)}, u32[]{:S(2)}, u32[]{:S(2)}) async-start(bf16[8,16,768]{2,1,0:T(8,128)(2,1)} %bitcast.32), calls=%async_computation.6 | async-start | bytes 393216 | tf_op jit(solution)/shard_map/all_to_all | solution.py:120
  160.2 1.5 collective-permute-start.16
  161.8 6.1 %all-to-all-done.6 = bf16[8,16,768]{2,1,0:T(8,128)(2,1)S(1)} async-done(((bf16[8,16,768]{2,1,0:T(8,128)(2,1)}), bf16[8,16,768]{2,1,0:T(8,128)(2,1)S(1)}, u32[]{:S(2)}, u32[]{:S(2)}) %all-to-all-start.6) | async-done | bytes 196640 | tf_op jit(solution)/shard_map/all_to_all | solution.py:120
  168.2 1.5 collective-permute-start.18
  169.9 4.0 %collective-permute-done.18 = bf16[1,16,6144]{2,1,0:T(8,128)(2,1)S(1)} collective-permute-done((bf16[1,16,6144]{2,1,0:T(8,128)(2,1)S(1)}, bf16[1,16,6144]{2,1,0:T(8,128)(2,1)S(1)}, u32[]{:S(2)}, u32[]{:S(2)}) %collective-permute-start.18) | collective-permute-done | bytes 196640 | tf_op jit(solution)/shard_map/ppermute | solution.py:77
  174.8 1.0 collective-permute-done.19
  175.9 2.3 %maximum_maximum_fusion = bf16[4,72,6144]{2,1,0:T(8,128)(2,1)} fusion(bf16[1,16,6144]{2,1,0:T(8,128)(2,1)S(1)} %get-tuple-element.41, bf16[1,24,6144]{2,1,0:T(8,128)(2,1)S(1)} %get-tuple-element.23, bf16[1,32,6144]{2,1,0:T(8,128)(2,1)S(1)} %get-tuple-element.13, bf16[1,16,6144]{2,1,0:T(8,128)(2,1)S(1)} %get-tuple-element.42, ...), kind=kLoop, calls=%fused_computation | loop fusion | flops 42467328 | bytes 7077888 | tf_op jit(solution)/shard_map/concatenate | solution.py:133
  (75 shorter events, 4.8 us)
Async XLA Ops:
  0.6 18.5 %copy-start.1 = (bf16[1,72,6144]{2,1,0:T(8,128)(2,1)S(1)}, bf16[1,72,6144]{2,1,0:T(8,128)(2,1)}, u32[]{:S(2)}) copy-start(bf16[1,72,6144]{2,1,0:T(8,128)(2,1)} %param.3) | copy-start | bytes 2654212
  3.5 15.8 %copy-start = (f32[1,72,6144]{2,1,0:T(8,128)}, f32[1,72,6144]{2,1,0:T(8,128)S(1)}, u32[]{:S(2)}) copy-start(f32[1,72,6144]{2,1,0:T(8,128)S(1)} %get-tuple-element.11) | copy-start | bytes 5308420
  20.6 24.8 %all-to-all-start.1 = ((bf16[72,8,768]{2,0,1:T(8,128)(2,1)}), bf16[72,8,768]{2,0,1:T(8,128)(2,1)S(1)}, u32[]{:S(2)}, u32[]{:S(2)}) async-start(bf16[72,8,768]{2,0,1:T(8,128)(2,1)} %copy.45), calls=%async_computation.1 | async-start | bytes 1769472 | tf_op jit(solution)/shard_map/all_to_all | solution.py:90
  46.9 7.9 %collective-permute-start = (f32[37,576]{1,0:T(8,128)S(1)}, f32[37,576]{1,0:T(8,128)S(1)}, u32[]{:S(2)}, u32[]{:S(2)}) collective-permute-start(f32[37,576]{1,0:T(8,128)S(1)} %get-tuple-element.33), channel_id=1, source_target_pairs={{0,1},{1,2},{2,3},{3,4},{4,5},{5,6},{6,7},{7,0},{8,9},{9,10},{10,1... | collective-permute-start | bytes 255752 | tf_op jit(solution)/shard_map/ppermute | solution.py:52
  48.2 6.7 %collective-permute-start.6 = (f32[37,576]{1,0:T(8,128)S(1)}, f32[37,576]{1,0:T(8,128)S(1)}, u32[]{:S(2)}, u32[]{:S(2)}) collective-permute-start(f32[37,576]{1,0:T(8,128)S(1)} %get-tuple-element.34), channel_id=1, source_target_pairs={{0,7},{1,0},{2,1},{3,2},{4,3},{5,4},{6,5},{7,6},{8,15},{9,8},{10,9... | collective-permute-start | bytes 255752 | tf_op jit(solution)/shard_map/ppermute | solution.py:52
  51.7 5.2 %collective-permute-start.5 = (f32[37,576]{1,0:T(8,128)S(1)}, f32[37,576]{1,0:T(8,128)S(1)}, u32[]{:S(2)}, u32[]{:S(2)}) collective-permute-start(f32[37,576]{1,0:T(8,128)S(1)} %get-tuple-element.35), channel_id=1, source_target_pairs={{0,6},{1,7},{2,0},{3,1},{4,2},{5,3},{6,4},{7,5},{8,14},{9,15},{10,... | collective-permute-start | bytes 255752 | tf_op jit(solution)/shard_map/ppermute | solution.py:52
  51.7 7.4 %collective-permute-start.4 = (f32[37,576]{1,0:T(8,128)S(1)}, f32[37,576]{1,0:T(8,128)S(1)}, u32[]{:S(2)}, u32[]{:S(2)}) collective-permute-start(f32[37,576]{1,0:T(8,128)S(1)} %get-tuple-element.36), channel_id=1, source_target_pairs={{0,5},{1,6},{2,7},{3,0},{4,1},{5,2},{6,3},{7,4},{8,13},{9,14},{10,... | collective-permute-start | bytes 255752 | tf_op jit(solution)/shard_map/ppermute | solution.py:52
  51.7 15.3 %collective-permute-start.3 = (f32[37,576]{1,0:T(8,128)S(1)}, f32[37,576]{1,0:T(8,128)S(1)}, u32[]{:S(2)}, u32[]{:S(2)}) collective-permute-start(f32[37,576]{1,0:T(8,128)S(1)} %get-tuple-element.37), channel_id=1, source_target_pairs={{0,4},{1,5},{2,6},{3,7},{4,0},{5,1},{6,2},{7,3},{8,12},{9,13},{10,... | collective-permute-start | bytes 255752 | tf_op jit(solution)/shard_map/ppermute | solution.py:52
  54.8 12.8 %collective-permute-start.2 = (f32[37,576]{1,0:T(8,128)S(1)}, f32[37,576]{1,0:T(8,128)S(1)}, u32[]{:S(2)}, u32[]{:S(2)}) collective-permute-start(f32[37,576]{1,0:T(8,128)S(1)} %get-tuple-element.38), channel_id=1, source_target_pairs={{0,3},{1,4},{2,5},{3,6},{4,7},{5,0},{6,1},{7,2},{8,11},{9,12},{10,... | collective-permute-start | bytes 255752 | tf_op jit(solution)/shard_map/ppermute | solution.py:52
  54.9 12.8 %collective-permute-start.1 = (f32[37,576]{1,0:T(8,128)S(1)}, f32[37,576]{1,0:T(8,128)S(1)}, u32[]{:S(2)}, u32[]{:S(2)}) collective-permute-start(f32[37,576]{1,0:T(8,128)S(1)} %get-tuple-element.39), channel_id=1, source_target_pairs={{0,2},{1,3},{2,4},{3,5},{4,6},{5,7},{6,0},{7,1},{8,10},{9,11},{10,... | collective-permute-start | bytes 255752 | tf_op jit(solution)/shard_map/ppermute | solution.py:52
  87.8 8.4 %collective-permute-start.7 = (f32[37,576]{1,0:T(8,128)S(1)}, f32[37,576]{1,0:T(8,128)S(1)}, u32[]{:S(2)}, u32[]{:S(2)}) collective-permute-start(f32[37,576]{1,0:T(8,128)S(1)} %get-tuple-element.26), channel_id=1, source_target_pairs={{0,1},{1,2},{2,3},{3,4},{4,5},{5,6},{6,7},{7,0},{8,9},{9,10},{10,1... | collective-permute-start | bytes 255752 | tf_op jit(solution)/shard_map/ppermute | solution.py:52
  89.1 7.2 %collective-permute-start.13 = (f32[37,576]{1,0:T(8,128)S(1)}, f32[37,576]{1,0:T(8,128)S(1)}, u32[]{:S(2)}, u32[]{:S(2)}) collective-permute-start(f32[37,576]{1,0:T(8,128)S(1)} %get-tuple-element.27), channel_id=1, source_target_pairs={{0,7},{1,0},{2,1},{3,2},{4,3},{5,4},{6,5},{7,6},{8,15},{9,8},{10,9... | collective-permute-start | bytes 255752 | tf_op jit(solution)/shard_map/ppermute | solution.py:52
  92.6 5.5 %collective-permute-start.12 = (f32[37,576]{1,0:T(8,128)S(1)}, f32[37,576]{1,0:T(8,128)S(1)}, u32[]{:S(2)}, u32[]{:S(2)}) collective-permute-start(f32[37,576]{1,0:T(8,128)S(1)} %get-tuple-element.28), channel_id=1, source_target_pairs={{0,6},{1,7},{2,0},{3,1},{4,2},{5,3},{6,4},{7,5},{8,14},{9,15},{10,... | collective-permute-start | bytes 255752 | tf_op jit(solution)/shard_map/ppermute | solution.py:52
  92.6 7.7 %collective-permute-start.11 = (f32[37,576]{1,0:T(8,128)S(1)}, f32[37,576]{1,0:T(8,128)S(1)}, u32[]{:S(2)}, u32[]{:S(2)}) collective-permute-start(f32[37,576]{1,0:T(8,128)S(1)} %get-tuple-element.29), channel_id=1, source_target_pairs={{0,5},{1,6},{2,7},{3,0},{4,1},{5,2},{6,3},{7,4},{8,13},{9,14},{10,... | collective-permute-start | bytes 255752 | tf_op jit(solution)/shard_map/ppermute | solution.py:52
  92.6 16.3 %collective-permute-start.10 = (f32[37,576]{1,0:T(8,128)S(1)}, f32[37,576]{1,0:T(8,128)S(1)}, u32[]{:S(2)}, u32[]{:S(2)}) collective-permute-start(f32[37,576]{1,0:T(8,128)S(1)} %get-tuple-element.30), channel_id=1, source_target_pairs={{0,4},{1,5},{2,6},{3,7},{4,0},{5,1},{6,2},{7,3},{8,12},{9,13},{10,... | collective-permute-start | bytes 255752 | tf_op jit(solution)/shard_map/ppermute | solution.py:52
  96.3 12.8 %collective-permute-start.9 = (f32[37,576]{1,0:T(8,128)S(1)}, f32[37,576]{1,0:T(8,128)S(1)}, u32[]{:S(2)}, u32[]{:S(2)}) collective-permute-start(f32[37,576]{1,0:T(8,128)S(1)} %get-tuple-element.31), channel_id=1, source_target_pairs={{0,3},{1,4},{2,5},{3,6},{4,7},{5,0},{6,1},{7,2},{8,11},{9,12},{10,... | collective-permute-start | bytes 255752 | tf_op jit(solution)/shard_map/ppermute | solution.py:52
  96.3 12.8 %collective-permute-start.8 = (f32[37,576]{1,0:T(8,128)S(1)}, f32[37,576]{1,0:T(8,128)S(1)}, u32[]{:S(2)}, u32[]{:S(2)}) collective-permute-start(f32[37,576]{1,0:T(8,128)S(1)} %get-tuple-element.32), channel_id=1, source_target_pairs={{0,2},{1,3},{2,4},{3,5},{4,6},{5,7},{6,0},{7,1},{8,10},{9,11},{10,... | collective-permute-start | bytes 255752 | tf_op jit(solution)/shard_map/ppermute | solution.py:52
  127.6 4.3 %copy-start.2 = (s32[4]{0:T(128)S(1)}, s32[4]{0:T(128)}, u32[]{:S(2)}) copy-start(s32[4]{0:T(128)} %param.5) | copy-start | bytes 52
  128.3 14.9 %all-to-all-start.4 = ((bf16[8,32,768]{2,1,0:T(8,128)(2,1)}), bf16[8,32,768]{2,1,0:T(8,128)(2,1)S(1)}, u32[]{:S(2)}, u32[]{:S(2)}) async-start(bf16[8,32,768]{2,1,0:T(8,128)(2,1)} %slice.121), calls=%async_computation.4 | async-start | bytes 786432 | tf_op jit(solution)/shard_map/all_to_all | solution.py:120
  143.2 13.3 %all-to-all-start.5 = ((bf16[8,24,768]{2,1,0:T(8,128)(2,1)}), bf16[8,24,768]{2,1,0:T(8,128)(2,1)S(1)}, u32[]{:S(2)}, u32[]{:S(2)}) async-start(bf16[8,24,768]{2,1,0:T(8,128)(2,1)} %bitcast.29), calls=%async_computation.5 | async-start | bytes 589824 | tf_op jit(solution)/shard_map/all_to_all | solution.py:120
  147.8 13.9 %collective-permute-start.14 = (bf16[1,32,6144]{2,1,0:T(8,128)(2,1)S(1)}, bf16[1,32,6144]{2,1,0:T(8,128)(2,1)S(1)}, u32[]{:S(2)}, u32[]{:S(2)}) collective-permute-start(bf16[1,32,6144]{2,1,0:T(8,128)(2,1)S(1)} %fusion.38), channel_id=1, source_target_pairs={{0,16},{8,24},{16,0},{24,8},{1,17},{9,25},{17,1},{25,9},{2,18},{10... | collective-permute-start | bytes 1179656 | tf_op jit(solution)/shard_map/ppermute | solution.py:77
  156.6 11.3 %all-to-all-start.6 = ((bf16[8,16,768]{2,1,0:T(8,128)(2,1)}), bf16[8,16,768]{2,1,0:T(8,128)(2,1)S(1)}, u32[]{:S(2)}, u32[]{:S(2)}) async-start(bf16[8,16,768]{2,1,0:T(8,128)(2,1)} %bitcast.32), calls=%async_computation.6 | async-start | bytes 393216 | tf_op jit(solution)/shard_map/all_to_all | solution.py:120
  160.2 9.5 %collective-permute-start.16 = (bf16[1,24,6144]{2,1,0:T(8,128)(2,1)S(1)}, bf16[1,24,6144]{2,1,0:T(8,128)(2,1)S(1)}, u32[]{:S(2)}, u32[]{:S(2)}) collective-permute-start(bf16[1,24,6144]{2,1,0:T(8,128)(2,1)S(1)} %fusion.39), channel_id=1, source_target_pairs={{0,16},{8,24},{16,0},{24,8},{1,17},{9,25},{17,1},{25,9},{2,18},{10... | collective-permute-start | bytes 884744 | tf_op jit(solution)/shard_map/ppermute | solution.py:77
  161.7 12.3 %collective-permute-start.15 = (bf16[2,32,6144]{2,1,0:T(8,128)(2,1)S(1)}, bf16[2,32,6144]{2,1,0:T(8,128)(2,1)S(1)}, u32[]{:S(2)}, u32[]{:S(2)}) collective-permute-start(bf16[2,32,6144]{2,1,0:T(8,128)(2,1)S(1)} %pad_maximum_fusion.2), channel_id=1, source_target_pairs={{0,8},{8,0},{16,24},{24,16},{1,9},{9,1},{17,25},{25,17},{2,10},{10... | collective-permute-start | bytes 2359304 | tf_op jit(solution)/shard_map/ppermute | solution.py:77
  168.2 5.7 %collective-permute-start.18 = (bf16[1,16,6144]{2,1,0:T(8,128)(2,1)S(1)}, bf16[1,16,6144]{2,1,0:T(8,128)(2,1)S(1)}, u32[]{:S(2)}, u32[]{:S(2)}) collective-permute-start(bf16[1,16,6144]{2,1,0:T(8,128)(2,1)S(1)} %convert_element_type.101), channel_id=1, source_target_pairs={{0,16},{8,24},{16,0},{24,8},{1,17},{9,25},{17,1},{25,9},{2,18},{10... | collective-permute-start | bytes 589832 | tf_op jit(solution)/shard_map/ppermute | solution.py:77
  169.8 4.7 %collective-permute-start.17 = (bf16[2,24,6144]{2,1,0:T(8,128)(2,1)S(1)}, bf16[2,24,6144]{2,1,0:T(8,128)(2,1)S(1)}, u32[]{:S(2)}, u32[]{:S(2)}) collective-permute-start(bf16[2,24,6144]{2,1,0:T(8,128)(2,1)S(1)} %pad_maximum_fusion.4), channel_id=1, source_target_pairs={{0,8},{8,0},{16,24},{24,16},{1,9},{9,1},{17,25},{25,17},{2,10},{10... | collective-permute-start | bytes 1769480 | tf_op jit(solution)/shard_map/ppermute | solution.py:77
  173.9 1.8 %collective-permute-start.19 = (bf16[2,16,6144]{2,1,0:T(8,128)(2,1)S(1)}, bf16[2,16,6144]{2,1,0:T(8,128)(2,1)S(1)}, u32[]{:S(2)}, u32[]{:S(2)}) collective-permute-start(bf16[2,16,6144]{2,1,0:T(8,128)(2,1)S(1)} %pad_maximum_fusion.5), channel_id=1, source_target_pairs={{0,8},{8,0},{16,24},{24,16},{1,9},{9,1},{17,25},{25,17},{2,10},{10... | collective-permute-start | bytes 1179656 | tf_op jit(solution)/shard_map/ppermute | solution.py:77
